TPU v7x, 512 devices: a whole 4x8x8 slice. The times are simulated.
512 devices in a mesh: tgt: 32 (over z_hi, x, core), src: 16 (over z_lo, y).
Axes of the slice: x: 4, y: 8, z: 8 (z_hi: 4, z_lo: 2; z = z_hi * 2 + z_lo), core: 2. Of those that a mesh axis runs over, the one named last changes fastest.
Arguments:
- states_late: bfloat16 [32768, 128], P('src'), may hold values from -12 to 12
- offset_late: bfloat16 [32768], P('src'), may hold values from 0 to 2
- values_late: bfloat16 [32768, 64], P('src'), may hold values from -6 to 6
- states_mid: bfloat16 [32768, 128], P('tgt'), may hold values from -12 to 12
- offset_mid: bfloat16 [32768], P('src'), may hold values from 0 to 2
- exercise_mid: bfloat16 [32768, 64], P('tgt'), may hold values from -6 to 6
- mask_mid: int32 [64, 64], replicated, may hold values from 0 to 1, as said below
- states_early: bfloat16 [32768, 128], P('tgt'), may hold values from -12 to 12
- exercise_early: bfloat16 [32768, 64], P('tgt'), may hold values from -6 to 6
- mask_early: int32 [64, 64], replicated, may hold values from 0 to 1, as said below
Outputs:
- value_mid: bfloat16 [32768, 64], P('tgt')
- value_early: bfloat16 [32768, 64], P('tgt')
Inputs may be any that keep to these rules, and one draw needn't show every extreme that they name: `mask_mid`: 1 marks a live tile of 512 x 512 paths; every diagonal tile is live. `mask_early`: 1 marks a live tile of 512 x 512 paths; every diagonal tile is live.
All inputs are finite; a program needn't handle non-finite values.
Results may differ from a plain program's by a relative error of at most 0.0055.
Values may be sent and summed in bfloat16 or wider, within the bound.
No kernel may reach another device: no remote copies, remote signals or barrier semaphores. Data moves between devices by JAX's collectives and lax.ppermute only.
A program may use at most 64 MiB of HBM per device.

v0:
```python
import jax
import jax.numpy as jnp
from jax import lax
from jax.sharding import PartitionSpec as P

BLOCK = 512


sharpness = 3.5
very_low = -1e30


def date_partials(targets, sources, offsets, values, tile_mask):
    row_count = targets.shape[0]
    col_count = sources.shape[0]
    factors = targets.shape[1]
    value_width = values.shape[1]
    row_tiles = row_count // BLOCK
    col_tiles = col_count // BLOCK
    score_scale = sharpness / factors**0.5
    local_mask = lax.dynamic_slice(
        tile_mask,
        (lax.axis_index("tgt") * row_tiles, lax.axis_index("src") * col_tiles),
        (row_tiles, col_tiles),
    )
    source_tiles = sources.reshape(col_tiles, BLOCK, factors)
    offset_tiles = offsets.astype(jnp.float32).reshape(col_tiles, BLOCK)
    value_tiles = values.reshape(col_tiles, BLOCK, value_width)
    peaks, sums, weighted_all = ([], [], [])
    for row_block in range(row_tiles):
        target_rows = targets[row_block * BLOCK : (row_block + 1) * BLOCK]

        def step(carry, inputs):
            source_tile, offset_tile, value_tile, tile_live = inputs

            def active(carry_in):
                row_peak, weight_sum, weighted = carry_in
                scores = lax.dot_general(
                    target_rows,
                    source_tile,
                    (((1,), (1,)), ((), ())),
                    preferred_element_type=jnp.float32,
                )
                scores = scores * score_scale - offset_tile[None, :]
                new_peak = jnp.maximum(row_peak, jnp.max(scores, axis=1))
                shrink = jnp.exp(row_peak - new_peak)
                weights = jnp.exp(scores - new_peak[:, None])
                new_sum = weight_sum * shrink + jnp.sum(weights, axis=1)
                new_weighted = weighted * shrink[:, None] + jnp.dot(
                    weights.astype(jnp.bfloat16), value_tile, preferred_element_type=jnp.float32
                )
                return (new_peak, new_sum, new_weighted)

            def skipped(carry_in):
                return carry_in

            return (lax.cond(tile_live > 0, active, skipped, carry), None)

        start = (
            jnp.full((BLOCK,), very_low, jnp.float32),
            jnp.zeros((BLOCK,), jnp.float32),
            jnp.zeros((BLOCK, value_width), jnp.float32),
        )
        result, _ = lax.scan(
            step, start, (source_tiles, offset_tiles, value_tiles, local_mask[row_block])
        )
        peaks.append(result[0])
        sums.append(result[1])
        weighted_all.append(result[2])
    return (jnp.concatenate(peaks, 0), jnp.concatenate(sums, 0), jnp.concatenate(weighted_all, 0))


def finish(partials, exercise):
    row_peak, weight_sum, weighted = partials
    peak_all = lax.pmax(row_peak, "src")
    shrink = jnp.exp(row_peak - peak_all)
    weight_sum, weighted = lax.psum((weight_sum * shrink, weighted * shrink[:, None]), "src")
    continuation = weighted / weight_sum[:, None]
    return jnp.maximum(continuation, exercise.astype(jnp.float32)).astype(jnp.bfloat16)


def regroup(block_rows):
    per_owner = lax.axis_size("tgt") // lax.axis_size("src")
    gathered = lax.all_gather(block_rows, "tgt", axis=0, tiled=True)
    row_count = block_rows.shape[0] * per_owner
    return lax.dynamic_slice_in_dim(gathered, lax.axis_index("src") * row_count, row_count, 0)


def per_device(
    states_late,
    offset_late,
    values_late,
    states_mid,
    offset_mid,
    exercise_mid,
    mask_mid,
    states_early,
    exercise_early,
    mask_early,
):
    mid_sources = regroup(states_mid)
    value_mid = finish(
        date_partials(states_mid, states_late, offset_late, values_late, mask_mid), exercise_mid
    )
    mid_values = regroup(value_mid)
    value_early = finish(
        date_partials(states_early, mid_sources, offset_mid, mid_values, mask_early), exercise_early
    )
    return (value_mid, value_early)


def solution(mesh):
    in_specs = (
        P("src", None),
        P("src"),
        P("src", None),
        P("tgt", None),
        P("src"),
        P("tgt", None),
        P(),
        P("tgt", None),
        P("tgt", None),
        P(),
    )
    out_specs = (P("tgt", None), P("tgt", None))
    return jax.shard_map(
        per_device, mesh=mesh, in_specs=in_specs, out_specs=out_specs, check_vma=False
    )
```

profile of v0, /device:TPU:6, one launch (start us, length us, event | category | flops | bytes accessed | tf_op | source)
XLA Modules:
  0.0 559.3 jit_solution(17759028767299258301)
XLA Ops:
  11.0 11.1 %while.57 = (s32[]{:T(128)}, f32[512]{0:T(512)S(1)}, f32[512]{0:T(512)S(1)}, f32[512,64]{0,1:T(8,128)S(1)}, s32[4]{0:T(128)S(1)}, /*index=5*/bf16[4,512,128]{2,1...) while((s32[]{:T(128)}, f32[512]{0:T(512)S(1)}, ...), condition=%wide.region_11.12_spmd, body=%wide.region_6.11_spmd.sunk | while | flops 102564864 | bytes 3840783 | solution.py:64
  12.3 1.8 conditional.9
  17.0 1.8 conditional.9
  17.0 1.2 fusion.45
  20.2 1.8 conditional.9
  22.1 12.0 %while.56 = (s32[]{:T(128)}, f32[512]{0:T(512)S(1)}, f32[512]{0:T(512)S(1)}, f32[512,64]{0,1:T(8,128)S(1)}, s32[4]{0:T(128)S(1)}, /*index=5*/bf16[4,512,128]{2,1...) while((s32[]{:T(128)}, f32[512]{0:T(512)S(1)}, ...), condition=%wide.region_5.6_spmd, body=%wide.region_0.5_spmd.sunk | while | flops 102564864 | bytes 3840783 | solution.py:64
  23.3 1.8 conditional.8
  23.3 1.2 fusion.44
  26.3 1.8 conditional.8
  26.3 1.2 fusion.44
  29.3 1.8 conditional.8
  32.3 1.8 conditional.8
  34.1 34.5 %pmax.14 = f32[1024]{0:T(1024)S(1)} all-reduce(f32[1024]{0:T(1024)S(1)} %constant_dynamic-update-slice_fusion), channel_id=1, replica_groups=mesh['tgt'=32,'src'=16] {'src'}, use_global_device_ids=true, to_apply=%region_12.13 | all-reduce | flops 1024 | bytes 8192 | tf_op jit(solution)/shard_map/pmax | solution.py:75
  69.4 30.6 %psum.29 = f32[1024]{0:T(1024)S(1)} all-reduce(f32[1024]{0:T(1024)S(1)} %get-tuple-element.638), channel_id=1, replica_groups=mesh['tgt'=32,'src'=16] {'src'}, use_global_device_ids=true, to_apply=%region_14.15 | all-reduce | flops 1024 | bytes 8192 | tf_op jit(solution)/shard_map/psum | solution.py:77
  100.0 111.0 %all-reduce.3.cloned.1.call-done = f32[1024,64]{0,1:T(8,128)} async-done(((f32[1024,64]{0,1:T(8,128)}), f32[1024,64]{0,1:T(8,128)}) %all-reduce.3.cloned.1.call-update) | async-done | bytes 262160 | tf_op jit(solution)/shard_map/psum | solution.py:77
  211.0 1.6 maximum_convert_fusion.1
  214.3 63.5 %all-gather.5.cloned.1.call-done = bf16[32768,64]{0,1:T(8,128)(2,1)} async-done(((bf16[1024,64]{0,1:T(8,128)(2,1)}), bf16[32768,64]{0,1:T(8,128)(2,1)}) %all-gather.5.cloned.1.call-update) | async-done | bytes 4194320 | tf_op jit(solution)/shard_map/all_gather | solution.py:84
  279.1 83.8 %all-gather.3.cloned.1.call-done = bf16[32768,128]{1,0:T(8,128)(2,1)} async-done(((bf16[1024,128]{1,0:T(8,128)(2,1)}), bf16[32768,128]{1,0:T(8,128)(2,1)}) %all-gather.3.cloned.1.call-update) | async-done | bytes 8388624 | tf_op jit(solution)/shard_map/all_gather | solution.py:84
  364.0 8.4 %while.59 = (s32[]{:T(128)}, f32[512]{0:T(512)S(1)}, f32[512]{0:T(512)S(1)}, f32[512,64]{0,1:T(8,128)S(1)}, s32[4]{0:T(128)S(1)}, /*index=5*/bf16[4,512,128]{2,1...) while((s32[]{:T(128)}, f32[512]{0:T(512)S(1)}, ...), condition=%wide.region_26.27_spmd, body=%wide.region_21.26_spmd.sunk | while | flops 102564864 | bytes 3840275 | solution.py:64
  372.5 7.8 %while.58 = (s32[]{:T(128)}, f32[512]{0:T(512)S(1)}, f32[512]{0:T(512)S(1)}, f32[512,64]{0,1:T(8,128)S(1)}, s32[4]{0:T(128)S(1)}, /*index=5*/bf16[4,512,128]{2,1...) while((s32[]{:T(128)}, f32[512]{0:T(512)S(1)}, ...), condition=%wide.region_20.21_spmd, body=%wide.region_15.20_spmd.sunk | while | flops 102564864 | bytes 3840275 | solution.py:64
  380.3 32.8 %pmax.15 = f32[1024]{0:T(1024)S(1)} all-reduce(f32[1024]{0:T(1024)S(1)} %constant_dynamic-update-slice_fusion.1), channel_id=1, replica_groups=mesh['tgt'=32,'src'=16] {'src'}, use_global_device_ids=true, to_apply=%region_27.28 | all-reduce | flops 1024 | bytes 8192 | tf_op jit(solution)/shard_map/pmax | solution.py:75
  413.8 31.8 %psum.31 = f32[1024]{0:T(1024)S(1)} all-reduce(f32[1024]{0:T(1024)S(1)} %get-tuple-element.636), channel_id=1, replica_groups=mesh['tgt'=32,'src'=16] {'src'}, use_global_device_ids=true, to_apply=%region_29.30 | all-reduce | flops 1024 | bytes 8192 | tf_op jit(solution)/shard_map/psum | solution.py:77
  445.6 105.5 %all-reduce.5.cloned.1.call-done = f32[1024,64]{0,1:T(8,128)} async-done(((f32[1024,64]{0,1:T(8,128)}), f32[1024,64]{0,1:T(8,128)}) %all-reduce.5.cloned.1.call-update) | async-done | bytes 262160 | tf_op jit(solution)/shard_map/psum | solution.py:77
  551.1 1.6 maximum_convert_fusion
  (170 shorter events, 40.3 us)
Async XLA Ops:
  7.2 203.9 %all-reduce.3.cloned.1.call-start = ((), (), s32[]{:S(2)}) async-start(), calls=%async_computation | async-start | bytes 524288 | tf_op jit(solution)/shard_map/psum | solution.py:77
  22.1 189.0 %copy-start.1 = (bf16[1024,64]{0,1:T(8,128)(2,1)S(1)}, bf16[1024,64]{0,1:T(8,128)(2,1)}, u32[]{:S(2)}) copy-start(bf16[1024,64]{0,1:T(8,128)(2,1)} %param.31) | copy-start | bytes 393220
  22.1 192.2 %copy-start.3 = (bf16[2048]{0:T(1024)(128)(2,1)S(1)}, bf16[2048]{0:T(1024)(128)(2,1)}, u32[]{:S(2)}) copy-start(bf16[2048]{0:T(1024)(128)(2,1)} %param.30) | copy-start | bytes 12292
  22.1 192.2 %copy-start = (bf16[1024,128]{1,0:T(8,128)(2,1)S(1)}, bf16[1024,128]{1,0:T(8,128)(2,1)}, u32[]{:S(2)}) copy-start(bf16[1024,128]{1,0:T(8,128)(2,1)} %param.33) | copy-start | bytes 786436
  69.3 208.5 %all-gather.5.cloned.1.call-start = ((), (), s32[]{:S(2)}) async-start(), calls=%async_computation.2 | async-start | bytes 4325376 | tf_op jit(solution)/shard_map/all_gather | solution.py:84
  212.7 150.2 %all-gather.3.cloned.1.call-start = ((), (), s32[]{:S(2)}) async-start(), calls=%async_computation.1 | async-start | bytes 8650752 | tf_op jit(solution)/shard_map/all_gather | solution.py:84
  213.4 337.7 %all-reduce.5.cloned.1.call-start = ((), (), s32[]{:S(2)}) async-start(), calls=%async_computation.3 | async-start | bytes 524288 | tf_op jit(solution)/shard_map/psum | solution.py:77
  372.5 178.7 %copy-start.2 = (bf16[1024,64]{0,1:T(8,128)(2,1)S(1)}, bf16[1024,64]{0,1:T(8,128)(2,1)}, u32[]{:S(2)}) copy-start(bf16[1024,64]{0,1:T(8,128)(2,1)} %param.34) | copy-start | bytes 393220
Sparse Core Ops, SparseCore 0:
  69.5 141.5 all-reduce.2
  214.8 63.0 all-gather.4
  281.0 81.8 all-gather.2
  414.0 137.1 all-reduce.4
where the time goes:
time: 560 us; the launch traced here: 559 us
  waiting for transfers between devices  365 us (65%)
  blocking collectives  130 us (23%)
  local copies, waits for them, and re-layouts  16.8 us (3%)
  matrix products  15.4 us (3%)
  between operations  14 us (2%)
  loops' own time  10.9 us (2%)
  other arithmetic  7.79 us (1%)
    psum x2, waiting for transfers between devices, finish(): lax.psum((weight_sum * shrink, weighted * shrink[:, None]), 'src')  217 us
    all_gather x2, waiting for transfers between devices, regroup(): gathered = lax.all_gather(block_rows, 'tgt', axis=0, tiled=True)  147 us
    pmax x2, blocking collectives, finish(): peak_all = lax.pmax(row_peak, 'src')  67.2 us
    psum x2, blocking collectives, finish(): lax.psum((weight_sum * shrink, weighted * shrink[:, None]), 'src')  62.4 us
  transfers between devices with their start and end apart: 4, of which 4 were waited for; matrix products, arithmetic and copies ran while one was open for 0% of the time, Pallas kernels for 0%

commit v1 on v0

--- a/solution.py
+++ b/solution.py
@@ -9,20 +9,18 @@
 sharpness = 3.5
 very_low = -1e30
 
+HALVING_BITS = (3, 0, 1, 2)
 
-def date_partials(targets, sources, offsets, values, tile_mask):
+
+def date_partials(targets, sources, offsets, values, tile_mask, col_tile_ids):
     row_count = targets.shape[0]
-    col_count = sources.shape[0]
     factors = targets.shape[1]
     value_width = values.shape[1]
     row_tiles = row_count // BLOCK
-    col_tiles = col_count // BLOCK
+    col_tiles = sources.shape[0] // BLOCK
     score_scale = sharpness / factors**0.5
-    local_mask = lax.dynamic_slice(
-        tile_mask,
-        (lax.axis_index("tgt") * row_tiles, lax.axis_index("src") * col_tiles),
-        (row_tiles, col_tiles),
-    )
+    row_ids = lax.axis_index("tgt") * row_tiles + jnp.arange(row_tiles)
+    local_mask = tile_mask[row_ids][:, col_tile_ids]
     source_tiles = sources.reshape(col_tiles, BLOCK, factors)
     offset_tiles = offsets.astype(jnp.float32).reshape(col_tiles, BLOCK)
     value_tiles = values.reshape(col_tiles, BLOCK, value_width)
@@ -70,20 +68,81 @@
     return (jnp.concatenate(peaks, 0), jnp.concatenate(sums, 0), jnp.concatenate(weighted_all, 0))
 
 
+def xor_perm(size, bit):
+    return [(i, i ^ (1 << bit)) for i in range(size)]
+
+
+def merge(mine, theirs):
+    width = mine.shape[1] - 2
+    peak_a, peak_b = mine[:, width + 1], theirs[:, width + 1]
+    peak = jnp.maximum(peak_a, peak_b)
+    scale_a = jnp.exp(peak_a - peak)
+    scale_b = jnp.exp(peak_b - peak)
+    body = mine[:, : width + 1] * scale_a[:, None] + theirs[:, : width + 1] * scale_b[:, None]
+    return jnp.concatenate([body, peak[:, None]], axis=1)
+
+
 def finish(partials, exercise):
     row_peak, weight_sum, weighted = partials
-    peak_all = lax.pmax(row_peak, "src")
-    shrink = jnp.exp(row_peak - peak_all)
-    weight_sum, weighted = lax.psum((weight_sum * shrink, weighted * shrink[:, None]), "src")
-    continuation = weighted / weight_sum[:, None]
-    return jnp.maximum(continuation, exercise.astype(jnp.float32)).astype(jnp.bfloat16)
+    src_size = lax.axis_size("src")
+    me = lax.axis_index("src")
+    packed = jnp.concatenate([weighted, weight_sum[:, None], row_peak[:, None]], axis=1)
+    exercise = exercise.astype(jnp.float32)
+    for bit in HALVING_BITS:
+        half = packed.shape[0] // 2
+        mine_hi = (me >> bit) & 1
+        low, high = packed[:half], packed[half:]
+        keep = jnp.where(mine_hi == 1, high, low)
+        send = jnp.where(mine_hi == 1, low, high)
+        got = lax.ppermute(send, "src", xor_perm(src_size, bit))
+        packed = merge(keep, got)
+        exercise = jnp.where(mine_hi == 1, exercise[half:], exercise[:half])
+    width = packed.shape[1] - 2
+    continuation = packed[:, :width] / packed[:, width : width + 1]
+    value = jnp.maximum(continuation, exercise).astype(jnp.bfloat16)
+    for bit in reversed(HALVING_BITS):
+        mine_hi = (me >> bit) & 1
+        got = lax.ppermute(value, "src", xor_perm(src_size, bit))
+        value = jnp.where(
+            mine_hi == 1,
+            jnp.concatenate([got, value], 0),
+            jnp.concatenate([value, got], 0),
+        )
+    return value
 
 
 def regroup(block_rows):
-    per_owner = lax.axis_size("tgt") // lax.axis_size("src")
-    gathered = lax.all_gather(block_rows, "tgt", axis=0, tiled=True)
-    row_count = block_rows.shape[0] * per_owner
-    return lax.dynamic_slice_in_dim(gathered, lax.axis_index("src") * row_count, row_count, 0)
+    tgt_size = lax.axis_size("tgt")
+    src_size = lax.axis_size("src")
+    per_owner = tgt_size // src_size
+
+    def lin(t, s):
+        return t * src_size + s
+
+    perms = []
+    for flip in range(per_owner):
+        pairs = []
+        for u in range(tgt_size):
+            for v in range(src_size):
+                part = u % per_owner
+                t = per_owner * v + ((part + flip) % per_owner)
+                pairs.append((lin(u, v), lin(t, u // per_owner)))
+        perms.append(pairs)
+    got = [lax.ppermute(block_rows, ("tgt", "src"), p) for p in perms]
+    return got
+
+
+def regroup_order(got):
+    per_owner = len(got)
+    t = lax.axis_index("tgt")
+    ordered = []
+    for part in range(per_owner):
+        flip = (t - part) % per_owner
+        pick = got[0]
+        for f in range(1, per_owner):
+            pick = jnp.where(flip == f, got[f], pick)
+        ordered.append(pick)
+    return jnp.concatenate(ordered, 0)
 
 
 def per_device(
@@ -98,13 +157,17 @@
     exercise_early,
     mask_early,
 ):
-    mid_sources = regroup(states_mid)
+    src_tiles = states_late.shape[0] // BLOCK
+    col_ids = lax.axis_index("src") * src_tiles + jnp.arange(src_tiles)
+    mid_sources = regroup_order(regroup(states_mid))
     value_mid = finish(
-        date_partials(states_mid, states_late, offset_late, values_late, mask_mid), exercise_mid
+        date_partials(states_mid, states_late, offset_late, values_late, mask_mid, col_ids),
+        exercise_mid,
     )
-    mid_values = regroup(value_mid)
+    mid_values = regroup_order(regroup(value_mid))
     value_early = finish(
-        date_partials(states_early, mid_sources, offset_mid, mid_values, mask_early), exercise_early
+        date_partials(states_early, mid_sources, offset_mid, mid_values, mask_early, col_ids),
+        exercise_early,
     )
     return (value_mid, value_early)
 

time: 560 us -> 288 us (0.51)
  waiting for transfers between devices: 365 us -> 47.8 us
  starting transfers between devices: 0.16 us -> 196 us
  blocking collectives: 130 us -> 0 us
  between operations: 14 us -> 1.5 us
  matrix products: 15.4 us -> 6.41 us
    psum x2 -> x0, waiting for transfers between devices: 217 us -> none  [finish(): lax.psum((weight_sum * shrink, weighted * shrink[:, None]), 'src')]
    ppermute x0 -> x20, starting transfers between devices: none -> 196 us  [the longest x8 99.3 us: finish(): got = lax.ppermute(send, 'src', xor_perm(src_size, bit))]
    all_gather x2 -> x0, waiting for transfers between devices: 147 us -> none  [regroup(): gathered = lax.all_gather(block_rows, 'tgt', axis=0, tiled=True)]
    pmax x2 -> x0, blocking collectives: 67.2 us -> none  [finish(): peak_all = lax.pmax(row_peak, 'src')]
    psum x2 -> x0, blocking collectives: 62.4 us -> none  [finish(): lax.psum((weight_sum * shrink, weighted * shrink[:, None]), 'src')]
    ppermute x0 -> x20, waiting for transfers between devices: none -> 47.8 us  [the longest x8 26.3 us: finish(): got = lax.ppermute(send, 'src', xor_perm(src_size, bit))]
    dot_general x14 -> x10, matrix products: 10.8 us -> 3.21 us  [active(): lax.dot_general(target_rows, source_tile, (((1,), (1,)), ((), ())), prefe...]
  transfers between devices with their start and end apart: 4 -> 20, of which waited for: 4 -> 16; matrix products, arithmetic and copies ran while one was open for 0% -> 1% of each run, Pallas kernels for 0% -> 0%
where the time goes in v1:
time: 288 us; the launch traced here: 285 us
  starting transfers between devices  196 us (68%)
  waiting for transfers between devices  47.8 us (17%)
  local copies, waits for them, and re-layouts  18 us (6%)
  loops' own time  11 us (4%)
  matrix products  6.41 us (2%)
  other arithmetic  4.06 us (1%)
    ppermute x8, starting transfers between devices, finish(): got = lax.ppermute(send, 'src', xor_perm(src_size, bit))  99.3 us
    ppermute x8, starting transfers between devices, finish(): got = lax.ppermute(value, 'src', xor_perm(src_size, bit))  78.4 us
    ppermute x8, waiting for transfers between devices, finish(): got = lax.ppermute(send, 'src', xor_perm(src_size, bit))  26.3 us
    ppermute x4, starting transfers between devices, regroup(): got = [lax.ppermute(block_rows, ('tgt', 'src'), p) for p in perms]  18.4 us
    ppermute x8, waiting for transfers between devices, finish(): got = lax.ppermute(value, 'src', xor_perm(src_size, bit))  17.4 us
    another operation x4, loops' own time, date_partials(): lax.scan(step, start, (source_tiles, offset_tiles, value_tiles, local_mas...  10.4 us
    dynamic_slice x26, local copies, waits for them, and re-layouts, date_partials(): lax.scan(step, start, (source_tiles, offset_tiles, value_tiles, local_mas...  10.4 us
  transfers between devices with their start and end apart: 20, of which 16 were waited for; matrix products, arithmetic and copies ran while one was open for 1% of the time, Pallas kernels for 0%

profile of v1, /device:TPU:6, one launch (start us, length us, event | category | flops | bytes accessed | tf_op | source)
XLA Modules:
  0.0 284.8 jit_solution(13897426580363340046)
XLA Ops:
  5.2 6.1 %while.56 = (s32[]{:T(128)}, f32[512]{0:T(512)S(1)}, f32[512]{0:T(512)S(1)}, f32[512,64]{0,1:T(8,128)S(1)}, s32[4]{0:T(128)S(1)}, /*index=5*/bf16[4,512,128]{2,1...) while((s32[]{:T(128)}, f32[512]{0:T(512)S(1)}, ...), condition=%wide.region_5.6_spmd, body=%wide.region_0.5_spmd.sunk | while | flops 102564864 | bytes 3840267 | solution.py:62
  11.3 8.8 %while.57 = (s32[]{:T(128)}, f32[512]{0:T(512)S(1)}, f32[512]{0:T(512)S(1)}, f32[512,64]{0,1:T(8,128)S(1)}, s32[4]{0:T(128)S(1)}, /*index=5*/bf16[4,512,128]{2,1...) while((s32[]{:T(128)}, f32[512]{0:T(512)S(1)}, ...), condition=%wide.region_11.12_spmd, body=%wide.region_6.11_spmd.sunk | while | flops 102564864 | bytes 3840267 | solution.py:62
  20.3 5.2 %collective-permute-start = (f32[512,66]{0,1:T(8,128)S(1)}, f32[512,66]{0,1:T(8,128)S(1)}, u32[]{:S(2)}, u32[]{:S(2)}) collective-permute-start(f32[512,66]{0,1:T(8,128)S(1)} %get-tuple-element.682), channel_id=1, source_target_pairs={{0,8},{1,9},{2,10},{3,11},{4,12},{5,13},{6,14},{7,15},{8,0},{9,1},... | collective-permute-start | bytes 405512 | tf_op jit(solution)/shard_map/ppermute | solution.py:97
  31.4 3.6 %collective-permute-done.1 = f32[256,66]{0,1:T(8,128)S(1)} collective-permute-done((f32[256,66]{0,1:T(8,128)S(1)}, f32[256,66]{0,1:T(8,128)S(1)}, u32[]{:S(2)}, u32[]{:S(2)}) %collective-permute-start.1) | collective-permute-done | bytes 67616 | tf_op jit(solution)/shard_map/ppermute | solution.py:97
  35.1 5.9 %collective-permute-start.2 = (f32[128,66]{0,1:T(8,128)S(1)}, f32[128,66]{0,1:T(8,128)S(1)}, u32[]{:S(2)}, u32[]{:S(2)}) collective-permute-start(f32[128,66]{0,1:T(8,128)S(1)} %get-tuple-element.696), channel_id=1, source_target_pairs={{0,2},{1,3},{2,0},{3,1},{4,6},{5,7},{6,4},{7,5},{8,10},{9,11},{10,... | collective-permute-start | bytes 101384 | tf_op jit(solution)/shard_map/ppermute | solution.py:97
  43.0 7.6 %collective-permute-start.3 = (f32[64,66]{0,1:T(8,128)S(1)}, f32[64,66]{0,1:T(8,128)S(1)}, u32[]{:S(2)}, u32[]{:S(2)}) collective-permute-start(f32[64,66]{0,1:T(8,128)S(1)} %get-tuple-element.705), channel_id=1, source_target_pairs={{0,4},{1,5},{2,6},{3,7},{4,0},{5,1},{6,2},{7,3},{8,12},{9,13},{10,... | collective-permute-start | bytes 50696 | tf_op jit(solution)/shard_map/ppermute | solution.py:97
  52.9 8.0 %collective-permute-start.4 = (bf16[64,64]{0,1:T(8,128)(2,1)S(1)}, bf16[64,64]{0,1:T(8,128)(2,1)S(1)}, u32[]{:S(2)}, u32[]{:S(2)}) collective-permute-start(bf16[64,64]{0,1:T(8,128)(2,1)S(1)} %fusion.59), channel_id=1, source_target_pairs={{0,4},{1,5},{2,6},{3,7},{4,0},{5,1},{6,2},{7,3},{8,12},{9,13},{10,... | collective-permute-start | bytes 24584 | tf_op jit(solution)/shard_map/ppermute | solution.py:105
  64.9 4.5 %collective-permute-start.5 = (bf16[128,64]{0,1:T(8,128)(2,1)S(1)}, bf16[128,64]{0,1:T(8,128)(2,1)S(1)}, u32[]{:S(2)}, u32[]{:S(2)}) collective-permute-start(bf16[128,64]{0,1:T(8,128)(2,1)S(1)} %maximum_select_fusion.6), channel_id=1, source_target_pairs={{0,2},{1,3},{2,0},{3,1},{4,6},{5,7},{6,4},{7,5},{8,10},{9,11},{10,... | collective-permute-start | bytes 49160 | tf_op jit(solution)/shard_map/ppermute | solution.py:105
  71.6 17.2 %collective-permute-start.6 = (bf16[256,64]{0,1:T(8,128)(2,1)S(1)}, bf16[256,64]{0,1:T(8,128)(2,1)S(1)}, u32[]{:S(2)}, u32[]{:S(2)}) collective-permute-start(bf16[256,64]{0,1:T(8,128)(2,1)S(1)} %maximum_select_fusion.4), channel_id=1, source_target_pairs={{0,1},{1,0},{2,3},{3,2},{4,5},{5,4},{6,7},{7,6},{8,9},{9,8},{10,11... | collective-permute-start | bytes 98312 | tf_op jit(solution)/shard_map/ppermute | solution.py:105
  90.7 34.8 %collective-permute-start.7 = (bf16[512,64]{0,1:T(8,128)(2,1)S(1)}, bf16[512,64]{0,1:T(8,128)(2,1)S(1)}, u32[]{:S(2)}, u32[]{:S(2)}) collective-permute-start(bf16[512,64]{0,1:T(8,128)(2,1)S(1)} %maximum_select_fusion.2), channel_id=1, source_target_pairs={{0,8},{1,9},{2,10},{3,11},{4,12},{5,13},{6,14},{7,15},{8,0},{9,1},... | collective-permute-start | bytes 196616 | tf_op jit(solution)/shard_map/ppermute | solution.py:105
  127.8 7.1 %collective-permute-start.10 = (bf16[1024,64]{0,1:T(8,128)(2,1)S(1)}, bf16[1024,64]{0,1:T(8,128)(2,1)S(1)}, u32[]{:S(2)}, u32[]{:S(2)}) collective-permute-start(bf16[1024,64]{0,1:T(8,128)(2,1)S(1)} %maximum_select_fusion), channel_id=1, source_target_pairs={{0,16},{1,48},{2,80},{3,112},{4,144},{5,176},{6,208},{7,240},{8,27... | collective-permute-start | bytes 393224 | tf_op jit(solution)/shard_map/ppermute | solution.py:131
  134.9 7.4 %collective-permute-start.11 = (bf16[1024,64]{0,1:T(8,128)(2,1)S(1)}, bf16[1024,64]{0,1:T(8,128)(2,1)S(1)}, u32[]{:S(2)}, u32[]{:S(2)}) collective-permute-start(bf16[1024,64]{0,1:T(8,128)(2,1)S(1)} %maximum_select_fusion), channel_id=1, source_target_pairs={{0,0},{1,32},{2,64},{3,96},{4,128},{5,160},{6,192},{7,224},{8,256}... | collective-permute-start | bytes 393224 | tf_op jit(solution)/shard_map/ppermute | solution.py:131
  142.4 4.1 %collective-permute-done.11 = bf16[1024,64]{0,1:T(8,128)(2,1)S(1)} collective-permute-done((bf16[1024,64]{0,1:T(8,128)(2,1)S(1)}, bf16[1024,64]{0,1:T(8,128)(2,1)S(1)}, u32[]{:S(2)}, u32[]{:S(2)}) %collective-permute-start.11) | collective-permute-done | bytes 131104 | tf_op jit(solution)/shard_map/ppermute | solution.py:131
  146.8 7.9 %while.58 = (s32[]{:T(128)}, f32[512]{0:T(512)S(1)}, f32[512]{0:T(512)S(1)}, f32[512,64]{0,1:T(8,128)S(1)}, s32[4]{0:T(128)S(1)}, /*index=5*/bf16[4,512,128]{2,1...) while((s32[]{:T(128)}, f32[512]{0:T(512)S(1)}, ...), condition=%wide.region_17.18_spmd, body=%wide.region_12.17_spmd.sunk | while | flops 102564864 | bytes 3840267 | solution.py:62
  154.8 7.0 %while.59 = (s32[]{:T(128)}, f32[512]{0:T(512)S(1)}, f32[512]{0:T(512)S(1)}, f32[512,64]{0,1:T(8,128)S(1)}, s32[4]{0:T(128)S(1)}, /*index=5*/bf16[4,512,128]{2,1...) while((s32[]{:T(128)}, f32[512]{0:T(512)S(1)}, ...), condition=%wide.region_23.24_spmd, body=%wide.region_18.23_spmd.sunk | while | flops 102564864 | bytes 3840267 | solution.py:62
  162.0 16.8 %collective-permute-start.12 = (f32[512,66]{0,1:T(8,128)S(1)}, f32[512,66]{0,1:T(8,128)S(1)}, u32[]{:S(2)}, u32[]{:S(2)}) collective-permute-start(f32[512,66]{0,1:T(8,128)S(1)} %get-tuple-element.680), channel_id=1, source_target_pairs={{0,8},{1,9},{2,10},{3,11},{4,12},{5,13},{6,14},{7,15},{8,0},{9,1},... | collective-permute-start | bytes 405512 | tf_op jit(solution)/shard_map/ppermute | solution.py:97
  178.8 3.1 %collective-permute-done.12 = f32[512,66]{0,1:T(8,128)S(1)} collective-permute-done((f32[512,66]{0,1:T(8,128)S(1)}, f32[512,66]{0,1:T(8,128)S(1)}, u32[]{:S(2)}, u32[]{:S(2)}) %collective-permute-start.12) | collective-permute-done | bytes 135200 | tf_op jit(solution)/shard_map/ppermute | solution.py:97
  182.0 41.1 %collective-permute-start.13 = (f32[256,66]{0,1:T(8,128)S(1)}, f32[256,66]{0,1:T(8,128)S(1)}, u32[]{:S(2)}, u32[]{:S(2)}) collective-permute-start(f32[256,66]{0,1:T(8,128)S(1)} %get-tuple-element.690), channel_id=1, source_target_pairs={{0,1},{1,0},{2,3},{3,2},{4,5},{5,4},{6,7},{7,6},{8,9},{9,8},{10,11... | collective-permute-start | bytes 202760 | tf_op jit(solution)/shard_map/ppermute | solution.py:97
  225.4 18.2 %collective-permute-start.14 = (f32[128,66]{0,1:T(8,128)S(1)}, f32[128,66]{0,1:T(8,128)S(1)}, u32[]{:S(2)}, u32[]{:S(2)}) collective-permute-start(f32[128,66]{0,1:T(8,128)S(1)} %get-tuple-element.694), channel_id=1, source_target_pairs={{0,2},{1,3},{2,0},{3,1},{4,6},{5,7},{6,4},{7,5},{8,10},{9,11},{10,... | collective-permute-start | bytes 101384 | tf_op jit(solution)/shard_map/ppermute | solution.py:97
  247.6 8.2 %collective-permute-done.15 = f32[64,66]{0,1:T(8,128)S(1)} collective-permute-done((f32[64,66]{0,1:T(8,128)S(1)}, f32[64,66]{0,1:T(8,128)S(1)}, u32[]{:S(2)}, u32[]{:S(2)}) %collective-permute-start.15) | collective-permute-done | bytes 16928 | tf_op jit(solution)/shard_map/ppermute | solution.py:97
  257.9 7.6 %collective-permute-done.16 = bf16[64,64]{0,1:T(8,128)(2,1)S(1)} collective-permute-done((bf16[64,64]{0,1:T(8,128)(2,1)S(1)}, bf16[64,64]{0,1:T(8,128)(2,1)S(1)}, u32[]{:S(2)}, u32[]{:S(2)}) %collective-permute-start.16) | collective-permute-done | bytes 8224 | tf_op jit(solution)/shard_map/ppermute | solution.py:105
  265.6 4.6 %collective-permute-start.17 = (bf16[128,64]{0,1:T(8,128)(2,1)S(1)}, bf16[128,64]{0,1:T(8,128)(2,1)S(1)}, u32[]{:S(2)}, u32[]{:S(2)}) collective-permute-start(bf16[128,64]{0,1:T(8,128)(2,1)S(1)} %maximum_select_fusion.7), channel_id=1, source_target_pairs={{0,2},{1,3},{2,0},{3,1},{4,6},{5,7},{6,4},{7,5},{8,10},{9,11},{10,... | collective-permute-start | bytes 49160 | tf_op jit(solution)/shard_map/ppermute | solution.py:105
  272.2 3.4 %collective-permute-start.18 = (bf16[256,64]{0,1:T(8,128)(2,1)S(1)}, bf16[256,64]{0,1:T(8,128)(2,1)S(1)}, u32[]{:S(2)}, u32[]{:S(2)}) collective-permute-start(bf16[256,64]{0,1:T(8,128)(2,1)S(1)} %maximum_select_fusion.5), channel_id=1, source_target_pairs={{0,1},{1,0},{2,3},{3,2},{4,5},{5,4},{6,7},{7,6},{8,9},{9,8},{10,11... | collective-permute-start | bytes 98312 | tf_op jit(solution)/shard_map/ppermute | solution.py:105
  278.0 3.9 %collective-permute-start.19 = (bf16[512,64]{0,1:T(8,128)(2,1)S(1)}, bf16[512,64]{0,1:T(8,128)(2,1)S(1)}, u32[]{:S(2)}, u32[]{:S(2)}) collective-permute-start(bf16[512,64]{0,1:T(8,128)(2,1)S(1)} %maximum_select_fusion.3), channel_id=1, source_target_pairs={{0,8},{1,9},{2,10},{3,11},{4,12},{5,13},{6,14},{7,15},{8,0},{9,1},... | collective-permute-start | bytes 196616 | tf_op jit(solution)/shard_map/ppermute | solution.py:105
  (227 shorter events, 69.3 us)
Async XLA Ops:
  20.3 8.3 %collective-permute-start = (f32[512,66]{0,1:T(8,128)S(1)}, f32[512,66]{0,1:T(8,128)S(1)}, u32[]{:S(2)}, u32[]{:S(2)}) collective-permute-start(f32[512,66]{0,1:T(8,128)S(1)} %get-tuple-element.682), channel_id=1, source_target_pairs={{0,8},{1,9},{2,10},{3,11},{4,12},{5,13},{6,14},{7,15},{8,0},{9,1},... | collective-permute-start | bytes 405512 | tf_op jit(solution)/shard_map/ppermute | solution.py:97
  28.6 2.8 copy-start.4
  28.7 6.4 %collective-permute-start.1 = (f32[256,66]{0,1:T(8,128)S(1)}, f32[256,66]{0,1:T(8,128)S(1)}, u32[]{:S(2)}, u32[]{:S(2)}) collective-permute-start(f32[256,66]{0,1:T(8,128)S(1)} %get-tuple-element.692), channel_id=1, source_target_pairs={{0,1},{1,0},{2,3},{3,2},{4,5},{5,4},{6,7},{7,6},{8,9},{9,8},{10,11... | collective-permute-start | bytes 202760 | tf_op jit(solution)/shard_map/ppermute | solution.py:97
  35.1 7.8 %collective-permute-start.2 = (f32[128,66]{0,1:T(8,128)S(1)}, f32[128,66]{0,1:T(8,128)S(1)}, u32[]{:S(2)}, u32[]{:S(2)}) collective-permute-start(f32[128,66]{0,1:T(8,128)S(1)} %get-tuple-element.696), channel_id=1, source_target_pairs={{0,2},{1,3},{2,0},{3,1},{4,6},{5,7},{6,4},{7,5},{8,10},{9,11},{10,... | collective-permute-start | bytes 101384 | tf_op jit(solution)/shard_map/ppermute | solution.py:97
  42.9 26.5 %copy-start.2 = (bf16[1024,128]{1,0:T(8,128)(2,1)S(1)}, bf16[1024,128]{1,0:T(8,128)(2,1)}, u32[]{:S(2)}) copy-start(bf16[1024,128]{1,0:T(8,128)(2,1)} %param.33) | copy-start | bytes 786436
  43.0 9.8 %collective-permute-start.3 = (f32[64,66]{0,1:T(8,128)S(1)}, f32[64,66]{0,1:T(8,128)S(1)}, u32[]{:S(2)}, u32[]{:S(2)}) collective-permute-start(f32[64,66]{0,1:T(8,128)S(1)} %get-tuple-element.705), channel_id=1, source_target_pairs={{0,4},{1,5},{2,6},{3,7},{4,0},{5,1},{6,2},{7,3},{8,12},{9,13},{10,... | collective-permute-start | bytes 50696 | tf_op jit(solution)/shard_map/ppermute | solution.py:97
  52.9 11.8 %collective-permute-start.4 = (bf16[64,64]{0,1:T(8,128)(2,1)S(1)}, bf16[64,64]{0,1:T(8,128)(2,1)S(1)}, u32[]{:S(2)}, u32[]{:S(2)}) collective-permute-start(bf16[64,64]{0,1:T(8,128)(2,1)S(1)} %fusion.59), channel_id=1, source_target_pairs={{0,4},{1,5},{2,6},{3,7},{4,0},{5,1},{6,2},{7,3},{8,12},{9,13},{10,... | collective-permute-start | bytes 24584 | tf_op jit(solution)/shard_map/ppermute | solution.py:105
  60.9 64.6 %collective-permute-start.8 = (bf16[1024,128]{1,0:T(8,128)(2,1)S(1)}, bf16[1024,128]{1,0:T(8,128)(2,1)S(1)}, u32[]{:S(2)}, u32[]{:S(2)}) collective-permute-start(bf16[1024,128]{1,0:T(8,128)(2,1)S(1)} %copy-done.3), channel_id=1, source_target_pairs={{0,16},{1,48},{2,80},{3,112},{4,144},{5,176},{6,208},{7,240},{8,27... | collective-permute-start | bytes 786440 | tf_op jit(solution)/shard_map/ppermute | solution.py:131
  62.8 62.7 %collective-permute-start.9 = (bf16[1024,128]{1,0:T(8,128)(2,1)S(1)}, bf16[1024,128]{1,0:T(8,128)(2,1)S(1)}, u32[]{:S(2)}, u32[]{:S(2)}) collective-permute-start(bf16[1024,128]{1,0:T(8,128)(2,1)S(1)} %copy-done.3), channel_id=1, source_target_pairs={{0,0},{1,32},{2,64},{3,96},{4,128},{5,160},{6,192},{7,224},{8,256}... | collective-permute-start | bytes 786440 | tf_op jit(solution)/shard_map/ppermute | solution.py:131
  64.9 6.8 %collective-permute-start.5 = (bf16[128,64]{0,1:T(8,128)(2,1)S(1)}, bf16[128,64]{0,1:T(8,128)(2,1)S(1)}, u32[]{:S(2)}, u32[]{:S(2)}) collective-permute-start(bf16[128,64]{0,1:T(8,128)(2,1)S(1)} %maximum_select_fusion.6), channel_id=1, source_target_pairs={{0,2},{1,3},{2,0},{3,1},{4,6},{5,7},{6,4},{7,5},{8,10},{9,11},{10,... | collective-permute-start | bytes 49160 | tf_op jit(solution)/shard_map/ppermute | solution.py:105
  71.6 19.0 %collective-permute-start.6 = (bf16[256,64]{0,1:T(8,128)(2,1)S(1)}, bf16[256,64]{0,1:T(8,128)(2,1)S(1)}, u32[]{:S(2)}, u32[]{:S(2)}) collective-permute-start(bf16[256,64]{0,1:T(8,128)(2,1)S(1)} %maximum_select_fusion.4), channel_id=1, source_target_pairs={{0,1},{1,0},{2,3},{3,2},{4,5},{5,4},{6,7},{7,6},{8,9},{9,8},{10,11... | collective-permute-start | bytes 98312 | tf_op jit(solution)/shard_map/ppermute | solution.py:105
  90.7 37.0 %collective-permute-start.7 = (bf16[512,64]{0,1:T(8,128)(2,1)S(1)}, bf16[512,64]{0,1:T(8,128)(2,1)S(1)}, u32[]{:S(2)}, u32[]{:S(2)}) collective-permute-start(bf16[512,64]{0,1:T(8,128)(2,1)S(1)} %maximum_select_fusion.2), channel_id=1, source_target_pairs={{0,8},{1,9},{2,10},{3,11},{4,12},{5,13},{6,14},{7,15},{8,0},{9,1},... | collective-permute-start | bytes 196616 | tf_op jit(solution)/shard_map/ppermute | solution.py:105
  127.8 14.6 %copy-start.6 = (bf16[1024,64]{0,1:T(8,128)(2,1)}, bf16[1024,64]{0,1:T(8,128)(2,1)S(1)}, u32[]{:S(2)}) copy-start(bf16[1024,64]{0,1:T(8,128)(2,1)S(1)} %maximum_select_fusion) | copy-start | bytes 393220
  127.8 14.6 %collective-permute-start.10 = (bf16[1024,64]{0,1:T(8,128)(2,1)S(1)}, bf16[1024,64]{0,1:T(8,128)(2,1)S(1)}, u32[]{:S(2)}, u32[]{:S(2)}) collective-permute-start(bf16[1024,64]{0,1:T(8,128)(2,1)S(1)} %maximum_select_fusion), channel_id=1, source_target_pairs={{0,16},{1,48},{2,80},{3,112},{4,144},{5,176},{6,208},{7,240},{8,27... | collective-permute-start | bytes 393224 | tf_op jit(solution)/shard_map/ppermute | solution.py:131
  134.9 11.6 %collective-permute-start.11 = (bf16[1024,64]{0,1:T(8,128)(2,1)S(1)}, bf16[1024,64]{0,1:T(8,128)(2,1)S(1)}, u32[]{:S(2)}, u32[]{:S(2)}) collective-permute-start(bf16[1024,64]{0,1:T(8,128)(2,1)S(1)} %maximum_select_fusion), channel_id=1, source_target_pairs={{0,0},{1,32},{2,64},{3,96},{4,128},{5,160},{6,192},{7,224},{8,256}... | collective-permute-start | bytes 393224 | tf_op jit(solution)/shard_map/ppermute | solution.py:131
  162.0 19.9 %collective-permute-start.12 = (f32[512,66]{0,1:T(8,128)S(1)}, f32[512,66]{0,1:T(8,128)S(1)}, u32[]{:S(2)}, u32[]{:S(2)}) collective-permute-start(f32[512,66]{0,1:T(8,128)S(1)} %get-tuple-element.680), channel_id=1, source_target_pairs={{0,8},{1,9},{2,10},{3,11},{4,12},{5,13},{6,14},{7,15},{8,0},{9,1},... | collective-permute-start | bytes 405512 | tf_op jit(solution)/shard_map/ppermute | solution.py:97
  181.9 41.1 %copy-start.5 = (bf16[1024,64]{0,1:T(8,128)(2,1)S(1)}, bf16[1024,64]{0,1:T(8,128)(2,1)}, u32[]{:S(2)}) copy-start(bf16[1024,64]{0,1:T(8,128)(2,1)} %param.34) | copy-start | bytes 393220
  182.0 43.4 %collective-permute-start.13 = (f32[256,66]{0,1:T(8,128)S(1)}, f32[256,66]{0,1:T(8,128)S(1)}, u32[]{:S(2)}, u32[]{:S(2)}) collective-permute-start(f32[256,66]{0,1:T(8,128)S(1)} %get-tuple-element.690), channel_id=1, source_target_pairs={{0,1},{1,0},{2,3},{3,2},{4,5},{5,4},{6,7},{7,6},{8,9},{9,8},{10,11... | collective-permute-start | bytes 202760 | tf_op jit(solution)/shard_map/ppermute | solution.py:97
  225.4 20.2 %collective-permute-start.14 = (f32[128,66]{0,1:T(8,128)S(1)}, f32[128,66]{0,1:T(8,128)S(1)}, u32[]{:S(2)}, u32[]{:S(2)}) collective-permute-start(f32[128,66]{0,1:T(8,128)S(1)} %get-tuple-element.694), channel_id=1, source_target_pairs={{0,2},{1,3},{2,0},{3,1},{4,6},{5,7},{6,4},{7,5},{8,10},{9,11},{10,... | collective-permute-start | bytes 101384 | tf_op jit(solution)/shard_map/ppermute | solution.py:97
  245.7 10.2 %collective-permute-start.15 = (f32[64,66]{0,1:T(8,128)S(1)}, f32[64,66]{0,1:T(8,128)S(1)}, u32[]{:S(2)}, u32[]{:S(2)}) collective-permute-start(f32[64,66]{0,1:T(8,128)S(1)} %get-tuple-element.703), channel_id=1, source_target_pairs={{0,4},{1,5},{2,6},{3,7},{4,0},{5,1},{6,2},{7,3},{8,12},{9,13},{10,... | collective-permute-start | bytes 50696 | tf_op jit(solution)/shard_map/ppermute | solution.py:97
  256.0 9.5 %collective-permute-start.16 = (bf16[64,64]{0,1:T(8,128)(2,1)S(1)}, bf16[64,64]{0,1:T(8,128)(2,1)S(1)}, u32[]{:S(2)}, u32[]{:S(2)}) collective-permute-start(bf16[64,64]{0,1:T(8,128)(2,1)S(1)} %fusion.57), channel_id=1, source_target_pairs={{0,4},{1,5},{2,6},{3,7},{4,0},{5,1},{6,2},{7,3},{8,12},{9,13},{10,... | collective-permute-start | bytes 24584 | tf_op jit(solution)/shard_map/ppermute | solution.py:105
  265.6 6.5 %collective-permute-start.17 = (bf16[128,64]{0,1:T(8,128)(2,1)S(1)}, bf16[128,64]{0,1:T(8,128)(2,1)S(1)}, u32[]{:S(2)}, u32[]{:S(2)}) collective-permute-start(bf16[128,64]{0,1:T(8,128)(2,1)S(1)} %maximum_select_fusion.7), channel_id=1, source_target_pairs={{0,2},{1,3},{2,0},{3,1},{4,6},{5,7},{6,4},{7,5},{8,10},{9,11},{10,... | collective-permute-start | bytes 49160 | tf_op jit(solution)/shard_map/ppermute | solution.py:105
  272.2 5.8 %collective-permute-start.18 = (bf16[256,64]{0,1:T(8,128)(2,1)S(1)}, bf16[256,64]{0,1:T(8,128)(2,1)S(1)}, u32[]{:S(2)}, u32[]{:S(2)}) collective-permute-start(bf16[256,64]{0,1:T(8,128)(2,1)S(1)} %maximum_select_fusion.5), channel_id=1, source_target_pairs={{0,1},{1,0},{2,3},{3,2},{4,5},{5,4},{6,7},{7,6},{8,9},{9,8},{10,11... | collective-permute-start | bytes 98312 | tf_op jit(solution)/shard_map/ppermute | solution.py:105
  278.0 6.2 %collective-permute-start.19 = (bf16[512,64]{0,1:T(8,128)(2,1)S(1)}, bf16[512,64]{0,1:T(8,128)(2,1)S(1)}, u32[]{:S(2)}, u32[]{:S(2)}) collective-permute-start(bf16[512,64]{0,1:T(8,128)(2,1)S(1)} %maximum_select_fusion.3), channel_id=1, source_target_pairs={{0,8},{1,9},{2,10},{3,11},{4,12},{5,13},{6,14},{7,15},{8,0},{9,1},... | collective-permute-start | bytes 196616 | tf_op jit(solution)/shard_map/ppermute | solution.py:105
  (5 other events, 5.1 us)

commit v2 on v1

--- a/solution.py
+++ b/solution.py
@@ -111,38 +111,43 @@
     return value
 
 
+def lin(t, s):
+    return t * lax.axis_size("src") + s
+
+
+def source_pair(t, s):
+    x_count = lax.axis_size("tgt") // 8
+    z_hi, x = t // (2 * x_count), (t // 2) % x_count
+    return ((z_hi + s // 4) % 4) * x_count + (x + s % 4) % x_count
+
+
 def regroup(block_rows):
     tgt_size = lax.axis_size("tgt")
     src_size = lax.axis_size("src")
-    per_owner = tgt_size // src_size
-
-    def lin(t, s):
-        return t * src_size + s
-
-    perms = []
-    for flip in range(per_owner):
-        pairs = []
-        for u in range(tgt_size):
-            for v in range(src_size):
-                part = u % per_owner
-                t = per_owner * v + ((part + flip) % per_owner)
-                pairs.append((lin(u, v), lin(t, u // per_owner)))
-        perms.append(pairs)
-    got = [lax.ppermute(block_rows, ("tgt", "src"), p) for p in perms]
-    return got
+    perms = ([], [])
+    for t in range(tgt_size):
+        for s in range(src_size):
+            pair = source_pair(t, s)
+            for flip in range(2):
+                u = 2 * pair + ((t % 2) ^ flip)
+                perms[flip].append((lin(u, s), lin(t, s)))
+    return [lax.ppermute(block_rows, ("tgt", "src"), p) for p in perms]
 
 
 def regroup_order(got):
-    per_owner = len(got)
-    t = lax.axis_index("tgt")
-    ordered = []
-    for part in range(per_owner):
-        flip = (t - part) % per_owner
-        pick = got[0]
-        for f in range(1, per_owner):
-            pick = jnp.where(flip == f, got[f], pick)
-        ordered.append(pick)
-    return jnp.concatenate(ordered, 0)
+    odd = lax.axis_index("tgt") % 2 == 1
+    return jnp.concatenate(
+        [jnp.where(odd, got[1], got[0]), jnp.where(odd, got[0], got[1])], 0
+    )
+
+
+def regroup_offsets(offsets):
+    tgt_size = lax.axis_size("tgt")
+    src_size = lax.axis_size("src")
+    pairs = [
+        (lin(t, source_pair(t, s)), lin(t, s)) for t in range(tgt_size) for s in range(src_size)
+    ]
+    return lax.ppermute(offsets, ("tgt", "src"), pairs)
 
 
 def per_device(
@@ -159,14 +164,20 @@
 ):
     src_tiles = states_late.shape[0] // BLOCK
     col_ids = lax.axis_index("src") * src_tiles + jnp.arange(src_tiles)
+    pair = source_pair(lax.axis_index("tgt"), lax.axis_index("src"))
+    early_col_ids = pair * src_tiles + jnp.arange(src_tiles)
     mid_sources = regroup_order(regroup(states_mid))
-    value_mid = finish(
-        date_partials(states_mid, states_late, offset_late, values_late, mask_mid, col_ids),
-        exercise_mid,
-    )
+    mid_offsets = regroup_offsets(offset_mid)
+    partials = date_partials(states_mid, states_late, offset_late, values_late, mask_mid, col_ids)
+    partials, mid_sources, mid_offsets = lax.optimization_barrier(
+        (partials, mid_sources, mid_offsets)
+    )
+    value_mid = finish(partials, exercise_mid)
     mid_values = regroup_order(regroup(value_mid))
     value_early = finish(
-        date_partials(states_early, mid_sources, offset_mid, mid_values, mask_early, col_ids),
+        date_partials(
+            states_early, mid_sources, mid_offsets, mid_values, mask_early, early_col_ids
+        ),
         exercise_early,
     )
     return (value_mid, value_early)

time: 288 us -> 196 us (0.68)
  the two profiles are of different devices: /device:TPU:6 before, /device:TPU:146 now
where the time goes in v2:
time: 196 us; the launch traced here: 195 us
  waiting for transfers between devices  87.7 us (45%)
  starting transfers between devices  65 us (33%)
  local copies, waits for them, and re-layouts  16.1 us (8%)
  loops' own time  11.1 us (6%)
  matrix products  8.34 us (4%)
  other arithmetic  4.74 us (2%)
    ppermute x8, waiting for transfers between devices, finish(): got = lax.ppermute(send, 'src', xor_perm(src_size, bit))  44 us
    ppermute x8, waiting for transfers between devices, finish(): got = lax.ppermute(value, 'src', xor_perm(src_size, bit))  38.6 us
    ppermute x8, starting transfers between devices, finish(): got = lax.ppermute(send, 'src', xor_perm(src_size, bit))  23.6 us
    ppermute x8, starting transfers between devices, finish(): got = lax.ppermute(value, 'src', xor_perm(src_size, bit))  17.6 us
    ppermute x1, starting transfers between devices, regroup_offsets(): return lax.ppermute(offsets, ('tgt', 'src'), pairs)  13.1 us
    ppermute x4, starting transfers between devices, regroup(): return [lax.ppermute(block_rows, ('tgt', 'src'), p) for p in perms]  10.6 us
    another operation x4, loops' own time, date_partials(): lax.scan(step, start, (source_tiles, offset_tiles, value_tiles, local_mas...  10.4 us
    dynamic_slice x29, local copies, waits for them, and re-layouts, date_partials(): lax.scan(step, start, (source_tiles, offset_tiles, value_tiles, local_mas...  10.4 us
  transfers between devices with their start and end apart: 21, of which 18 were waited for; matrix products, arithmetic and copies ran while one was open for 8% of the time, Pallas kernels for 0%

profile of v2, /device:TPU:146, one launch (start us, length us, event | category | flops | bytes accessed | tf_op | source)
XLA Modules:
  0.0 194.5 jit_solution(5370659003445036894)
XLA Ops:
  0.6 3.5 %collective-permute-start = (bf16[1024,128]{1,0:T(8,128)(2,1)}, bf16[1024,128]{1,0:T(8,128)(2,1)S(1)}, u32[]{:S(2)}, u32[]{:S(2)}) collective-permute-start(bf16[1024,128]{1,0:T(8,128)(2,1)} %param.29), channel_id=1, source_target_pairs={{16,0},{49,1},{82,2},{115,3},{148,4},{181,5},{214,6},{247,7},{280,... | collective-permute-start | bytes 786440 | tf_op jit(solution)/shard_map/ppermute | solution.py:134
  4.1 3.3 %collective-permute-start.1 = (bf16[1024,128]{1,0:T(8,128)(2,1)}, bf16[1024,128]{1,0:T(8,128)(2,1)S(1)}, u32[]{:S(2)}, u32[]{:S(2)}) collective-permute-start(bf16[1024,128]{1,0:T(8,128)(2,1)} %param.29), channel_id=1, source_target_pairs={{0,0},{33,1},{66,2},{99,3},{132,4},{165,5},{198,6},{231,7},{264,8}... | collective-permute-start | bytes 786440 | tf_op jit(solution)/shard_map/ppermute | solution.py:134
  7.4 13.1 %collective-permute-start.2 = (bf16[2048]{0:T(1024)(128)(2,1)}, bf16[2048]{0:T(1024)(128)(2,1)S(1)}, u32[]{:S(2)}, u32[]{:S(2)}) collective-permute-start(bf16[2048]{0:T(1024)(128)(2,1)} %param.30), channel_id=1, source_target_pairs={{0,0},{1,1},{2,2},{3,3},{4,4},{5,5},{6,6},{7,7},{8,8},{9,9},{10,10... | collective-permute-start | bytes 12296 | tf_op jit(solution)/shard_map/ppermute | solution.py:150
  23.9 6.1 %while.56 = (s32[]{:T(128)}, f32[512]{0:T(512)S(1)}, f32[512]{0:T(512)S(1)}, f32[512,64]{0,1:T(8,128)S(1)}, s32[4]{0:T(128)S(1)}, /*index=5*/bf16[4,512,128]{2,1...) while((s32[]{:T(128)}, f32[512]{0:T(512)S(1)}, ...), condition=%wide.region_5.6_spmd, body=%wide.region_0.5_spmd.sunk | while | flops 102564864 | bytes 3840267 | solution.py:62
  30.1 8.8 %while.57 = (s32[]{:T(128)}, f32[512]{0:T(512)S(1)}, f32[512]{0:T(512)S(1)}, f32[512,64]{0,1:T(8,128)S(1)}, s32[4]{0:T(128)S(1)}, /*index=5*/bf16[4,512,128]{2,1...) while((s32[]{:T(128)}, f32[512]{0:T(512)S(1)}, ...), condition=%wide.region_11.12_spmd, body=%wide.region_6.11_spmd.sunk | while | flops 102564864 | bytes 3840267 | solution.py:62
  41.1 6.6 %collective-permute-done.3 = f32[512,66]{0,1:T(8,128)S(1)} collective-permute-done((f32[512,66]{0,1:T(8,128)S(1)}, f32[512,66]{0,1:T(8,128)S(1)}, u32[]{:S(2)}, u32[]{:S(2)}) %collective-permute-start.3) | collective-permute-done | bytes 135200 | tf_op jit(solution)/shard_map/ppermute | solution.py:97
  49.9 4.3 %collective-permute-done.4 = f32[256,66]{0,1:T(8,128)S(1)} collective-permute-done((f32[256,66]{0,1:T(8,128)S(1)}, f32[256,66]{0,1:T(8,128)S(1)}, u32[]{:S(2)}, u32[]{:S(2)}) %collective-permute-start.4) | collective-permute-done | bytes 67616 | tf_op jit(solution)/shard_map/ppermute | solution.py:97
  56.2 4.8 %collective-permute-done.5 = f32[128,66]{0,1:T(8,128)S(1)} collective-permute-done((f32[128,66]{0,1:T(8,128)S(1)}, f32[128,66]{0,1:T(8,128)S(1)}, u32[]{:S(2)}, u32[]{:S(2)}) %collective-permute-start.5) | collective-permute-done | bytes 33824 | tf_op jit(solution)/shard_map/ppermute | solution.py:97
  63.1 8.1 %collective-permute-done.6 = f32[64,66]{0,1:T(8,128)S(1)} collective-permute-done((f32[64,66]{0,1:T(8,128)S(1)}, f32[64,66]{0,1:T(8,128)S(1)}, u32[]{:S(2)}, u32[]{:S(2)}) %collective-permute-start.6) | collective-permute-done | bytes 16928 | tf_op jit(solution)/shard_map/ppermute | solution.py:97
  73.2 7.9 %collective-permute-done.7 = bf16[64,64]{0,1:T(8,128)(2,1)S(1)} collective-permute-done((bf16[64,64]{0,1:T(8,128)(2,1)S(1)}, bf16[64,64]{0,1:T(8,128)(2,1)S(1)}, u32[]{:S(2)}, u32[]{:S(2)}) %collective-permute-start.7) | collective-permute-done | bytes 8224 | tf_op jit(solution)/shard_map/ppermute | solution.py:105
  83.1 4.6 %collective-permute-done.8 = bf16[128,64]{0,1:T(8,128)(2,1)S(1)} collective-permute-done((bf16[128,64]{0,1:T(8,128)(2,1)S(1)}, bf16[128,64]{0,1:T(8,128)(2,1)S(1)}, u32[]{:S(2)}, u32[]{:S(2)}) %collective-permute-start.8) | collective-permute-done | bytes 16416 | tf_op jit(solution)/shard_map/ppermute | solution.py:105
  89.8 3.8 %collective-permute-done.9 = bf16[256,64]{0,1:T(8,128)(2,1)S(1)} collective-permute-done((bf16[256,64]{0,1:T(8,128)(2,1)S(1)}, bf16[256,64]{0,1:T(8,128)(2,1)S(1)}, u32[]{:S(2)}, u32[]{:S(2)}) %collective-permute-start.9) | collective-permute-done | bytes 32800 | tf_op jit(solution)/shard_map/ppermute | solution.py:105
  95.5 4.2 %collective-permute-done.10 = bf16[512,64]{0,1:T(8,128)(2,1)S(1)} collective-permute-done((bf16[512,64]{0,1:T(8,128)(2,1)S(1)}, bf16[512,64]{0,1:T(8,128)(2,1)S(1)}, u32[]{:S(2)}, u32[]{:S(2)}) %collective-permute-start.10) | collective-permute-done | bytes 65568 | tf_op jit(solution)/shard_map/ppermute | solution.py:105
  107.5 3.3 %collective-permute-done.12 = bf16[1024,64]{0,1:T(8,128)(2,1)S(1)} collective-permute-done((bf16[1024,64]{0,1:T(8,128)(2,1)S(1)}, bf16[1024,64]{0,1:T(8,128)(2,1)S(1)}, u32[]{:S(2)}, u32[]{:S(2)}) %collective-permute-start.12) | collective-permute-done | bytes 131104 | tf_op jit(solution)/shard_map/ppermute | solution.py:134
  111.3 8.8 %while.58 = (s32[]{:T(128)}, f32[512]{0:T(512)S(1)}, f32[512]{0:T(512)S(1)}, f32[512,64]{0,1:T(8,128)S(1)}, s32[4]{0:T(128)S(1)}, /*index=5*/bf16[4,512,128]{2,1...) while((s32[]{:T(128)}, f32[512]{0:T(512)S(1)}, ...), condition=%wide.region_17.18_spmd, body=%wide.region_12.17_spmd.sunk | while | flops 102564864 | bytes 3840267 | solution.py:62
  120.1 8.9 %while.59 = (s32[]{:T(128)}, f32[512]{0:T(512)S(1)}, f32[512]{0:T(512)S(1)}, f32[512,64]{0,1:T(8,128)S(1)}, s32[4]{0:T(128)S(1)}, /*index=5*/bf16[4,512,128]{2,1...) while((s32[]{:T(128)}, f32[512]{0:T(512)S(1)}, ...), condition=%wide.region_23.24_spmd, body=%wide.region_18.23_spmd.sunk | while | flops 102564864 | bytes 3840267 | solution.py:62
  129.1 9.9 %collective-permute-start.13 = (f32[512,66]{0,1:T(8,128)S(1)}, f32[512,66]{0,1:T(8,128)S(1)}, u32[]{:S(2)}, u32[]{:S(2)}) collective-permute-start(f32[512,66]{0,1:T(8,128)S(1)} %get-tuple-element.690), channel_id=1, source_target_pairs={{0,8},{1,9},{2,10},{3,11},{4,12},{5,13},{6,14},{7,15},{8,0},{9,1},... | collective-permute-start | bytes 405512 | tf_op jit(solution)/shard_map/ppermute | solution.py:97
  144.3 4.3 %collective-permute-done.14 = f32[256,66]{0,1:T(8,128)S(1)} collective-permute-done((f32[256,66]{0,1:T(8,128)S(1)}, f32[256,66]{0,1:T(8,128)S(1)}, u32[]{:S(2)}, u32[]{:S(2)}) %collective-permute-start.14) | collective-permute-done | bytes 67616 | tf_op jit(solution)/shard_map/ppermute | solution.py:97
  150.6 4.8 %collective-permute-done.15 = f32[128,66]{0,1:T(8,128)S(1)} collective-permute-done((f32[128,66]{0,1:T(8,128)S(1)}, f32[128,66]{0,1:T(8,128)S(1)}, u32[]{:S(2)}, u32[]{:S(2)}) %collective-permute-start.15) | collective-permute-done | bytes 33824 | tf_op jit(solution)/shard_map/ppermute | solution.py:97
  157.5 8.1 %collective-permute-done.16 = f32[64,66]{0,1:T(8,128)S(1)} collective-permute-done((f32[64,66]{0,1:T(8,128)S(1)}, f32[64,66]{0,1:T(8,128)S(1)}, u32[]{:S(2)}, u32[]{:S(2)}) %collective-permute-start.16) | collective-permute-done | bytes 16928 | tf_op jit(solution)/shard_map/ppermute | solution.py:97
  167.6 7.6 %collective-permute-done.17 = bf16[64,64]{0,1:T(8,128)(2,1)S(1)} collective-permute-done((bf16[64,64]{0,1:T(8,128)(2,1)S(1)}, bf16[64,64]{0,1:T(8,128)(2,1)S(1)}, u32[]{:S(2)}, u32[]{:S(2)}) %collective-permute-start.17) | collective-permute-done | bytes 8224 | tf_op jit(solution)/shard_map/ppermute | solution.py:105
  177.4 4.4 %collective-permute-done.18 = bf16[128,64]{0,1:T(8,128)(2,1)S(1)} collective-permute-done((bf16[128,64]{0,1:T(8,128)(2,1)S(1)}, bf16[128,64]{0,1:T(8,128)(2,1)S(1)}, u32[]{:S(2)}, u32[]{:S(2)}) %collective-permute-start.18) | collective-permute-done | bytes 16416 | tf_op jit(solution)/shard_map/ppermute | solution.py:105
  183.8 3.9 %collective-permute-done.19 = bf16[256,64]{0,1:T(8,128)(2,1)S(1)} collective-permute-done((bf16[256,64]{0,1:T(8,128)(2,1)S(1)}, bf16[256,64]{0,1:T(8,128)(2,1)S(1)}, u32[]{:S(2)}, u32[]{:S(2)}) %collective-permute-start.19) | collective-permute-done | bytes 32800 | tf_op jit(solution)/shard_map/ppermute | solution.py:105
  187.7 3.9 %collective-permute-start.20 = (bf16[512,64]{0,1:T(8,128)(2,1)S(1)}, bf16[512,64]{0,1:T(8,128)(2,1)S(1)}, u32[]{:S(2)}, u32[]{:S(2)}) collective-permute-start(bf16[512,64]{0,1:T(8,128)(2,1)S(1)} %maximum_select_fusion.3), channel_id=1, source_target_pairs={{0,8},{1,9},{2,10},{3,11},{4,12},{5,13},{6,14},{7,15},{8,0},{9,1},... | collective-permute-start | bytes 196616 | tf_op jit(solution)/shard_map/ppermute | solution.py:105
  (251 shorter events, 79.4 us)
Async XLA Ops:
  0.6 21.1 %copy-start = (s32[64,64]{1,0:T(8,128)S(1)}, s32[64,64]{1,0:T(8,128)}, u32[]{:S(2)}) copy-start(s32[64,64]{1,0:T(8,128)} %param.32) | copy-start | bytes 49156
  0.6 38.3 %collective-permute-start = (bf16[1024,128]{1,0:T(8,128)(2,1)}, bf16[1024,128]{1,0:T(8,128)(2,1)S(1)}, u32[]{:S(2)}, u32[]{:S(2)}) collective-permute-start(bf16[1024,128]{1,0:T(8,128)(2,1)} %param.29), channel_id=1, source_target_pairs={{16,0},{49,1},{82,2},{115,3},{148,4},{181,5},{214,6},{247,7},{280,... | collective-permute-start | bytes 786440 | tf_op jit(solution)/shard_map/ppermute | solution.py:134
  4.1 34.9 %collective-permute-start.1 = (bf16[1024,128]{1,0:T(8,128)(2,1)}, bf16[1024,128]{1,0:T(8,128)(2,1)S(1)}, u32[]{:S(2)}, u32[]{:S(2)}) collective-permute-start(bf16[1024,128]{1,0:T(8,128)(2,1)} %param.29), channel_id=1, source_target_pairs={{0,0},{33,1},{66,2},{99,3},{132,4},{165,5},{198,6},{231,7},{264,8}... | collective-permute-start | bytes 786440 | tf_op jit(solution)/shard_map/ppermute | solution.py:134
  7.4 31.6 %collective-permute-start.2 = (bf16[2048]{0:T(1024)(128)(2,1)}, bf16[2048]{0:T(1024)(128)(2,1)S(1)}, u32[]{:S(2)}, u32[]{:S(2)}) collective-permute-start(bf16[2048]{0:T(1024)(128)(2,1)} %param.30), channel_id=1, source_target_pairs={{0,0},{1,1},{2,2},{3,3},{4,4},{5,5},{6,6},{7,7},{8,8},{9,9},{10,10... | collective-permute-start | bytes 12296 | tf_op jit(solution)/shard_map/ppermute | solution.py:150
  39.2 8.6 %collective-permute-start.3 = (f32[512,66]{0,1:T(8,128)S(1)}, f32[512,66]{0,1:T(8,128)S(1)}, u32[]{:S(2)}, u32[]{:S(2)}) collective-permute-start(f32[512,66]{0,1:T(8,128)S(1)} %get-tuple-element.692), channel_id=1, source_target_pairs={{0,8},{1,9},{2,10},{3,11},{4,12},{5,13},{6,14},{7,15},{8,0},{9,1},... | collective-permute-start | bytes 405512 | tf_op jit(solution)/shard_map/ppermute | solution.py:97
  47.8 6.4 %collective-permute-start.4 = (f32[256,66]{0,1:T(8,128)S(1)}, f32[256,66]{0,1:T(8,128)S(1)}, u32[]{:S(2)}, u32[]{:S(2)}) collective-permute-start(f32[256,66]{0,1:T(8,128)S(1)} %get-tuple-element.702), channel_id=1, source_target_pairs={{0,1},{1,0},{2,3},{3,2},{4,5},{5,4},{6,7},{7,6},{8,9},{9,8},{10,11... | collective-permute-start | bytes 202760 | tf_op jit(solution)/shard_map/ppermute | solution.py:97
  54.3 6.8 %collective-permute-start.5 = (f32[128,66]{0,1:T(8,128)S(1)}, f32[128,66]{0,1:T(8,128)S(1)}, u32[]{:S(2)}, u32[]{:S(2)}) collective-permute-start(f32[128,66]{0,1:T(8,128)S(1)} %get-tuple-element.706), channel_id=1, source_target_pairs={{0,2},{1,3},{2,0},{3,1},{4,6},{5,7},{6,4},{7,5},{8,10},{9,11},{10,... | collective-permute-start | bytes 101384 | tf_op jit(solution)/shard_map/ppermute | solution.py:97
  61.1 28.6 %copy-start.3 = (bf16[1024,128]{1,0:T(8,128)(2,1)S(1)}, bf16[1024,128]{1,0:T(8,128)(2,1)}, u32[]{:S(2)}) copy-start(bf16[1024,128]{1,0:T(8,128)(2,1)} %param.33) | copy-start | bytes 786436
  61.2 10.0 %collective-permute-start.6 = (f32[64,66]{0,1:T(8,128)S(1)}, f32[64,66]{0,1:T(8,128)S(1)}, u32[]{:S(2)}, u32[]{:S(2)}) collective-permute-start(f32[64,66]{0,1:T(8,128)S(1)} %get-tuple-element.715), channel_id=1, source_target_pairs={{0,4},{1,5},{2,6},{3,7},{4,0},{5,1},{6,2},{7,3},{8,12},{9,13},{10,... | collective-permute-start | bytes 50696 | tf_op jit(solution)/shard_map/ppermute | solution.py:97
  71.3 9.8 %collective-permute-start.7 = (bf16[64,64]{0,1:T(8,128)(2,1)S(1)}, bf16[64,64]{0,1:T(8,128)(2,1)S(1)}, u32[]{:S(2)}, u32[]{:S(2)}) collective-permute-start(bf16[64,64]{0,1:T(8,128)(2,1)S(1)} %fusion.59), channel_id=1, source_target_pairs={{0,4},{1,5},{2,6},{3,7},{4,0},{5,1},{6,2},{7,3},{8,12},{9,13},{10,... | collective-permute-start | bytes 24584 | tf_op jit(solution)/shard_map/ppermute | solution.py:105
  81.2 6.5 %collective-permute-start.8 = (bf16[128,64]{0,1:T(8,128)(2,1)S(1)}, bf16[128,64]{0,1:T(8,128)(2,1)S(1)}, u32[]{:S(2)}, u32[]{:S(2)}) collective-permute-start(bf16[128,64]{0,1:T(8,128)(2,1)S(1)} %maximum_select_fusion.6), channel_id=1, source_target_pairs={{0,2},{1,3},{2,0},{3,1},{4,6},{5,7},{6,4},{7,5},{8,10},{9,11},{10,... | collective-permute-start | bytes 49160 | tf_op jit(solution)/shard_map/ppermute | solution.py:105
  87.7 5.8 %collective-permute-start.9 = (bf16[256,64]{0,1:T(8,128)(2,1)S(1)}, bf16[256,64]{0,1:T(8,128)(2,1)S(1)}, u32[]{:S(2)}, u32[]{:S(2)}) collective-permute-start(bf16[256,64]{0,1:T(8,128)(2,1)S(1)} %maximum_select_fusion.4), channel_id=1, source_target_pairs={{0,1},{1,0},{2,3},{3,2},{4,5},{5,4},{6,7},{7,6},{8,9},{9,8},{10,11... | collective-permute-start | bytes 98312 | tf_op jit(solution)/shard_map/ppermute | solution.py:105
  93.5 6.2 %collective-permute-start.10 = (bf16[512,64]{0,1:T(8,128)(2,1)S(1)}, bf16[512,64]{0,1:T(8,128)(2,1)S(1)}, u32[]{:S(2)}, u32[]{:S(2)}) collective-permute-start(bf16[512,64]{0,1:T(8,128)(2,1)S(1)} %maximum_select_fusion.2), channel_id=1, source_target_pairs={{0,8},{1,9},{2,10},{3,11},{4,12},{5,13},{6,14},{7,15},{8,0},{9,1},... | collective-permute-start | bytes 196616 | tf_op jit(solution)/shard_map/ppermute | solution.py:105
  99.7 11.2 %copy-start.6 = (bf16[1024,64]{0,1:T(8,128)(2,1)}, bf16[1024,64]{0,1:T(8,128)(2,1)S(1)}, u32[]{:S(2)}) copy-start(bf16[1024,64]{0,1:T(8,128)(2,1)S(1)} %maximum_select_fusion) | copy-start | bytes 393220
  99.7 7.8 %collective-permute-start.11 = (bf16[1024,64]{0,1:T(8,128)(2,1)S(1)}, bf16[1024,64]{0,1:T(8,128)(2,1)S(1)}, u32[]{:S(2)}, u32[]{:S(2)}) collective-permute-start(bf16[1024,64]{0,1:T(8,128)(2,1)S(1)} %maximum_select_fusion), channel_id=1, source_target_pairs={{16,0},{49,1},{82,2},{115,3},{148,4},{181,5},{214,6},{247,7},{280,... | collective-permute-start | bytes 393224 | tf_op jit(solution)/shard_map/ppermute | solution.py:134
  101.7 9.2 %collective-permute-start.12 = (bf16[1024,64]{0,1:T(8,128)(2,1)S(1)}, bf16[1024,64]{0,1:T(8,128)(2,1)S(1)}, u32[]{:S(2)}, u32[]{:S(2)}) collective-permute-start(bf16[1024,64]{0,1:T(8,128)(2,1)S(1)} %maximum_select_fusion), channel_id=1, source_target_pairs={{0,0},{33,1},{66,2},{99,3},{132,4},{165,5},{198,6},{231,7},{264,8}... | collective-permute-start | bytes 393224 | tf_op jit(solution)/shard_map/ppermute | solution.py:134
  129.1 13.1 %collective-permute-start.13 = (f32[512,66]{0,1:T(8,128)S(1)}, f32[512,66]{0,1:T(8,128)S(1)}, u32[]{:S(2)}, u32[]{:S(2)}) collective-permute-start(f32[512,66]{0,1:T(8,128)S(1)} %get-tuple-element.690), channel_id=1, source_target_pairs={{0,8},{1,9},{2,10},{3,11},{4,12},{5,13},{6,14},{7,15},{8,0},{9,1},... | collective-permute-start | bytes 405512 | tf_op jit(solution)/shard_map/ppermute | solution.py:97
  142.3 6.4 %collective-permute-start.14 = (f32[256,66]{0,1:T(8,128)S(1)}, f32[256,66]{0,1:T(8,128)S(1)}, u32[]{:S(2)}, u32[]{:S(2)}) collective-permute-start(f32[256,66]{0,1:T(8,128)S(1)} %get-tuple-element.700), channel_id=1, source_target_pairs={{0,1},{1,0},{2,3},{3,2},{4,5},{5,4},{6,7},{7,6},{8,9},{9,8},{10,11... | collective-permute-start | bytes 202760 | tf_op jit(solution)/shard_map/ppermute | solution.py:97
  148.7 6.8 %collective-permute-start.15 = (f32[128,66]{0,1:T(8,128)S(1)}, f32[128,66]{0,1:T(8,128)S(1)}, u32[]{:S(2)}, u32[]{:S(2)}) collective-permute-start(f32[128,66]{0,1:T(8,128)S(1)} %get-tuple-element.704), channel_id=1, source_target_pairs={{0,2},{1,3},{2,0},{3,1},{4,6},{5,7},{6,4},{7,5},{8,10},{9,11},{10,... | collective-permute-start | bytes 101384 | tf_op jit(solution)/shard_map/ppermute | solution.py:97
  155.6 10.0 %collective-permute-start.16 = (f32[64,66]{0,1:T(8,128)S(1)}, f32[64,66]{0,1:T(8,128)S(1)}, u32[]{:S(2)}, u32[]{:S(2)}) collective-permute-start(f32[64,66]{0,1:T(8,128)S(1)} %get-tuple-element.713), channel_id=1, source_target_pairs={{0,4},{1,5},{2,6},{3,7},{4,0},{5,1},{6,2},{7,3},{8,12},{9,13},{10,... | collective-permute-start | bytes 50696 | tf_op jit(solution)/shard_map/ppermute | solution.py:97
  165.7 9.5 %collective-permute-start.17 = (bf16[64,64]{0,1:T(8,128)(2,1)S(1)}, bf16[64,64]{0,1:T(8,128)(2,1)S(1)}, u32[]{:S(2)}, u32[]{:S(2)}) collective-permute-start(bf16[64,64]{0,1:T(8,128)(2,1)S(1)} %fusion.57), channel_id=1, source_target_pairs={{0,4},{1,5},{2,6},{3,7},{4,0},{5,1},{6,2},{7,3},{8,12},{9,13},{10,... | collective-permute-start | bytes 24584 | tf_op jit(solution)/shard_map/ppermute | solution.py:105
  175.3 6.5 %collective-permute-start.18 = (bf16[128,64]{0,1:T(8,128)(2,1)S(1)}, bf16[128,64]{0,1:T(8,128)(2,1)S(1)}, u32[]{:S(2)}, u32[]{:S(2)}) collective-permute-start(bf16[128,64]{0,1:T(8,128)(2,1)S(1)} %maximum_select_fusion.7), channel_id=1, source_target_pairs={{0,2},{1,3},{2,0},{3,1},{4,6},{5,7},{6,4},{7,5},{8,10},{9,11},{10,... | collective-permute-start | bytes 49160 | tf_op jit(solution)/shard_map/ppermute | solution.py:105
  181.9 5.8 %collective-permute-start.19 = (bf16[256,64]{0,1:T(8,128)(2,1)S(1)}, bf16[256,64]{0,1:T(8,128)(2,1)S(1)}, u32[]{:S(2)}, u32[]{:S(2)}) collective-permute-start(bf16[256,64]{0,1:T(8,128)(2,1)S(1)} %maximum_select_fusion.5), channel_id=1, source_target_pairs={{0,1},{1,0},{2,3},{3,2},{4,5},{5,4},{6,7},{7,6},{8,9},{9,8},{10,11... | collective-permute-start | bytes 98312 | tf_op jit(solution)/shard_map/ppermute | solution.py:105
  187.7 6.2 %collective-permute-start.20 = (bf16[512,64]{0,1:T(8,128)(2,1)S(1)}, bf16[512,64]{0,1:T(8,128)(2,1)S(1)}, u32[]{:S(2)}, u32[]{:S(2)}) collective-permute-start(bf16[512,64]{0,1:T(8,128)(2,1)S(1)} %maximum_select_fusion.3), channel_id=1, source_target_pairs={{0,8},{1,9},{2,10},{3,11},{4,12},{5,13},{6,14},{7,15},{8,0},{9,1},... | collective-permute-start | bytes 196616 | tf_op jit(solution)/shard_map/ppermute | solution.py:105
  (5 other events, 9.6 us)

commit v3 on v2

--- a/solution.py
+++ b/solution.py
@@ -8,9 +8,6 @@
 
 sharpness = 3.5
 very_low = -1e30
-
-HALVING_BITS = (3, 0, 1, 2)
-
 
 def date_partials(targets, sources, offsets, values, tile_mask, col_tile_ids):
     row_count = targets.shape[0]
@@ -68,17 +65,33 @@
     return (jnp.concatenate(peaks, 0), jnp.concatenate(sums, 0), jnp.concatenate(weighted_all, 0))
 
 
-def xor_perm(size, bit):
-    return [(i, i ^ (1 << bit)) for i in range(size)]
-
-
-def merge(mine, theirs):
-    width = mine.shape[1] - 2
-    peak_a, peak_b = mine[:, width + 1], theirs[:, width + 1]
-    peak = jnp.maximum(peak_a, peak_b)
-    scale_a = jnp.exp(peak_a - peak)
-    scale_b = jnp.exp(peak_b - peak)
-    body = mine[:, : width + 1] * scale_a[:, None] + theirs[:, : width + 1] * scale_b[:, None]
+DIGIT_GROUPS = ((3, 0), (1, 2))
+
+
+def digit_of(me, bits):
+    return sum(((me >> b) & 1) << i for i, b in enumerate(bits))
+
+
+def partner_perm(size, bits, k):
+    pairs = []
+    for i in range(size):
+        j = i
+        for n, b in enumerate(bits):
+            if (k >> n) & 1:
+                j ^= 1 << b
+        pairs.append((i, j))
+    return pairs
+
+
+def merge_all(parts):
+    width = parts[0].shape[1] - 2
+    peaks = [p[:, width + 1] for p in parts]
+    peak = peaks[0]
+    for other in peaks[1:]:
+        peak = jnp.maximum(peak, other)
+    body = parts[0][:, : width + 1] * jnp.exp(peaks[0] - peak)[:, None]
+    for p, pk in zip(parts[1:], peaks[1:]):
+        body = body + p[:, : width + 1] * jnp.exp(pk - peak)[:, None]
     return jnp.concatenate([body, peak[:, None]], axis=1)
 
 
@@ -88,26 +101,29 @@
     me = lax.axis_index("src")
     packed = jnp.concatenate([weighted, weight_sum[:, None], row_peak[:, None]], axis=1)
     exercise = exercise.astype(jnp.float32)
-    for bit in HALVING_BITS:
-        half = packed.shape[0] // 2
-        mine_hi = (me >> bit) & 1
-        low, high = packed[:half], packed[half:]
-        keep = jnp.where(mine_hi == 1, high, low)
-        send = jnp.where(mine_hi == 1, low, high)
-        got = lax.ppermute(send, "src", xor_perm(src_size, bit))
-        packed = merge(keep, got)
-        exercise = jnp.where(mine_hi == 1, exercise[half:], exercise[:half])
+    for bits in DIGIT_GROUPS:
+        radix = 1 << len(bits)
+        rows = packed.shape[0] // radix
+        d = digit_of(me, bits)
+        parts = [lax.dynamic_slice_in_dim(packed, d * rows, rows, 0)]
+        for k in range(1, radix):
+            send = lax.dynamic_slice_in_dim(packed, (d ^ k) * rows, rows, 0)
+            parts.append(lax.ppermute(send, "src", partner_perm(src_size, bits, k)))
+        packed = merge_all(parts)
+        exercise = lax.dynamic_slice_in_dim(exercise, d * rows, rows, 0)
     width = packed.shape[1] - 2
     continuation = packed[:, :width] / packed[:, width : width + 1]
     value = jnp.maximum(continuation, exercise).astype(jnp.bfloat16)
-    for bit in reversed(HALVING_BITS):
-        mine_hi = (me >> bit) & 1
-        got = lax.ppermute(value, "src", xor_perm(src_size, bit))
-        value = jnp.where(
-            mine_hi == 1,
-            jnp.concatenate([got, value], 0),
-            jnp.concatenate([value, got], 0),
-        )
+    for bits in reversed(DIGIT_GROUPS):
+        radix = 1 << len(bits)
+        rows = value.shape[0]
+        d = digit_of(me, bits)
+        whole = jnp.zeros((rows * radix, value.shape[1]), value.dtype)
+        whole = lax.dynamic_update_slice_in_dim(whole, value, d * rows, 0)
+        for k in range(1, radix):
+            got = lax.ppermute(value, "src", partner_perm(src_size, bits, k))
+            whole = lax.dynamic_update_slice_in_dim(whole, got, (d ^ k) * rows, 0)
+        value = whole
     return value
 
 

time: 196 us -> 197 us (level)
  the two profiles are of different devices: /device:TPU:146 before, /device:TPU:12 now
where the time goes in v3:
time: 197 us; the launch traced here: 196 us
  starting transfers between devices  121 us (61%)
  waiting for transfers between devices  34.7 us (18%)
  local copies, waits for them, and re-layouts  18.2 us (9%)
  loops' own time  11.2 us (6%)
  matrix products  5.13 us (3%)
  other arithmetic  4.28 us (2%)
    ppermute x12, starting transfers between devices, finish(): parts.append(lax.ppermute(send, 'src', partner_perm(src_size, bits, k)))  64.4 us
    ppermute x12, starting transfers between devices, finish(): got = lax.ppermute(value, 'src', partner_perm(src_size, bits, k))  43.1 us
    ppermute x12, waiting for transfers between devices, finish(): parts.append(lax.ppermute(send, 'src', partner_perm(src_size, bits, k)))  15.7 us
    ppermute x12, waiting for transfers between devices, finish(): got = lax.ppermute(value, 'src', partner_perm(src_size, bits, k))  12.8 us
    another operation x4, loops' own time, date_partials(): lax.scan(step, start, (source_tiles, offset_tiles, value_tiles, local_mas...  10.7 us
    dynamic_slice x24, local copies, waits for them, and re-layouts, date_partials(): lax.scan(step, start, (source_tiles, offset_tiles, value_tiles, local_mas...  9.8 us
    ppermute x4, starting transfers between devices, regroup(): return [lax.ppermute(block_rows, ('tgt', 'src'), p) for p in perms]  8.19 us
    ppermute x4, waiting for transfers between devices, regroup(): return [lax.ppermute(block_rows, ('tgt', 'src'), p) for p in perms]  6.28 us
  transfers between devices with their start and end apart: 29, of which 13 were waited for; matrix products, arithmetic and copies ran while one was open for 7% of the time, Pallas kernels for 0%

profile of v3, /device:TPU:12, one launch (start us, length us, event | category | flops | bytes accessed | tf_op | source)
XLA Modules:
  0.0 196.2 jit_solution(13863025184667067380)
XLA Ops:
  5.0 5.2 %collective-permute-start.2 = (bf16[2048]{0:T(1024)(128)(2,1)}, bf16[2048]{0:T(1024)(128)(2,1)S(1)}, u32[]{:S(2)}, u32[]{:S(2)}) collective-permute-start(bf16[2048]{0:T(1024)(128)(2,1)} %param.30), channel_id=1, source_target_pairs={{0,0},{1,1},{2,2},{3,3},{4,4},{5,5},{6,6},{7,7},{8,8},{9,9},{10,10... | collective-permute-start | bytes 12296 | tf_op jit(solution)/shard_map/ppermute | solution.py:166
  15.6 6.1 %while.56 = (s32[]{:T(128)}, f32[512]{0:T(512)S(1)}, f32[512]{0:T(512)S(1)}, f32[512,64]{0,1:T(8,128)S(1)}, s32[4]{0:T(128)S(1)}, /*index=5*/bf16[4,512,128]{2,1...) while((s32[]{:T(128)}, f32[512]{0:T(512)S(1)}, ...), condition=%wide.region_5.6_spmd, body=%wide.region_0.5_spmd.sunk | while | flops 102564864 | bytes 3840267 | solution.py:59
  21.8 6.0 %while.57 = (s32[]{:T(128)}, f32[512]{0:T(512)S(1)}, f32[512]{0:T(512)S(1)}, f32[512,64]{0,1:T(8,128)S(1)}, s32[4]{0:T(128)S(1)}, /*index=5*/bf16[4,512,128]{2,1...) while((s32[]{:T(128)}, f32[512]{0:T(512)S(1)}, ...), condition=%wide.region_11.12_spmd, body=%wide.region_6.11_spmd.sunk | while | flops 102564864 | bytes 3840267 | solution.py:59
  28.1 15.4 %collective-permute-start.3 = (f32[256,66]{0,1:T(8,128)S(1)}, f32[256,66]{0,1:T(8,128)S(1)}, u32[]{:S(2)}, u32[]{:S(2)}) collective-permute-start(f32[256,66]{0,1:T(8,128)S(1)} %get-tuple-element.689), channel_id=1, source_target_pairs={{0,8},{1,9},{2,10},{3,11},{4,12},{5,13},{6,14},{7,15},{8,0},{9,1},... | collective-permute-start | bytes 202760 | tf_op jit(solution)/shard_map/ppermute | solution.py:111
  45.5 3.4 %collective-permute-start.5 = (f32[256,66]{0,1:T(8,128)S(1)}, f32[256,66]{0,1:T(8,128)S(1)}, u32[]{:S(2)}, u32[]{:S(2)}) collective-permute-start(f32[256,66]{0,1:T(8,128)S(1)} %get-tuple-element.690), channel_id=1, source_target_pairs={{0,9},{1,8},{2,11},{3,10},{4,13},{5,12},{6,15},{7,14},{8,1},{9,0},... | collective-permute-start | bytes 202760 | tf_op jit(solution)/shard_map/ppermute | solution.py:111
  54.8 7.2 %collective-permute-start.7 = (f32[64,66]{0,1:T(8,128)S(1)}, f32[64,66]{0,1:T(8,128)S(1)}, u32[]{:S(2)}, u32[]{:S(2)}) collective-permute-start(f32[64,66]{0,1:T(8,128)S(1)} %get-tuple-element.704), channel_id=1, source_target_pairs={{0,4},{1,5},{2,6},{3,7},{4,0},{5,1},{6,2},{7,3},{8,12},{9,13},{10,... | collective-permute-start | bytes 50696 | tf_op jit(solution)/shard_map/ppermute | solution.py:111
  62.0 3.1 %collective-permute-start.8 = (f32[64,66]{0,1:T(8,128)S(1)}, f32[64,66]{0,1:T(8,128)S(1)}, u32[]{:S(2)}, u32[]{:S(2)}) collective-permute-start(f32[64,66]{0,1:T(8,128)S(1)} %get-tuple-element.705), channel_id=1, source_target_pairs={{0,6},{1,7},{2,4},{3,5},{4,2},{5,3},{6,0},{7,1},{8,14},{9,15},{10,... | collective-permute-start | bytes 50696 | tf_op jit(solution)/shard_map/ppermute | solution.py:111
  65.2 5.2 %collective-permute-done.8 = f32[64,66]{0,1:T(8,128)S(1)} collective-permute-done((f32[64,66]{0,1:T(8,128)S(1)}, f32[64,66]{0,1:T(8,128)S(1)}, u32[]{:S(2)}, u32[]{:S(2)}) %collective-permute-start.8) | collective-permute-done | bytes 16928 | tf_op jit(solution)/shard_map/ppermute | solution.py:111
  71.3 4.4 %collective-permute-start.9 = (bf16[64,64]{0,1:T(8,128)(2,1)S(1)}, bf16[64,64]{0,1:T(8,128)(2,1)S(1)}, u32[]{:S(2)}, u32[]{:S(2)}) collective-permute-start(bf16[64,64]{0,1:T(8,128)(2,1)S(1)} %fusion.67), channel_id=1, source_target_pairs={{0,2},{1,3},{2,0},{3,1},{4,6},{5,7},{6,4},{7,5},{8,10},{9,11},{10,... | collective-permute-start | bytes 24584 | tf_op jit(solution)/shard_map/ppermute | solution.py:124
  78.3 5.3 %collective-permute-start.11 = (bf16[64,64]{0,1:T(8,128)(2,1)S(1)}, bf16[64,64]{0,1:T(8,128)(2,1)S(1)}, u32[]{:S(2)}, u32[]{:S(2)}) collective-permute-start(bf16[64,64]{0,1:T(8,128)(2,1)S(1)} %fusion.67), channel_id=1, source_target_pairs={{0,6},{1,7},{2,4},{3,5},{4,2},{5,3},{6,0},{7,1},{8,14},{9,15},{10,... | collective-permute-start | bytes 24584 | tf_op jit(solution)/shard_map/ppermute | solution.py:124
  88.8 3.8 %collective-permute-start.13 = (bf16[256,64]{0,1:T(8,128)(2,1)S(1)}, bf16[256,64]{0,1:T(8,128)(2,1)S(1)}, u32[]{:S(2)}, u32[]{:S(2)}) collective-permute-start(bf16[256,64]{0,1:T(8,128)(2,1)S(1)} %dynamic_update_slice.51), channel_id=1, source_target_pairs={{0,1},{1,0},{2,3},{3,2},{4,5},{5,4},{6,7},{7,6},{8,9},{9,8},{10,11... | collective-permute-start | bytes 98312 | tf_op jit(solution)/shard_map/ppermute | solution.py:124
  92.6 3.0 %collective-permute-start.14 = (bf16[256,64]{0,1:T(8,128)(2,1)S(1)}, bf16[256,64]{0,1:T(8,128)(2,1)S(1)}, u32[]{:S(2)}, u32[]{:S(2)}) collective-permute-start(bf16[256,64]{0,1:T(8,128)(2,1)S(1)} %dynamic_update_slice.51), channel_id=1, source_target_pairs={{0,9},{1,8},{2,11},{3,10},{4,13},{5,12},{6,15},{7,14},{8,1},{9,0},... | collective-permute-start | bytes 98312 | tf_op jit(solution)/shard_map/ppermute | solution.py:124
  95.6 3.6 %collective-permute-done.14 = bf16[256,64]{0,1:T(8,128)(2,1)S(1)} collective-permute-done((bf16[256,64]{0,1:T(8,128)(2,1)S(1)}, bf16[256,64]{0,1:T(8,128)(2,1)S(1)}, u32[]{:S(2)}, u32[]{:S(2)}) %collective-permute-start.14) | collective-permute-done | bytes 32800 | tf_op jit(solution)/shard_map/ppermute | solution.py:124
  103.2 3.6 %collective-permute-done.15 = bf16[1024,64]{0,1:T(8,128)(2,1)S(1)} collective-permute-done((bf16[1024,64]{0,1:T(8,128)(2,1)S(1)}, bf16[1024,64]{0,1:T(8,128)(2,1)S(1)}, u32[]{:S(2)}, u32[]{:S(2)}) %collective-permute-start.15) | collective-permute-done | bytes 131104 | tf_op jit(solution)/shard_map/ppermute | solution.py:150
  109.8 7.9 %while.58 = (s32[]{:T(128)}, f32[512]{0:T(512)S(1)}, f32[512]{0:T(512)S(1)}, f32[512,64]{0,1:T(8,128)S(1)}, s32[4]{0:T(128)S(1)}, /*index=5*/bf16[4,512,128]{2,1...) while((s32[]{:T(128)}, f32[512]{0:T(512)S(1)}, ...), condition=%wide.region_17.18_spmd, body=%wide.region_12.17_spmd.sunk | while | flops 102564864 | bytes 3840267 | solution.py:59
  117.8 7.9 %while.59 = (s32[]{:T(128)}, f32[512]{0:T(512)S(1)}, f32[512]{0:T(512)S(1)}, f32[512,64]{0,1:T(8,128)S(1)}, s32[4]{0:T(128)S(1)}, /*index=5*/bf16[4,512,128]{2,1...) while((s32[]{:T(128)}, f32[512]{0:T(512)S(1)}, ...), condition=%wide.region_23.24_spmd, body=%wide.region_18.23_spmd.sunk | while | flops 102564864 | bytes 3840267 | solution.py:59
  125.8 13.9 %collective-permute-start.17 = (f32[256,66]{0,1:T(8,128)S(1)}, f32[256,66]{0,1:T(8,128)S(1)}, u32[]{:S(2)}, u32[]{:S(2)}) collective-permute-start(f32[256,66]{0,1:T(8,128)S(1)} %get-tuple-element.686), channel_id=1, source_target_pairs={{0,8},{1,9},{2,10},{3,11},{4,12},{5,13},{6,14},{7,15},{8,0},{9,1},... | collective-permute-start | bytes 202760 | tf_op jit(solution)/shard_map/ppermute | solution.py:111
  141.6 3.4 %collective-permute-start.19 = (f32[256,66]{0,1:T(8,128)S(1)}, f32[256,66]{0,1:T(8,128)S(1)}, u32[]{:S(2)}, u32[]{:S(2)}) collective-permute-start(f32[256,66]{0,1:T(8,128)S(1)} %get-tuple-element.687), channel_id=1, source_target_pairs={{0,9},{1,8},{2,11},{3,10},{4,13},{5,12},{6,15},{7,14},{8,1},{9,0},... | collective-permute-start | bytes 202760 | tf_op jit(solution)/shard_map/ppermute | solution.py:111
  153.3 8.0 %collective-permute-start.22 = (f32[64,66]{0,1:T(8,128)S(1)}, f32[64,66]{0,1:T(8,128)S(1)}, u32[]{:S(2)}, u32[]{:S(2)}) collective-permute-start(f32[64,66]{0,1:T(8,128)S(1)} %get-tuple-element.701), channel_id=1, source_target_pairs={{0,6},{1,7},{2,4},{3,5},{4,2},{5,3},{6,0},{7,1},{8,14},{9,15},{10,... | collective-permute-start | bytes 50696 | tf_op jit(solution)/shard_map/ppermute | solution.py:111
  167.1 7.4 %collective-permute-start.24 = (bf16[64,64]{0,1:T(8,128)(2,1)S(1)}, bf16[64,64]{0,1:T(8,128)(2,1)S(1)}, u32[]{:S(2)}, u32[]{:S(2)}) collective-permute-start(bf16[64,64]{0,1:T(8,128)(2,1)S(1)} %fusion.65), channel_id=1, source_target_pairs={{0,4},{1,5},{2,6},{3,7},{4,0},{5,1},{6,2},{7,3},{8,12},{9,13},{10,... | collective-permute-start | bytes 24584 | tf_op jit(solution)/shard_map/ppermute | solution.py:124
  178.1 4.1 %collective-permute-done.25 = bf16[64,64]{0,1:T(8,128)(2,1)S(1)} collective-permute-done((bf16[64,64]{0,1:T(8,128)(2,1)S(1)}, bf16[64,64]{0,1:T(8,128)(2,1)S(1)}, u32[]{:S(2)}, u32[]{:S(2)}) %collective-permute-start.25) | collective-permute-done | bytes 8224 | tf_op jit(solution)/shard_map/ppermute | solution.py:124
  185.0 3.8 %collective-permute-start.27 = (bf16[256,64]{0,1:T(8,128)(2,1)S(1)}, bf16[256,64]{0,1:T(8,128)(2,1)S(1)}, u32[]{:S(2)}, u32[]{:S(2)}) collective-permute-start(bf16[256,64]{0,1:T(8,128)(2,1)S(1)} %dynamic_update_slice.59), channel_id=1, source_target_pairs={{0,1},{1,0},{2,3},{3,2},{4,5},{5,4},{6,7},{7,6},{8,9},{9,8},{10,11... | collective-permute-start | bytes 98312 | tf_op jit(solution)/shard_map/ppermute | solution.py:124
  188.8 3.3 %collective-permute-start.28 = (bf16[256,64]{0,1:T(8,128)(2,1)S(1)}, bf16[256,64]{0,1:T(8,128)(2,1)S(1)}, u32[]{:S(2)}, u32[]{:S(2)}) collective-permute-start(bf16[256,64]{0,1:T(8,128)(2,1)S(1)} %dynamic_update_slice.59), channel_id=1, source_target_pairs={{0,9},{1,8},{2,11},{3,10},{4,13},{5,12},{6,15},{7,14},{8,1},{9,0},... | collective-permute-start | bytes 98312 | tf_op jit(solution)/shard_map/ppermute | solution.py:124
  192.1 3.4 %collective-permute-done.28 = bf16[256,64]{0,1:T(8,128)(2,1)S(1)} collective-permute-done((bf16[256,64]{0,1:T(8,128)(2,1)S(1)}, bf16[256,64]{0,1:T(8,128)(2,1)S(1)}, u32[]{:S(2)}, u32[]{:S(2)}) %collective-permute-start.28) | collective-permute-done | bytes 32800 | tf_op jit(solution)/shard_map/ppermute | solution.py:124
  (222 shorter events, 80.3 us)
Async XLA Ops:
  0.6 27.2 %collective-permute-start = (bf16[1024,128]{1,0:T(8,128)(2,1)}, bf16[1024,128]{1,0:T(8,128)(2,1)S(1)}, u32[]{:S(2)}, u32[]{:S(2)}) collective-permute-start(bf16[1024,128]{1,0:T(8,128)(2,1)} %param.29), channel_id=1, source_target_pairs={{16,0},{49,1},{82,2},{115,3},{148,4},{181,5},{214,6},{247,7},{280,... | collective-permute-start | bytes 786440 | tf_op jit(solution)/shard_map/ppermute | solution.py:150
  2.6 25.3 %collective-permute-start.1 = (bf16[1024,128]{1,0:T(8,128)(2,1)}, bf16[1024,128]{1,0:T(8,128)(2,1)S(1)}, u32[]{:S(2)}, u32[]{:S(2)}) collective-permute-start(bf16[1024,128]{1,0:T(8,128)(2,1)} %param.29), channel_id=1, source_target_pairs={{0,0},{33,1},{66,2},{99,3},{132,4},{165,5},{198,6},{231,7},{264,8}... | collective-permute-start | bytes 786440 | tf_op jit(solution)/shard_map/ppermute | solution.py:150
  5.0 23.0 %collective-permute-start.2 = (bf16[2048]{0:T(1024)(128)(2,1)}, bf16[2048]{0:T(1024)(128)(2,1)S(1)}, u32[]{:S(2)}, u32[]{:S(2)}) collective-permute-start(bf16[2048]{0:T(1024)(128)(2,1)} %param.30), channel_id=1, source_target_pairs={{0,0},{1,1},{2,2},{3,3},{4,4},{5,5},{6,6},{7,7},{8,8},{9,9},{10,10... | collective-permute-start | bytes 12296 | tf_op jit(solution)/shard_map/ppermute | solution.py:166
  28.1 20.8 %collective-permute-start.3 = (f32[256,66]{0,1:T(8,128)S(1)}, f32[256,66]{0,1:T(8,128)S(1)}, u32[]{:S(2)}, u32[]{:S(2)}) collective-permute-start(f32[256,66]{0,1:T(8,128)S(1)} %get-tuple-element.689), channel_id=1, source_target_pairs={{0,8},{1,9},{2,10},{3,11},{4,12},{5,13},{6,14},{7,15},{8,0},{9,1},... | collective-permute-start | bytes 202760 | tf_op jit(solution)/shard_map/ppermute | solution.py:111
  45.5 7.1 %collective-permute-start.5 = (f32[256,66]{0,1:T(8,128)S(1)}, f32[256,66]{0,1:T(8,128)S(1)}, u32[]{:S(2)}, u32[]{:S(2)}) collective-permute-start(f32[256,66]{0,1:T(8,128)S(1)} %get-tuple-element.690), channel_id=1, source_target_pairs={{0,9},{1,8},{2,11},{3,10},{4,13},{5,12},{6,15},{7,14},{8,1},{9,0},... | collective-permute-start | bytes 202760 | tf_op jit(solution)/shard_map/ppermute | solution.py:111
  52.9 12.3 %collective-permute-start.6 = (f32[64,66]{0,1:T(8,128)S(1)}, f32[64,66]{0,1:T(8,128)S(1)}, u32[]{:S(2)}, u32[]{:S(2)}) collective-permute-start(f32[64,66]{0,1:T(8,128)S(1)} %get-tuple-element.703), channel_id=1, source_target_pairs={{0,2},{1,3},{2,0},{3,1},{4,6},{5,7},{6,4},{7,5},{8,10},{9,11},{10,... | collective-permute-start | bytes 50696 | tf_op jit(solution)/shard_map/ppermute | solution.py:111
  54.8 10.3 %collective-permute-start.7 = (f32[64,66]{0,1:T(8,128)S(1)}, f32[64,66]{0,1:T(8,128)S(1)}, u32[]{:S(2)}, u32[]{:S(2)}) collective-permute-start(f32[64,66]{0,1:T(8,128)S(1)} %get-tuple-element.704), channel_id=1, source_target_pairs={{0,4},{1,5},{2,6},{3,7},{4,0},{5,1},{6,2},{7,3},{8,12},{9,13},{10,... | collective-permute-start | bytes 50696 | tf_op jit(solution)/shard_map/ppermute | solution.py:111
  62.0 8.4 %collective-permute-start.8 = (f32[64,66]{0,1:T(8,128)S(1)}, f32[64,66]{0,1:T(8,128)S(1)}, u32[]{:S(2)}, u32[]{:S(2)}) collective-permute-start(f32[64,66]{0,1:T(8,128)S(1)} %get-tuple-element.705), channel_id=1, source_target_pairs={{0,6},{1,7},{2,4},{3,5},{4,2},{5,3},{6,0},{7,1},{8,14},{9,15},{10,... | collective-permute-start | bytes 50696 | tf_op jit(solution)/shard_map/ppermute | solution.py:111
  71.3 12.5 %collective-permute-start.9 = (bf16[64,64]{0,1:T(8,128)(2,1)S(1)}, bf16[64,64]{0,1:T(8,128)(2,1)S(1)}, u32[]{:S(2)}, u32[]{:S(2)}) collective-permute-start(bf16[64,64]{0,1:T(8,128)(2,1)S(1)} %fusion.67), channel_id=1, source_target_pairs={{0,2},{1,3},{2,0},{3,1},{4,6},{5,7},{6,4},{7,5},{8,10},{9,11},{10,... | collective-permute-start | bytes 24584 | tf_op jit(solution)/shard_map/ppermute | solution.py:124
  75.7 9.6 %collective-permute-start.10 = (bf16[64,64]{0,1:T(8,128)(2,1)S(1)}, bf16[64,64]{0,1:T(8,128)(2,1)S(1)}, u32[]{:S(2)}, u32[]{:S(2)}) collective-permute-start(bf16[64,64]{0,1:T(8,128)(2,1)S(1)} %fusion.67), channel_id=1, source_target_pairs={{0,4},{1,5},{2,6},{3,7},{4,0},{5,1},{6,2},{7,3},{8,12},{9,13},{10,... | collective-permute-start | bytes 24584 | tf_op jit(solution)/shard_map/ppermute | solution.py:124
  78.3 7.7 %collective-permute-start.11 = (bf16[64,64]{0,1:T(8,128)(2,1)S(1)}, bf16[64,64]{0,1:T(8,128)(2,1)S(1)}, u32[]{:S(2)}, u32[]{:S(2)}) collective-permute-start(bf16[64,64]{0,1:T(8,128)(2,1)S(1)} %fusion.67), channel_id=1, source_target_pairs={{0,6},{1,7},{2,4},{3,5},{4,2},{5,3},{6,0},{7,1},{8,14},{9,15},{10,... | collective-permute-start | bytes 24584 | tf_op jit(solution)/shard_map/ppermute | solution.py:124
  86.3 9.3 %collective-permute-start.12 = (bf16[256,64]{0,1:T(8,128)(2,1)S(1)}, bf16[256,64]{0,1:T(8,128)(2,1)S(1)}, u32[]{:S(2)}, u32[]{:S(2)}) collective-permute-start(bf16[256,64]{0,1:T(8,128)(2,1)S(1)} %dynamic_update_slice.51), channel_id=1, source_target_pairs={{0,8},{1,9},{2,10},{3,11},{4,12},{5,13},{6,14},{7,15},{8,0},{9,1},... | collective-permute-start | bytes 98312 | tf_op jit(solution)/shard_map/ppermute | solution.py:124
  99.3 7.5 %collective-permute-start.15 = (bf16[1024,64]{0,1:T(8,128)(2,1)S(1)}, bf16[1024,64]{0,1:T(8,128)(2,1)S(1)}, u32[]{:S(2)}, u32[]{:S(2)}) collective-permute-start(bf16[1024,64]{0,1:T(8,128)(2,1)S(1)} %constant_dynamic-update-slice_fusion.4), channel_id=1, source_target_pairs={{16,0},{49,1},{82,2},{115,3},{148,4},{181,5},{214,6},{247,7},{280,... | collective-permute-start | bytes 393224 | tf_op jit(solution)/shard_map/ppermute | solution.py:150
  101.2 8.3 %collective-permute-start.16 = (bf16[1024,64]{0,1:T(8,128)(2,1)S(1)}, bf16[1024,64]{0,1:T(8,128)(2,1)S(1)}, u32[]{:S(2)}, u32[]{:S(2)}) collective-permute-start(bf16[1024,64]{0,1:T(8,128)(2,1)S(1)} %constant_dynamic-update-slice_fusion.4), channel_id=1, source_target_pairs={{0,0},{33,1},{66,2},{99,3},{132,4},{165,5},{198,6},{231,7},{264,8}... | collective-permute-start | bytes 393224 | tf_op jit(solution)/shard_map/ppermute | solution.py:150
  125.8 19.2 %collective-permute-start.17 = (f32[256,66]{0,1:T(8,128)S(1)}, f32[256,66]{0,1:T(8,128)S(1)}, u32[]{:S(2)}, u32[]{:S(2)}) collective-permute-start(f32[256,66]{0,1:T(8,128)S(1)} %get-tuple-element.686), channel_id=1, source_target_pairs={{0,8},{1,9},{2,10},{3,11},{4,12},{5,13},{6,14},{7,15},{8,0},{9,1},... | collective-permute-start | bytes 202760 | tf_op jit(solution)/shard_map/ppermute | solution.py:111
  141.6 7.2 %collective-permute-start.19 = (f32[256,66]{0,1:T(8,128)S(1)}, f32[256,66]{0,1:T(8,128)S(1)}, u32[]{:S(2)}, u32[]{:S(2)}) collective-permute-start(f32[256,66]{0,1:T(8,128)S(1)} %get-tuple-element.687), channel_id=1, source_target_pairs={{0,9},{1,8},{2,11},{3,10},{4,13},{5,12},{6,15},{7,14},{8,1},{9,0},... | collective-permute-start | bytes 202760 | tf_op jit(solution)/shard_map/ppermute | solution.py:111
  149.1 12.2 %collective-permute-start.20 = (f32[64,66]{0,1:T(8,128)S(1)}, f32[64,66]{0,1:T(8,128)S(1)}, u32[]{:S(2)}, u32[]{:S(2)}) collective-permute-start(f32[64,66]{0,1:T(8,128)S(1)} %get-tuple-element.699), channel_id=1, source_target_pairs={{0,2},{1,3},{2,0},{3,1},{4,6},{5,7},{6,4},{7,5},{8,10},{9,11},{10,... | collective-permute-start | bytes 50696 | tf_op jit(solution)/shard_map/ppermute | solution.py:111
  151.0 10.3 %collective-permute-start.21 = (f32[64,66]{0,1:T(8,128)S(1)}, f32[64,66]{0,1:T(8,128)S(1)}, u32[]{:S(2)}, u32[]{:S(2)}) collective-permute-start(f32[64,66]{0,1:T(8,128)S(1)} %get-tuple-element.700), channel_id=1, source_target_pairs={{0,4},{1,5},{2,6},{3,7},{4,0},{5,1},{6,2},{7,3},{8,12},{9,13},{10,... | collective-permute-start | bytes 50696 | tf_op jit(solution)/shard_map/ppermute | solution.py:111
  153.3 10.9 %collective-permute-start.22 = (f32[64,66]{0,1:T(8,128)S(1)}, f32[64,66]{0,1:T(8,128)S(1)}, u32[]{:S(2)}, u32[]{:S(2)}) collective-permute-start(f32[64,66]{0,1:T(8,128)S(1)} %get-tuple-element.701), channel_id=1, source_target_pairs={{0,6},{1,7},{2,4},{3,5},{4,2},{5,3},{6,0},{7,1},{8,14},{9,15},{10,... | collective-permute-start | bytes 50696 | tf_op jit(solution)/shard_map/ppermute | solution.py:111
  165.1 12.4 %collective-permute-start.23 = (bf16[64,64]{0,1:T(8,128)(2,1)S(1)}, bf16[64,64]{0,1:T(8,128)(2,1)S(1)}, u32[]{:S(2)}, u32[]{:S(2)}) collective-permute-start(bf16[64,64]{0,1:T(8,128)(2,1)S(1)} %fusion.65), channel_id=1, source_target_pairs={{0,2},{1,3},{2,0},{3,1},{4,6},{5,7},{6,4},{7,5},{8,10},{9,11},{10,... | collective-permute-start | bytes 24584 | tf_op jit(solution)/shard_map/ppermute | solution.py:124
  167.1 10.9 %collective-permute-start.24 = (bf16[64,64]{0,1:T(8,128)(2,1)S(1)}, bf16[64,64]{0,1:T(8,128)(2,1)S(1)}, u32[]{:S(2)}, u32[]{:S(2)}) collective-permute-start(bf16[64,64]{0,1:T(8,128)(2,1)S(1)} %fusion.65), channel_id=1, source_target_pairs={{0,4},{1,5},{2,6},{3,7},{4,0},{5,1},{6,2},{7,3},{8,12},{9,13},{10,... | collective-permute-start | bytes 24584 | tf_op jit(solution)/shard_map/ppermute | solution.py:124
  174.5 7.7 %collective-permute-start.25 = (bf16[64,64]{0,1:T(8,128)(2,1)S(1)}, bf16[64,64]{0,1:T(8,128)(2,1)S(1)}, u32[]{:S(2)}, u32[]{:S(2)}) collective-permute-start(bf16[64,64]{0,1:T(8,128)(2,1)S(1)} %fusion.65), channel_id=1, source_target_pairs={{0,6},{1,7},{2,4},{3,5},{4,2},{5,3},{6,0},{7,1},{8,14},{9,15},{10,... | collective-permute-start | bytes 24584 | tf_op jit(solution)/shard_map/ppermute | solution.py:124
  182.5 9.6 %collective-permute-start.26 = (bf16[256,64]{0,1:T(8,128)(2,1)S(1)}, bf16[256,64]{0,1:T(8,128)(2,1)S(1)}, u32[]{:S(2)}, u32[]{:S(2)}) collective-permute-start(bf16[256,64]{0,1:T(8,128)(2,1)S(1)} %dynamic_update_slice.59), channel_id=1, source_target_pairs={{0,8},{1,9},{2,10},{3,11},{4,12},{5,13},{6,14},{7,15},{8,0},{9,1},... | collective-permute-start | bytes 98312 | tf_op jit(solution)/shard_map/ppermute | solution.py:124
  185.0 7.1 %collective-permute-start.27 = (bf16[256,64]{0,1:T(8,128)(2,1)S(1)}, bf16[256,64]{0,1:T(8,128)(2,1)S(1)}, u32[]{:S(2)}, u32[]{:S(2)}) collective-permute-start(bf16[256,64]{0,1:T(8,128)(2,1)S(1)} %dynamic_update_slice.59), channel_id=1, source_target_pairs={{0,1},{1,0},{2,3},{3,2},{4,5},{5,4},{6,7},{7,6},{8,9},{9,8},{10,11... | collective-permute-start | bytes 98312 | tf_op jit(solution)/shard_map/ppermute | solution.py:124
  (12 other events, 75.7 us)

commit v4 on v2

--- a/solution.py
+++ b/solution.py
@@ -8,9 +8,6 @@
 
 sharpness = 3.5
 very_low = -1e30
-
-HALVING_BITS = (3, 0, 1, 2)
-
 
 def date_partials(targets, sources, offsets, values, tile_mask, col_tile_ids):
     row_count = targets.shape[0]
@@ -68,6 +65,10 @@
     return (jnp.concatenate(peaks, 0), jnp.concatenate(sums, 0), jnp.concatenate(weighted_all, 0))
 
 
+HALVING_BITS = (3,)
+EXCHANGE_BITS = (0, 1, 2)
+
+
 def xor_perm(size, bit):
     return [(i, i ^ (1 << bit)) for i in range(size)]
 
@@ -91,12 +92,12 @@
     for bit in HALVING_BITS:
         half = packed.shape[0] // 2
         mine_hi = (me >> bit) & 1
-        low, high = packed[:half], packed[half:]
-        keep = jnp.where(mine_hi == 1, high, low)
-        send = jnp.where(mine_hi == 1, low, high)
-        got = lax.ppermute(send, "src", xor_perm(src_size, bit))
-        packed = merge(keep, got)
-        exercise = jnp.where(mine_hi == 1, exercise[half:], exercise[:half])
+        keep = lax.dynamic_slice_in_dim(packed, mine_hi * half, half, 0)
+        send = lax.dynamic_slice_in_dim(packed, (1 - mine_hi) * half, half, 0)
+        packed = merge(keep, lax.ppermute(send, "src", xor_perm(src_size, bit)))
+        exercise = lax.dynamic_slice_in_dim(exercise, mine_hi * half, half, 0)
+    for bit in EXCHANGE_BITS:
+        packed = merge(packed, lax.ppermute(packed, "src", xor_perm(src_size, bit)))
     width = packed.shape[1] - 2
     continuation = packed[:, :width] / packed[:, width : width + 1]
     value = jnp.maximum(continuation, exercise).astype(jnp.bfloat16)

time: 196 us -> 167 us (0.85)
  the two profiles are of different devices: /device:TPU:146 before, /device:TPU:1 now
where the time goes in v4:
time: 167 us; the launch traced here: 166 us
  starting transfers between devices  67.2 us (40%)
  waiting for transfers between devices  56.2 us (34%)
  local copies, waits for them, and re-layouts  17 us (10%)
  loops' own time  10.3 us (6%)
  matrix products  8.98 us (5%)
  other arithmetic  4.65 us (3%)
    ppermute x6, waiting for transfers between devices, finish(): packed = merge(packed, lax.ppermute(packed, 'src', xor_perm(src_size, bit)))  44.5 us
    ppermute x2, starting transfers between devices, finish(): packed = merge(keep, lax.ppermute(send, 'src', xor_perm(src_size, bit)))  22.8 us
    ppermute x6, starting transfers between devices, finish(): packed = merge(packed, lax.ppermute(packed, 'src', xor_perm(src_size, bit)))  21.8 us
    ppermute x4, starting transfers between devices, regroup(): return [lax.ppermute(block_rows, ('tgt', 'src'), p) for p in perms]  15.4 us
    another operation x4, loops' own time, date_partials(): lax.scan(step, start, (source_tiles, offset_tiles, value_tiles, local_mas...  9.65 us
    dynamic_slice x30, local copies, waits for them, and re-layouts, date_partials(): lax.scan(step, start, (source_tiles, offset_tiles, value_tiles, local_mas...  9.58 us
    ppermute x2, waiting for transfers between devices, finish(): packed = merge(keep, lax.ppermute(send, 'src', xor_perm(src_size, bit)))  7 us
    ppermute x2, starting transfers between devices, finish(): got = lax.ppermute(value, 'src', xor_perm(src_size, bit))  5.86 us
  transfers between devices with their start and end apart: 15, of which 10 were waited for; matrix products, arithmetic and copies ran while one was open for 10% of the time, Pallas kernels for 0%

profile of v4, /device:TPU:1, one launch (start us, length us, event | category | flops | bytes accessed | tf_op | source)
XLA Modules:
  0.0 165.9 jit_solution(17668539337586787302)
XLA Ops:
  0.6 8.7 %collective-permute-start = (bf16[1024,128]{1,0:T(8,128)(2,1)}, bf16[1024,128]{1,0:T(8,128)(2,1)S(1)}, u32[]{:S(2)}, u32[]{:S(2)}) collective-permute-start(bf16[1024,128]{1,0:T(8,128)(2,1)} %param.29), channel_id=1, source_target_pairs={{16,0},{49,1},{82,2},{115,3},{148,4},{181,5},{214,6},{247,7},{280,... | collective-permute-start | bytes 786440 | tf_op jit(solution)/shard_map/ppermute | solution.py:135
  15.6 8.4 %while.56 = (s32[]{:T(128)}, f32[512]{0:T(512)S(1)}, f32[512]{0:T(512)S(1)}, f32[512,64]{0,1:T(8,128)S(1)}, s32[4]{0:T(128)S(1)}, /*index=5*/bf16[4,512,128]{2,1...) while((s32[]{:T(128)}, f32[512]{0:T(512)S(1)}, ...), condition=%wide.region_5.6_spmd, body=%wide.region_0.5_spmd.sunk | while | flops 102564864 | bytes 3840267 | solution.py:59
  24.1 7.5 %while.57 = (s32[]{:T(128)}, f32[512]{0:T(512)S(1)}, f32[512]{0:T(512)S(1)}, f32[512,64]{0,1:T(8,128)S(1)}, s32[4]{0:T(128)S(1)}, /*index=5*/bf16[4,512,128]{2,1...) while((s32[]{:T(128)}, f32[512]{0:T(512)S(1)}, ...), condition=%wide.region_11.12_spmd, body=%wide.region_6.11_spmd.sunk | while | flops 102564864 | bytes 3840267 | solution.py:59
  31.9 6.7 %collective-permute-start.3 = (f32[512,66]{0,1:T(8,128)S(1)}, f32[512,66]{0,1:T(8,128)S(1)}, u32[]{:S(2)}, u32[]{:S(2)}) collective-permute-start(f32[512,66]{0,1:T(8,128)S(1)} %constant_dynamic-slice_fusion.5), channel_id=1, source_target_pairs={{0,8},{1,9},{2,10},{3,11},{4,12},{5,13},{6,14},{7,15},{8,0},{9,1},... | collective-permute-start | bytes 405512 | tf_op jit(solution)/shard_map/ppermute | solution.py:97
  38.6 3.0 %collective-permute-done.3 = f32[512,66]{0,1:T(8,128)S(1)} collective-permute-done((f32[512,66]{0,1:T(8,128)S(1)}, f32[512,66]{0,1:T(8,128)S(1)}, u32[]{:S(2)}, u32[]{:S(2)}) %collective-permute-start.3) | collective-permute-done | bytes 135200 | tf_op jit(solution)/shard_map/ppermute | solution.py:97
  41.9 6.7 %collective-permute-start.4 = (f32[512,66]{0,1:T(8,128)S(1)}, f32[512,66]{0,1:T(8,128)S(1)}, u32[]{:S(2)}, u32[]{:S(2)}) collective-permute-start(f32[512,66]{0,1:T(8,128)S(1)} %pad_maximum_fusion.5), channel_id=1, source_target_pairs={{0,1},{1,0},{2,3},{3,2},{4,5},{5,4},{6,7},{7,6},{8,9},{9,8},{10,11... | collective-permute-start | bytes 405512 | tf_op jit(solution)/shard_map/ppermute | solution.py:100
  48.6 3.2 %collective-permute-done.4 = f32[512,66]{0,1:T(8,128)S(1)} collective-permute-done((f32[512,66]{0,1:T(8,128)S(1)}, f32[512,66]{0,1:T(8,128)S(1)}, u32[]{:S(2)}, u32[]{:S(2)}) %collective-permute-start.4) | collective-permute-done | bytes 135200 | tf_op jit(solution)/shard_map/ppermute | solution.py:100
  51.9 5.4 %collective-permute-start.5 = (f32[512,66]{0,1:T(8,128)S(1)}, f32[512,66]{0,1:T(8,128)S(1)}, u32[]{:S(2)}, u32[]{:S(2)}) collective-permute-start(f32[512,66]{0,1:T(8,128)S(1)} %pad_maximum_fusion.6), channel_id=1, source_target_pairs={{0,2},{1,3},{2,0},{3,1},{4,6},{5,7},{6,4},{7,5},{8,10},{9,11},{10,... | collective-permute-start | bytes 405512 | tf_op jit(solution)/shard_map/ppermute | solution.py:100
  57.3 7.4 %collective-permute-done.5 = f32[512,66]{0,1:T(8,128)S(1)} collective-permute-done((f32[512,66]{0,1:T(8,128)S(1)}, f32[512,66]{0,1:T(8,128)S(1)}, u32[]{:S(2)}, u32[]{:S(2)}) %collective-permute-start.5) | collective-permute-done | bytes 135200 | tf_op jit(solution)/shard_map/ppermute | solution.py:100
  64.8 1.9 %collective-permute-start.6 = (f32[512,66]{0,1:T(8,128)S(1)}, f32[512,66]{0,1:T(8,128)S(1)}, u32[]{:S(2)}, u32[]{:S(2)}) collective-permute-start(f32[512,66]{0,1:T(8,128)S(1)} %pad_maximum_fusion.7), channel_id=1, source_target_pairs={{0,4},{1,5},{2,6},{3,7},{4,0},{5,1},{6,2},{7,3},{8,12},{9,13},{10,... | collective-permute-start | bytes 405512 | tf_op jit(solution)/shard_map/ppermute | solution.py:100
  66.8 10.4 %collective-permute-done.6 = f32[512,66]{0,1:T(8,128)S(1)} collective-permute-done((f32[512,66]{0,1:T(8,128)S(1)}, f32[512,66]{0,1:T(8,128)S(1)}, u32[]{:S(2)}, u32[]{:S(2)}) %collective-permute-start.6) | collective-permute-done | bytes 135200 | tf_op jit(solution)/shard_map/ppermute | solution.py:100
  78.1 3.9 %collective-permute-start.7 = (bf16[512,64]{0,1:T(8,128)(2,1)S(1)}, bf16[512,64]{0,1:T(8,128)(2,1)S(1)}, u32[]{:S(2)}, u32[]{:S(2)}) collective-permute-start(bf16[512,64]{0,1:T(8,128)(2,1)S(1)} %fusion.55), channel_id=1, source_target_pairs={{0,8},{1,9},{2,10},{3,11},{4,12},{5,13},{6,14},{7,15},{8,0},{9,1},... | collective-permute-start | bytes 196616 | tf_op jit(solution)/shard_map/ppermute | solution.py:106
  83.7 4.4 %collective-permute-start.8 = (bf16[1024,64]{0,1:T(8,128)(2,1)S(1)}, bf16[1024,64]{0,1:T(8,128)(2,1)S(1)}, u32[]{:S(2)}, u32[]{:S(2)}) collective-permute-start(bf16[1024,64]{0,1:T(8,128)(2,1)S(1)} %maximum_select_fusion), channel_id=1, source_target_pairs={{16,0},{49,1},{82,2},{115,3},{148,4},{181,5},{214,6},{247,7},{280,... | collective-permute-start | bytes 393224 | tf_op jit(solution)/shard_map/ppermute | solution.py:135
  91.3 8.4 %while.58 = (s32[]{:T(128)}, f32[512]{0:T(512)S(1)}, f32[512]{0:T(512)S(1)}, f32[512,64]{0,1:T(8,128)S(1)}, s32[4]{0:T(128)S(1)}, /*index=5*/bf16[4,512,128]{2,1...) while((s32[]{:T(128)}, f32[512]{0:T(512)S(1)}, ...), condition=%wide.region_17.18_spmd, body=%wide.region_12.17_spmd.sunk | while | flops 102564864 | bytes 3840267 | solution.py:59
  99.8 7.5 %while.59 = (s32[]{:T(128)}, f32[512]{0:T(512)S(1)}, f32[512]{0:T(512)S(1)}, f32[512,64]{0,1:T(8,128)S(1)}, s32[4]{0:T(128)S(1)}, /*index=5*/bf16[4,512,128]{2,1...) while((s32[]{:T(128)}, f32[512]{0:T(512)S(1)}, ...), condition=%wide.region_23.24_spmd, body=%wide.region_18.23_spmd.sunk | while | flops 102564864 | bytes 3840267 | solution.py:59
  107.5 16.1 %collective-permute-start.10 = (f32[512,66]{0,1:T(8,128)S(1)}, f32[512,66]{0,1:T(8,128)S(1)}, u32[]{:S(2)}, u32[]{:S(2)}) collective-permute-start(f32[512,66]{0,1:T(8,128)S(1)} %constant_dynamic-slice_fusion.4), channel_id=1, source_target_pairs={{0,8},{1,9},{2,10},{3,11},{4,12},{5,13},{6,14},{7,15},{8,0},{9,1},... | collective-permute-start | bytes 405512 | tf_op jit(solution)/shard_map/ppermute | solution.py:97
  123.6 3.9 %collective-permute-done.10 = f32[512,66]{0,1:T(8,128)S(1)} collective-permute-done((f32[512,66]{0,1:T(8,128)S(1)}, f32[512,66]{0,1:T(8,128)S(1)}, u32[]{:S(2)}, u32[]{:S(2)}) %collective-permute-start.10) | collective-permute-done | bytes 135200 | tf_op jit(solution)/shard_map/ppermute | solution.py:97
  129.6 4.5 %collective-permute-done.11 = f32[512,66]{0,1:T(8,128)S(1)} collective-permute-done((f32[512,66]{0,1:T(8,128)S(1)}, f32[512,66]{0,1:T(8,128)S(1)}, u32[]{:S(2)}, u32[]{:S(2)}) %collective-permute-start.11) | collective-permute-done | bytes 135200 | tf_op jit(solution)/shard_map/ppermute | solution.py:100
  134.2 2.4 %collective-permute-start.12 = (f32[512,66]{0,1:T(8,128)S(1)}, f32[512,66]{0,1:T(8,128)S(1)}, u32[]{:S(2)}, u32[]{:S(2)}) collective-permute-start(f32[512,66]{0,1:T(8,128)S(1)} %pad_maximum_fusion.9), channel_id=1, source_target_pairs={{0,2},{1,3},{2,0},{3,1},{4,6},{5,7},{6,4},{7,5},{8,10},{9,11},{10,... | collective-permute-start | bytes 405512 | tf_op jit(solution)/shard_map/ppermute | solution.py:100
  136.7 9.1 %collective-permute-done.12 = f32[512,66]{0,1:T(8,128)S(1)} collective-permute-done((f32[512,66]{0,1:T(8,128)S(1)}, f32[512,66]{0,1:T(8,128)S(1)}, u32[]{:S(2)}, u32[]{:S(2)}) %collective-permute-start.12) | collective-permute-done | bytes 135200 | tf_op jit(solution)/shard_map/ppermute | solution.py:100
  145.8 3.4 %collective-permute-start.13 = (f32[512,66]{0,1:T(8,128)S(1)}, f32[512,66]{0,1:T(8,128)S(1)}, u32[]{:S(2)}, u32[]{:S(2)}) collective-permute-start(f32[512,66]{0,1:T(8,128)S(1)} %pad_maximum_fusion.10), channel_id=1, source_target_pairs={{0,4},{1,5},{2,6},{3,7},{4,0},{5,1},{6,2},{7,3},{8,12},{9,13},{10,... | collective-permute-start | bytes 405512 | tf_op jit(solution)/shard_map/ppermute | solution.py:100
  149.3 9.9 %collective-permute-done.13 = f32[512,66]{0,1:T(8,128)S(1)} collective-permute-done((f32[512,66]{0,1:T(8,128)S(1)}, f32[512,66]{0,1:T(8,128)S(1)}, u32[]{:S(2)}, u32[]{:S(2)}) %collective-permute-start.13) | collective-permute-done | bytes 135200 | tf_op jit(solution)/shard_map/ppermute | solution.py:100
  160.2 1.9 %collective-permute-start.14 = (bf16[512,64]{0,1:T(8,128)(2,1)S(1)}, bf16[512,64]{0,1:T(8,128)(2,1)S(1)}, u32[]{:S(2)}, u32[]{:S(2)}) collective-permute-start(bf16[512,64]{0,1:T(8,128)(2,1)S(1)} %fusion.53), channel_id=1, source_target_pairs={{0,8},{1,9},{2,10},{3,11},{4,12},{5,13},{6,14},{7,15},{8,0},{9,1},... | collective-permute-start | bytes 196616 | tf_op jit(solution)/shard_map/ppermute | solution.py:106
  162.1 3.1 %collective-permute-done.14 = bf16[512,64]{0,1:T(8,128)(2,1)S(1)} collective-permute-done((bf16[512,64]{0,1:T(8,128)(2,1)S(1)}, bf16[512,64]{0,1:T(8,128)(2,1)S(1)}, u32[]{:S(2)}, u32[]{:S(2)}) %collective-permute-start.14) | collective-permute-done | bytes 65568 | tf_op jit(solution)/shard_map/ppermute | solution.py:106
  (234 shorter events, 50.7 us)
Async XLA Ops:
  0.6 12.8 %copy-start = (s32[64,64]{1,0:T(8,128)S(1)}, s32[64,64]{1,0:T(8,128)}, u32[]{:S(2)}) copy-start(s32[64,64]{1,0:T(8,128)} %param.32) | copy-start | bytes 49156
  0.6 31.1 %collective-permute-start = (bf16[1024,128]{1,0:T(8,128)(2,1)}, bf16[1024,128]{1,0:T(8,128)(2,1)S(1)}, u32[]{:S(2)}, u32[]{:S(2)}) collective-permute-start(bf16[1024,128]{1,0:T(8,128)(2,1)} %param.29), channel_id=1, source_target_pairs={{16,0},{49,1},{82,2},{115,3},{148,4},{181,5},{214,6},{247,7},{280,... | collective-permute-start | bytes 786440 | tf_op jit(solution)/shard_map/ppermute | solution.py:135
  9.4 22.4 %collective-permute-start.1 = (bf16[1024,128]{1,0:T(8,128)(2,1)}, bf16[1024,128]{1,0:T(8,128)(2,1)S(1)}, u32[]{:S(2)}, u32[]{:S(2)}) collective-permute-start(bf16[1024,128]{1,0:T(8,128)(2,1)} %param.29), channel_id=1, source_target_pairs={{0,0},{33,1},{66,2},{99,3},{132,4},{165,5},{198,6},{231,7},{264,8}... | collective-permute-start | bytes 786440 | tf_op jit(solution)/shard_map/ppermute | solution.py:135
  11.0 20.9 %collective-permute-start.2 = (bf16[2048]{0:T(1024)(128)(2,1)}, bf16[2048]{0:T(1024)(128)(2,1)S(1)}, u32[]{:S(2)}, u32[]{:S(2)}) collective-permute-start(bf16[2048]{0:T(1024)(128)(2,1)} %param.30), channel_id=1, source_target_pairs={{0,0},{1,1},{2,2},{3,3},{4,4},{5,5},{6,6},{7,7},{8,8},{9,9},{10,10... | collective-permute-start | bytes 12296 | tf_op jit(solution)/shard_map/ppermute | solution.py:151
  12.3 2.5 %copy-start.2 = (bf16[2048,64]{0,1:T(8,128)(2,1)S(1)}, bf16[2048,64]{0,1:T(8,128)(2,1)}, u32[]{:S(2)}) copy-start(bf16[2048,64]{0,1:T(8,128)(2,1)} %param.28) | copy-start | bytes 786436
  13.4 2.2 %copy-start.1 = (bf16[2048,128]{1,0:T(8,128)(2,1)S(1)}, bf16[2048,128]{1,0:T(8,128)(2,1)}, u32[]{:S(2)}) copy-start(bf16[2048,128]{1,0:T(8,128)(2,1)} %param.26) | copy-start | bytes 1572868
  14.9 0.7 copy-start.7
  31.9 9.8 %collective-permute-start.3 = (f32[512,66]{0,1:T(8,128)S(1)}, f32[512,66]{0,1:T(8,128)S(1)}, u32[]{:S(2)}, u32[]{:S(2)}) collective-permute-start(f32[512,66]{0,1:T(8,128)S(1)} %constant_dynamic-slice_fusion.5), channel_id=1, source_target_pairs={{0,8},{1,9},{2,10},{3,11},{4,12},{5,13},{6,14},{7,15},{8,0},{9,1},... | collective-permute-start | bytes 405512 | tf_op jit(solution)/shard_map/ppermute | solution.py:97
  41.9 9.9 %collective-permute-start.4 = (f32[512,66]{0,1:T(8,128)S(1)}, f32[512,66]{0,1:T(8,128)S(1)}, u32[]{:S(2)}, u32[]{:S(2)}) collective-permute-start(f32[512,66]{0,1:T(8,128)S(1)} %pad_maximum_fusion.5), channel_id=1, source_target_pairs={{0,1},{1,0},{2,3},{3,2},{4,5},{5,4},{6,7},{7,6},{8,9},{9,8},{10,11... | collective-permute-start | bytes 405512 | tf_op jit(solution)/shard_map/ppermute | solution.py:100
  51.9 12.9 %collective-permute-start.5 = (f32[512,66]{0,1:T(8,128)S(1)}, f32[512,66]{0,1:T(8,128)S(1)}, u32[]{:S(2)}, u32[]{:S(2)}) collective-permute-start(f32[512,66]{0,1:T(8,128)S(1)} %pad_maximum_fusion.6), channel_id=1, source_target_pairs={{0,2},{1,3},{2,0},{3,1},{4,6},{5,7},{6,4},{7,5},{8,10},{9,11},{10,... | collective-permute-start | bytes 405512 | tf_op jit(solution)/shard_map/ppermute | solution.py:100
  64.8 12.3 %collective-permute-start.6 = (f32[512,66]{0,1:T(8,128)S(1)}, f32[512,66]{0,1:T(8,128)S(1)}, u32[]{:S(2)}, u32[]{:S(2)}) collective-permute-start(f32[512,66]{0,1:T(8,128)S(1)} %pad_maximum_fusion.7), channel_id=1, source_target_pairs={{0,4},{1,5},{2,6},{3,7},{4,0},{5,1},{6,2},{7,3},{8,12},{9,13},{10,... | collective-permute-start | bytes 405512 | tf_op jit(solution)/shard_map/ppermute | solution.py:100
  77.1 0.9 copy-start.5
  77.1 4.9 %copy-start.3 = (bf16[1024,128]{1,0:T(8,128)(2,1)S(1)}, bf16[1024,128]{1,0:T(8,128)(2,1)}, u32[]{:S(2)}) copy-start(bf16[1024,128]{1,0:T(8,128)(2,1)} %param.33) | copy-start | bytes 786436
  78.1 5.6 %collective-permute-start.7 = (bf16[512,64]{0,1:T(8,128)(2,1)S(1)}, bf16[512,64]{0,1:T(8,128)(2,1)S(1)}, u32[]{:S(2)}, u32[]{:S(2)}) collective-permute-start(bf16[512,64]{0,1:T(8,128)(2,1)S(1)} %fusion.55), channel_id=1, source_target_pairs={{0,8},{1,9},{2,10},{3,11},{4,12},{5,13},{6,14},{7,15},{8,0},{9,1},... | collective-permute-start | bytes 196616 | tf_op jit(solution)/shard_map/ppermute | solution.py:106
  83.7 7.3 %copy-start.4 = (bf16[1024,64]{0,1:T(8,128)(2,1)}, bf16[1024,64]{0,1:T(8,128)(2,1)S(1)}, u32[]{:S(2)}) copy-start(bf16[1024,64]{0,1:T(8,128)(2,1)S(1)} %maximum_select_fusion) | copy-start | bytes 393220
  83.7 7.2 %collective-permute-start.8 = (bf16[1024,64]{0,1:T(8,128)(2,1)S(1)}, bf16[1024,64]{0,1:T(8,128)(2,1)S(1)}, u32[]{:S(2)}, u32[]{:S(2)}) collective-permute-start(bf16[1024,64]{0,1:T(8,128)(2,1)S(1)} %maximum_select_fusion), channel_id=1, source_target_pairs={{16,0},{49,1},{82,2},{115,3},{148,4},{181,5},{214,6},{247,7},{280,... | collective-permute-start | bytes 393224 | tf_op jit(solution)/shard_map/ppermute | solution.py:135
  88.1 2.9 %collective-permute-start.9 = (bf16[1024,64]{0,1:T(8,128)(2,1)S(1)}, bf16[1024,64]{0,1:T(8,128)(2,1)S(1)}, u32[]{:S(2)}, u32[]{:S(2)}) collective-permute-start(bf16[1024,64]{0,1:T(8,128)(2,1)S(1)} %maximum_select_fusion), channel_id=1, source_target_pairs={{0,0},{33,1},{66,2},{99,3},{132,4},{165,5},{198,6},{231,7},{264,8}... | collective-permute-start | bytes 393224 | tf_op jit(solution)/shard_map/ppermute | solution.py:135
  107.5 20.1 %collective-permute-start.10 = (f32[512,66]{0,1:T(8,128)S(1)}, f32[512,66]{0,1:T(8,128)S(1)}, u32[]{:S(2)}, u32[]{:S(2)}) collective-permute-start(f32[512,66]{0,1:T(8,128)S(1)} %constant_dynamic-slice_fusion.4), channel_id=1, source_target_pairs={{0,8},{1,9},{2,10},{3,11},{4,12},{5,13},{6,14},{7,15},{8,0},{9,1},... | collective-permute-start | bytes 405512 | tf_op jit(solution)/shard_map/ppermute | solution.py:97
  127.7 6.5 %collective-permute-start.11 = (f32[512,66]{0,1:T(8,128)S(1)}, f32[512,66]{0,1:T(8,128)S(1)}, u32[]{:S(2)}, u32[]{:S(2)}) collective-permute-start(f32[512,66]{0,1:T(8,128)S(1)} %pad_maximum_fusion.8), channel_id=1, source_target_pairs={{0,1},{1,0},{2,3},{3,2},{4,5},{5,4},{6,7},{7,6},{8,9},{9,8},{10,11... | collective-permute-start | bytes 405512 | tf_op jit(solution)/shard_map/ppermute | solution.py:100
  134.2 11.5 %collective-permute-start.12 = (f32[512,66]{0,1:T(8,128)S(1)}, f32[512,66]{0,1:T(8,128)S(1)}, u32[]{:S(2)}, u32[]{:S(2)}) collective-permute-start(f32[512,66]{0,1:T(8,128)S(1)} %pad_maximum_fusion.9), channel_id=1, source_target_pairs={{0,2},{1,3},{2,0},{3,1},{4,6},{5,7},{6,4},{7,5},{8,10},{9,11},{10,... | collective-permute-start | bytes 405512 | tf_op jit(solution)/shard_map/ppermute | solution.py:100
  145.8 13.4 %collective-permute-start.13 = (f32[512,66]{0,1:T(8,128)S(1)}, f32[512,66]{0,1:T(8,128)S(1)}, u32[]{:S(2)}, u32[]{:S(2)}) collective-permute-start(f32[512,66]{0,1:T(8,128)S(1)} %pad_maximum_fusion.10), channel_id=1, source_target_pairs={{0,4},{1,5},{2,6},{3,7},{4,0},{5,1},{6,2},{7,3},{8,12},{9,13},{10,... | collective-permute-start | bytes 405512 | tf_op jit(solution)/shard_map/ppermute | solution.py:100
  159.2 0.9 copy-start.6
  160.2 5.0 %collective-permute-start.14 = (bf16[512,64]{0,1:T(8,128)(2,1)S(1)}, bf16[512,64]{0,1:T(8,128)(2,1)S(1)}, u32[]{:S(2)}, u32[]{:S(2)}) collective-permute-start(bf16[512,64]{0,1:T(8,128)(2,1)S(1)} %fusion.53), channel_id=1, source_target_pairs={{0,8},{1,9},{2,10},{3,11},{4,12},{5,13},{6,14},{7,15},{8,0},{9,1},... | collective-permute-start | bytes 196616 | tf_op jit(solution)/shard_map/ppermute | solution.py:106

commit v5 on v4

--- a/solution.py
+++ b/solution.py
@@ -1,6 +1,8 @@
 import jax
 import jax.numpy as jnp
 from jax import lax
+from jax.experimental import pallas as pl
+from jax.experimental.pallas import tpu as pltpu
 from jax.sharding import PartitionSpec as P
 
 BLOCK = 512
@@ -9,60 +11,70 @@
 sharpness = 3.5
 very_low = -1e30
 
+def partials_kernel(mask_ref, x_ref, y_ref, off_ref, v_ref, out_ref, m_ref, l_ref, acc_ref, *, scale, col_tiles):
+    i = pl.program_id(0)
+    j = pl.program_id(1)
+
+    @pl.when(j == 0)
+    def _():
+        m_ref[...] = jnp.full(m_ref.shape, very_low, jnp.float32)
+        l_ref[...] = jnp.zeros(l_ref.shape, jnp.float32)
+        acc_ref[...] = jnp.zeros(acc_ref.shape, jnp.float32)
+
+    @pl.when(mask_ref[i * col_tiles + j] > 0)
+    def _():
+        s = lax.dot_general(x_ref[...], y_ref[...], (((1,), (1,)), ((), ())), preferred_element_type=jnp.float32)
+        s = s * scale - off_ref[...]
+        m_old = m_ref[...]
+        m_new = jnp.maximum(m_old, jnp.max(s, axis=1, keepdims=True))
+        shrink = jnp.exp(m_old - m_new)
+        p = jnp.exp(s - m_new)
+        l_ref[...] = l_ref[...] * shrink + jnp.sum(p, axis=1, keepdims=True)
+        acc_ref[...] = acc_ref[...] * shrink + jnp.dot(p.astype(jnp.bfloat16), v_ref[...], preferred_element_type=jnp.float32)
+        m_ref[...] = m_new
+
+    @pl.when(j == col_tiles - 1)
+    def _():
+        w = acc_ref.shape[1]
+        out_ref[:, 0:w] = acc_ref[...]
+        out_ref[:, w:w + 1] = l_ref[...]
+        out_ref[:, w + 1:w + 2] = m_ref[...]
+
+
+def date_partials_kernel(targets, sources, offsets, values, live):
+    rows, factors = targets.shape
+    cols = sources.shape[0]
+    width = values.shape[1]
+    row_tiles, col_tiles = rows // BLOCK, cols // BLOCK
+    kernel = lambda *refs: partials_kernel(*refs, scale=sharpness / factors**0.5, col_tiles=col_tiles)
+    return pl.pallas_call(
+        kernel,
+        out_shape=jax.ShapeDtypeStruct((rows, width + 2), jnp.float32),
+        grid_spec=pltpu.PrefetchScalarGridSpec(
+            num_scalar_prefetch=1,
+            grid=(row_tiles, col_tiles),
+            in_specs=[
+                pl.BlockSpec((BLOCK, factors), lambda i, j, m: (i, 0)),
+                pl.BlockSpec((BLOCK, factors), lambda i, j, m: (j, 0)),
+                pl.BlockSpec((1, BLOCK), lambda i, j, m: (0, j)),
+                pl.BlockSpec((BLOCK, width), lambda i, j, m: (j, 0)),
+            ],
+            out_specs=pl.BlockSpec((BLOCK, width + 2), lambda i, j, m: (i, 0)),
+            scratch_shapes=[
+                pltpu.VMEM((BLOCK, 1), jnp.float32),
+                pltpu.VMEM((BLOCK, 1), jnp.float32),
+                pltpu.VMEM((BLOCK, width), jnp.float32),
+            ],
+        ),
+        compiler_params=pltpu.CompilerParams(dimension_semantics=("arbitrary", "arbitrary")),
+    )(live.reshape(-1).astype(jnp.int32), targets, sources, offsets.astype(jnp.float32).reshape(1, cols), values)
+
+
 def date_partials(targets, sources, offsets, values, tile_mask, col_tile_ids):
-    row_count = targets.shape[0]
-    factors = targets.shape[1]
-    value_width = values.shape[1]
-    row_tiles = row_count // BLOCK
-    col_tiles = sources.shape[0] // BLOCK
-    score_scale = sharpness / factors**0.5
+    row_tiles = targets.shape[0] // BLOCK
     row_ids = lax.axis_index("tgt") * row_tiles + jnp.arange(row_tiles)
-    local_mask = tile_mask[row_ids][:, col_tile_ids]
-    source_tiles = sources.reshape(col_tiles, BLOCK, factors)
-    offset_tiles = offsets.astype(jnp.float32).reshape(col_tiles, BLOCK)
-    value_tiles = values.reshape(col_tiles, BLOCK, value_width)
-    peaks, sums, weighted_all = ([], [], [])
-    for row_block in range(row_tiles):
-        target_rows = targets[row_block * BLOCK : (row_block + 1) * BLOCK]
-
-        def step(carry, inputs):
-            source_tile, offset_tile, value_tile, tile_live = inputs
-
-            def active(carry_in):
-                row_peak, weight_sum, weighted = carry_in
-                scores = lax.dot_general(
-                    target_rows,
-                    source_tile,
-                    (((1,), (1,)), ((), ())),
-                    preferred_element_type=jnp.float32,
-                )
-                scores = scores * score_scale - offset_tile[None, :]
-                new_peak = jnp.maximum(row_peak, jnp.max(scores, axis=1))
-                shrink = jnp.exp(row_peak - new_peak)
-                weights = jnp.exp(scores - new_peak[:, None])
-                new_sum = weight_sum * shrink + jnp.sum(weights, axis=1)
-                new_weighted = weighted * shrink[:, None] + jnp.dot(
-                    weights.astype(jnp.bfloat16), value_tile, preferred_element_type=jnp.float32
-                )
-                return (new_peak, new_sum, new_weighted)
-
-            def skipped(carry_in):
-                return carry_in
-
-            return (lax.cond(tile_live > 0, active, skipped, carry), None)
-
-        start = (
-            jnp.full((BLOCK,), very_low, jnp.float32),
-            jnp.zeros((BLOCK,), jnp.float32),
-            jnp.zeros((BLOCK, value_width), jnp.float32),
-        )
-        result, _ = lax.scan(
-            step, start, (source_tiles, offset_tiles, value_tiles, local_mask[row_block])
-        )
-        peaks.append(result[0])
-        sums.append(result[1])
-        weighted_all.append(result[2])
-    return (jnp.concatenate(peaks, 0), jnp.concatenate(sums, 0), jnp.concatenate(weighted_all, 0))
+    live = tile_mask[row_ids][:, col_tile_ids]
+    return date_partials_kernel(targets, sources, offsets, values, live)
 
 
 HALVING_BITS = (3,)
@@ -84,10 +96,9 @@
 
 
 def finish(partials, exercise):
-    row_peak, weight_sum, weighted = partials
     src_size = lax.axis_size("src")
     me = lax.axis_index("src")
-    packed = jnp.concatenate([weighted, weight_sum[:, None], row_peak[:, None]], axis=1)
+    packed = partials
     exercise = exercise.astype(jnp.float32)
     for bit in HALVING_BITS:
         half = packed.shape[0] // 2

time: 167 us -> 210 us (1.26)
  the two profiles are of different devices: /device:TPU:1 before, /device:TPU:4 now
where the time goes in v5:
time: 210 us; the launch traced here: 209 us
  waiting for transfers between devices  87.6 us (42%)
  starting transfers between devices  78.4 us (37%)
  Pallas kernels  23.4 us (11%)
  local copies, waits for them, and re-layouts  10.1 us (5%)
  other arithmetic  8.65 us (4%)
    ppermute x6, waiting for transfers between devices, finish(): packed = merge(packed, lax.ppermute(packed, 'src', xor_perm(src_size, bit)))  68.3 us
    ppermute x2, starting transfers between devices, finish(): packed = merge(keep, lax.ppermute(send, 'src', xor_perm(src_size, bit)))  37.6 us
    pallas_call x2, Pallas kernels, date_partials_kernel(): pl.pallas_call(kernel, out_shape=jax.ShapeDtypeStruct((rows, width + 2),...  23.4 us
    ppermute x6, starting transfers between devices, finish(): packed = merge(packed, lax.ppermute(packed, 'src', xor_perm(src_size, bit)))  20.5 us
    ppermute x2, waiting for transfers between devices, finish(): packed = merge(keep, lax.ppermute(send, 'src', xor_perm(src_size, bit)))  12.6 us
    ppermute x1, starting transfers between devices, regroup_offsets(): return lax.ppermute(offsets, ('tgt', 'src'), pairs)  7.76 us
    ppermute x2, waiting for transfers between devices, finish(): got = lax.ppermute(value, 'src', xor_perm(src_size, bit))  6.66 us
    ppermute x4, starting transfers between devices, regroup(): return [lax.ppermute(block_rows, ('tgt', 'src'), p) for p in perms]  6.26 us
  transfers between devices with their start and end apart: 15, of which 10 were waited for; matrix products, arithmetic and copies ran while one was open for 5% of the time, Pallas kernels for 6%

profile of v5, /device:TPU:4, one launch (start us, length us, event | category | flops | bytes accessed | tf_op | source)
XLA Modules:
  0.0 209.2 jit_solution(10334625478483349855)
XLA Ops:
  0.7 2.1 collective-permute-start
  4.3 7.8 %collective-permute-start.2 = (bf16[2048]{0:T(1024)(128)(2,1)}, bf16[2048]{0:T(1024)(128)(2,1)S(1)}, u32[]{:S(2)}, u32[]{:S(2)}) collective-permute-start(bf16[2048]{0:T(1024)(128)(2,1)} %param.14), channel_id=1, source_target_pairs={{0,0},{1,1},{2,2},{3,3},{4,4},{5,5},{6,6},{7,7},{8,8},{9,9},{10,10... | collective-permute-start | bytes 12296 | tf_op jit(solution)/shard_map/ppermute | solution.py:162
  16.5 13.3 %shard_map.113 = f32[1024,66]{1,0:T(8,128)} custom-call(s32[8]{0:T(128)} %reshape.68.refs_0_, bf16[1024,128]{1,0:T(8,128)(2,1)} %refs_1_.2, bf16[2048,128]{1,0:T(8,128)(2,1)} %refs_2_.1, f32[1,2048]{1,0:T(1,128)} %bitcast.11, bf16[2048,64]{1,0:T(8,128)(2,1)} %copy.32.refs_4_), custom_call_target="tpu_custom_call" | custom-call | tf_op jit(solution)/shard_map/pallas_call | solution.py:50
  31.1 9.0 %collective-permute-start.3 = (f32[512,66]{1,0:T(8,128)S(1)}, f32[512,66]{1,0:T(8,128)S(1)}, u32[]{:S(2)}, u32[]{:S(2)}) collective-permute-start(f32[512,66]{1,0:T(8,128)S(1)} %constant_dynamic-slice_fusion.1), channel_id=1, source_target_pairs={{0,8},{1,9},{2,10},{3,11},{4,12},{5,13},{6,14},{7,15},{8,0},{9,1},... | collective-permute-start | bytes 405512 | tf_op jit(solution)/shard_map/ppermute | solution.py:108
  40.1 5.5 %collective-permute-done.3 = f32[512,66]{1,0:T(8,128)S(1)} collective-permute-done((f32[512,66]{1,0:T(8,128)S(1)}, f32[512,66]{1,0:T(8,128)S(1)}, u32[]{:S(2)}, u32[]{:S(2)}) %collective-permute-start.3) | collective-permute-done | bytes 135200 | tf_op jit(solution)/shard_map/ppermute | solution.py:108
  46.3 5.4 %collective-permute-start.4 = (f32[512,66]{1,0:T(8,128)S(1)}, f32[512,66]{1,0:T(8,128)S(1)}, u32[]{:S(2)}, u32[]{:S(2)}) collective-permute-start(f32[512,66]{1,0:T(8,128)S(1)} %pad_maximum_fusion.2), channel_id=1, source_target_pairs={{0,1},{1,0},{2,3},{3,2},{4,5},{5,4},{6,7},{7,6},{8,9},{9,8},{10,11... | collective-permute-start | bytes 405512 | tf_op jit(solution)/shard_map/ppermute | solution.py:111
  51.7 6.3 %collective-permute-done.4 = f32[512,66]{1,0:T(8,128)S(1)} collective-permute-done((f32[512,66]{1,0:T(8,128)S(1)}, f32[512,66]{1,0:T(8,128)S(1)}, u32[]{:S(2)}, u32[]{:S(2)}) %collective-permute-start.4) | collective-permute-done | bytes 135200 | tf_op jit(solution)/shard_map/ppermute | solution.py:111
  58.6 3.6 %collective-permute-start.5 = (f32[512,66]{1,0:T(8,128)S(1)}, f32[512,66]{1,0:T(8,128)S(1)}, u32[]{:S(2)}, u32[]{:S(2)}) collective-permute-start(f32[512,66]{1,0:T(8,128)S(1)} %pad_maximum_fusion.3), channel_id=1, source_target_pairs={{0,2},{1,3},{2,0},{3,1},{4,6},{5,7},{6,4},{7,5},{8,10},{9,11},{10,... | collective-permute-start | bytes 405512 | tf_op jit(solution)/shard_map/ppermute | solution.py:111
  62.2 12.2 %collective-permute-done.5 = f32[512,66]{1,0:T(8,128)S(1)} collective-permute-done((f32[512,66]{1,0:T(8,128)S(1)}, f32[512,66]{1,0:T(8,128)S(1)}, u32[]{:S(2)}, u32[]{:S(2)}) %collective-permute-start.5) | collective-permute-done | bytes 135200 | tf_op jit(solution)/shard_map/ppermute | solution.py:111
  75.1 5.8 %collective-permute-start.6 = (f32[512,66]{1,0:T(8,128)S(1)}, f32[512,66]{1,0:T(8,128)S(1)}, u32[]{:S(2)}, u32[]{:S(2)}) collective-permute-start(f32[512,66]{1,0:T(8,128)S(1)} %pad_maximum_fusion.4), channel_id=1, source_target_pairs={{0,4},{1,5},{2,6},{3,7},{4,0},{5,1},{6,2},{7,3},{8,12},{9,13},{10,... | collective-permute-start | bytes 405512 | tf_op jit(solution)/shard_map/ppermute | solution.py:111
  81.1 12.8 %collective-permute-done.6 = f32[512,66]{1,0:T(8,128)S(1)} collective-permute-done((f32[512,66]{1,0:T(8,128)S(1)}, f32[512,66]{1,0:T(8,128)S(1)}, u32[]{:S(2)}, u32[]{:S(2)}) %collective-permute-start.6) | collective-permute-done | bytes 135200 | tf_op jit(solution)/shard_map/ppermute | solution.py:111
  94.8 3.2 %collective-permute-start.7 = (bf16[512,64]{1,0:T(8,128)(2,1)S(1)}, bf16[512,64]{1,0:T(8,128)(2,1)S(1)}, u32[]{:S(2)}, u32[]{:S(2)}) collective-permute-start(bf16[512,64]{1,0:T(8,128)(2,1)S(1)} %fusion.15), channel_id=1, source_target_pairs={{0,8},{1,9},{2,10},{3,11},{4,12},{5,13},{6,14},{7,15},{8,0},{9,1},... | collective-permute-start | bytes 196616 | tf_op jit(solution)/shard_map/ppermute | solution.py:117
  98.0 3.7 %collective-permute-done.7 = bf16[512,64]{1,0:T(8,128)(2,1)S(1)} collective-permute-done((bf16[512,64]{1,0:T(8,128)(2,1)S(1)}, bf16[512,64]{1,0:T(8,128)(2,1)S(1)}, u32[]{:S(2)}, u32[]{:S(2)}) %collective-permute-start.7) | collective-permute-done | bytes 65568 | tf_op jit(solution)/shard_map/ppermute | solution.py:117
  101.8 1.9 collective-permute-start.8
  108.7 10.1 %shard_map.114 = f32[1024,66]{1,0:T(8,128)} custom-call(s32[8]{0:T(128)} %reshape.71.refs_0_, bf16[1024,128]{1,0:T(8,128)(2,1)} %refs_1_.3, bf16[2048,128]{1,0:T(8,128)(2,1)} %pad_maximum_fusion.refs_2_, f32[1,2048]{1,0:T(1,128)} %bitcast.10, bf16[2048,64]{1,0:T(8,128)(2,1)} %pad_maximum_fusion.1.refs_4_), custom_call_target="tpu_custom_call" | custom-call | tf_op jit(solution)/shard_map/pallas_call | solution.py:50
  119.8 28.7 %collective-permute-start.10 = (f32[512,66]{1,0:T(8,128)S(1)}, f32[512,66]{1,0:T(8,128)S(1)}, u32[]{:S(2)}, u32[]{:S(2)}) collective-permute-start(f32[512,66]{1,0:T(8,128)S(1)} %constant_dynamic-slice_fusion), channel_id=1, source_target_pairs={{0,8},{1,9},{2,10},{3,11},{4,12},{5,13},{6,14},{7,15},{8,0},{9,1},... | collective-permute-start | bytes 405512 | tf_op jit(solution)/shard_map/ppermute | solution.py:108
  148.4 7.1 %collective-permute-done.10 = f32[512,66]{1,0:T(8,128)S(1)} collective-permute-done((f32[512,66]{1,0:T(8,128)S(1)}, f32[512,66]{1,0:T(8,128)S(1)}, u32[]{:S(2)}, u32[]{:S(2)}) %collective-permute-start.10) | collective-permute-done | bytes 135200 | tf_op jit(solution)/shard_map/ppermute | solution.py:108
  156.3 1.9 collective-permute-start.11
  158.2 8.3 %collective-permute-done.11 = f32[512,66]{1,0:T(8,128)S(1)} collective-permute-done((f32[512,66]{1,0:T(8,128)S(1)}, f32[512,66]{1,0:T(8,128)S(1)}, u32[]{:S(2)}, u32[]{:S(2)}) %collective-permute-start.11) | collective-permute-done | bytes 135200 | tf_op jit(solution)/shard_map/ppermute | solution.py:111
  167.1 1.9 collective-permute-start.12
  169.1 13.9 %collective-permute-done.12 = f32[512,66]{1,0:T(8,128)S(1)} collective-permute-done((f32[512,66]{1,0:T(8,128)S(1)}, f32[512,66]{1,0:T(8,128)S(1)}, u32[]{:S(2)}, u32[]{:S(2)}) %collective-permute-start.12) | collective-permute-done | bytes 135200 | tf_op jit(solution)/shard_map/ppermute | solution.py:111
  185.7 14.8 %collective-permute-done.13 = f32[512,66]{1,0:T(8,128)S(1)} collective-permute-done((f32[512,66]{1,0:T(8,128)S(1)}, f32[512,66]{1,0:T(8,128)S(1)}, u32[]{:S(2)}, u32[]{:S(2)}) %collective-permute-start.13) | collective-permute-done | bytes 135200 | tf_op jit(solution)/shard_map/ppermute | solution.py:111
  201.5 3.1 %collective-permute-start.14 = (bf16[512,64]{1,0:T(8,128)(2,1)S(1)}, bf16[512,64]{1,0:T(8,128)(2,1)S(1)}, u32[]{:S(2)}, u32[]{:S(2)}) collective-permute-start(bf16[512,64]{1,0:T(8,128)(2,1)S(1)} %fusion.9), channel_id=1, source_target_pairs={{0,8},{1,9},{2,10},{3,11},{4,12},{5,13},{6,14},{7,15},{8,0},{9,1},... | collective-permute-start | bytes 196616 | tf_op jit(solution)/shard_map/ppermute | solution.py:117
  205.4 3.0 %collective-permute-done.14 = bf16[512,64]{1,0:T(8,128)(2,1)S(1)} collective-permute-done((bf16[512,64]{1,0:T(8,128)(2,1)S(1)}, bf16[512,64]{1,0:T(8,128)(2,1)S(1)}, u32[]{:S(2)}, u32[]{:S(2)}) %collective-permute-start.14) | collective-permute-done | bytes 65568 | tf_op jit(solution)/shard_map/ppermute | solution.py:117
  (78 shorter events, 23.0 us)
Async XLA Ops:
  0.6 80.3 %copy-start = (bf16[1024,64]{0,1:T(8,128)(2,1)S(1)}, bf16[1024,64]{0,1:T(8,128)(2,1)}, u32[]{:S(2)}) copy-start(bf16[1024,64]{0,1:T(8,128)(2,1)} %param.15) | copy-start | bytes 393220
  0.6 14.3 %copy-start.3 = (bf16[2048,64]{0,1:T(8,128)(2,1)S(1)}, bf16[2048,64]{0,1:T(8,128)(2,1)}, u32[]{:S(2)}) copy-start(bf16[2048,64]{0,1:T(8,128)(2,1)} %param.12) | copy-start | bytes 786436
  0.7 29.2 %collective-permute-start = (bf16[1024,128]{1,0:T(8,128)(2,1)}, bf16[1024,128]{1,0:T(8,128)(2,1)S(1)}, u32[]{:S(2)}, u32[]{:S(2)}) collective-permute-start(bf16[1024,128]{1,0:T(8,128)(2,1)} %refs_1_.2), channel_id=1, source_target_pairs={{16,0},{49,1},{82,2},{115,3},{148,4},{181,5},{214,6},{247,7},{280,... | collective-permute-start | bytes 786440 | tf_op jit(solution)/shard_map/ppermute | solution.py:146
  2.7 27.1 %collective-permute-start.1 = (bf16[1024,128]{1,0:T(8,128)(2,1)}, bf16[1024,128]{1,0:T(8,128)(2,1)S(1)}, u32[]{:S(2)}, u32[]{:S(2)}) collective-permute-start(bf16[1024,128]{1,0:T(8,128)(2,1)} %refs_1_.2), channel_id=1, source_target_pairs={{0,0},{33,1},{66,2},{99,3},{132,4},{165,5},{198,6},{231,7},{264,8}... | collective-permute-start | bytes 786440 | tf_op jit(solution)/shard_map/ppermute | solution.py:146
  4.3 26.4 %collective-permute-start.2 = (bf16[2048]{0:T(1024)(128)(2,1)}, bf16[2048]{0:T(1024)(128)(2,1)S(1)}, u32[]{:S(2)}, u32[]{:S(2)}) collective-permute-start(bf16[2048]{0:T(1024)(128)(2,1)} %param.14), channel_id=1, source_target_pairs={{0,0},{1,1},{2,2},{3,3},{4,4},{5,5},{6,6},{7,7},{8,8},{9,9},{10,10... | collective-permute-start | bytes 12296 | tf_op jit(solution)/shard_map/ppermute | solution.py:162
  14.9 1.0 copy-start.5
  29.9 1.2 copy-start.1
  31.1 14.4 %collective-permute-start.3 = (f32[512,66]{1,0:T(8,128)S(1)}, f32[512,66]{1,0:T(8,128)S(1)}, u32[]{:S(2)}, u32[]{:S(2)}) collective-permute-start(f32[512,66]{1,0:T(8,128)S(1)} %constant_dynamic-slice_fusion.1), channel_id=1, source_target_pairs={{0,8},{1,9},{2,10},{3,11},{4,12},{5,13},{6,14},{7,15},{8,0},{9,1},... | collective-permute-start | bytes 405512 | tf_op jit(solution)/shard_map/ppermute | solution.py:108
  46.3 11.6 %collective-permute-start.4 = (f32[512,66]{1,0:T(8,128)S(1)}, f32[512,66]{1,0:T(8,128)S(1)}, u32[]{:S(2)}, u32[]{:S(2)}) collective-permute-start(f32[512,66]{1,0:T(8,128)S(1)} %pad_maximum_fusion.2), channel_id=1, source_target_pairs={{0,1},{1,0},{2,3},{3,2},{4,5},{5,4},{6,7},{7,6},{8,9},{9,8},{10,11... | collective-permute-start | bytes 405512 | tf_op jit(solution)/shard_map/ppermute | solution.py:111
  58.6 15.8 %collective-permute-start.5 = (f32[512,66]{1,0:T(8,128)S(1)}, f32[512,66]{1,0:T(8,128)S(1)}, u32[]{:S(2)}, u32[]{:S(2)}) collective-permute-start(f32[512,66]{1,0:T(8,128)S(1)} %pad_maximum_fusion.3), channel_id=1, source_target_pairs={{0,2},{1,3},{2,0},{3,1},{4,6},{5,7},{6,4},{7,5},{8,10},{9,11},{10,... | collective-permute-start | bytes 405512 | tf_op jit(solution)/shard_map/ppermute | solution.py:111
  75.1 18.8 %collective-permute-start.6 = (f32[512,66]{1,0:T(8,128)S(1)}, f32[512,66]{1,0:T(8,128)S(1)}, u32[]{:S(2)}, u32[]{:S(2)}) collective-permute-start(f32[512,66]{1,0:T(8,128)S(1)} %pad_maximum_fusion.4), channel_id=1, source_target_pairs={{0,4},{1,5},{2,6},{3,7},{4,0},{5,1},{6,2},{7,3},{8,12},{9,13},{10,... | collective-permute-start | bytes 405512 | tf_op jit(solution)/shard_map/ppermute | solution.py:111
  94.8 6.9 %collective-permute-start.7 = (bf16[512,64]{1,0:T(8,128)(2,1)S(1)}, bf16[512,64]{1,0:T(8,128)(2,1)S(1)}, u32[]{:S(2)}, u32[]{:S(2)}) collective-permute-start(bf16[512,64]{1,0:T(8,128)(2,1)S(1)} %fusion.15), channel_id=1, source_target_pairs={{0,8},{1,9},{2,10},{3,11},{4,12},{5,13},{6,14},{7,15},{8,0},{9,1},... | collective-permute-start | bytes 196616 | tf_op jit(solution)/shard_map/ppermute | solution.py:117
  101.8 5.9 %collective-permute-start.8 = (bf16[1024,64]{1,0:T(8,128)(2,1)S(1)}, bf16[1024,64]{1,0:T(8,128)(2,1)S(1)}, u32[]{:S(2)}, u32[]{:S(2)}) collective-permute-start(bf16[1024,64]{1,0:T(8,128)(2,1)S(1)} %maximum_select_fusion), channel_id=1, source_target_pairs={{16,0},{49,1},{82,2},{115,3},{148,4},{181,5},{214,6},{247,7},{280,... | collective-permute-start | bytes 393224 | tf_op jit(solution)/shard_map/ppermute | solution.py:146
  103.7 4.0 %collective-permute-start.9 = (bf16[1024,64]{1,0:T(8,128)(2,1)S(1)}, bf16[1024,64]{1,0:T(8,128)(2,1)S(1)}, u32[]{:S(2)}, u32[]{:S(2)}) collective-permute-start(bf16[1024,64]{1,0:T(8,128)(2,1)S(1)} %maximum_select_fusion), channel_id=1, source_target_pairs={{0,0},{33,1},{66,2},{99,3},{132,4},{165,5},{198,6},{231,7},{264,8}... | collective-permute-start | bytes 393224 | tf_op jit(solution)/shard_map/ppermute | solution.py:146
  118.7 36.8 %copy-start.2 = (f32[1024,66]{1,0:T(8,128)S(1)}, f32[1024,66]{1,0:T(8,128)}, u32[]{:S(2)}) copy-start(f32[1024,66]{1,0:T(8,128)} %shard_map.114) | copy-start | bytes 811012
  119.8 35.8 %collective-permute-start.10 = (f32[512,66]{1,0:T(8,128)S(1)}, f32[512,66]{1,0:T(8,128)S(1)}, u32[]{:S(2)}, u32[]{:S(2)}) collective-permute-start(f32[512,66]{1,0:T(8,128)S(1)} %constant_dynamic-slice_fusion), channel_id=1, source_target_pairs={{0,8},{1,9},{2,10},{3,11},{4,12},{5,13},{6,14},{7,15},{8,0},{9,1},... | collective-permute-start | bytes 405512 | tf_op jit(solution)/shard_map/ppermute | solution.py:108
  156.3 10.2 %collective-permute-start.11 = (f32[512,66]{1,0:T(8,128)S(1)}, f32[512,66]{1,0:T(8,128)S(1)}, u32[]{:S(2)}, u32[]{:S(2)}) collective-permute-start(f32[512,66]{1,0:T(8,128)S(1)} %pad_maximum_fusion.5), channel_id=1, source_target_pairs={{0,1},{1,0},{2,3},{3,2},{4,5},{5,4},{6,7},{7,6},{8,9},{9,8},{10,11... | collective-permute-start | bytes 405512 | tf_op jit(solution)/shard_map/ppermute | solution.py:111
  167.1 15.8 %collective-permute-start.12 = (f32[512,66]{1,0:T(8,128)S(1)}, f32[512,66]{1,0:T(8,128)S(1)}, u32[]{:S(2)}, u32[]{:S(2)}) collective-permute-start(f32[512,66]{1,0:T(8,128)S(1)} %pad_maximum_fusion.6), channel_id=1, source_target_pairs={{0,2},{1,3},{2,0},{3,1},{4,6},{5,7},{6,4},{7,5},{8,10},{9,11},{10,... | collective-permute-start | bytes 405512 | tf_op jit(solution)/shard_map/ppermute | solution.py:111
  183.5 2.1 copy-start.4
  183.7 16.9 %collective-permute-start.13 = (f32[512,66]{1,0:T(8,128)S(1)}, f32[512,66]{1,0:T(8,128)S(1)}, u32[]{:S(2)}, u32[]{:S(2)}) collective-permute-start(f32[512,66]{1,0:T(8,128)S(1)} %pad_maximum_fusion.7), channel_id=1, source_target_pairs={{0,4},{1,5},{2,6},{3,7},{4,0},{5,1},{6,2},{7,3},{8,12},{9,13},{10,... | collective-permute-start | bytes 405512 | tf_op jit(solution)/shard_map/ppermute | solution.py:111
  201.5 6.9 %collective-permute-start.14 = (bf16[512,64]{1,0:T(8,128)(2,1)S(1)}, bf16[512,64]{1,0:T(8,128)(2,1)S(1)}, u32[]{:S(2)}, u32[]{:S(2)}) collective-permute-start(bf16[512,64]{1,0:T(8,128)(2,1)S(1)} %fusion.9), channel_id=1, source_target_pairs={{0,8},{1,9},{2,10},{3,11},{4,12},{5,13},{6,14},{7,15},{8,0},{9,1},... | collective-permute-start | bytes 196616 | tf_op jit(solution)/shard_map/ppermute | solution.py:117

commit v6 on v5

v6 whole, which is shorter than its diff:
```python
import jax
import jax.numpy as jnp
from jax import lax
from jax.experimental import pallas as pl
from jax.experimental.pallas import tpu as pltpu
from jax.sharding import PartitionSpec as P

BLOCK = 512


sharpness = 3.5
very_low = -1e30

def partials_kernel(mask_ref, x_ref, y_ref, off_ref, v_ref, out_ref, m_ref, l_ref, acc_ref, *, scale, col_tiles):
    i = pl.program_id(0)
    j = pl.program_id(1)

    @pl.when(j == 0)
    def _():
        m_ref[...] = jnp.full(m_ref.shape, very_low, jnp.float32)
        l_ref[...] = jnp.zeros(l_ref.shape, jnp.float32)
        acc_ref[...] = jnp.zeros(acc_ref.shape, jnp.float32)

    @pl.when(mask_ref[i * col_tiles + j] > 0)
    def _():
        s = lax.dot_general(y_ref[...], x_ref[...], (((1,), (1,)), ((), ())), preferred_element_type=jnp.float32)
        s = s * scale - off_ref[...]
        m_old = m_ref[...]
        m_new = jnp.maximum(m_old, jnp.max(s, axis=0, keepdims=True))
        shrink = jnp.exp(m_old - m_new)
        p = jnp.exp(s - m_new)
        l_ref[...] = l_ref[...] * shrink + jnp.sum(p, axis=0, keepdims=True)
        acc_ref[...] = acc_ref[...] * shrink + jnp.dot(v_ref[...], p.astype(jnp.bfloat16), preferred_element_type=jnp.float32)
        m_ref[...] = m_new

    @pl.when(j == col_tiles - 1)
    def _():
        w = acc_ref.shape[0]
        out_ref[0:w, :] = acc_ref[...]
        out_ref[w:w + 1, :] = l_ref[...]
        out_ref[w + 1:w + 2, :] = m_ref[...]


def date_partials_kernel(targets, sources, offsets, values_t, live):
    rows, factors = targets.shape
    cols = sources.shape[0]
    width = values_t.shape[0]
    row_tiles, col_tiles = rows // BLOCK, cols // BLOCK
    kernel = lambda *refs: partials_kernel(*refs, scale=sharpness / factors**0.5, col_tiles=col_tiles)
    return pl.pallas_call(
        kernel,
        out_shape=jax.ShapeDtypeStruct((width + 2, rows), jnp.float32),
        grid_spec=pltpu.PrefetchScalarGridSpec(
            num_scalar_prefetch=1,
            grid=(row_tiles, col_tiles),
            in_specs=[
                pl.BlockSpec((BLOCK, factors), lambda i, j, m: (i, 0)),
                pl.BlockSpec((BLOCK, factors), lambda i, j, m: (j, 0)),
                pl.BlockSpec((BLOCK, 1), lambda i, j, m: (j, 0)),
                pl.BlockSpec((width, BLOCK), lambda i, j, m: (0, j)),
            ],
            out_specs=pl.BlockSpec((width + 2, BLOCK), lambda i, j, m: (0, i)),
            scratch_shapes=[
                pltpu.VMEM((1, BLOCK), jnp.float32),
                pltpu.VMEM((1, BLOCK), jnp.float32),
                pltpu.VMEM((width, BLOCK), jnp.float32),
            ],
        ),
        compiler_params=pltpu.CompilerParams(dimension_semantics=("arbitrary", "arbitrary")),
    )(live.reshape(-1).astype(jnp.int32), targets, sources, offsets.astype(jnp.float32).reshape(cols, 1), values_t)


def date_partials(targets, sources, offsets, values_t, tile_mask, col_tile_ids):
    row_tiles = targets.shape[0] // BLOCK
    row_ids = lax.axis_index("tgt") * row_tiles + jnp.arange(row_tiles)
    live = tile_mask[row_ids][:, col_tile_ids]
    return date_partials_kernel(targets, sources, offsets, values_t, live)


HALVING_BITS = (3,)
EXCHANGE_BITS = (0, 1, 2)


def xor_perm(size, bit):
    return [(i, i ^ (1 << bit)) for i in range(size)]


def merge(mine, theirs):
    width = mine.shape[0] - 2
    peak_a, peak_b = mine[width + 1 :], theirs[width + 1 :]
    peak = jnp.maximum(peak_a, peak_b)
    scale_a = jnp.exp(peak_a - peak)
    scale_b = jnp.exp(peak_b - peak)
    body = mine[: width + 1] * scale_a + theirs[: width + 1] * scale_b
    return jnp.concatenate([body, peak], axis=0)


def finish(packed, exercise):
    src_size = lax.axis_size("src")
    me = lax.axis_index("src")
    exercise = exercise.astype(jnp.float32)
    for bit in HALVING_BITS:
        half = packed.shape[1] // 2
        mine_hi = (me >> bit) & 1
        keep = lax.dynamic_slice_in_dim(packed, mine_hi * half, half, 1)
        send = lax.dynamic_slice_in_dim(packed, (1 - mine_hi) * half, half, 1)
        packed = merge(keep, lax.ppermute(send, "src", xor_perm(src_size, bit)))
        exercise = lax.dynamic_slice_in_dim(exercise, mine_hi * half, half, 0)
    for bit in EXCHANGE_BITS:
        packed = merge(packed, lax.ppermute(packed, "src", xor_perm(src_size, bit)))
    width = packed.shape[0] - 2
    continuation = packed[:width] / packed[width : width + 1]
    value = jnp.maximum(continuation, exercise.T).astype(jnp.bfloat16)
    for bit in reversed(HALVING_BITS):
        mine_hi = (me >> bit) & 1
        got = lax.ppermute(value, "src", xor_perm(src_size, bit))
        value = jnp.where(
            mine_hi == 1,
            jnp.concatenate([got, value], 1),
            jnp.concatenate([value, got], 1),
        )
    return value


def lin(t, s):
    return t * lax.axis_size("src") + s


def source_pair(t, s):
    x_count = lax.axis_size("tgt") // 8
    z_hi, x = t // (2 * x_count), (t // 2) % x_count
    return ((z_hi + s // 4) % 4) * x_count + (x + s % 4) % x_count


def regroup(block_rows):
    tgt_size = lax.axis_size("tgt")
    src_size = lax.axis_size("src")
    perms = ([], [])
    for t in range(tgt_size):
        for s in range(src_size):
            pair = source_pair(t, s)
            for flip in range(2):
                u = 2 * pair + ((t % 2) ^ flip)
                perms[flip].append((lin(u, s), lin(t, s)))
    return [lax.ppermute(block_rows, ("tgt", "src"), p) for p in perms]


def regroup_order(got, axis=0):
    odd = lax.axis_index("tgt") % 2 == 1
    return jnp.concatenate(
        [jnp.where(odd, got[1], got[0]), jnp.where(odd, got[0], got[1])], axis
    )


def regroup_offsets(offsets):
    tgt_size = lax.axis_size("tgt")
    src_size = lax.axis_size("src")
    pairs = [
        (lin(t, source_pair(t, s)), lin(t, s)) for t in range(tgt_size) for s in range(src_size)
    ]
    return lax.ppermute(offsets, ("tgt", "src"), pairs)


def per_device(
    states_late,
    offset_late,
    values_late,
    states_mid,
    offset_mid,
    exercise_mid,
    mask_mid,
    states_early,
    exercise_early,
    mask_early,
):
    src_tiles = states_late.shape[0] // BLOCK
    col_ids = lax.axis_index("src") * src_tiles + jnp.arange(src_tiles)
    pair = source_pair(lax.axis_index("tgt"), lax.axis_index("src"))
    early_col_ids = pair * src_tiles + jnp.arange(src_tiles)
    mid_sources = regroup_order(regroup(states_mid))
    mid_offsets = regroup_offsets(offset_mid)
    partials = date_partials(states_mid, states_late, offset_late, values_late.T, mask_mid, col_ids)
    partials, mid_sources, mid_offsets = lax.optimization_barrier(
        (partials, mid_sources, mid_offsets)
    )
    value_mid_t = finish(partials, exercise_mid)
    mid_values_t = regroup_order(regroup(value_mid_t), axis=1)
    value_early_t = finish(
        date_partials(
            states_early, mid_sources, mid_offsets, mid_values_t, mask_early, early_col_ids
        ),
        exercise_early,
    )
    value_mid, value_early = value_mid_t.T, value_early_t.T
    return (value_mid, value_early)


def solution(mesh):
    in_specs = (
        P("src", None),
        P("src"),
        P("src", None),
        P("tgt", None),
        P("src"),
        P("tgt", None),
        P(),
        P("tgt", None),
        P("tgt", None),
        P(),
    )
    out_specs = (P("tgt", None), P("tgt", None))
    return jax.shard_map(
        per_device, mesh=mesh, in_specs=in_specs, out_specs=out_specs, check_vma=False
    )
```

time: 210 us -> 163 us (0.78)
  the two profiles are of different devices: /device:TPU:4 before, /device:TPU:136 now
where the time goes in v6:
time: 163 us; the launch traced here: 162 us
  starting transfers between devices  71.9 us (44%)
  waiting for transfers between devices  60 us (37%)
  Pallas kernels  14.9 us (9%)
  local copies, waits for them, and re-layouts  10.9 us (7%)
  other arithmetic  3.03 us (2%)
    ppermute x6, waiting for transfers between devices, finish(): packed = merge(packed, lax.ppermute(packed, 'src', xor_perm(src_size, bit)))  46.4 us
    ppermute x6, starting transfers between devices, finish(): packed = merge(packed, lax.ppermute(packed, 'src', xor_perm(src_size, bit)))  20.2 us
    ppermute x2, starting transfers between devices, finish(): packed = merge(keep, lax.ppermute(send, 'src', xor_perm(src_size, bit)))  16.7 us
    pallas_call x2, Pallas kernels, date_partials_kernel(): pl.pallas_call(kernel, out_shape=jax.ShapeDtypeStruct((width + 2, rows),...  14.9 us
    ppermute x1, starting transfers between devices, regroup_offsets(): return lax.ppermute(offsets, ('tgt', 'src'), pairs)  14.4 us
    ppermute x4, starting transfers between devices, regroup(): return [lax.ppermute(block_rows, ('tgt', 'src'), p) for p in perms]  13.8 us
    ppermute x2, waiting for transfers between devices, finish(): packed = merge(keep, lax.ppermute(send, 'src', xor_perm(src_size, bit)))  7.83 us
    ppermute x2, starting transfers between devices, finish(): got = lax.ppermute(value, 'src', xor_perm(src_size, bit))  6.83 us
  transfers between devices with their start and end apart: 15, of which 11 were waited for; matrix products, arithmetic and copies ran while one was open for 5% of the time, Pallas kernels for 5%

profile of v6, /device:TPU:136, one launch (start us, length us, event | category | flops | bytes accessed | tf_op | source)
XLA Modules:
  0.0 161.9 jit_solution(1944262471835122297)
XLA Ops:
  0.6 4.7 %collective-permute-start.1 = (bf16[1024,128]{1,0:T(8,128)(2,1)}, bf16[1024,128]{1,0:T(8,128)(2,1)S(1)}, u32[]{:S(2)}, u32[]{:S(2)}) collective-permute-start(bf16[1024,128]{1,0:T(8,128)(2,1)} %refs_1_.2), channel_id=1, source_target_pairs={{0,0},{33,1},{66,2},{99,3},{132,4},{165,5},{198,6},{231,7},{264,8}... | collective-permute-start | bytes 786440 | tf_op jit(solution)/shard_map/ppermute | solution.py:145
  5.3 1.9 %collective-permute-start = (bf16[1024,128]{1,0:T(8,128)(2,1)}, bf16[1024,128]{1,0:T(8,128)(2,1)S(1)}, u32[]{:S(2)}, u32[]{:S(2)}) collective-permute-start(bf16[1024,128]{1,0:T(8,128)(2,1)} %refs_1_.2), channel_id=1, source_target_pairs={{16,0},{49,1},{82,2},{115,3},{148,4},{181,5},{214,6},{247,7},{280,... | collective-permute-start | bytes 786440 | tf_op jit(solution)/shard_map/ppermute | solution.py:145
  7.3 14.4 %collective-permute-start.2 = (bf16[2048]{0:T(1024)(128)(2,1)}, bf16[2048]{0:T(1024)(128)(2,1)S(1)}, u32[]{:S(2)}, u32[]{:S(2)}) collective-permute-start(bf16[2048]{0:T(1024)(128)(2,1)} %param.14), channel_id=1, source_target_pairs={{0,0},{1,1},{2,2},{3,3},{4,4},{5,5},{6,6},{7,7},{8,8},{9,9},{10,10... | collective-permute-start | bytes 12296 | tf_op jit(solution)/shard_map/ppermute | solution.py:161
  25.7 7.8 %shard_map.113 = f32[66,1024]{1,0:T(8,128)} custom-call(s32[8]{0:T(128)} %reshape.68.refs_0_, bf16[1024,128]{1,0:T(8,128)(2,1)} %refs_1_.2, bf16[2048,128]{1,0:T(8,128)(2,1)} %refs_2_.1, f32[2048,1]{1,0:T(8,128)} %copy.18.refs_3_, bf16[64,2048]{1,0:T(8,128)(2,1)} %bitcast.36), custom_call_target="tpu_custom_call" | custom-call | tf_op jit(solution)/shard_map/pallas_call | solution.py:50
  34.7 3.5 %collective-permute-start.3 = (f32[66,512]{1,0:T(8,128)S(1)}, f32[66,512]{1,0:T(8,128)S(1)}, u32[]{:S(2)}, u32[]{:S(2)}) collective-permute-start(f32[66,512]{1,0:T(8,128)S(1)} %constant_dynamic-slice_fusion.1), channel_id=1, source_target_pairs={{0,8},{1,9},{2,10},{3,11},{4,12},{5,13},{6,14},{7,15},{8,0},{9,1},... | collective-permute-start | bytes 405512 | tf_op jit(solution)/shard_map/ppermute | solution.py:107
  38.2 4.7 %collective-permute-done.3 = f32[66,512]{1,0:T(8,128)S(1)} collective-permute-done((f32[66,512]{1,0:T(8,128)S(1)}, f32[66,512]{1,0:T(8,128)S(1)}, u32[]{:S(2)}, u32[]{:S(2)}) %collective-permute-start.3) | collective-permute-done | bytes 135200 | tf_op jit(solution)/shard_map/ppermute | solution.py:107
  43.1 1.9 %collective-permute-start.4 = (f32[66,512]{1,0:T(8,128)S(1)}, f32[66,512]{1,0:T(8,128)S(1)}, u32[]{:S(2)}, u32[]{:S(2)}) collective-permute-start(f32[66,512]{1,0:T(8,128)S(1)} %pad_maximum_fusion.2), channel_id=1, source_target_pairs={{0,1},{1,0},{2,3},{3,2},{4,5},{5,4},{6,7},{7,6},{8,9},{9,8},{10,11... | collective-permute-start | bytes 405512 | tf_op jit(solution)/shard_map/ppermute | solution.py:110
  45.0 5.5 %collective-permute-done.4 = f32[66,512]{1,0:T(8,128)S(1)} collective-permute-done((f32[66,512]{1,0:T(8,128)S(1)}, f32[66,512]{1,0:T(8,128)S(1)}, u32[]{:S(2)}, u32[]{:S(2)}) %collective-permute-start.4) | collective-permute-done | bytes 135200 | tf_op jit(solution)/shard_map/ppermute | solution.py:110
  50.6 4.2 %collective-permute-start.5 = (f32[66,512]{1,0:T(8,128)S(1)}, f32[66,512]{1,0:T(8,128)S(1)}, u32[]{:S(2)}, u32[]{:S(2)}) collective-permute-start(f32[66,512]{1,0:T(8,128)S(1)} %pad_maximum_fusion.3), channel_id=1, source_target_pairs={{0,2},{1,3},{2,0},{3,1},{4,6},{5,7},{6,4},{7,5},{8,10},{9,11},{10,... | collective-permute-start | bytes 405512 | tf_op jit(solution)/shard_map/ppermute | solution.py:110
  54.8 4.8 %collective-permute-done.5 = f32[66,512]{1,0:T(8,128)S(1)} collective-permute-done((f32[66,512]{1,0:T(8,128)S(1)}, f32[66,512]{1,0:T(8,128)S(1)}, u32[]{:S(2)}, u32[]{:S(2)}) %collective-permute-start.5) | collective-permute-done | bytes 135200 | tf_op jit(solution)/shard_map/ppermute | solution.py:110
  61.7 12.2 %collective-permute-done.6 = f32[66,512]{1,0:T(8,128)S(1)} collective-permute-done((f32[66,512]{1,0:T(8,128)S(1)}, f32[66,512]{1,0:T(8,128)S(1)}, u32[]{:S(2)}, u32[]{:S(2)}) %collective-permute-start.6) | collective-permute-done | bytes 135200 | tf_op jit(solution)/shard_map/ppermute | solution.py:110
  74.8 3.2 %collective-permute-start.7 = (bf16[64,512]{1,0:T(8,128)(2,1)S(1)}, bf16[64,512]{1,0:T(8,128)(2,1)S(1)}, u32[]{:S(2)}, u32[]{:S(2)}) collective-permute-start(bf16[64,512]{1,0:T(8,128)(2,1)S(1)} %fusion.11), channel_id=1, source_target_pairs={{0,8},{1,9},{2,10},{3,11},{4,12},{5,13},{6,14},{7,15},{8,0},{9,1},... | collective-permute-start | bytes 196616 | tf_op jit(solution)/shard_map/ppermute | solution.py:116
  78.0 3.0 %collective-permute-done.7 = bf16[64,512]{1,0:T(8,128)(2,1)S(1)} collective-permute-done((bf16[64,512]{1,0:T(8,128)(2,1)S(1)}, bf16[64,512]{1,0:T(8,128)(2,1)S(1)}, u32[]{:S(2)}, u32[]{:S(2)}) %collective-permute-start.7) | collective-permute-done | bytes 65568 | tf_op jit(solution)/shard_map/ppermute | solution.py:116
  81.0 5.3 %collective-permute-start.9 = (bf16[64,1024]{1,0:T(8,128)(2,1)S(1)}, bf16[64,1024]{1,0:T(8,128)(2,1)S(1)}, u32[]{:S(2)}, u32[]{:S(2)}) collective-permute-start(bf16[64,1024]{1,0:T(8,128)(2,1)S(1)} %maximum_select_fusion), channel_id=1, source_target_pairs={{0,0},{33,1},{66,2},{99,3},{132,4},{165,5},{198,6},{231,7},{264,8}... | collective-permute-start | bytes 393224 | tf_op jit(solution)/shard_map/ppermute | solution.py:145
  93.3 7.1 %shard_map.114 = f32[66,1024]{1,0:T(8,128)} custom-call(s32[8]{0:T(128)} %reshape.71.refs_0_, bf16[1024,128]{1,0:T(8,128)(2,1)} %refs_1_.3, bf16[2048,128]{1,0:T(8,128)(2,1)} %pad_maximum_fusion.refs_2_, f32[2048,1]{1,0:T(8,128)} %copy.21.refs_3_, bf16[64,2048]{1,0:T(8,128)(2,1)} %pad_maximum_fusion.1.refs_4_), custom_call_target="tpu_custom_call" | custom-call | tf_op jit(solution)/shard_map/pallas_call | solution.py:50
  101.4 13.2 %collective-permute-start.10 = (f32[66,512]{1,0:T(8,128)S(1)}, f32[66,512]{1,0:T(8,128)S(1)}, u32[]{:S(2)}, u32[]{:S(2)}) collective-permute-start(f32[66,512]{1,0:T(8,128)S(1)} %constant_dynamic-slice_fusion), channel_id=1, source_target_pairs={{0,8},{1,9},{2,10},{3,11},{4,12},{5,13},{6,14},{7,15},{8,0},{9,1},... | collective-permute-start | bytes 405512 | tf_op jit(solution)/shard_map/ppermute | solution.py:107
  114.6 3.1 %collective-permute-done.10 = f32[66,512]{1,0:T(8,128)S(1)} collective-permute-done((f32[66,512]{1,0:T(8,128)S(1)}, f32[66,512]{1,0:T(8,128)S(1)}, u32[]{:S(2)}, u32[]{:S(2)}) %collective-permute-start.10) | collective-permute-done | bytes 135200 | tf_op jit(solution)/shard_map/ppermute | solution.py:107
  117.9 1.9 %collective-permute-start.11 = (f32[66,512]{1,0:T(8,128)S(1)}, f32[66,512]{1,0:T(8,128)S(1)}, u32[]{:S(2)}, u32[]{:S(2)}) collective-permute-start(f32[66,512]{1,0:T(8,128)S(1)} %pad_maximum_fusion.5), channel_id=1, source_target_pairs={{0,1},{1,0},{2,3},{3,2},{4,5},{5,4},{6,7},{7,6},{8,9},{9,8},{10,11... | collective-permute-start | bytes 405512 | tf_op jit(solution)/shard_map/ppermute | solution.py:110
  119.8 5.1 %collective-permute-done.11 = f32[66,512]{1,0:T(8,128)S(1)} collective-permute-done((f32[66,512]{1,0:T(8,128)S(1)}, f32[66,512]{1,0:T(8,128)S(1)}, u32[]{:S(2)}, u32[]{:S(2)}) %collective-permute-start.11) | collective-permute-done | bytes 135200 | tf_op jit(solution)/shard_map/ppermute | solution.py:110
  125.0 8.3 %collective-permute-start.12 = (f32[66,512]{1,0:T(8,128)S(1)}, f32[66,512]{1,0:T(8,128)S(1)}, u32[]{:S(2)}, u32[]{:S(2)}) collective-permute-start(f32[66,512]{1,0:T(8,128)S(1)} %pad_maximum_fusion.6), channel_id=1, source_target_pairs={{0,2},{1,3},{2,0},{3,1},{4,6},{5,7},{6,4},{7,5},{8,10},{9,11},{10,... | collective-permute-start | bytes 405512 | tf_op jit(solution)/shard_map/ppermute | solution.py:110
  133.3 6.0 %collective-permute-done.12 = f32[66,512]{1,0:T(8,128)S(1)} collective-permute-done((f32[66,512]{1,0:T(8,128)S(1)}, f32[66,512]{1,0:T(8,128)S(1)}, u32[]{:S(2)}, u32[]{:S(2)}) %collective-permute-start.12) | collective-permute-done | bytes 135200 | tf_op jit(solution)/shard_map/ppermute | solution.py:110
  141.3 12.8 %collective-permute-done.13 = f32[66,512]{1,0:T(8,128)S(1)} collective-permute-done((f32[66,512]{1,0:T(8,128)S(1)}, f32[66,512]{1,0:T(8,128)S(1)}, u32[]{:S(2)}, u32[]{:S(2)}) %collective-permute-start.13) | collective-permute-done | bytes 135200 | tf_op jit(solution)/shard_map/ppermute | solution.py:110
  155.1 3.6 %collective-permute-start.14 = (bf16[64,512]{1,0:T(8,128)(2,1)S(1)}, bf16[64,512]{1,0:T(8,128)(2,1)S(1)}, u32[]{:S(2)}, u32[]{:S(2)}) collective-permute-start(bf16[64,512]{1,0:T(8,128)(2,1)S(1)} %fusion.9), channel_id=1, source_target_pairs={{0,8},{1,9},{2,10},{3,11},{4,12},{5,13},{6,14},{7,15},{8,0},{9,1},... | collective-permute-start | bytes 196616 | tf_op jit(solution)/shard_map/ppermute | solution.py:116
  158.7 2.5 %collective-permute-done.14 = bf16[64,512]{1,0:T(8,128)(2,1)S(1)} collective-permute-done((bf16[64,512]{1,0:T(8,128)(2,1)S(1)}, bf16[64,512]{1,0:T(8,128)(2,1)S(1)}, u32[]{:S(2)}, u32[]{:S(2)}) %collective-permute-start.14) | collective-permute-done | bytes 65568 | tf_op jit(solution)/shard_map/ppermute | solution.py:116
  (81 shorter events, 20.0 us)
Async XLA Ops:
  0.6 21.8 %copy-start = (s32[64,64]{1,0:T(8,128)S(1)}, s32[64,64]{1,0:T(8,128)}, u32[]{:S(2)}) copy-start(s32[64,64]{1,0:T(8,128)} %param.16) | copy-start | bytes 49156
  0.6 32.9 %collective-permute-start.1 = (bf16[1024,128]{1,0:T(8,128)(2,1)}, bf16[1024,128]{1,0:T(8,128)(2,1)S(1)}, u32[]{:S(2)}, u32[]{:S(2)}) collective-permute-start(bf16[1024,128]{1,0:T(8,128)(2,1)} %refs_1_.2), channel_id=1, source_target_pairs={{0,0},{33,1},{66,2},{99,3},{132,4},{165,5},{198,6},{231,7},{264,8}... | collective-permute-start | bytes 786440 | tf_op jit(solution)/shard_map/ppermute | solution.py:145
  5.3 28.2 %collective-permute-start = (bf16[1024,128]{1,0:T(8,128)(2,1)}, bf16[1024,128]{1,0:T(8,128)(2,1)S(1)}, u32[]{:S(2)}, u32[]{:S(2)}) collective-permute-start(bf16[1024,128]{1,0:T(8,128)(2,1)} %refs_1_.2), channel_id=1, source_target_pairs={{16,0},{49,1},{82,2},{115,3},{148,4},{181,5},{214,6},{247,7},{280,... | collective-permute-start | bytes 786440 | tf_op jit(solution)/shard_map/ppermute | solution.py:145
  7.3 27.2 %collective-permute-start.2 = (bf16[2048]{0:T(1024)(128)(2,1)}, bf16[2048]{0:T(1024)(128)(2,1)S(1)}, u32[]{:S(2)}, u32[]{:S(2)}) collective-permute-start(bf16[2048]{0:T(1024)(128)(2,1)} %param.14), channel_id=1, source_target_pairs={{0,0},{1,1},{2,2},{3,3},{4,4},{5,5},{6,6},{7,7},{8,8},{9,9},{10,10... | collective-permute-start | bytes 12296 | tf_op jit(solution)/shard_map/ppermute | solution.py:161
  21.8 0.7 copy-start.6
  33.6 1.0 copy-start.1
  34.7 8.3 %collective-permute-start.3 = (f32[66,512]{1,0:T(8,128)S(1)}, f32[66,512]{1,0:T(8,128)S(1)}, u32[]{:S(2)}, u32[]{:S(2)}) collective-permute-start(f32[66,512]{1,0:T(8,128)S(1)} %constant_dynamic-slice_fusion.1), channel_id=1, source_target_pairs={{0,8},{1,9},{2,10},{3,11},{4,12},{5,13},{6,14},{7,15},{8,0},{9,1},... | collective-permute-start | bytes 405512 | tf_op jit(solution)/shard_map/ppermute | solution.py:107
  43.1 7.4 %collective-permute-start.4 = (f32[66,512]{1,0:T(8,128)S(1)}, f32[66,512]{1,0:T(8,128)S(1)}, u32[]{:S(2)}, u32[]{:S(2)}) collective-permute-start(f32[66,512]{1,0:T(8,128)S(1)} %pad_maximum_fusion.2), channel_id=1, source_target_pairs={{0,1},{1,0},{2,3},{3,2},{4,5},{5,4},{6,7},{7,6},{8,9},{9,8},{10,11... | collective-permute-start | bytes 405512 | tf_op jit(solution)/shard_map/ppermute | solution.py:110
  50.6 9.0 %collective-permute-start.5 = (f32[66,512]{1,0:T(8,128)S(1)}, f32[66,512]{1,0:T(8,128)S(1)}, u32[]{:S(2)}, u32[]{:S(2)}) collective-permute-start(f32[66,512]{1,0:T(8,128)S(1)} %pad_maximum_fusion.3), channel_id=1, source_target_pairs={{0,2},{1,3},{2,0},{3,1},{4,6},{5,7},{6,4},{7,5},{8,10},{9,11},{10,... | collective-permute-start | bytes 405512 | tf_op jit(solution)/shard_map/ppermute | solution.py:110
  59.7 14.1 %collective-permute-start.6 = (f32[66,512]{1,0:T(8,128)S(1)}, f32[66,512]{1,0:T(8,128)S(1)}, u32[]{:S(2)}, u32[]{:S(2)}) collective-permute-start(f32[66,512]{1,0:T(8,128)S(1)} %pad_maximum_fusion.4), channel_id=1, source_target_pairs={{0,4},{1,5},{2,6},{3,7},{4,0},{5,1},{6,2},{7,3},{8,12},{9,13},{10,... | collective-permute-start | bytes 405512 | tf_op jit(solution)/shard_map/ppermute | solution.py:110
  73.9 0.9 copy-start.4
  74.8 6.2 %collective-permute-start.7 = (bf16[64,512]{1,0:T(8,128)(2,1)S(1)}, bf16[64,512]{1,0:T(8,128)(2,1)S(1)}, u32[]{:S(2)}, u32[]{:S(2)}) collective-permute-start(bf16[64,512]{1,0:T(8,128)(2,1)S(1)} %fusion.11), channel_id=1, source_target_pairs={{0,8},{1,9},{2,10},{3,11},{4,12},{5,13},{6,14},{7,15},{8,0},{9,1},... | collective-permute-start | bytes 196616 | tf_op jit(solution)/shard_map/ppermute | solution.py:116
  81.0 11.3 %copy-start.3 = (bf16[64,1024]{1,0:T(8,128)(2,1)}, bf16[64,1024]{1,0:T(8,128)(2,1)S(1)}, u32[]{:S(2)}) copy-start(bf16[64,1024]{1,0:T(8,128)(2,1)S(1)} %maximum_select_fusion) | copy-start | bytes 393220
  81.0 11.3 %collective-permute-start.9 = (bf16[64,1024]{1,0:T(8,128)(2,1)S(1)}, bf16[64,1024]{1,0:T(8,128)(2,1)S(1)}, u32[]{:S(2)}, u32[]{:S(2)}) collective-permute-start(bf16[64,1024]{1,0:T(8,128)(2,1)S(1)} %maximum_select_fusion), channel_id=1, source_target_pairs={{0,0},{33,1},{66,2},{99,3},{132,4},{165,5},{198,6},{231,7},{264,8}... | collective-permute-start | bytes 393224 | tf_op jit(solution)/shard_map/ppermute | solution.py:145
  86.3 6.3 %collective-permute-start.8 = (bf16[64,1024]{1,0:T(8,128)(2,1)S(1)}, bf16[64,1024]{1,0:T(8,128)(2,1)S(1)}, u32[]{:S(2)}, u32[]{:S(2)}) collective-permute-start(bf16[64,1024]{1,0:T(8,128)(2,1)S(1)} %maximum_select_fusion), channel_id=1, source_target_pairs={{16,0},{49,1},{82,2},{115,3},{148,4},{181,5},{214,6},{247,7},{280,... | collective-permute-start | bytes 393224 | tf_op jit(solution)/shard_map/ppermute | solution.py:145
  100.4 17.3 %copy-start.2 = (f32[66,1024]{1,0:T(8,128)S(1)}, f32[66,1024]{1,0:T(8,128)}, u32[]{:S(2)}) copy-start(f32[66,1024]{1,0:T(8,128)} %shard_map.114) | copy-start | bytes 811012
  101.4 16.3 %collective-permute-start.10 = (f32[66,512]{1,0:T(8,128)S(1)}, f32[66,512]{1,0:T(8,128)S(1)}, u32[]{:S(2)}, u32[]{:S(2)}) collective-permute-start(f32[66,512]{1,0:T(8,128)S(1)} %constant_dynamic-slice_fusion), channel_id=1, source_target_pairs={{0,8},{1,9},{2,10},{3,11},{4,12},{5,13},{6,14},{7,15},{8,0},{9,1},... | collective-permute-start | bytes 405512 | tf_op jit(solution)/shard_map/ppermute | solution.py:107
  117.9 7.0 %collective-permute-start.11 = (f32[66,512]{1,0:T(8,128)S(1)}, f32[66,512]{1,0:T(8,128)S(1)}, u32[]{:S(2)}, u32[]{:S(2)}) collective-permute-start(f32[66,512]{1,0:T(8,128)S(1)} %pad_maximum_fusion.5), channel_id=1, source_target_pairs={{0,1},{1,0},{2,3},{3,2},{4,5},{5,4},{6,7},{7,6},{8,9},{9,8},{10,11... | collective-permute-start | bytes 405512 | tf_op jit(solution)/shard_map/ppermute | solution.py:110
  125.0 14.3 %collective-permute-start.12 = (f32[66,512]{1,0:T(8,128)S(1)}, f32[66,512]{1,0:T(8,128)S(1)}, u32[]{:S(2)}, u32[]{:S(2)}) collective-permute-start(f32[66,512]{1,0:T(8,128)S(1)} %pad_maximum_fusion.6), channel_id=1, source_target_pairs={{0,2},{1,3},{2,0},{3,1},{4,6},{5,7},{6,4},{7,5},{8,10},{9,11},{10,... | collective-permute-start | bytes 405512 | tf_op jit(solution)/shard_map/ppermute | solution.py:110
  139.4 14.8 %collective-permute-start.13 = (f32[66,512]{1,0:T(8,128)S(1)}, f32[66,512]{1,0:T(8,128)S(1)}, u32[]{:S(2)}, u32[]{:S(2)}) collective-permute-start(f32[66,512]{1,0:T(8,128)S(1)} %pad_maximum_fusion.7), channel_id=1, source_target_pairs={{0,4},{1,5},{2,6},{3,7},{4,0},{5,1},{6,2},{7,3},{8,12},{9,13},{10,... | collective-permute-start | bytes 405512 | tf_op jit(solution)/shard_map/ppermute | solution.py:110
  154.1 0.9 copy-start.5
  155.1 6.2 %collective-permute-start.14 = (bf16[64,512]{1,0:T(8,128)(2,1)S(1)}, bf16[64,512]{1,0:T(8,128)(2,1)S(1)}, u32[]{:S(2)}, u32[]{:S(2)}) collective-permute-start(bf16[64,512]{1,0:T(8,128)(2,1)S(1)} %fusion.9), channel_id=1, source_target_pairs={{0,8},{1,9},{2,10},{3,11},{4,12},{5,13},{6,14},{7,15},{8,0},{9,1},... | collective-permute-start | bytes 196616 | tf_op jit(solution)/shard_map/ppermute | solution.py:116

commit v7 on v6

--- a/solution.py
+++ b/solution.py
@@ -70,10 +70,74 @@
     )(live.reshape(-1).astype(jnp.int32), targets, sources, offsets.astype(jnp.float32).reshape(cols, 1), values_t)
 
 
-def date_partials(targets, sources, offsets, values_t, tile_mask, col_tile_ids):
+def weights_kernel(mask_ref, x_ref, y_ref, off_ref, p_ref, stats_ref, *, scale, col_tiles):
+    i = pl.program_id(0)
+
+    def scores(j):
+        y = y_ref[j * BLOCK : (j + 1) * BLOCK, :]
+        s = lax.dot_general(y, x_ref[...], (((1,), (1,)), ((), ())), preferred_element_type=jnp.float32)
+        return s * scale - off_ref[j * BLOCK : (j + 1) * BLOCK, :]
+
+    stats_ref[...] = jnp.concatenate(
+        [jnp.zeros((1, BLOCK), jnp.float32), jnp.full((1, BLOCK), very_low, jnp.float32)], 0
+    )
+    for j in range(col_tiles):
+
+        @pl.when(mask_ref[i * col_tiles + j] > 0)
+        def _():
+            tile_peak = jnp.max(scores(j), axis=0, keepdims=True)
+            stats_ref[1:2, :] = jnp.maximum(stats_ref[1:2, :], tile_peak)
+
+    for j in range(col_tiles):
+        live = mask_ref[i * col_tiles + j] > 0
+
+        @pl.when(live)
+        def _():
+            p = jnp.exp(scores(j) - stats_ref[1:2, :])
+            p_ref[j * BLOCK : (j + 1) * BLOCK, :] = p.astype(jnp.bfloat16)
+            stats_ref[0:1, :] = stats_ref[0:1, :] + jnp.sum(p, axis=0, keepdims=True)
+
+        @pl.when(jnp.logical_not(live))
+        def _():
+            p_ref[j * BLOCK : (j + 1) * BLOCK, :] = jnp.zeros((BLOCK, BLOCK), jnp.bfloat16)
+
+
+def date_weights_kernel(targets, sources, offsets, live):
+    rows, factors = targets.shape
+    cols = sources.shape[0]
+    row_tiles, col_tiles = rows // BLOCK, cols // BLOCK
+    kernel = lambda *refs: weights_kernel(*refs, scale=sharpness / factors**0.5, col_tiles=col_tiles)
+    return pl.pallas_call(
+        kernel,
+        out_shape=(
+            jax.ShapeDtypeStruct((cols, rows), jnp.bfloat16),
+            jax.ShapeDtypeStruct((2, rows), jnp.float32),
+        ),
+        grid_spec=pltpu.PrefetchScalarGridSpec(
+            num_scalar_prefetch=1,
+            grid=(row_tiles,),
+            in_specs=[
+                pl.BlockSpec((BLOCK, factors), lambda i, m: (i, 0)),
+                pl.BlockSpec((cols, factors), lambda i, m: (0, 0)),
+                pl.BlockSpec((cols, 1), lambda i, m: (0, 0)),
+            ],
+            out_specs=(
+                pl.BlockSpec((cols, BLOCK), lambda i, m: (0, i)),
+                pl.BlockSpec((2, BLOCK), lambda i, m: (0, i)),
+            ),
+        ),
+        compiler_params=pltpu.CompilerParams(dimension_semantics=("arbitrary",)),
+    )(live.reshape(-1).astype(jnp.int32), targets, sources, offsets.astype(jnp.float32).reshape(cols, 1))
+
+
+def local_live(targets, tile_mask, col_tile_ids):
     row_tiles = targets.shape[0] // BLOCK
     row_ids = lax.axis_index("tgt") * row_tiles + jnp.arange(row_tiles)
-    live = tile_mask[row_ids][:, col_tile_ids]
+    return tile_mask[row_ids][:, col_tile_ids]
+
+
+def date_partials(targets, sources, offsets, values_t, tile_mask, col_tile_ids):
+    live = local_live(targets, tile_mask, col_tile_ids)
     return date_partials_kernel(targets, sources, offsets, values_t, live)
 
 
@@ -183,14 +247,13 @@
     partials, mid_sources, mid_offsets = lax.optimization_barrier(
         (partials, mid_sources, mid_offsets)
     )
+    early_weights, early_stats = date_weights_kernel(
+        states_early, mid_sources, mid_offsets, local_live(states_early, mask_early, early_col_ids)
+    )
     value_mid_t = finish(partials, exercise_mid)
     mid_values_t = regroup_order(regroup(value_mid_t), axis=1)
-    value_early_t = finish(
-        date_partials(
-            states_early, mid_sources, mid_offsets, mid_values_t, mask_early, early_col_ids
-        ),
-        exercise_early,
-    )
+    early_weighted = jnp.dot(mid_values_t, early_weights, preferred_element_type=jnp.float32)
+    value_early_t = finish(jnp.concatenate([early_weighted, early_stats], 0), exercise_early)
     value_mid, value_early = value_mid_t.T, value_early_t.T
     return (value_mid, value_early)
 

time: 163 us -> 158 us (0.969)
  the two profiles are of different devices: /device:TPU:136 before, /device:TPU:6 now
where the time goes in v7:
time: 158 us; the launch traced here: 156 us
  starting transfers between devices  73.3 us (46%)
  waiting for transfers between devices  50.1 us (32%)
  Pallas kernels  15.1 us (10%)
  local copies, waits for them, and re-layouts  8.3 us (5%)
  other arithmetic  4.59 us (3%)
  matrix products  3.06 us (2%)
    ppermute x6, waiting for transfers between devices, finish(): packed = merge(packed, lax.ppermute(packed, 'src', xor_perm(src_size, bit)))  36.6 us
    ppermute x2, starting transfers between devices, finish(): packed = merge(keep, lax.ppermute(send, 'src', xor_perm(src_size, bit)))  31.3 us
    ppermute x6, starting transfers between devices, finish(): packed = merge(packed, lax.ppermute(packed, 'src', xor_perm(src_size, bit)))  26.2 us
    pallas_call x1, Pallas kernels, date_partials_kernel(): pl.pallas_call(kernel, out_shape=jax.ShapeDtypeStruct((width + 2, rows),...  7.73 us
    pallas_call x1, Pallas kernels, date_weights_kernel(): pl.pallas_call(kernel, out_shape=(jax.ShapeDtypeStruct((cols, rows), jnp....  7.4 us
    ppermute x2, waiting for transfers between devices, finish(): got = lax.ppermute(value, 'src', xor_perm(src_size, bit))  7.19 us
    ppermute x2, waiting for transfers between devices, finish(): packed = merge(keep, lax.ppermute(send, 'src', xor_perm(src_size, bit)))  6.3 us
    ppermute x4, starting transfers between devices, regroup(): return [lax.ppermute(block_rows, ('tgt', 'src'), p) for p in perms]  6.12 us
  transfers between devices with their start and end apart: 15, of which 10 were waited for; matrix products, arithmetic and copies ran while one was open for 6% of the time, Pallas kernels for 10%

profile of v7, /device:TPU:6, one launch (start us, length us, event | category | flops | bytes accessed | tf_op | source)
XLA Modules:
  0.0 155.6 jit_solution(17896857258886874489)
XLA Ops:
  4.2 4.6 %collective-permute-start.2 = (bf16[2048]{0:T(1024)(128)(2,1)}, bf16[2048]{0:T(1024)(128)(2,1)S(1)}, u32[]{:S(2)}, u32[]{:S(2)}) collective-permute-start(bf16[2048]{0:T(1024)(128)(2,1)} %param.14), channel_id=1, source_target_pairs={{0,0},{1,1},{2,2},{3,3},{4,4},{5,5},{6,6},{7,7},{8,8},{9,9},{10,10... | collective-permute-start | bytes 12296 | tf_op jit(solution)/shard_map/ppermute | solution.py:225
  12.9 7.7 %shard_map.113 = f32[66,1024]{1,0:T(8,128)} custom-call(s32[8]{0:T(128)} %reshape.68.refs_0_, bf16[1024,128]{1,0:T(8,128)(2,1)} %refs_1_.2, bf16[2048,128]{1,0:T(8,128)(2,1)} %refs_2_.1, f32[2048,1]{1,0:T(8,128)} %copy.18.refs_3_, bf16[64,2048]{1,0:T(8,128)(2,1)} %bitcast.37), custom_call_target="tpu_custom_call" | custom-call | tf_op jit(solution)/shard_map/pallas_call | solution.py:50
  22.5 17.9 %collective-permute-start.3 = (f32[66,512]{1,0:T(8,128)S(1)}, f32[66,512]{1,0:T(8,128)S(1)}, u32[]{:S(2)}, u32[]{:S(2)}) collective-permute-start(f32[66,512]{1,0:T(8,128)S(1)} %constant_dynamic-slice_fusion), channel_id=1, source_target_pairs={{0,8},{1,9},{2,10},{3,11},{4,12},{5,13},{6,14},{7,15},{8,0},{9,1},... | collective-permute-start | bytes 405512 | tf_op jit(solution)/shard_map/ppermute | solution.py:171
  40.4 3.2 %collective-permute-done.3 = f32[66,512]{1,0:T(8,128)S(1)} collective-permute-done((f32[66,512]{1,0:T(8,128)S(1)}, f32[66,512]{1,0:T(8,128)S(1)}, u32[]{:S(2)}, u32[]{:S(2)}) %collective-permute-start.3) | collective-permute-done | bytes 135200 | tf_op jit(solution)/shard_map/ppermute | solution.py:171
  45.3 3.7 %collective-permute-start.4 = (f32[66,512]{1,0:T(8,128)S(1)}, f32[66,512]{1,0:T(8,128)S(1)}, u32[]{:S(2)}, u32[]{:S(2)}) collective-permute-start(f32[66,512]{1,0:T(8,128)S(1)} %pad_maximum_fusion.1), channel_id=1, source_target_pairs={{0,1},{1,0},{2,3},{3,2},{4,5},{5,4},{6,7},{7,6},{8,9},{9,8},{10,11... | collective-permute-start | bytes 405512 | tf_op jit(solution)/shard_map/ppermute | solution.py:174
  49.1 3.3 %collective-permute-done.4 = f32[66,512]{1,0:T(8,128)S(1)} collective-permute-done((f32[66,512]{1,0:T(8,128)S(1)}, f32[66,512]{1,0:T(8,128)S(1)}, u32[]{:S(2)}, u32[]{:S(2)}) %collective-permute-start.4) | collective-permute-done | bytes 135200 | tf_op jit(solution)/shard_map/ppermute | solution.py:174
  52.5 5.8 %collective-permute-start.5 = (f32[66,512]{1,0:T(8,128)S(1)}, f32[66,512]{1,0:T(8,128)S(1)}, u32[]{:S(2)}, u32[]{:S(2)}) collective-permute-start(f32[66,512]{1,0:T(8,128)S(1)} %pad_maximum_fusion.2), channel_id=1, source_target_pairs={{0,2},{1,3},{2,0},{3,1},{4,6},{5,7},{6,4},{7,5},{8,10},{9,11},{10,... | collective-permute-start | bytes 405512 | tf_op jit(solution)/shard_map/ppermute | solution.py:174
  58.3 5.4 %collective-permute-done.5 = f32[66,512]{1,0:T(8,128)S(1)} collective-permute-done((f32[66,512]{1,0:T(8,128)S(1)}, f32[66,512]{1,0:T(8,128)S(1)}, u32[]{:S(2)}, u32[]{:S(2)}) %collective-permute-start.5) | collective-permute-done | bytes 135200 | tf_op jit(solution)/shard_map/ppermute | solution.py:174
  63.7 4.5 %collective-permute-start.6 = (f32[66,512]{1,0:T(8,128)S(1)}, f32[66,512]{1,0:T(8,128)S(1)}, u32[]{:S(2)}, u32[]{:S(2)}) collective-permute-start(f32[66,512]{1,0:T(8,128)S(1)} %pad_maximum_fusion.3), channel_id=1, source_target_pairs={{0,4},{1,5},{2,6},{3,7},{4,0},{5,1},{6,2},{7,3},{8,12},{9,13},{10,... | collective-permute-start | bytes 405512 | tf_op jit(solution)/shard_map/ppermute | solution.py:174
  68.2 8.5 %collective-permute-done.6 = f32[66,512]{1,0:T(8,128)S(1)} collective-permute-done((f32[66,512]{1,0:T(8,128)S(1)}, f32[66,512]{1,0:T(8,128)S(1)}, u32[]{:S(2)}, u32[]{:S(2)}) %collective-permute-start.6) | collective-permute-done | bytes 135200 | tf_op jit(solution)/shard_map/ppermute | solution.py:174
  76.9 2.4 %collective-permute-start.7 = (bf16[64,512]{1,0:T(8,128)(2,1)S(1)}, bf16[64,512]{1,0:T(8,128)(2,1)S(1)}, u32[]{:S(2)}, u32[]{:S(2)}) collective-permute-start(bf16[64,512]{1,0:T(8,128)(2,1)S(1)} %fusion.17), channel_id=1, source_target_pairs={{0,8},{1,9},{2,10},{3,11},{4,12},{5,13},{6,14},{7,15},{8,0},{9,1},... | collective-permute-start | bytes 196616 | tf_op jit(solution)/shard_map/ppermute | solution.py:180
  79.3 3.7 %collective-permute-done.7 = bf16[64,512]{1,0:T(8,128)(2,1)S(1)} collective-permute-done((bf16[64,512]{1,0:T(8,128)(2,1)S(1)}, bf16[64,512]{1,0:T(8,128)(2,1)S(1)}, u32[]{:S(2)}, u32[]{:S(2)}) %collective-permute-start.7) | collective-permute-done | bytes 65568 | tf_op jit(solution)/shard_map/ppermute | solution.py:180
  89.8 7.4 %shard_map.114 = (bf16[2048,1024]{1,0:T(8,128)(2,1)}, f32[2,1024]{1,0:T(2,128)}) custom-call(s32[8]{0:T(128)} %reshape.71.refs_0_, bf16[1024,128]{1,0:T(8,128)(2,1)} %refs_1_.3, bf16[2048,128]{1,0:T(8,128)(2,1)} %pad_maximum_fusion.refs_2_, f32[2048,1]{1,0:T(8,128)} %copy.21.refs_3_), custom_call_target="tpu_custom_call" | custom-call | tf_op jit(solution)/shard_map/pallas_call | solution.py:110
  97.2 3.1 %fusion = f32[64,1024]{1,0:T(8,128)S(1)} fusion(bf16[2048,1024]{1,0:T(8,128)(2,1)} %get-tuple-element.10, bf16[64,1024]{1,0:T(8,128)(2,1)S(1)} %get-tuple-element.29, bf16[64,1024]{1,0:T(8,128)(2,1)S(1)} %get-tuple-element.28), kind=kOutput, calls=%fused_computation.9 | convolution fusion | flops 268959744 | bytes 4718592 | tf_op jit(solution)/shard_map/dot_general | solution.py:255
  100.4 13.4 %collective-permute-start.10 = (f32[66,512]{1,0:T(8,128)S(1)}, f32[66,512]{1,0:T(8,128)S(1)}, u32[]{:S(2)}, u32[]{:S(2)}) collective-permute-start(f32[66,512]{1,0:T(8,128)S(1)} %get-tuple-element.26), channel_id=1, source_target_pairs={{0,8},{1,9},{2,10},{3,11},{4,12},{5,13},{6,14},{7,15},{8,0},{9,1},... | collective-permute-start | bytes 405512 | tf_op jit(solution)/shard_map/ppermute | solution.py:171
  113.7 3.1 %collective-permute-done.10 = f32[66,512]{1,0:T(8,128)S(1)} collective-permute-done((f32[66,512]{1,0:T(8,128)S(1)}, f32[66,512]{1,0:T(8,128)S(1)}, u32[]{:S(2)}, u32[]{:S(2)}) %collective-permute-start.10) | collective-permute-done | bytes 135200 | tf_op jit(solution)/shard_map/ppermute | solution.py:171
  116.9 4.0 %collective-permute-start.11 = (f32[66,512]{1,0:T(8,128)S(1)}, f32[66,512]{1,0:T(8,128)S(1)}, u32[]{:S(2)}, u32[]{:S(2)}) collective-permute-start(f32[66,512]{1,0:T(8,128)S(1)} %pad_maximum_fusion.4), channel_id=1, source_target_pairs={{0,1},{1,0},{2,3},{3,2},{4,5},{5,4},{6,7},{7,6},{8,9},{9,8},{10,11... | collective-permute-start | bytes 405512 | tf_op jit(solution)/shard_map/ppermute | solution.py:174
  120.9 4.1 %collective-permute-done.11 = f32[66,512]{1,0:T(8,128)S(1)} collective-permute-done((f32[66,512]{1,0:T(8,128)S(1)}, f32[66,512]{1,0:T(8,128)S(1)}, u32[]{:S(2)}, u32[]{:S(2)}) %collective-permute-start.11) | collective-permute-done | bytes 135200 | tf_op jit(solution)/shard_map/ppermute | solution.py:174
  125.1 4.8 %collective-permute-start.12 = (f32[66,512]{1,0:T(8,128)S(1)}, f32[66,512]{1,0:T(8,128)S(1)}, u32[]{:S(2)}, u32[]{:S(2)}) collective-permute-start(f32[66,512]{1,0:T(8,128)S(1)} %pad_maximum_fusion.5), channel_id=1, source_target_pairs={{0,2},{1,3},{2,0},{3,1},{4,6},{5,7},{6,4},{7,5},{8,10},{9,11},{10,... | collective-permute-start | bytes 405512 | tf_op jit(solution)/shard_map/ppermute | solution.py:174
  129.9 6.4 %collective-permute-done.12 = f32[66,512]{1,0:T(8,128)S(1)} collective-permute-done((f32[66,512]{1,0:T(8,128)S(1)}, f32[66,512]{1,0:T(8,128)S(1)}, u32[]{:S(2)}, u32[]{:S(2)}) %collective-permute-start.12) | collective-permute-done | bytes 135200 | tf_op jit(solution)/shard_map/ppermute | solution.py:174
  136.4 3.3 %collective-permute-start.13 = (f32[66,512]{1,0:T(8,128)S(1)}, f32[66,512]{1,0:T(8,128)S(1)}, u32[]{:S(2)}, u32[]{:S(2)}) collective-permute-start(f32[66,512]{1,0:T(8,128)S(1)} %pad_maximum_fusion.6), channel_id=1, source_target_pairs={{0,4},{1,5},{2,6},{3,7},{4,0},{5,1},{6,2},{7,3},{8,12},{9,13},{10,... | collective-permute-start | bytes 405512 | tf_op jit(solution)/shard_map/ppermute | solution.py:174
  139.8 8.8 %collective-permute-done.13 = f32[66,512]{1,0:T(8,128)S(1)} collective-permute-done((f32[66,512]{1,0:T(8,128)S(1)}, f32[66,512]{1,0:T(8,128)S(1)}, u32[]{:S(2)}, u32[]{:S(2)}) %collective-permute-start.13) | collective-permute-done | bytes 135200 | tf_op jit(solution)/shard_map/ppermute | solution.py:174
  148.7 2.7 %collective-permute-start.14 = (bf16[64,512]{1,0:T(8,128)(2,1)S(1)}, bf16[64,512]{1,0:T(8,128)(2,1)S(1)}, u32[]{:S(2)}, u32[]{:S(2)}) collective-permute-start(bf16[64,512]{1,0:T(8,128)(2,1)S(1)} %fusion.15), channel_id=1, source_target_pairs={{0,8},{1,9},{2,10},{3,11},{4,12},{5,13},{6,14},{7,15},{8,0},{9,1},... | collective-permute-start | bytes 196616 | tf_op jit(solution)/shard_map/ppermute | solution.py:180
  151.4 3.5 %collective-permute-done.14 = bf16[64,512]{1,0:T(8,128)(2,1)S(1)} collective-permute-done((bf16[64,512]{1,0:T(8,128)(2,1)S(1)}, bf16[64,512]{1,0:T(8,128)(2,1)S(1)}, u32[]{:S(2)}, u32[]{:S(2)}) %collective-permute-start.14) | collective-permute-done | bytes 65568 | tf_op jit(solution)/shard_map/ppermute | solution.py:180
  (77 shorter events, 19.0 us)
Async XLA Ops:
  0.6 8.3 %copy-start = (s32[64,64]{1,0:T(8,128)S(1)}, s32[64,64]{1,0:T(8,128)}, u32[]{:S(2)}) copy-start(s32[64,64]{1,0:T(8,128)} %param.16) | copy-start | bytes 49156
  0.6 20.0 %collective-permute-start = (bf16[1024,128]{1,0:T(8,128)(2,1)}, bf16[1024,128]{1,0:T(8,128)(2,1)S(1)}, u32[]{:S(2)}, u32[]{:S(2)}) collective-permute-start(bf16[1024,128]{1,0:T(8,128)(2,1)} %refs_1_.2), channel_id=1, source_target_pairs={{16,0},{49,1},{82,2},{115,3},{148,4},{181,5},{214,6},{247,7},{280,... | collective-permute-start | bytes 786440 | tf_op jit(solution)/shard_map/ppermute | solution.py:209
  2.6 18.1 %collective-permute-start.1 = (bf16[1024,128]{1,0:T(8,128)(2,1)}, bf16[1024,128]{1,0:T(8,128)(2,1)S(1)}, u32[]{:S(2)}, u32[]{:S(2)}) collective-permute-start(bf16[1024,128]{1,0:T(8,128)(2,1)} %refs_1_.2), channel_id=1, source_target_pairs={{0,0},{33,1},{66,2},{99,3},{132,4},{165,5},{198,6},{231,7},{264,8}... | collective-permute-start | bytes 786440 | tf_op jit(solution)/shard_map/ppermute | solution.py:209
  4.2 17.4 %collective-permute-start.2 = (bf16[2048]{0:T(1024)(128)(2,1)}, bf16[2048]{0:T(1024)(128)(2,1)S(1)}, u32[]{:S(2)}, u32[]{:S(2)}) collective-permute-start(bf16[2048]{0:T(1024)(128)(2,1)} %param.14), channel_id=1, source_target_pairs={{0,0},{1,1},{2,2},{3,3},{4,4},{5,5},{6,6},{7,7},{8,8},{9,9},{10,10... | collective-permute-start | bytes 12296 | tf_op jit(solution)/shard_map/ppermute | solution.py:225
  11.6 65.3 %copy-start.2 = (bf16[1024,64]{0,1:T(8,128)(2,1)S(1)}, bf16[1024,64]{0,1:T(8,128)(2,1)}, u32[]{:S(2)}) copy-start(bf16[1024,64]{0,1:T(8,128)(2,1)} %param.15) | copy-start | bytes 393220
  22.5 21.1 %collective-permute-start.3 = (f32[66,512]{1,0:T(8,128)S(1)}, f32[66,512]{1,0:T(8,128)S(1)}, u32[]{:S(2)}, u32[]{:S(2)}) collective-permute-start(f32[66,512]{1,0:T(8,128)S(1)} %constant_dynamic-slice_fusion), channel_id=1, source_target_pairs={{0,8},{1,9},{2,10},{3,11},{4,12},{5,13},{6,14},{7,15},{8,0},{9,1},... | collective-permute-start | bytes 405512 | tf_op jit(solution)/shard_map/ppermute | solution.py:171
  45.3 7.1 %collective-permute-start.4 = (f32[66,512]{1,0:T(8,128)S(1)}, f32[66,512]{1,0:T(8,128)S(1)}, u32[]{:S(2)}, u32[]{:S(2)}) collective-permute-start(f32[66,512]{1,0:T(8,128)S(1)} %pad_maximum_fusion.1), channel_id=1, source_target_pairs={{0,1},{1,0},{2,3},{3,2},{4,5},{5,4},{6,7},{7,6},{8,9},{9,8},{10,11... | collective-permute-start | bytes 405512 | tf_op jit(solution)/shard_map/ppermute | solution.py:174
  52.5 11.1 %collective-permute-start.5 = (f32[66,512]{1,0:T(8,128)S(1)}, f32[66,512]{1,0:T(8,128)S(1)}, u32[]{:S(2)}, u32[]{:S(2)}) collective-permute-start(f32[66,512]{1,0:T(8,128)S(1)} %pad_maximum_fusion.2), channel_id=1, source_target_pairs={{0,2},{1,3},{2,0},{3,1},{4,6},{5,7},{6,4},{7,5},{8,10},{9,11},{10,... | collective-permute-start | bytes 405512 | tf_op jit(solution)/shard_map/ppermute | solution.py:174
  63.7 13.1 %collective-permute-start.6 = (f32[66,512]{1,0:T(8,128)S(1)}, f32[66,512]{1,0:T(8,128)S(1)}, u32[]{:S(2)}, u32[]{:S(2)}) collective-permute-start(f32[66,512]{1,0:T(8,128)S(1)} %pad_maximum_fusion.3), channel_id=1, source_target_pairs={{0,4},{1,5},{2,6},{3,7},{4,0},{5,1},{6,2},{7,3},{8,12},{9,13},{10,... | collective-permute-start | bytes 405512 | tf_op jit(solution)/shard_map/ppermute | solution.py:174
  76.9 6.2 %collective-permute-start.7 = (bf16[64,512]{1,0:T(8,128)(2,1)S(1)}, bf16[64,512]{1,0:T(8,128)(2,1)S(1)}, u32[]{:S(2)}, u32[]{:S(2)}) collective-permute-start(bf16[64,512]{1,0:T(8,128)(2,1)S(1)} %fusion.17), channel_id=1, source_target_pairs={{0,8},{1,9},{2,10},{3,11},{4,12},{5,13},{6,14},{7,15},{8,0},{9,1},... | collective-permute-start | bytes 196616 | tf_op jit(solution)/shard_map/ppermute | solution.py:180
  83.1 17.3 %copy-start.1 = (bf16[64,1024]{1,0:T(8,128)(2,1)}, bf16[64,1024]{1,0:T(8,128)(2,1)S(1)}, u32[]{:S(2)}) copy-start(bf16[64,1024]{1,0:T(8,128)(2,1)S(1)} %maximum_select_fusion) | copy-start | bytes 393220
  83.1 14.1 %collective-permute-start.8 = (bf16[64,1024]{1,0:T(8,128)(2,1)S(1)}, bf16[64,1024]{1,0:T(8,128)(2,1)S(1)}, u32[]{:S(2)}, u32[]{:S(2)}) collective-permute-start(bf16[64,1024]{1,0:T(8,128)(2,1)S(1)} %maximum_select_fusion), channel_id=1, source_target_pairs={{16,0},{49,1},{82,2},{115,3},{148,4},{181,5},{214,6},{247,7},{280,... | collective-permute-start | bytes 393224 | tf_op jit(solution)/shard_map/ppermute | solution.py:209
  85.0 12.2 %collective-permute-start.9 = (bf16[64,1024]{1,0:T(8,128)(2,1)S(1)}, bf16[64,1024]{1,0:T(8,128)(2,1)S(1)}, u32[]{:S(2)}, u32[]{:S(2)}) collective-permute-start(bf16[64,1024]{1,0:T(8,128)(2,1)S(1)} %maximum_select_fusion), channel_id=1, source_target_pairs={{0,0},{33,1},{66,2},{99,3},{132,4},{165,5},{198,6},{231,7},{264,8}... | collective-permute-start | bytes 393224 | tf_op jit(solution)/shard_map/ppermute | solution.py:209
  97.2 3.1 %copy-start.4 = (f32[2,1024]{1,0:T(2,128)S(1)}, f32[2,1024]{1,0:T(2,128)}, u32[]{:S(2)}) copy-start(f32[2,1024]{1,0:T(2,128)} %get-tuple-element.11) | copy-start | bytes 24580
  97.2 51.5 %copy-start.3 = (bf16[1024,64]{0,1:T(8,128)(2,1)S(1)}, bf16[1024,64]{0,1:T(8,128)(2,1)}, u32[]{:S(2)}) copy-start(bf16[1024,64]{0,1:T(8,128)(2,1)} %param.18) | copy-start | bytes 393220
  100.4 16.5 %collective-permute-start.10 = (f32[66,512]{1,0:T(8,128)S(1)}, f32[66,512]{1,0:T(8,128)S(1)}, u32[]{:S(2)}, u32[]{:S(2)}) collective-permute-start(f32[66,512]{1,0:T(8,128)S(1)} %get-tuple-element.26), channel_id=1, source_target_pairs={{0,8},{1,9},{2,10},{3,11},{4,12},{5,13},{6,14},{7,15},{8,0},{9,1},... | collective-permute-start | bytes 405512 | tf_op jit(solution)/shard_map/ppermute | solution.py:171
  116.9 8.1 %collective-permute-start.11 = (f32[66,512]{1,0:T(8,128)S(1)}, f32[66,512]{1,0:T(8,128)S(1)}, u32[]{:S(2)}, u32[]{:S(2)}) collective-permute-start(f32[66,512]{1,0:T(8,128)S(1)} %pad_maximum_fusion.4), channel_id=1, source_target_pairs={{0,1},{1,0},{2,3},{3,2},{4,5},{5,4},{6,7},{7,6},{8,9},{9,8},{10,11... | collective-permute-start | bytes 405512 | tf_op jit(solution)/shard_map/ppermute | solution.py:174
  125.1 11.2 %collective-permute-start.12 = (f32[66,512]{1,0:T(8,128)S(1)}, f32[66,512]{1,0:T(8,128)S(1)}, u32[]{:S(2)}, u32[]{:S(2)}) collective-permute-start(f32[66,512]{1,0:T(8,128)S(1)} %pad_maximum_fusion.5), channel_id=1, source_target_pairs={{0,2},{1,3},{2,0},{3,1},{4,6},{5,7},{6,4},{7,5},{8,10},{9,11},{10,... | collective-permute-start | bytes 405512 | tf_op jit(solution)/shard_map/ppermute | solution.py:174
  136.4 12.2 %collective-permute-start.13 = (f32[66,512]{1,0:T(8,128)S(1)}, f32[66,512]{1,0:T(8,128)S(1)}, u32[]{:S(2)}, u32[]{:S(2)}) collective-permute-start(f32[66,512]{1,0:T(8,128)S(1)} %pad_maximum_fusion.6), channel_id=1, source_target_pairs={{0,4},{1,5},{2,6},{3,7},{4,0},{5,1},{6,2},{7,3},{8,12},{9,13},{10,... | collective-permute-start | bytes 405512 | tf_op jit(solution)/shard_map/ppermute | solution.py:174
  148.7 6.2 %collective-permute-start.14 = (bf16[64,512]{1,0:T(8,128)(2,1)S(1)}, bf16[64,512]{1,0:T(8,128)(2,1)S(1)}, u32[]{:S(2)}, u32[]{:S(2)}) collective-permute-start(bf16[64,512]{1,0:T(8,128)(2,1)S(1)} %fusion.15), channel_id=1, source_target_pairs={{0,8},{1,9},{2,10},{3,11},{4,12},{5,13},{6,14},{7,15},{8,0},{9,1},... | collective-permute-start | bytes 196616 | tf_op jit(solution)/shard_map/ppermute | solution.py:180

commit v8 on v7

--- a/solution.py
+++ b/solution.py
@@ -190,10 +190,30 @@
     return t * lax.axis_size("src") + s
 
 
+Z_PLAN = ((3, 1, 1), (3, 1, 1), (3, 1, 1), (3, 1, 1), (2, 2, 1), (2, 2, 1), (0, 0, 0), (0, 0, 0))
+
+
+def column_offset(s):
+    y, z_lo = s % 8, s // 8
+    dz = Z_PLAN[y][z_lo]
+    same_dz = [(yy, zz) for yy in range(8) for zz in range(2) if Z_PLAN[yy][zz] == dz]
+    return dz, same_dz.index((y, z_lo))
+
+
+def holder(s):
+    return s ^ (8 * Z_PLAN[s % 8][2])
+
+
 def source_pair(t, s):
     x_count = lax.axis_size("tgt") // 8
     z_hi, x = t // (2 * x_count), (t // 2) % x_count
-    return ((z_hi + s // 4) % 4) * x_count + (x + s % 4) % x_count
+    if isinstance(s, int):
+        dz, dx = column_offset(s)
+    else:
+        table = [column_offset(v) for v in range(lax.axis_size("src"))]
+        dz = jnp.array([d for d, _ in table])[s]
+        dx = jnp.array([d for _, d in table])[s]
+    return ((z_hi + dz) % 4) * x_count + (x + dx) % x_count
 
 
 def regroup(block_rows):
@@ -205,7 +225,7 @@
             pair = source_pair(t, s)
             for flip in range(2):
                 u = 2 * pair + ((t % 2) ^ flip)
-                perms[flip].append((lin(u, s), lin(t, s)))
+                perms[flip].append((lin(u, holder(s)), lin(t, s)))
     return [lax.ppermute(block_rows, ("tgt", "src"), p) for p in perms]
 
 

time: 158 us -> 158 us (level); the launches traced: 156 us -> 157 us
  local copies, waits for them, and re-layouts: 8.3 us -> 10.8 us
  starting transfers between devices: 73.3 us -> 71.1 us
  Pallas kernels: 15.1 us -> 17.2 us
  waiting for transfers between devices: 50.1 us -> 48.1 us
    ppermute x2, starting transfers between devices: 31.3 us -> 9.51 us  [finish(): packed = merge(keep, lax.ppermute(send, 'src', xor_perm(src_size, bit)))]
    ppermute x4, starting transfers between devices: 6.12 us -> 22.7 us  [regroup(): return [lax.ppermute(block_rows, ('tgt', 'src'), p) for p in perms]]
    ppermute x6, starting transfers between devices: 26.2 us -> 30.6 us  [finish(): packed = merge(packed, lax.ppermute(packed, 'src', xor_perm(src_size, bit)))]
    ppermute x6, waiting for transfers between devices: 36.6 us -> 33.2 us  [finish(): packed = merge(packed, lax.ppermute(packed, 'src', xor_perm(src_size, bit)))]
    ppermute x1, starting transfers between devices: 4.62 us -> 1.92 us  [regroup_offsets(): return lax.ppermute(offsets, ('tgt', 'src'), pairs)]
    ppermute x2, waiting for transfers between devices: 6.3 us -> 8.98 us  [finish(): packed = merge(keep, lax.ppermute(send, 'src', xor_perm(src_size, bit)))]
    dynamic_slice x0 -> x2, local copies, waits for them, and re-layouts: none -> 2.49 us  [the longest x1 1.24 us: source_pair(): dz = jnp.array([d for d, _ in table])[s]]
  transfers between devices with their start and end apart: 15 -> 15, of which waited for: 10 -> 10; matrix products, arithmetic and copies ran while one was open for 6% -> 7% of each run, Pallas kernels for 10% -> 11%
where the time goes in v8:
time: 158 us; the launch traced here: 157 us
  starting transfers between devices  71.1 us (45%)
  waiting for transfers between devices  48.1 us (30%)
  Pallas kernels  17.2 us (11%)
  local copies, waits for them, and re-layouts  10.8 us (7%)
  other arithmetic  4.59 us (3%)
  matrix products  3.06 us (2%)
  between operations  2.48 us (2%)
    ppermute x6, waiting for transfers between devices, finish(): packed = merge(packed, lax.ppermute(packed, 'src', xor_perm(src_size, bit)))  33.2 us
    ppermute x6, starting transfers between devices, finish(): packed = merge(packed, lax.ppermute(packed, 'src', xor_perm(src_size, bit)))  30.6 us
    ppermute x4, starting transfers between devices, regroup(): return [lax.ppermute(block_rows, ('tgt', 'src'), p) for p in perms]  22.7 us
    ppermute x2, starting transfers between devices, finish(): packed = merge(keep, lax.ppermute(send, 'src', xor_perm(src_size, bit)))  9.51 us
    ppermute x2, waiting for transfers between devices, finish(): packed = merge(keep, lax.ppermute(send, 'src', xor_perm(src_size, bit)))  8.98 us
    pallas_call x1, Pallas kernels, date_weights_kernel(): pl.pallas_call(kernel, out_shape=(jax.ShapeDtypeStruct((cols, rows), jnp....  8.76 us
    pallas_call x1, Pallas kernels, date_partials_kernel(): pl.pallas_call(kernel, out_shape=jax.ShapeDtypeStruct((width + 2, rows),...  8.48 us
    ppermute x2, starting transfers between devices, finish(): got = lax.ppermute(value, 'src', xor_perm(src_size, bit))  6.38 us
  transfers between devices with their start and end apart: 15, of which 10 were waited for; matrix products, arithmetic and copies ran while one was open for 7% of the time, Pallas kernels for 11%

profile of v8, /device:TPU:6, one launch (start us, length us, event | category | flops | bytes accessed | tf_op | source)
XLA Modules:
  0.0 157.3 jit_solution(62843808924256120)
XLA Ops:
  0.6 10.4 %collective-permute-start = (bf16[1024,128]{1,0:T(8,128)(2,1)}, bf16[1024,128]{1,0:T(8,128)(2,1)S(1)}, u32[]{:S(2)}, u32[]{:S(2)}) collective-permute-start(bf16[1024,128]{1,0:T(8,128)(2,1)} %refs_1_.2), channel_id=1, source_target_pairs={{408,0},{441,1},{474,2},{507,3},{284,4},{349,5},{22,6},{87,7},{144... | collective-permute-start | bytes 786440 | tf_op jit(solution)/shard_map/ppermute | solution.py:229
  11.0 2.5 %collective-permute-start.1 = (bf16[1024,128]{1,0:T(8,128)(2,1)}, bf16[1024,128]{1,0:T(8,128)(2,1)S(1)}, u32[]{:S(2)}, u32[]{:S(2)}) collective-permute-start(bf16[1024,128]{1,0:T(8,128)(2,1)} %refs_1_.2), channel_id=1, source_target_pairs={{392,0},{425,1},{458,2},{491,3},{268,4},{333,5},{6,6},{71,7},{128,... | collective-permute-start | bytes 786440 | tf_op jit(solution)/shard_map/ppermute | solution.py:229
  23.3 8.5 %shard_map.131 = f32[66,1024]{1,0:T(8,128)} custom-call(s32[8]{0:T(128)} %reshape.68.refs_0_, bf16[1024,128]{1,0:T(8,128)(2,1)} %refs_1_.2, bf16[2048,128]{1,0:T(8,128)(2,1)} %refs_2_.1, f32[2048,1]{1,0:T(8,128)} %copy.20.refs_3_, bf16[64,2048]{1,0:T(8,128)(2,1)} %bitcast.39), custom_call_target="tpu_custom_call" | custom-call | tf_op jit(solution)/shard_map/pallas_call | solution.py:50
  33.7 7.6 %collective-permute-start.3 = (f32[66,512]{1,0:T(8,128)S(1)}, f32[66,512]{1,0:T(8,128)S(1)}, u32[]{:S(2)}, u32[]{:S(2)}) collective-permute-start(f32[66,512]{1,0:T(8,128)S(1)} %constant_dynamic-slice_fusion), channel_id=1, source_target_pairs={{0,8},{1,9},{2,10},{3,11},{4,12},{5,13},{6,14},{7,15},{8,0},{9,1},... | collective-permute-start | bytes 405512 | tf_op jit(solution)/shard_map/ppermute | solution.py:171
  41.3 3.1 %collective-permute-done.3 = f32[66,512]{1,0:T(8,128)S(1)} collective-permute-done((f32[66,512]{1,0:T(8,128)S(1)}, f32[66,512]{1,0:T(8,128)S(1)}, u32[]{:S(2)}, u32[]{:S(2)}) %collective-permute-start.3) | collective-permute-done | bytes 135200 | tf_op jit(solution)/shard_map/ppermute | solution.py:171
  46.2 3.9 %collective-permute-start.4 = (f32[66,512]{1,0:T(8,128)S(1)}, f32[66,512]{1,0:T(8,128)S(1)}, u32[]{:S(2)}, u32[]{:S(2)}) collective-permute-start(f32[66,512]{1,0:T(8,128)S(1)} %pad_maximum_fusion.1), channel_id=1, source_target_pairs={{0,1},{1,0},{2,3},{3,2},{4,5},{5,4},{6,7},{7,6},{8,9},{9,8},{10,11... | collective-permute-start | bytes 405512 | tf_op jit(solution)/shard_map/ppermute | solution.py:174
  50.1 3.1 %collective-permute-done.4 = f32[66,512]{1,0:T(8,128)S(1)} collective-permute-done((f32[66,512]{1,0:T(8,128)S(1)}, f32[66,512]{1,0:T(8,128)S(1)}, u32[]{:S(2)}, u32[]{:S(2)}) %collective-permute-start.4) | collective-permute-done | bytes 135200 | tf_op jit(solution)/shard_map/ppermute | solution.py:174
  53.3 3.5 %collective-permute-start.5 = (f32[66,512]{1,0:T(8,128)S(1)}, f32[66,512]{1,0:T(8,128)S(1)}, u32[]{:S(2)}, u32[]{:S(2)}) collective-permute-start(f32[66,512]{1,0:T(8,128)S(1)} %pad_maximum_fusion.2), channel_id=1, source_target_pairs={{0,2},{1,3},{2,0},{3,1},{4,6},{5,7},{6,4},{7,5},{8,10},{9,11},{10,... | collective-permute-start | bytes 405512 | tf_op jit(solution)/shard_map/ppermute | solution.py:174
  56.8 6.0 %collective-permute-done.5 = f32[66,512]{1,0:T(8,128)S(1)} collective-permute-done((f32[66,512]{1,0:T(8,128)S(1)}, f32[66,512]{1,0:T(8,128)S(1)}, u32[]{:S(2)}, u32[]{:S(2)}) %collective-permute-start.5) | collective-permute-done | bytes 135200 | tf_op jit(solution)/shard_map/ppermute | solution.py:174
  62.9 7.5 %collective-permute-start.6 = (f32[66,512]{1,0:T(8,128)S(1)}, f32[66,512]{1,0:T(8,128)S(1)}, u32[]{:S(2)}, u32[]{:S(2)}) collective-permute-start(f32[66,512]{1,0:T(8,128)S(1)} %pad_maximum_fusion.3), channel_id=1, source_target_pairs={{0,4},{1,5},{2,6},{3,7},{4,0},{5,1},{6,2},{7,3},{8,12},{9,13},{10,... | collective-permute-start | bytes 405512 | tf_op jit(solution)/shard_map/ppermute | solution.py:174
  70.4 5.0 %collective-permute-done.6 = f32[66,512]{1,0:T(8,128)S(1)} collective-permute-done((f32[66,512]{1,0:T(8,128)S(1)}, f32[66,512]{1,0:T(8,128)S(1)}, u32[]{:S(2)}, u32[]{:S(2)}) %collective-permute-start.6) | collective-permute-done | bytes 135200 | tf_op jit(solution)/shard_map/ppermute | solution.py:174
  75.5 3.9 %collective-permute-start.7 = (bf16[64,512]{1,0:T(8,128)(2,1)S(1)}, bf16[64,512]{1,0:T(8,128)(2,1)S(1)}, u32[]{:S(2)}, u32[]{:S(2)}) collective-permute-start(bf16[64,512]{1,0:T(8,128)(2,1)S(1)} %fusion.17), channel_id=1, source_target_pairs={{0,8},{1,9},{2,10},{3,11},{4,12},{5,13},{6,14},{7,15},{8,0},{9,1},... | collective-permute-start | bytes 196616 | tf_op jit(solution)/shard_map/ppermute | solution.py:180
  81.8 4.9 %collective-permute-start.8 = (bf16[64,1024]{1,0:T(8,128)(2,1)S(1)}, bf16[64,1024]{1,0:T(8,128)(2,1)S(1)}, u32[]{:S(2)}, u32[]{:S(2)}) collective-permute-start(bf16[64,1024]{1,0:T(8,128)(2,1)S(1)} %maximum_select_fusion), channel_id=1, source_target_pairs={{408,0},{441,1},{474,2},{507,3},{284,4},{349,5},{22,6},{87,7},{144... | collective-permute-start | bytes 393224 | tf_op jit(solution)/shard_map/ppermute | solution.py:229
  86.7 4.9 %collective-permute-start.9 = (bf16[64,1024]{1,0:T(8,128)(2,1)S(1)}, bf16[64,1024]{1,0:T(8,128)(2,1)S(1)}, u32[]{:S(2)}, u32[]{:S(2)}) collective-permute-start(bf16[64,1024]{1,0:T(8,128)(2,1)S(1)} %maximum_select_fusion), channel_id=1, source_target_pairs={{392,0},{425,1},{458,2},{491,3},{268,4},{333,5},{6,6},{71,7},{128,... | collective-permute-start | bytes 393224 | tf_op jit(solution)/shard_map/ppermute | solution.py:229
  95.7 8.8 %shard_map.132 = (bf16[2048,1024]{1,0:T(8,128)(2,1)}, f32[2,1024]{1,0:T(2,128)}) custom-call(s32[8]{0:T(128)} %reshape.71.refs_0_, bf16[1024,128]{1,0:T(8,128)(2,1)} %refs_1_.3, bf16[2048,128]{1,0:T(8,128)(2,1)} %pad_maximum_fusion.refs_2_, f32[2048,1]{1,0:T(8,128)} %copy.23.refs_3_), custom_call_target="tpu_custom_call" | custom-call | tf_op jit(solution)/shard_map/pallas_call | solution.py:110
  104.5 3.1 %fusion = f32[64,1024]{1,0:T(8,128)S(1)} fusion(bf16[2048,1024]{1,0:T(8,128)(2,1)} %get-tuple-element.10, bf16[64,1024]{1,0:T(8,128)(2,1)S(1)} %get-tuple-element.29, bf16[64,1024]{1,0:T(8,128)(2,1)S(1)} %get-tuple-element.28), kind=kOutput, calls=%fused_computation.9 | convolution fusion | flops 268959744 | bytes 4718592 | tf_op jit(solution)/shard_map/dot_general | solution.py:275
  109.5 5.8 %collective-permute-done.10 = f32[66,512]{1,0:T(8,128)S(1)} collective-permute-done((f32[66,512]{1,0:T(8,128)S(1)}, f32[66,512]{1,0:T(8,128)S(1)}, u32[]{:S(2)}, u32[]{:S(2)}) %collective-permute-start.10) | collective-permute-done | bytes 135200 | tf_op jit(solution)/shard_map/ppermute | solution.py:171
  117.4 5.1 %collective-permute-done.11 = f32[66,512]{1,0:T(8,128)S(1)} collective-permute-done((f32[66,512]{1,0:T(8,128)S(1)}, f32[66,512]{1,0:T(8,128)S(1)}, u32[]{:S(2)}, u32[]{:S(2)}) %collective-permute-start.11) | collective-permute-done | bytes 135200 | tf_op jit(solution)/shard_map/ppermute | solution.py:174
  122.6 5.1 %collective-permute-start.12 = (f32[66,512]{1,0:T(8,128)S(1)}, f32[66,512]{1,0:T(8,128)S(1)}, u32[]{:S(2)}, u32[]{:S(2)}) collective-permute-start(f32[66,512]{1,0:T(8,128)S(1)} %pad_maximum_fusion.5), channel_id=1, source_target_pairs={{0,2},{1,3},{2,0},{3,1},{4,6},{5,7},{6,4},{7,5},{8,10},{9,11},{10,... | collective-permute-start | bytes 405512 | tf_op jit(solution)/shard_map/ppermute | solution.py:174
  127.6 6.9 %collective-permute-done.12 = f32[66,512]{1,0:T(8,128)S(1)} collective-permute-done((f32[66,512]{1,0:T(8,128)S(1)}, f32[66,512]{1,0:T(8,128)S(1)}, u32[]{:S(2)}, u32[]{:S(2)}) %collective-permute-start.12) | collective-permute-done | bytes 135200 | tf_op jit(solution)/shard_map/ppermute | solution.py:174
  134.6 8.8 %collective-permute-start.13 = (f32[66,512]{1,0:T(8,128)S(1)}, f32[66,512]{1,0:T(8,128)S(1)}, u32[]{:S(2)}, u32[]{:S(2)}) collective-permute-start(f32[66,512]{1,0:T(8,128)S(1)} %pad_maximum_fusion.6), channel_id=1, source_target_pairs={{0,4},{1,5},{2,6},{3,7},{4,0},{5,1},{6,2},{7,3},{8,12},{9,13},{10,... | collective-permute-start | bytes 405512 | tf_op jit(solution)/shard_map/ppermute | solution.py:174
  143.4 7.0 %collective-permute-done.13 = f32[66,512]{1,0:T(8,128)S(1)} collective-permute-done((f32[66,512]{1,0:T(8,128)S(1)}, f32[66,512]{1,0:T(8,128)S(1)}, u32[]{:S(2)}, u32[]{:S(2)}) %collective-permute-start.13) | collective-permute-done | bytes 135200 | tf_op jit(solution)/shard_map/ppermute | solution.py:174
  150.5 2.5 %collective-permute-start.14 = (bf16[64,512]{1,0:T(8,128)(2,1)S(1)}, bf16[64,512]{1,0:T(8,128)(2,1)S(1)}, u32[]{:S(2)}, u32[]{:S(2)}) collective-permute-start(bf16[64,512]{1,0:T(8,128)(2,1)S(1)} %fusion.15), channel_id=1, source_target_pairs={{0,8},{1,9},{2,10},{3,11},{4,12},{5,13},{6,14},{7,15},{8,0},{9,1},... | collective-permute-start | bytes 196616 | tf_op jit(solution)/shard_map/ppermute | solution.py:180
  153.0 3.7 %collective-permute-done.14 = bf16[64,512]{1,0:T(8,128)(2,1)S(1)} collective-permute-done((bf16[64,512]{1,0:T(8,128)(2,1)S(1)}, bf16[64,512]{1,0:T(8,128)(2,1)S(1)}, u32[]{:S(2)}, u32[]{:S(2)}) %collective-permute-start.14) | collective-permute-done | bytes 65568 | tf_op jit(solution)/shard_map/ppermute | solution.py:180
  (79 shorter events, 23.4 us)
Async XLA Ops:
  0.6 18.7 %copy-start = (s32[64,64]{1,0:T(8,128)S(1)}, s32[64,64]{1,0:T(8,128)}, u32[]{:S(2)}) copy-start(s32[64,64]{1,0:T(8,128)} %param.18) | copy-start | bytes 49156
  0.6 31.2 %collective-permute-start = (bf16[1024,128]{1,0:T(8,128)(2,1)}, bf16[1024,128]{1,0:T(8,128)(2,1)S(1)}, u32[]{:S(2)}, u32[]{:S(2)}) collective-permute-start(bf16[1024,128]{1,0:T(8,128)(2,1)} %refs_1_.2), channel_id=1, source_target_pairs={{408,0},{441,1},{474,2},{507,3},{284,4},{349,5},{22,6},{87,7},{144... | collective-permute-start | bytes 786440 | tf_op jit(solution)/shard_map/ppermute | solution.py:229
  11.0 20.8 %collective-permute-start.1 = (bf16[1024,128]{1,0:T(8,128)(2,1)}, bf16[1024,128]{1,0:T(8,128)(2,1)S(1)}, u32[]{:S(2)}, u32[]{:S(2)}) collective-permute-start(bf16[1024,128]{1,0:T(8,128)(2,1)} %refs_1_.2), channel_id=1, source_target_pairs={{392,0},{425,1},{458,2},{491,3},{268,4},{333,5},{6,6},{71,7},{128,... | collective-permute-start | bytes 786440 | tf_op jit(solution)/shard_map/ppermute | solution.py:229
  13.5 19.2 %collective-permute-start.2 = (bf16[2048]{0:T(1024)(128)(2,1)}, bf16[2048]{0:T(1024)(128)(2,1)S(1)}, u32[]{:S(2)}, u32[]{:S(2)}) collective-permute-start(bf16[2048]{0:T(1024)(128)(2,1)} %param.16), channel_id=1, source_target_pairs={{12,0},{13,1},{14,2},{15,3},{8,4},{10,5},{0,6},{2,7},{4,8},{5,9},{... | collective-permute-start | bytes 12296 | tf_op jit(solution)/shard_map/ppermute | solution.py:245
  22.0 53.5 %copy-start.2 = (bf16[1024,64]{0,1:T(8,128)(2,1)S(1)}, bf16[1024,64]{0,1:T(8,128)(2,1)}, u32[]{:S(2)}) copy-start(bf16[1024,64]{0,1:T(8,128)(2,1)} %param.17) | copy-start | bytes 393220
  33.7 10.7 %collective-permute-start.3 = (f32[66,512]{1,0:T(8,128)S(1)}, f32[66,512]{1,0:T(8,128)S(1)}, u32[]{:S(2)}, u32[]{:S(2)}) collective-permute-start(f32[66,512]{1,0:T(8,128)S(1)} %constant_dynamic-slice_fusion), channel_id=1, source_target_pairs={{0,8},{1,9},{2,10},{3,11},{4,12},{5,13},{6,14},{7,15},{8,0},{9,1},... | collective-permute-start | bytes 405512 | tf_op jit(solution)/shard_map/ppermute | solution.py:171
  46.2 7.0 %collective-permute-start.4 = (f32[66,512]{1,0:T(8,128)S(1)}, f32[66,512]{1,0:T(8,128)S(1)}, u32[]{:S(2)}, u32[]{:S(2)}) collective-permute-start(f32[66,512]{1,0:T(8,128)S(1)} %pad_maximum_fusion.1), channel_id=1, source_target_pairs={{0,1},{1,0},{2,3},{3,2},{4,5},{5,4},{6,7},{7,6},{8,9},{9,8},{10,11... | collective-permute-start | bytes 405512 | tf_op jit(solution)/shard_map/ppermute | solution.py:174
  53.3 9.5 %collective-permute-start.5 = (f32[66,512]{1,0:T(8,128)S(1)}, f32[66,512]{1,0:T(8,128)S(1)}, u32[]{:S(2)}, u32[]{:S(2)}) collective-permute-start(f32[66,512]{1,0:T(8,128)S(1)} %pad_maximum_fusion.2), channel_id=1, source_target_pairs={{0,2},{1,3},{2,0},{3,1},{4,6},{5,7},{6,4},{7,5},{8,10},{9,11},{10,... | collective-permute-start | bytes 405512 | tf_op jit(solution)/shard_map/ppermute | solution.py:174
  62.9 12.5 %collective-permute-start.6 = (f32[66,512]{1,0:T(8,128)S(1)}, f32[66,512]{1,0:T(8,128)S(1)}, u32[]{:S(2)}, u32[]{:S(2)}) collective-permute-start(f32[66,512]{1,0:T(8,128)S(1)} %pad_maximum_fusion.3), channel_id=1, source_target_pairs={{0,4},{1,5},{2,6},{3,7},{4,0},{5,1},{6,2},{7,3},{8,12},{9,13},{10,... | collective-permute-start | bytes 405512 | tf_op jit(solution)/shard_map/ppermute | solution.py:174
  75.5 6.2 %collective-permute-start.7 = (bf16[64,512]{1,0:T(8,128)(2,1)S(1)}, bf16[64,512]{1,0:T(8,128)(2,1)S(1)}, u32[]{:S(2)}, u32[]{:S(2)}) collective-permute-start(bf16[64,512]{1,0:T(8,128)(2,1)S(1)} %fusion.17), channel_id=1, source_target_pairs={{0,8},{1,9},{2,10},{3,11},{4,12},{5,13},{6,14},{7,15},{8,0},{9,1},... | collective-permute-start | bytes 196616 | tf_op jit(solution)/shard_map/ppermute | solution.py:180
  81.7 25.8 %copy-start.1 = (bf16[64,1024]{1,0:T(8,128)(2,1)}, bf16[64,1024]{1,0:T(8,128)(2,1)S(1)}, u32[]{:S(2)}) copy-start(bf16[64,1024]{1,0:T(8,128)(2,1)S(1)} %maximum_select_fusion) | copy-start | bytes 393220
  81.8 22.7 %collective-permute-start.8 = (bf16[64,1024]{1,0:T(8,128)(2,1)S(1)}, bf16[64,1024]{1,0:T(8,128)(2,1)S(1)}, u32[]{:S(2)}, u32[]{:S(2)}) collective-permute-start(bf16[64,1024]{1,0:T(8,128)(2,1)S(1)} %maximum_select_fusion), channel_id=1, source_target_pairs={{408,0},{441,1},{474,2},{507,3},{284,4},{349,5},{22,6},{87,7},{144... | collective-permute-start | bytes 393224 | tf_op jit(solution)/shard_map/ppermute | solution.py:229
  86.7 17.7 %collective-permute-start.9 = (bf16[64,1024]{1,0:T(8,128)(2,1)S(1)}, bf16[64,1024]{1,0:T(8,128)(2,1)S(1)}, u32[]{:S(2)}, u32[]{:S(2)}) collective-permute-start(bf16[64,1024]{1,0:T(8,128)(2,1)S(1)} %maximum_select_fusion), channel_id=1, source_target_pairs={{392,0},{425,1},{458,2},{491,3},{268,4},{333,5},{6,6},{71,7},{128,... | collective-permute-start | bytes 393224 | tf_op jit(solution)/shard_map/ppermute | solution.py:229
  104.4 3.1 %copy-start.4 = (f32[2,1024]{1,0:T(2,128)S(1)}, f32[2,1024]{1,0:T(2,128)}, u32[]{:S(2)}) copy-start(f32[2,1024]{1,0:T(2,128)} %get-tuple-element.11) | copy-start | bytes 24580
  104.4 46.0 %copy-start.3 = (bf16[1024,64]{0,1:T(8,128)(2,1)S(1)}, bf16[1024,64]{0,1:T(8,128)(2,1)}, u32[]{:S(2)}) copy-start(bf16[1024,64]{0,1:T(8,128)(2,1)} %param.20) | copy-start | bytes 393220
  107.6 7.8 %collective-permute-start.10 = (f32[66,512]{1,0:T(8,128)S(1)}, f32[66,512]{1,0:T(8,128)S(1)}, u32[]{:S(2)}, u32[]{:S(2)}) collective-permute-start(f32[66,512]{1,0:T(8,128)S(1)} %get-tuple-element.26), channel_id=1, source_target_pairs={{0,8},{1,9},{2,10},{3,11},{4,12},{5,13},{6,14},{7,15},{8,0},{9,1},... | collective-permute-start | bytes 405512 | tf_op jit(solution)/shard_map/ppermute | solution.py:171
  115.4 7.0 %collective-permute-start.11 = (f32[66,512]{1,0:T(8,128)S(1)}, f32[66,512]{1,0:T(8,128)S(1)}, u32[]{:S(2)}, u32[]{:S(2)}) collective-permute-start(f32[66,512]{1,0:T(8,128)S(1)} %pad_maximum_fusion.4), channel_id=1, source_target_pairs={{0,1},{1,0},{2,3},{3,2},{4,5},{5,4},{6,7},{7,6},{8,9},{9,8},{10,11... | collective-permute-start | bytes 405512 | tf_op jit(solution)/shard_map/ppermute | solution.py:174
  122.6 12.0 %collective-permute-start.12 = (f32[66,512]{1,0:T(8,128)S(1)}, f32[66,512]{1,0:T(8,128)S(1)}, u32[]{:S(2)}, u32[]{:S(2)}) collective-permute-start(f32[66,512]{1,0:T(8,128)S(1)} %pad_maximum_fusion.5), channel_id=1, source_target_pairs={{0,2},{1,3},{2,0},{3,1},{4,6},{5,7},{6,4},{7,5},{8,10},{9,11},{10,... | collective-permute-start | bytes 405512 | tf_op jit(solution)/shard_map/ppermute | solution.py:174
  134.6 15.8 %collective-permute-start.13 = (f32[66,512]{1,0:T(8,128)S(1)}, f32[66,512]{1,0:T(8,128)S(1)}, u32[]{:S(2)}, u32[]{:S(2)}) collective-permute-start(f32[66,512]{1,0:T(8,128)S(1)} %pad_maximum_fusion.6), channel_id=1, source_target_pairs={{0,4},{1,5},{2,6},{3,7},{4,0},{5,1},{6,2},{7,3},{8,12},{9,13},{10,... | collective-permute-start | bytes 405512 | tf_op jit(solution)/shard_map/ppermute | solution.py:174
  150.5 6.2 %collective-permute-start.14 = (bf16[64,512]{1,0:T(8,128)(2,1)S(1)}, bf16[64,512]{1,0:T(8,128)(2,1)S(1)}, u32[]{:S(2)}, u32[]{:S(2)}) collective-permute-start(bf16[64,512]{1,0:T(8,128)(2,1)S(1)} %fusion.15), channel_id=1, source_target_pairs={{0,8},{1,9},{2,10},{3,11},{4,12},{5,13},{6,14},{7,15},{8,0},{9,1},... | collective-permute-start | bytes 196616 | tf_op jit(solution)/shard_map/ppermute | solution.py:180

commit v9 on v8

--- a/solution.py
+++ b/solution.py
@@ -5,11 +5,13 @@
 from jax.experimental.pallas import tpu as pltpu
 from jax.sharding import PartitionSpec as P
 
+
 BLOCK = 512
 
 
 sharpness = 3.5
 very_low = -1e30
+
 
 def partials_kernel(mask_ref, x_ref, y_ref, off_ref, v_ref, out_ref, m_ref, l_ref, acc_ref, *, scale, col_tiles):
     i = pl.program_id(0)
@@ -168,10 +170,12 @@
         mine_hi = (me >> bit) & 1
         keep = lax.dynamic_slice_in_dim(packed, mine_hi * half, half, 1)
         send = lax.dynamic_slice_in_dim(packed, (1 - mine_hi) * half, half, 1)
-        packed = merge(keep, lax.ppermute(send, "src", xor_perm(src_size, bit)))
+        got = lax.ppermute(send, "src", xor_perm(src_size, bit))
+        packed = merge(keep, got)
         exercise = lax.dynamic_slice_in_dim(exercise, mine_hi * half, half, 0)
     for bit in EXCHANGE_BITS:
-        packed = merge(packed, lax.ppermute(packed, "src", xor_perm(src_size, bit)))
+        got = lax.ppermute(packed, "src", xor_perm(src_size, bit))
+        packed = merge(packed, got)
     width = packed.shape[0] - 2
     continuation = packed[:width] / packed[width : width + 1]
     value = jnp.maximum(continuation, exercise.T).astype(jnp.bfloat16)
@@ -210,9 +214,9 @@
     if isinstance(s, int):
         dz, dx = column_offset(s)
     else:
-        table = [column_offset(v) for v in range(lax.axis_size("src"))]
-        dz = jnp.array([d for d, _ in table])[s]
-        dx = jnp.array([d for _, d in table])[s]
+        y, z_lo = s % 8, s // 8
+        dz = jnp.where(y < 4, 3 - 2 * z_lo, jnp.where(y < 6, 2, 0))
+        dx = jnp.where(y < 4, y, (y % 2) * 2 + z_lo)
     return ((z_hi + dz) % 4) * x_count + (x + dx) % x_count
 
 
@@ -267,12 +271,19 @@
     partials, mid_sources, mid_offsets = lax.optimization_barrier(
         (partials, mid_sources, mid_offsets)
     )
-    early_weights, early_stats = date_weights_kernel(
-        states_early, mid_sources, mid_offsets, local_live(states_early, mask_early, early_col_ids)
-    )
+    early_live = local_live(states_early, mask_early, early_col_ids)
+    early_parts = []
+    for row_tile in range(early_live.shape[0]):
+        rows = states_early[row_tile * BLOCK : (row_tile + 1) * BLOCK]
+        early_parts.append(
+            date_weights_kernel(rows, mid_sources, mid_offsets, early_live[row_tile : row_tile + 1])
+        )
     value_mid_t = finish(partials, exercise_mid)
     mid_values_t = regroup_order(regroup(value_mid_t), axis=1)
-    early_weighted = jnp.dot(mid_values_t, early_weights, preferred_element_type=jnp.float32)
+    early_weighted = jnp.concatenate(
+        [jnp.dot(mid_values_t, w, preferred_element_type=jnp.float32) for w, _ in early_parts], 1
+    )
+    early_stats = jnp.concatenate([s for _, s in early_parts], 1)
     value_early_t = finish(jnp.concatenate([early_weighted, early_stats], 0), exercise_early)
     value_mid, value_early = value_mid_t.T, value_early_t.T
     return (value_mid, value_early)
@@ -292,6 +303,4 @@
         P(),
     )
     out_specs = (P("tgt", None), P("tgt", None))
-    return jax.shard_map(
-        per_device, mesh=mesh, in_specs=in_specs, out_specs=out_specs, check_vma=False
-    )
+    return jax.shard_map(per_device, mesh=mesh, in_specs=in_specs, out_specs=out_specs, check_vma=False)

time: 158 us -> 160 us (1.013)
  the two profiles are of different devices: /device:TPU:6 before, /device:TPU:1 now
where the time goes in v9:
time: 160 us; the launch traced here: 159 us
  starting transfers between devices  74.5 us (47%)
  waiting for transfers between devices  51 us (32%)
  Pallas kernels  19.2 us (12%)
  local copies, waits for them, and re-layouts  9.25 us (6%)
  other arithmetic  3.04 us (2%)
    ppermute x6, waiting for transfers between devices, finish(): got = lax.ppermute(packed, 'src', xor_perm(src_size, bit))  38.8 us
    ppermute x6, starting transfers between devices, finish(): got = lax.ppermute(packed, 'src', xor_perm(src_size, bit))  29.8 us
    ppermute x4, starting transfers between devices, regroup(): return [lax.ppermute(block_rows, ('tgt', 'src'), p) for p in perms]  23.1 us
    ppermute x2, starting transfers between devices, finish(): got = lax.ppermute(send, 'src', xor_perm(src_size, bit))  13.1 us
    pallas_call x2, Pallas kernels, date_weights_kernel(): pl.pallas_call(kernel, out_shape=(jax.ShapeDtypeStruct((cols, rows), jnp....  10.8 us
    pallas_call x1, Pallas kernels, date_partials_kernel(): pl.pallas_call(kernel, out_shape=jax.ShapeDtypeStruct((width + 2, rows),...  8.37 us
    ppermute x2, waiting for transfers between devices, finish(): got = lax.ppermute(send, 'src', xor_perm(src_size, bit))  8.3 us
    ppermute x2, starting transfers between devices, finish(): got = lax.ppermute(value, 'src', xor_perm(src_size, bit))  6.6 us
  transfers between devices with their start and end apart: 15, of which 10 were waited for; matrix products, arithmetic and copies ran while one was open for 6% of the time, Pallas kernels for 12%

profile of v9, /device:TPU:1, one launch (start us, length us, event | category | flops | bytes accessed | tf_op | source)
XLA Modules:
  0.0 159.2 jit_solution(5647446377425600576)
XLA Ops:
  0.6 11.5 %collective-permute-start.1 = (bf16[1024,128]{1,0:T(8,128)(2,1)}, bf16[1024,128]{1,0:T(8,128)(2,1)S(1)}, u32[]{:S(2)}, u32[]{:S(2)}) collective-permute-start(bf16[1024,128]{1,0:T(8,128)(2,1)} %refs_1_.1), channel_id=1, source_target_pairs={{392,0},{425,1},{458,2},{491,3},{268,4},{333,5},{6,6},{71,7},{128,... | collective-permute-start | bytes 786440 | tf_op jit(solution)/shard_map/ppermute | solution.py:233
  12.1 2.5 %collective-permute-start = (bf16[1024,128]{1,0:T(8,128)(2,1)}, bf16[1024,128]{1,0:T(8,128)(2,1)S(1)}, u32[]{:S(2)}, u32[]{:S(2)}) collective-permute-start(bf16[1024,128]{1,0:T(8,128)(2,1)} %refs_1_.1), channel_id=1, source_target_pairs={{408,0},{441,1},{474,2},{507,3},{284,4},{349,5},{22,6},{87,7},{144... | collective-permute-start | bytes 786440 | tf_op jit(solution)/shard_map/ppermute | solution.py:233
  20.7 8.4 %shard_map.113 = f32[66,1024]{1,0:T(8,128)} custom-call(s32[8]{0:T(128)} %reshape.72.refs_0_, bf16[1024,128]{1,0:T(8,128)(2,1)} %refs_1_.1, bf16[2048,128]{1,0:T(8,128)(2,1)} %refs_2_.1, f32[2048,1]{1,0:T(8,128)} %copy.17.refs_3_, bf16[64,2048]{1,0:T(8,128)(2,1)} %bitcast.38), custom_call_target="tpu_custom_call" | custom-call | tf_op jit(solution)/shard_map/pallas_call | solution.py:52
  30.1 10.2 %collective-permute-start.3 = (f32[66,512]{1,0:T(8,128)S(1)}, f32[66,512]{1,0:T(8,128)S(1)}, u32[]{:S(2)}, u32[]{:S(2)}) collective-permute-start(f32[66,512]{1,0:T(8,128)S(1)} %constant_dynamic-slice_fusion.1), channel_id=1, source_target_pairs={{0,8},{1,9},{2,10},{3,11},{4,12},{5,13},{6,14},{7,15},{8,0},{9,1},... | collective-permute-start | bytes 405512 | tf_op jit(solution)/shard_map/ppermute | solution.py:173
  40.2 3.6 %collective-permute-done.3 = f32[66,512]{1,0:T(8,128)S(1)} collective-permute-done((f32[66,512]{1,0:T(8,128)S(1)}, f32[66,512]{1,0:T(8,128)S(1)}, u32[]{:S(2)}, u32[]{:S(2)}) %collective-permute-start.3) | collective-permute-done | bytes 135200 | tf_op jit(solution)/shard_map/ppermute | solution.py:173
  46.0 5.1 %collective-permute-done.4 = f32[66,512]{1,0:T(8,128)S(1)} collective-permute-done((f32[66,512]{1,0:T(8,128)S(1)}, f32[66,512]{1,0:T(8,128)S(1)}, u32[]{:S(2)}, u32[]{:S(2)}) %collective-permute-start.4) | collective-permute-done | bytes 135200 | tf_op jit(solution)/shard_map/ppermute | solution.py:177
  53.1 9.8 %collective-permute-done.5 = f32[66,512]{1,0:T(8,128)S(1)} collective-permute-done((f32[66,512]{1,0:T(8,128)S(1)}, f32[66,512]{1,0:T(8,128)S(1)}, u32[]{:S(2)}, u32[]{:S(2)}) %collective-permute-start.5) | collective-permute-done | bytes 135200 | tf_op jit(solution)/shard_map/ppermute | solution.py:177
  63.0 7.1 %collective-permute-start.6 = (f32[66,512]{1,0:T(8,128)S(1)}, f32[66,512]{1,0:T(8,128)S(1)}, u32[]{:S(2)}, u32[]{:S(2)}) collective-permute-start(f32[66,512]{1,0:T(8,128)S(1)} %pad_maximum_fusion.6), channel_id=1, source_target_pairs={{0,4},{1,5},{2,6},{3,7},{4,0},{5,1},{6,2},{7,3},{8,12},{9,13},{10,... | collective-permute-start | bytes 405512 | tf_op jit(solution)/shard_map/ppermute | solution.py:177
  70.1 5.7 %collective-permute-done.6 = f32[66,512]{1,0:T(8,128)S(1)} collective-permute-done((f32[66,512]{1,0:T(8,128)S(1)}, f32[66,512]{1,0:T(8,128)S(1)}, u32[]{:S(2)}, u32[]{:S(2)}) %collective-permute-start.6) | collective-permute-done | bytes 135200 | tf_op jit(solution)/shard_map/ppermute | solution.py:177
  75.9 4.7 %collective-permute-start.7 = (bf16[64,512]{1,0:T(8,128)(2,1)S(1)}, bf16[64,512]{1,0:T(8,128)(2,1)S(1)}, u32[]{:S(2)}, u32[]{:S(2)}) collective-permute-start(bf16[64,512]{1,0:T(8,128)(2,1)S(1)} %fusion.13), channel_id=1, source_target_pairs={{0,8},{1,9},{2,10},{3,11},{4,12},{5,13},{6,14},{7,15},{8,0},{9,1},... | collective-permute-start | bytes 196616 | tf_op jit(solution)/shard_map/ppermute | solution.py:184
  82.3 4.9 %collective-permute-start.9 = (bf16[64,1024]{1,0:T(8,128)(2,1)S(1)}, bf16[64,1024]{1,0:T(8,128)(2,1)S(1)}, u32[]{:S(2)}, u32[]{:S(2)}) collective-permute-start(bf16[64,1024]{1,0:T(8,128)(2,1)S(1)} %maximum_select_fusion), channel_id=1, source_target_pairs={{392,0},{425,1},{458,2},{491,3},{268,4},{333,5},{6,6},{71,7},{128,... | collective-permute-start | bytes 393224 | tf_op jit(solution)/shard_map/ppermute | solution.py:233
  87.1 4.3 %collective-permute-start.8 = (bf16[64,1024]{1,0:T(8,128)(2,1)S(1)}, bf16[64,1024]{1,0:T(8,128)(2,1)S(1)}, u32[]{:S(2)}, u32[]{:S(2)}) collective-permute-start(bf16[64,1024]{1,0:T(8,128)(2,1)S(1)} %maximum_select_fusion), channel_id=1, source_target_pairs={{408,0},{441,1},{474,2},{507,3},{284,4},{349,5},{22,6},{87,7},{144... | collective-permute-start | bytes 393224 | tf_op jit(solution)/shard_map/ppermute | solution.py:233
  95.6 4.3 %shard_map.115 = (bf16[2048,512]{1,0:T(8,128)(2,1)}, f32[2,512]{1,0:T(2,128)}) custom-call(s32[4]{0:T(128)} %get-tuple-element.17.refs_0_, bf16[512,128]{1,0:T(8,128)(2,1)} %get-tuple-element.35.refs_1_, bf16[2048,128]{1,0:T(8,128)(2,1)} %pad_maximum_fusion.refs_2_, f32[2048,1]{1,0:T(8,128)} %copy.19.refs_3_), custom_call_target="tpu_custom_call" | custom-call | tf_op jit(solution)/shard_map/pallas_call | solution.py:112
  99.9 6.5 %shard_map.114 = (bf16[2048,512]{1,0:T(8,128)(2,1)}, f32[2,512]{1,0:T(2,128)}) custom-call(s32[4]{0:T(128)} %get-tuple-element.16.refs_0_, bf16[512,128]{1,0:T(8,128)(2,1)} %get-tuple-element.34.refs_1_, bf16[2048,128]{1,0:T(8,128)(2,1)} %pad_maximum_fusion.refs_2_, f32[2048,1]{1,0:T(8,128)} %copy.19.refs_3_), custom_call_target="tpu_custom_call" | custom-call | tf_op jit(solution)/shard_map/pallas_call | solution.py:112
  108.5 2.9 %collective-permute-start.10 = (f32[66,512]{1,0:T(8,128)S(1)}, f32[66,512]{1,0:T(8,128)S(1)}, u32[]{:S(2)}, u32[]{:S(2)}) collective-permute-start(f32[66,512]{1,0:T(8,128)S(1)} %constant_dynamic-slice_fusion), channel_id=1, source_target_pairs={{0,8},{1,9},{2,10},{3,11},{4,12},{5,13},{6,14},{7,15},{8,0},{9,1},... | collective-permute-start | bytes 405512 | tf_op jit(solution)/shard_map/ppermute | solution.py:173
  111.4 4.7 %collective-permute-done.10 = f32[66,512]{1,0:T(8,128)S(1)} collective-permute-done((f32[66,512]{1,0:T(8,128)S(1)}, f32[66,512]{1,0:T(8,128)S(1)}, u32[]{:S(2)}, u32[]{:S(2)}) %collective-permute-start.10) | collective-permute-done | bytes 135200 | tf_op jit(solution)/shard_map/ppermute | solution.py:173
  116.3 2.9 %collective-permute-start.11 = (f32[66,512]{1,0:T(8,128)S(1)}, f32[66,512]{1,0:T(8,128)S(1)}, u32[]{:S(2)}, u32[]{:S(2)}) collective-permute-start(f32[66,512]{1,0:T(8,128)S(1)} %pad_maximum_fusion.7), channel_id=1, source_target_pairs={{0,1},{1,0},{2,3},{3,2},{4,5},{5,4},{6,7},{7,6},{8,9},{9,8},{10,11... | collective-permute-start | bytes 405512 | tf_op jit(solution)/shard_map/ppermute | solution.py:177
  119.2 3.8 %collective-permute-done.11 = f32[66,512]{1,0:T(8,128)S(1)} collective-permute-done((f32[66,512]{1,0:T(8,128)S(1)}, f32[66,512]{1,0:T(8,128)S(1)}, u32[]{:S(2)}, u32[]{:S(2)}) %collective-permute-start.11) | collective-permute-done | bytes 135200 | tf_op jit(solution)/shard_map/ppermute | solution.py:177
  123.1 3.3 %collective-permute-start.12 = (f32[66,512]{1,0:T(8,128)S(1)}, f32[66,512]{1,0:T(8,128)S(1)}, u32[]{:S(2)}, u32[]{:S(2)}) collective-permute-start(f32[66,512]{1,0:T(8,128)S(1)} %pad_maximum_fusion.8), channel_id=1, source_target_pairs={{0,2},{1,3},{2,0},{3,1},{4,6},{5,7},{6,4},{7,5},{8,10},{9,11},{10,... | collective-permute-start | bytes 405512 | tf_op jit(solution)/shard_map/ppermute | solution.py:177
  126.3 7.8 %collective-permute-done.12 = f32[66,512]{1,0:T(8,128)S(1)} collective-permute-done((f32[66,512]{1,0:T(8,128)S(1)}, f32[66,512]{1,0:T(8,128)S(1)}, u32[]{:S(2)}, u32[]{:S(2)}) %collective-permute-start.12) | collective-permute-done | bytes 135200 | tf_op jit(solution)/shard_map/ppermute | solution.py:177
  134.2 12.7 %collective-permute-start.13 = (f32[66,512]{1,0:T(8,128)S(1)}, f32[66,512]{1,0:T(8,128)S(1)}, u32[]{:S(2)}, u32[]{:S(2)}) collective-permute-start(f32[66,512]{1,0:T(8,128)S(1)} %pad_maximum_fusion.9), channel_id=1, source_target_pairs={{0,4},{1,5},{2,6},{3,7},{4,0},{5,1},{6,2},{7,3},{8,12},{9,13},{10,... | collective-permute-start | bytes 405512 | tf_op jit(solution)/shard_map/ppermute | solution.py:177
  146.9 6.6 %collective-permute-done.13 = f32[66,512]{1,0:T(8,128)S(1)} collective-permute-done((f32[66,512]{1,0:T(8,128)S(1)}, f32[66,512]{1,0:T(8,128)S(1)}, u32[]{:S(2)}, u32[]{:S(2)}) %collective-permute-start.13) | collective-permute-done | bytes 135200 | tf_op jit(solution)/shard_map/ppermute | solution.py:177
  153.5 1.9 %collective-permute-start.14 = (bf16[64,512]{1,0:T(8,128)(2,1)S(1)}, bf16[64,512]{1,0:T(8,128)(2,1)S(1)}, u32[]{:S(2)}, u32[]{:S(2)}) collective-permute-start(bf16[64,512]{1,0:T(8,128)(2,1)S(1)} %fusion.11), channel_id=1, source_target_pairs={{0,8},{1,9},{2,10},{3,11},{4,12},{5,13},{6,14},{7,15},{8,0},{9,1},... | collective-permute-start | bytes 196616 | tf_op jit(solution)/shard_map/ppermute | solution.py:184
  155.5 3.1 %collective-permute-done.14 = bf16[64,512]{1,0:T(8,128)(2,1)S(1)} collective-permute-done((bf16[64,512]{1,0:T(8,128)(2,1)S(1)}, bf16[64,512]{1,0:T(8,128)(2,1)S(1)}, u32[]{:S(2)}, u32[]{:S(2)}) %collective-permute-start.14) | collective-permute-done | bytes 65568 | tf_op jit(solution)/shard_map/ppermute | solution.py:184
  (90 shorter events, 19.9 us)
Async XLA Ops:
  0.6 16.8 %copy-start = (s32[64,64]{1,0:T(8,128)S(1)}, s32[64,64]{1,0:T(8,128)}, u32[]{:S(2)}) copy-start(s32[64,64]{1,0:T(8,128)} %param.16) | copy-start | bytes 49156
  0.6 28.4 %collective-permute-start.1 = (bf16[1024,128]{1,0:T(8,128)(2,1)}, bf16[1024,128]{1,0:T(8,128)(2,1)S(1)}, u32[]{:S(2)}, u32[]{:S(2)}) collective-permute-start(bf16[1024,128]{1,0:T(8,128)(2,1)} %refs_1_.1), channel_id=1, source_target_pairs={{392,0},{425,1},{458,2},{491,3},{268,4},{333,5},{6,6},{71,7},{128,... | collective-permute-start | bytes 786440 | tf_op jit(solution)/shard_map/ppermute | solution.py:233
  12.1 16.9 %collective-permute-start = (bf16[1024,128]{1,0:T(8,128)(2,1)}, bf16[1024,128]{1,0:T(8,128)(2,1)S(1)}, u32[]{:S(2)}, u32[]{:S(2)}) collective-permute-start(bf16[1024,128]{1,0:T(8,128)(2,1)} %refs_1_.1), channel_id=1, source_target_pairs={{408,0},{441,1},{474,2},{507,3},{284,4},{349,5},{22,6},{87,7},{144... | collective-permute-start | bytes 786440 | tf_op jit(solution)/shard_map/ppermute | solution.py:233
  14.6 15.4 %collective-permute-start.2 = (bf16[2048]{0:T(1024)(128)(2,1)}, bf16[2048]{0:T(1024)(128)(2,1)S(1)}, u32[]{:S(2)}, u32[]{:S(2)}) collective-permute-start(bf16[2048]{0:T(1024)(128)(2,1)} %param.14), channel_id=1, source_target_pairs={{12,0},{13,1},{14,2},{15,3},{8,4},{10,5},{0,6},{2,7},{4,8},{5,9},{... | collective-permute-start | bytes 12296 | tf_op jit(solution)/shard_map/ppermute | solution.py:249
  29.1 46.7 %copy-start.6 = (bf16[1024,64]{0,1:T(8,128)(2,1)S(1)}, bf16[1024,64]{0,1:T(8,128)(2,1)}, u32[]{:S(2)}) copy-start(bf16[1024,64]{0,1:T(8,128)(2,1)} %param.15) | copy-start | bytes 393220
  29.2 51.4 %copy-start.4 = (bf16[1024,128]{1,0:T(8,128)(2,1)S(1)}, bf16[1024,128]{1,0:T(8,128)(2,1)}, u32[]{:S(2)}) copy-start(bf16[1024,128]{1,0:T(8,128)(2,1)} %param.17) | copy-start | bytes 786436
  30.1 13.8 %collective-permute-start.3 = (f32[66,512]{1,0:T(8,128)S(1)}, f32[66,512]{1,0:T(8,128)S(1)}, u32[]{:S(2)}, u32[]{:S(2)}) collective-permute-start(f32[66,512]{1,0:T(8,128)S(1)} %constant_dynamic-slice_fusion.1), channel_id=1, source_target_pairs={{0,8},{1,9},{2,10},{3,11},{4,12},{5,13},{6,14},{7,15},{8,0},{9,1},... | collective-permute-start | bytes 405512 | tf_op jit(solution)/shard_map/ppermute | solution.py:173
  44.0 7.1 %collective-permute-start.4 = (f32[66,512]{1,0:T(8,128)S(1)}, f32[66,512]{1,0:T(8,128)S(1)}, u32[]{:S(2)}, u32[]{:S(2)}) collective-permute-start(f32[66,512]{1,0:T(8,128)S(1)} %pad_maximum_fusion.4), channel_id=1, source_target_pairs={{0,1},{1,0},{2,3},{3,2},{4,5},{5,4},{6,7},{7,6},{8,9},{9,8},{10,11... | collective-permute-start | bytes 405512 | tf_op jit(solution)/shard_map/ppermute | solution.py:177
  51.2 11.7 %collective-permute-start.5 = (f32[66,512]{1,0:T(8,128)S(1)}, f32[66,512]{1,0:T(8,128)S(1)}, u32[]{:S(2)}, u32[]{:S(2)}) collective-permute-start(f32[66,512]{1,0:T(8,128)S(1)} %pad_maximum_fusion.5), channel_id=1, source_target_pairs={{0,2},{1,3},{2,0},{3,1},{4,6},{5,7},{6,4},{7,5},{8,10},{9,11},{10,... | collective-permute-start | bytes 405512 | tf_op jit(solution)/shard_map/ppermute | solution.py:177
  63.0 12.8 %collective-permute-start.6 = (f32[66,512]{1,0:T(8,128)S(1)}, f32[66,512]{1,0:T(8,128)S(1)}, u32[]{:S(2)}, u32[]{:S(2)}) collective-permute-start(f32[66,512]{1,0:T(8,128)S(1)} %pad_maximum_fusion.6), channel_id=1, source_target_pairs={{0,4},{1,5},{2,6},{3,7},{4,0},{5,1},{6,2},{7,3},{8,12},{9,13},{10,... | collective-permute-start | bytes 405512 | tf_op jit(solution)/shard_map/ppermute | solution.py:177
  75.9 6.3 %collective-permute-start.7 = (bf16[64,512]{1,0:T(8,128)(2,1)S(1)}, bf16[64,512]{1,0:T(8,128)(2,1)S(1)}, u32[]{:S(2)}, u32[]{:S(2)}) collective-permute-start(bf16[64,512]{1,0:T(8,128)(2,1)S(1)} %fusion.13), channel_id=1, source_target_pairs={{0,8},{1,9},{2,10},{3,11},{4,12},{5,13},{6,14},{7,15},{8,0},{9,1},... | collective-permute-start | bytes 196616 | tf_op jit(solution)/shard_map/ppermute | solution.py:184
  82.3 24.1 %copy-start.5 = (bf16[64,1024]{1,0:T(8,128)(2,1)}, bf16[64,1024]{1,0:T(8,128)(2,1)S(1)}, u32[]{:S(2)}) copy-start(bf16[64,1024]{1,0:T(8,128)(2,1)S(1)} %maximum_select_fusion) | copy-start | bytes 393220
  82.3 24.1 %collective-permute-start.9 = (bf16[64,1024]{1,0:T(8,128)(2,1)S(1)}, bf16[64,1024]{1,0:T(8,128)(2,1)S(1)}, u32[]{:S(2)}, u32[]{:S(2)}) collective-permute-start(bf16[64,1024]{1,0:T(8,128)(2,1)S(1)} %maximum_select_fusion), channel_id=1, source_target_pairs={{392,0},{425,1},{458,2},{491,3},{268,4},{333,5},{6,6},{71,7},{128,... | collective-permute-start | bytes 393224 | tf_op jit(solution)/shard_map/ppermute | solution.py:233
  87.1 19.2 %collective-permute-start.8 = (bf16[64,1024]{1,0:T(8,128)(2,1)S(1)}, bf16[64,1024]{1,0:T(8,128)(2,1)S(1)}, u32[]{:S(2)}, u32[]{:S(2)}) collective-permute-start(bf16[64,1024]{1,0:T(8,128)(2,1)S(1)} %maximum_select_fusion), channel_id=1, source_target_pairs={{408,0},{441,1},{474,2},{507,3},{284,4},{349,5},{22,6},{87,7},{144... | collective-permute-start | bytes 393224 | tf_op jit(solution)/shard_map/ppermute | solution.py:233
  99.9 6.5 %copy-start.1 = (bf16[2048,512]{1,0:T(8,128)(2,1)S(1)}, bf16[2048,512]{1,0:T(8,128)(2,1)}, u32[]{:S(2)}) copy-start(bf16[2048,512]{1,0:T(8,128)(2,1)} %get-tuple-element.13) | copy-start | bytes 6291460
  106.4 1.6 copy-start.2
  106.4 2.0 %copy-start.8 = (f32[2,512]{1,0:T(2,128)S(1)}, f32[2,512]{1,0:T(2,128)}, u32[]{:S(2)}) copy-start(f32[2,512]{1,0:T(2,128)} %get-tuple-element.15) | copy-start | bytes 12292
  106.4 2.0 %copy-start.9 = (f32[2,512]{1,0:T(2,128)S(1)}, f32[2,512]{1,0:T(2,128)}, u32[]{:S(2)}) copy-start(f32[2,512]{1,0:T(2,128)} %get-tuple-element.14) | copy-start | bytes 12292
  108.4 45.1 %copy-start.7 = (bf16[1024,64]{0,1:T(8,128)(2,1)S(1)}, bf16[1024,64]{0,1:T(8,128)(2,1)}, u32[]{:S(2)}) copy-start(bf16[1024,64]{0,1:T(8,128)(2,1)} %param.18) | copy-start | bytes 393220
  108.5 7.6 %collective-permute-start.10 = (f32[66,512]{1,0:T(8,128)S(1)}, f32[66,512]{1,0:T(8,128)S(1)}, u32[]{:S(2)}, u32[]{:S(2)}) collective-permute-start(f32[66,512]{1,0:T(8,128)S(1)} %constant_dynamic-slice_fusion), channel_id=1, source_target_pairs={{0,8},{1,9},{2,10},{3,11},{4,12},{5,13},{6,14},{7,15},{8,0},{9,1},... | collective-permute-start | bytes 405512 | tf_op jit(solution)/shard_map/ppermute | solution.py:173
  116.3 6.7 %collective-permute-start.11 = (f32[66,512]{1,0:T(8,128)S(1)}, f32[66,512]{1,0:T(8,128)S(1)}, u32[]{:S(2)}, u32[]{:S(2)}) collective-permute-start(f32[66,512]{1,0:T(8,128)S(1)} %pad_maximum_fusion.7), channel_id=1, source_target_pairs={{0,1},{1,0},{2,3},{3,2},{4,5},{5,4},{6,7},{7,6},{8,9},{9,8},{10,11... | collective-permute-start | bytes 405512 | tf_op jit(solution)/shard_map/ppermute | solution.py:177
  123.1 11.0 %collective-permute-start.12 = (f32[66,512]{1,0:T(8,128)S(1)}, f32[66,512]{1,0:T(8,128)S(1)}, u32[]{:S(2)}, u32[]{:S(2)}) collective-permute-start(f32[66,512]{1,0:T(8,128)S(1)} %pad_maximum_fusion.8), channel_id=1, source_target_pairs={{0,2},{1,3},{2,0},{3,1},{4,6},{5,7},{6,4},{7,5},{8,10},{9,11},{10,... | collective-permute-start | bytes 405512 | tf_op jit(solution)/shard_map/ppermute | solution.py:177
  134.2 19.2 %collective-permute-start.13 = (f32[66,512]{1,0:T(8,128)S(1)}, f32[66,512]{1,0:T(8,128)S(1)}, u32[]{:S(2)}, u32[]{:S(2)}) collective-permute-start(f32[66,512]{1,0:T(8,128)S(1)} %pad_maximum_fusion.9), channel_id=1, source_target_pairs={{0,4},{1,5},{2,6},{3,7},{4,0},{5,1},{6,2},{7,3},{8,12},{9,13},{10,... | collective-permute-start | bytes 405512 | tf_op jit(solution)/shard_map/ppermute | solution.py:177
  153.5 5.0 %collective-permute-start.14 = (bf16[64,512]{1,0:T(8,128)(2,1)S(1)}, bf16[64,512]{1,0:T(8,128)(2,1)S(1)}, u32[]{:S(2)}, u32[]{:S(2)}) collective-permute-start(bf16[64,512]{1,0:T(8,128)(2,1)S(1)} %fusion.11), channel_id=1, source_target_pairs={{0,8},{1,9},{2,10},{3,11},{4,12},{5,13},{6,14},{7,15},{8,0},{9,1},... | collective-permute-start | bytes 196616 | tf_op jit(solution)/shard_map/ppermute | solution.py:184
  (1 other events, 1.0 us)

commit v10 on v9

--- a/solution.py
+++ b/solution.py
@@ -26,13 +26,15 @@
     @pl.when(mask_ref[i * col_tiles + j] > 0)
     def _():
         s = lax.dot_general(y_ref[...], x_ref[...], (((1,), (1,)), ((), ())), preferred_element_type=jnp.float32)
-        s = s * scale - off_ref[...]
+        s = s * scale - jnp.transpose(off_ref[...])[:, 0:1]
         m_old = m_ref[...]
         m_new = jnp.maximum(m_old, jnp.max(s, axis=0, keepdims=True))
         shrink = jnp.exp(m_old - m_new)
         p = jnp.exp(s - m_new)
         l_ref[...] = l_ref[...] * shrink + jnp.sum(p, axis=0, keepdims=True)
-        acc_ref[...] = acc_ref[...] * shrink + jnp.dot(v_ref[...], p.astype(jnp.bfloat16), preferred_element_type=jnp.float32)
+        acc_ref[...] = acc_ref[...] * shrink + lax.dot_general(
+            v_ref[...], p.astype(jnp.bfloat16), (((0,), (0,)), ((), ())), preferred_element_type=jnp.float32
+        )
         m_ref[...] = m_new
 
     @pl.when(j == col_tiles - 1)
@@ -43,10 +45,14 @@
         out_ref[w + 1:w + 2, :] = m_ref[...]
 
 
-def date_partials_kernel(targets, sources, offsets, values_t, live):
+def lane_offsets(offsets):
+    return jnp.broadcast_to(offsets.astype(jnp.float32)[None, :], (8, offsets.shape[0]))
+
+
+def date_partials_kernel(targets, sources, offsets, values, live):
     rows, factors = targets.shape
     cols = sources.shape[0]
-    width = values_t.shape[0]
+    width = values.shape[1]
     row_tiles, col_tiles = rows // BLOCK, cols // BLOCK
     kernel = lambda *refs: partials_kernel(*refs, scale=sharpness / factors**0.5, col_tiles=col_tiles)
     return pl.pallas_call(
@@ -58,8 +64,8 @@
             in_specs=[
                 pl.BlockSpec((BLOCK, factors), lambda i, j, m: (i, 0)),
                 pl.BlockSpec((BLOCK, factors), lambda i, j, m: (j, 0)),
-                pl.BlockSpec((BLOCK, 1), lambda i, j, m: (j, 0)),
-                pl.BlockSpec((width, BLOCK), lambda i, j, m: (0, j)),
+                pl.BlockSpec((8, BLOCK), lambda i, j, m: (0, j)),
+                pl.BlockSpec((BLOCK, width), lambda i, j, m: (j, 0)),
             ],
             out_specs=pl.BlockSpec((width + 2, BLOCK), lambda i, j, m: (0, i)),
             scratch_shapes=[
@@ -69,7 +75,7 @@
             ],
         ),
         compiler_params=pltpu.CompilerParams(dimension_semantics=("arbitrary", "arbitrary")),
-    )(live.reshape(-1).astype(jnp.int32), targets, sources, offsets.astype(jnp.float32).reshape(cols, 1), values_t)
+    )(live.reshape(-1).astype(jnp.int32), targets, sources, lane_offsets(offsets), values)
 
 
 def weights_kernel(mask_ref, x_ref, y_ref, off_ref, p_ref, stats_ref, *, scale, col_tiles):
@@ -78,7 +84,7 @@
     def scores(j):
         y = y_ref[j * BLOCK : (j + 1) * BLOCK, :]
         s = lax.dot_general(y, x_ref[...], (((1,), (1,)), ((), ())), preferred_element_type=jnp.float32)
-        return s * scale - off_ref[j * BLOCK : (j + 1) * BLOCK, :]
+        return s * scale - jnp.transpose(off_ref[:, j * BLOCK : (j + 1) * BLOCK])[:, 0:1]
 
     stats_ref[...] = jnp.concatenate(
         [jnp.zeros((1, BLOCK), jnp.float32), jnp.full((1, BLOCK), very_low, jnp.float32)], 0
@@ -121,7 +127,7 @@
             in_specs=[
                 pl.BlockSpec((BLOCK, factors), lambda i, m: (i, 0)),
                 pl.BlockSpec((cols, factors), lambda i, m: (0, 0)),
-                pl.BlockSpec((cols, 1), lambda i, m: (0, 0)),
+                pl.BlockSpec((8, cols), lambda i, m: (0, 0)),
             ],
             out_specs=(
                 pl.BlockSpec((cols, BLOCK), lambda i, m: (0, i)),
@@ -129,7 +135,7 @@
             ),
         ),
         compiler_params=pltpu.CompilerParams(dimension_semantics=("arbitrary",)),
-    )(live.reshape(-1).astype(jnp.int32), targets, sources, offsets.astype(jnp.float32).reshape(cols, 1))
+    )(live.reshape(-1).astype(jnp.int32), targets, sources, lane_offsets(offsets))
 
 
 def local_live(targets, tile_mask, col_tile_ids):
@@ -138,9 +144,9 @@
     return tile_mask[row_ids][:, col_tile_ids]
 
 
-def date_partials(targets, sources, offsets, values_t, tile_mask, col_tile_ids):
+def date_partials(targets, sources, offsets, values, tile_mask, col_tile_ids):
     live = local_live(targets, tile_mask, col_tile_ids)
-    return date_partials_kernel(targets, sources, offsets, values_t, live)
+    return date_partials_kernel(targets, sources, offsets, values, live)
 
 
 HALVING_BITS = (3,)
@@ -267,7 +273,7 @@
     early_col_ids = pair * src_tiles + jnp.arange(src_tiles)
     mid_sources = regroup_order(regroup(states_mid))
     mid_offsets = regroup_offsets(offset_mid)
-    partials = date_partials(states_mid, states_late, offset_late, values_late.T, mask_mid, col_ids)
+    partials = date_partials(states_mid, states_late, offset_late, values_late, mask_mid, col_ids)
     partials, mid_sources, mid_offsets = lax.optimization_barrier(
         (partials, mid_sources, mid_offsets)
     )

time: 160 us -> 160 us (level)
  starting transfers between devices: 74.5 us -> 70.6 us
  waiting for transfers between devices: 51 us -> 54 us
  matrix products: 0.94 us -> 2.67 us
    ppermute x6, waiting for transfers between devices: 38.8 us -> 42.8 us  [finish(): got = lax.ppermute(packed, 'src', xor_perm(src_size, bit))]
    reshape x2 -> x0, local copies, waits for them, and re-layouts: 2.78 us -> none  [the longest x1 1.42 us: date_weights_kernel(): offsets.astype(jnp.float32).reshape(cols, 1)]
    ppermute x6, starting transfers between devices: 29.8 us -> 27.1 us  [finish(): got = lax.ppermute(packed, 'src', xor_perm(src_size, bit))]
    broadcast_in_dim x0 -> x2, local copies, waits for them, and re-layouts: none -> 1.95 us  [lane_offsets(): jnp.broadcast_to(offsets.astype(jnp.float32)[None, :], (8, offsets.shape[...]
    dot_general x2, matrix products: 0.94 us -> 2.67 us  [per_device(): jnp.dot(mid_values_t, w, preferred_element_type=jnp.float32)]
where the time goes in v10:
time: 160 us; the launch traced here: 159 us
  starting transfers between devices  70.6 us (44%)
  waiting for transfers between devices  54 us (34%)
  Pallas kernels  18.7 us (12%)
  local copies, waits for them, and re-layouts  9.37 us (6%)
  matrix products  2.67 us (2%)
  other arithmetic  2.35 us (1%)
    ppermute x6, waiting for transfers between devices, finish(): got = lax.ppermute(packed, 'src', xor_perm(src_size, bit))  42.8 us
    ppermute x6, starting transfers between devices, finish(): got = lax.ppermute(packed, 'src', xor_perm(src_size, bit))  27.1 us
    ppermute x4, starting transfers between devices, regroup(): return [lax.ppermute(block_rows, ('tgt', 'src'), p) for p in perms]  22.4 us
    ppermute x2, starting transfers between devices, finish(): got = lax.ppermute(send, 'src', xor_perm(src_size, bit))  13.3 us
    pallas_call x2, Pallas kernels, date_weights_kernel(): pl.pallas_call(kernel, out_shape=(jax.ShapeDtypeStruct((cols, rows), jnp....  10.3 us
    pallas_call x1, Pallas kernels, date_partials_kernel(): pl.pallas_call(kernel, out_shape=jax.ShapeDtypeStruct((width + 2, rows),...  8.4 us
    ppermute x2, waiting for transfers between devices, finish(): got = lax.ppermute(send, 'src', xor_perm(src_size, bit))  7.15 us
    ppermute x2, starting transfers between devices, finish(): got = lax.ppermute(value, 'src', xor_perm(src_size, bit))  5.93 us
  transfers between devices with their start and end apart: 15, of which 10 were waited for; matrix products, arithmetic and copies ran while one was open for 6% of the time, Pallas kernels for 12%

profile of v10, /device:TPU:1, one launch (start us, length us, event | category | flops | bytes accessed | tf_op | source)
XLA Modules:
  0.0 159.0 jit_solution(4119048723238114353)
XLA Ops:
  0.6 11.5 %collective-permute-start.1 = (bf16[1024,128]{1,0:T(8,128)(2,1)}, bf16[1024,128]{1,0:T(8,128)(2,1)S(1)}, u32[]{:S(2)}, u32[]{:S(2)}) collective-permute-start(bf16[1024,128]{1,0:T(8,128)(2,1)} %refs_1_.1), channel_id=1, source_target_pairs={{392,0},{425,1},{458,2},{491,3},{268,4},{333,5},{6,6},{71,7},{128,... | collective-permute-start | bytes 786440 | tf_op jit(solution)/shard_map/ppermute | solution.py:239
  12.1 2.5 %collective-permute-start = (bf16[1024,128]{1,0:T(8,128)(2,1)}, bf16[1024,128]{1,0:T(8,128)(2,1)S(1)}, u32[]{:S(2)}, u32[]{:S(2)}) collective-permute-start(bf16[1024,128]{1,0:T(8,128)(2,1)} %refs_1_.1), channel_id=1, source_target_pairs={{408,0},{441,1},{474,2},{507,3},{284,4},{349,5},{22,6},{87,7},{144... | collective-permute-start | bytes 786440 | tf_op jit(solution)/shard_map/ppermute | solution.py:239
  21.9 8.4 %shard_map.113 = f32[66,1024]{1,0:T(8,128)} custom-call(s32[8]{0:T(128)} %reshape.63.refs_0_, bf16[1024,128]{1,0:T(8,128)(2,1)} %refs_1_.1, bf16[2048,128]{1,0:T(8,128)(2,1)} %refs_2_.1, f32[8,2048]{1,0:T(8,128)} %broadcast_in_dim.4.refs_3_, bf16[2048,64]{1,0:T(8,128)(2,1)} %copy.18.refs_4_), custom_call_target="tpu_custom_call" | custom-call | tf_op jit(solution)/shard_map/pallas_call | solution.py:58
  31.3 10.1 %collective-permute-start.3 = (f32[66,512]{1,0:T(8,128)S(1)}, f32[66,512]{1,0:T(8,128)S(1)}, u32[]{:S(2)}, u32[]{:S(2)}) collective-permute-start(f32[66,512]{1,0:T(8,128)S(1)} %constant_dynamic-slice_fusion.1), channel_id=1, source_target_pairs={{0,8},{1,9},{2,10},{3,11},{4,12},{5,13},{6,14},{7,15},{8,0},{9,1},... | collective-permute-start | bytes 405512 | tf_op jit(solution)/shard_map/ppermute | solution.py:179
  41.4 3.5 %collective-permute-done.3 = f32[66,512]{1,0:T(8,128)S(1)} collective-permute-done((f32[66,512]{1,0:T(8,128)S(1)}, f32[66,512]{1,0:T(8,128)S(1)}, u32[]{:S(2)}, u32[]{:S(2)}) %collective-permute-start.3) | collective-permute-done | bytes 135200 | tf_op jit(solution)/shard_map/ppermute | solution.py:179
  47.1 5.2 %collective-permute-done.4 = f32[66,512]{1,0:T(8,128)S(1)} collective-permute-done((f32[66,512]{1,0:T(8,128)S(1)}, f32[66,512]{1,0:T(8,128)S(1)}, u32[]{:S(2)}, u32[]{:S(2)}) %collective-permute-start.4) | collective-permute-done | bytes 135200 | tf_op jit(solution)/shard_map/ppermute | solution.py:183
  54.3 9.8 %collective-permute-done.5 = f32[66,512]{1,0:T(8,128)S(1)} collective-permute-done((f32[66,512]{1,0:T(8,128)S(1)}, f32[66,512]{1,0:T(8,128)S(1)}, u32[]{:S(2)}, u32[]{:S(2)}) %collective-permute-start.5) | collective-permute-done | bytes 135200 | tf_op jit(solution)/shard_map/ppermute | solution.py:183
  64.2 5.9 %collective-permute-start.6 = (f32[66,512]{1,0:T(8,128)S(1)}, f32[66,512]{1,0:T(8,128)S(1)}, u32[]{:S(2)}, u32[]{:S(2)}) collective-permute-start(f32[66,512]{1,0:T(8,128)S(1)} %pad_maximum_fusion.6), channel_id=1, source_target_pairs={{0,4},{1,5},{2,6},{3,7},{4,0},{5,1},{6,2},{7,3},{8,12},{9,13},{10,... | collective-permute-start | bytes 405512 | tf_op jit(solution)/shard_map/ppermute | solution.py:183
  70.1 7.8 %collective-permute-done.6 = f32[66,512]{1,0:T(8,128)S(1)} collective-permute-done((f32[66,512]{1,0:T(8,128)S(1)}, f32[66,512]{1,0:T(8,128)S(1)}, u32[]{:S(2)}, u32[]{:S(2)}) %collective-permute-start.6) | collective-permute-done | bytes 135200 | tf_op jit(solution)/shard_map/ppermute | solution.py:183
  78.1 4.0 %collective-permute-start.7 = (bf16[64,512]{1,0:T(8,128)(2,1)S(1)}, bf16[64,512]{1,0:T(8,128)(2,1)S(1)}, u32[]{:S(2)}, u32[]{:S(2)}) collective-permute-start(bf16[64,512]{1,0:T(8,128)(2,1)S(1)} %fusion.13), channel_id=1, source_target_pairs={{0,8},{1,9},{2,10},{3,11},{4,12},{5,13},{6,14},{7,15},{8,0},{9,1},... | collective-permute-start | bytes 196616 | tf_op jit(solution)/shard_map/ppermute | solution.py:190
  83.8 3.4 %collective-permute-start.9 = (bf16[64,1024]{1,0:T(8,128)(2,1)S(1)}, bf16[64,1024]{1,0:T(8,128)(2,1)S(1)}, u32[]{:S(2)}, u32[]{:S(2)}) collective-permute-start(bf16[64,1024]{1,0:T(8,128)(2,1)S(1)} %maximum_select_fusion), channel_id=1, source_target_pairs={{392,0},{425,1},{458,2},{491,3},{268,4},{333,5},{6,6},{71,7},{128,... | collective-permute-start | bytes 393224 | tf_op jit(solution)/shard_map/ppermute | solution.py:239
  87.1 5.0 %collective-permute-start.8 = (bf16[64,1024]{1,0:T(8,128)(2,1)S(1)}, bf16[64,1024]{1,0:T(8,128)(2,1)S(1)}, u32[]{:S(2)}, u32[]{:S(2)}) collective-permute-start(bf16[64,1024]{1,0:T(8,128)(2,1)S(1)} %maximum_select_fusion), channel_id=1, source_target_pairs={{408,0},{441,1},{474,2},{507,3},{284,4},{349,5},{22,6},{87,7},{144... | collective-permute-start | bytes 393224 | tf_op jit(solution)/shard_map/ppermute | solution.py:239
  95.6 4.0 %shard_map.115 = (bf16[2048,512]{1,0:T(8,128)(2,1)}, f32[2,512]{1,0:T(2,128)}) custom-call(s32[4]{0:T(128)} %get-tuple-element.17.refs_0_, bf16[512,128]{1,0:T(8,128)(2,1)} %get-tuple-element.35.refs_1_, bf16[2048,128]{1,0:T(8,128)(2,1)} %pad_maximum_fusion.refs_2_, f32[8,2048]{1,0:T(8,128)} %broadcast_in_dim.5.refs_3_), custom_call_target="tpu_custom_call" | custom-call | tf_op jit(solution)/shard_map/pallas_call | solution.py:118
  99.6 6.3 %shard_map.114 = (bf16[2048,512]{1,0:T(8,128)(2,1)}, f32[2,512]{1,0:T(2,128)}) custom-call(s32[4]{0:T(128)} %get-tuple-element.16.refs_0_, bf16[512,128]{1,0:T(8,128)(2,1)} %get-tuple-element.34.refs_1_, bf16[2048,128]{1,0:T(8,128)(2,1)} %pad_maximum_fusion.refs_2_, f32[8,2048]{1,0:T(8,128)} %broadcast_in_dim.5.refs_3_), custom_call_target="tpu_custom_call" | custom-call | tf_op jit(solution)/shard_map/pallas_call | solution.py:118
  106.0 2.2 %fusion = f32[64,512]{1,0:T(8,128)S(1)} fusion(bf16[2048,512]{1,0:T(8,128)(2,1)} %get-tuple-element.13, bf16[64,1024]{1,0:T(8,128)(2,1)S(1)} %get-tuple-element.33, bf16[64,1024]{1,0:T(8,128)(2,1)S(1)} %get-tuple-element.32), kind=kOutput, calls=%fused_computation.9 | convolution fusion | flops 134742016 | bytes 2490368 | tf_op jit(solution)/shard_map/dot_general | solution.py:290
  108.8 3.2 %collective-permute-start.10 = (f32[66,512]{1,0:T(8,128)S(1)}, f32[66,512]{1,0:T(8,128)S(1)}, u32[]{:S(2)}, u32[]{:S(2)}) collective-permute-start(f32[66,512]{1,0:T(8,128)S(1)} %constant_dynamic-slice_fusion), channel_id=1, source_target_pairs={{0,8},{1,9},{2,10},{3,11},{4,12},{5,13},{6,14},{7,15},{8,0},{9,1},... | collective-permute-start | bytes 405512 | tf_op jit(solution)/shard_map/ppermute | solution.py:179
  112.0 3.6 %collective-permute-done.10 = f32[66,512]{1,0:T(8,128)S(1)} collective-permute-done((f32[66,512]{1,0:T(8,128)S(1)}, f32[66,512]{1,0:T(8,128)S(1)}, u32[]{:S(2)}, u32[]{:S(2)}) %collective-permute-start.10) | collective-permute-done | bytes 135200 | tf_op jit(solution)/shard_map/ppermute | solution.py:179
  115.7 2.8 %collective-permute-start.11 = (f32[66,512]{1,0:T(8,128)S(1)}, f32[66,512]{1,0:T(8,128)S(1)}, u32[]{:S(2)}, u32[]{:S(2)}) collective-permute-start(f32[66,512]{1,0:T(8,128)S(1)} %pad_maximum_fusion.7), channel_id=1, source_target_pairs={{0,1},{1,0},{2,3},{3,2},{4,5},{5,4},{6,7},{7,6},{8,9},{9,8},{10,11... | collective-permute-start | bytes 405512 | tf_op jit(solution)/shard_map/ppermute | solution.py:183
  118.6 4.3 %collective-permute-done.11 = f32[66,512]{1,0:T(8,128)S(1)} collective-permute-done((f32[66,512]{1,0:T(8,128)S(1)}, f32[66,512]{1,0:T(8,128)S(1)}, u32[]{:S(2)}, u32[]{:S(2)}) %collective-permute-start.11) | collective-permute-done | bytes 135200 | tf_op jit(solution)/shard_map/ppermute | solution.py:183
  122.9 2.4 %collective-permute-start.12 = (f32[66,512]{1,0:T(8,128)S(1)}, f32[66,512]{1,0:T(8,128)S(1)}, u32[]{:S(2)}, u32[]{:S(2)}) collective-permute-start(f32[66,512]{1,0:T(8,128)S(1)} %pad_maximum_fusion.8), channel_id=1, source_target_pairs={{0,2},{1,3},{2,0},{3,1},{4,6},{5,7},{6,4},{7,5},{8,10},{9,11},{10,... | collective-permute-start | bytes 405512 | tf_op jit(solution)/shard_map/ppermute | solution.py:183
  125.4 9.1 %collective-permute-done.12 = f32[66,512]{1,0:T(8,128)S(1)} collective-permute-done((f32[66,512]{1,0:T(8,128)S(1)}, f32[66,512]{1,0:T(8,128)S(1)}, u32[]{:S(2)}, u32[]{:S(2)}) %collective-permute-start.12) | collective-permute-done | bytes 135200 | tf_op jit(solution)/shard_map/ppermute | solution.py:183
  134.6 12.0 %collective-permute-start.13 = (f32[66,512]{1,0:T(8,128)S(1)}, f32[66,512]{1,0:T(8,128)S(1)}, u32[]{:S(2)}, u32[]{:S(2)}) collective-permute-start(f32[66,512]{1,0:T(8,128)S(1)} %pad_maximum_fusion.9), channel_id=1, source_target_pairs={{0,4},{1,5},{2,6},{3,7},{4,0},{5,1},{6,2},{7,3},{8,12},{9,13},{10,... | collective-permute-start | bytes 405512 | tf_op jit(solution)/shard_map/ppermute | solution.py:183
  146.6 6.6 %collective-permute-done.13 = f32[66,512]{1,0:T(8,128)S(1)} collective-permute-done((f32[66,512]{1,0:T(8,128)S(1)}, f32[66,512]{1,0:T(8,128)S(1)}, u32[]{:S(2)}, u32[]{:S(2)}) %collective-permute-start.13) | collective-permute-done | bytes 135200 | tf_op jit(solution)/shard_map/ppermute | solution.py:183
  155.2 3.1 %collective-permute-done.14 = bf16[64,512]{1,0:T(8,128)(2,1)S(1)} collective-permute-done((bf16[64,512]{1,0:T(8,128)(2,1)S(1)}, bf16[64,512]{1,0:T(8,128)(2,1)S(1)}, u32[]{:S(2)}, u32[]{:S(2)}) %collective-permute-start.14) | collective-permute-done | bytes 65568 | tf_op jit(solution)/shard_map/ppermute | solution.py:190
  (87 shorter events, 20.8 us)
Async XLA Ops:
  0.6 16.1 %copy-start = (s32[64,64]{1,0:T(8,128)S(1)}, s32[64,64]{1,0:T(8,128)}, u32[]{:S(2)}) copy-start(s32[64,64]{1,0:T(8,128)} %param.16) | copy-start | bytes 49156
  0.6 29.7 %collective-permute-start.1 = (bf16[1024,128]{1,0:T(8,128)(2,1)}, bf16[1024,128]{1,0:T(8,128)(2,1)S(1)}, u32[]{:S(2)}, u32[]{:S(2)}) collective-permute-start(bf16[1024,128]{1,0:T(8,128)(2,1)} %refs_1_.1), channel_id=1, source_target_pairs={{392,0},{425,1},{458,2},{491,3},{268,4},{333,5},{6,6},{71,7},{128,... | collective-permute-start | bytes 786440 | tf_op jit(solution)/shard_map/ppermute | solution.py:239
  12.1 18.2 %collective-permute-start = (bf16[1024,128]{1,0:T(8,128)(2,1)}, bf16[1024,128]{1,0:T(8,128)(2,1)S(1)}, u32[]{:S(2)}, u32[]{:S(2)}) collective-permute-start(bf16[1024,128]{1,0:T(8,128)(2,1)} %refs_1_.1), channel_id=1, source_target_pairs={{408,0},{441,1},{474,2},{507,3},{284,4},{349,5},{22,6},{87,7},{144... | collective-permute-start | bytes 786440 | tf_op jit(solution)/shard_map/ppermute | solution.py:239
  14.6 16.6 %collective-permute-start.2 = (bf16[2048]{0:T(1024)(128)(2,1)}, bf16[2048]{0:T(1024)(128)(2,1)S(1)}, u32[]{:S(2)}, u32[]{:S(2)}) collective-permute-start(bf16[2048]{0:T(1024)(128)(2,1)} %param.14), channel_id=1, source_target_pairs={{12,0},{13,1},{14,2},{15,3},{8,4},{10,5},{0,6},{2,7},{4,8},{5,9},{... | collective-permute-start | bytes 12296 | tf_op jit(solution)/shard_map/ppermute | solution.py:255
  30.3 1.0 copy-start.2
  30.4 47.6 %copy-start.5 = (bf16[1024,64]{0,1:T(8,128)(2,1)S(1)}, bf16[1024,64]{0,1:T(8,128)(2,1)}, u32[]{:S(2)}) copy-start(bf16[1024,64]{0,1:T(8,128)(2,1)} %param.15) | copy-start | bytes 393220
  30.4 51.7 %copy-start.3 = (bf16[1024,128]{1,0:T(8,128)(2,1)S(1)}, bf16[1024,128]{1,0:T(8,128)(2,1)}, u32[]{:S(2)}) copy-start(bf16[1024,128]{1,0:T(8,128)(2,1)} %param.17) | copy-start | bytes 786436
  31.3 13.7 %collective-permute-start.3 = (f32[66,512]{1,0:T(8,128)S(1)}, f32[66,512]{1,0:T(8,128)S(1)}, u32[]{:S(2)}, u32[]{:S(2)}) collective-permute-start(f32[66,512]{1,0:T(8,128)S(1)} %constant_dynamic-slice_fusion.1), channel_id=1, source_target_pairs={{0,8},{1,9},{2,10},{3,11},{4,12},{5,13},{6,14},{7,15},{8,0},{9,1},... | collective-permute-start | bytes 405512 | tf_op jit(solution)/shard_map/ppermute | solution.py:179
  45.1 7.2 %collective-permute-start.4 = (f32[66,512]{1,0:T(8,128)S(1)}, f32[66,512]{1,0:T(8,128)S(1)}, u32[]{:S(2)}, u32[]{:S(2)}) collective-permute-start(f32[66,512]{1,0:T(8,128)S(1)} %pad_maximum_fusion.4), channel_id=1, source_target_pairs={{0,1},{1,0},{2,3},{3,2},{4,5},{5,4},{6,7},{7,6},{8,9},{9,8},{10,11... | collective-permute-start | bytes 405512 | tf_op jit(solution)/shard_map/ppermute | solution.py:183
  52.4 11.7 %collective-permute-start.5 = (f32[66,512]{1,0:T(8,128)S(1)}, f32[66,512]{1,0:T(8,128)S(1)}, u32[]{:S(2)}, u32[]{:S(2)}) collective-permute-start(f32[66,512]{1,0:T(8,128)S(1)} %pad_maximum_fusion.5), channel_id=1, source_target_pairs={{0,2},{1,3},{2,0},{3,1},{4,6},{5,7},{6,4},{7,5},{8,10},{9,11},{10,... | collective-permute-start | bytes 405512 | tf_op jit(solution)/shard_map/ppermute | solution.py:183
  64.2 13.8 %collective-permute-start.6 = (f32[66,512]{1,0:T(8,128)S(1)}, f32[66,512]{1,0:T(8,128)S(1)}, u32[]{:S(2)}, u32[]{:S(2)}) collective-permute-start(f32[66,512]{1,0:T(8,128)S(1)} %pad_maximum_fusion.6), channel_id=1, source_target_pairs={{0,4},{1,5},{2,6},{3,7},{4,0},{5,1},{6,2},{7,3},{8,12},{9,13},{10,... | collective-permute-start | bytes 405512 | tf_op jit(solution)/shard_map/ppermute | solution.py:183
  78.1 5.7 %collective-permute-start.7 = (bf16[64,512]{1,0:T(8,128)(2,1)S(1)}, bf16[64,512]{1,0:T(8,128)(2,1)S(1)}, u32[]{:S(2)}, u32[]{:S(2)}) collective-permute-start(bf16[64,512]{1,0:T(8,128)(2,1)S(1)} %fusion.13), channel_id=1, source_target_pairs={{0,8},{1,9},{2,10},{3,11},{4,12},{5,13},{6,14},{7,15},{8,0},{9,1},... | collective-permute-start | bytes 196616 | tf_op jit(solution)/shard_map/ppermute | solution.py:190
  83.8 24.4 %copy-start.4 = (bf16[64,1024]{1,0:T(8,128)(2,1)}, bf16[64,1024]{1,0:T(8,128)(2,1)S(1)}, u32[]{:S(2)}) copy-start(bf16[64,1024]{1,0:T(8,128)(2,1)S(1)} %maximum_select_fusion) | copy-start | bytes 393220
  83.8 22.1 %collective-permute-start.9 = (bf16[64,1024]{1,0:T(8,128)(2,1)S(1)}, bf16[64,1024]{1,0:T(8,128)(2,1)S(1)}, u32[]{:S(2)}, u32[]{:S(2)}) collective-permute-start(bf16[64,1024]{1,0:T(8,128)(2,1)S(1)} %maximum_select_fusion), channel_id=1, source_target_pairs={{392,0},{425,1},{458,2},{491,3},{268,4},{333,5},{6,6},{71,7},{128,... | collective-permute-start | bytes 393224 | tf_op jit(solution)/shard_map/ppermute | solution.py:239
  87.1 18.8 %collective-permute-start.8 = (bf16[64,1024]{1,0:T(8,128)(2,1)S(1)}, bf16[64,1024]{1,0:T(8,128)(2,1)S(1)}, u32[]{:S(2)}, u32[]{:S(2)}) collective-permute-start(bf16[64,1024]{1,0:T(8,128)(2,1)S(1)} %maximum_select_fusion), channel_id=1, source_target_pairs={{408,0},{441,1},{474,2},{507,3},{284,4},{349,5},{22,6},{87,7},{144... | collective-permute-start | bytes 393224 | tf_op jit(solution)/shard_map/ppermute | solution.py:239
  105.9 2.3 %copy-start.1 = (bf16[2048,512]{1,0:T(8,128)(2,1)S(1)}, bf16[2048,512]{1,0:T(8,128)(2,1)}, u32[]{:S(2)}) copy-start(bf16[2048,512]{1,0:T(8,128)(2,1)} %get-tuple-element.12) | copy-start | bytes 6291460
  105.9 2.7 %copy-start.7 = (f32[2,512]{1,0:T(2,128)S(1)}, f32[2,512]{1,0:T(2,128)}, u32[]{:S(2)}) copy-start(f32[2,512]{1,0:T(2,128)} %get-tuple-element.15) | copy-start | bytes 12292
  105.9 2.7 %copy-start.8 = (f32[2,512]{1,0:T(2,128)S(1)}, f32[2,512]{1,0:T(2,128)}, u32[]{:S(2)}) copy-start(f32[2,512]{1,0:T(2,128)} %get-tuple-element.14) | copy-start | bytes 12292
  108.7 44.6 %copy-start.6 = (bf16[1024,64]{0,1:T(8,128)(2,1)S(1)}, bf16[1024,64]{0,1:T(8,128)(2,1)}, u32[]{:S(2)}) copy-start(bf16[1024,64]{0,1:T(8,128)(2,1)} %param.18) | copy-start | bytes 393220
  108.8 6.8 %collective-permute-start.10 = (f32[66,512]{1,0:T(8,128)S(1)}, f32[66,512]{1,0:T(8,128)S(1)}, u32[]{:S(2)}, u32[]{:S(2)}) collective-permute-start(f32[66,512]{1,0:T(8,128)S(1)} %constant_dynamic-slice_fusion), channel_id=1, source_target_pairs={{0,8},{1,9},{2,10},{3,11},{4,12},{5,13},{6,14},{7,15},{8,0},{9,1},... | collective-permute-start | bytes 405512 | tf_op jit(solution)/shard_map/ppermute | solution.py:179
  115.7 7.1 %collective-permute-start.11 = (f32[66,512]{1,0:T(8,128)S(1)}, f32[66,512]{1,0:T(8,128)S(1)}, u32[]{:S(2)}, u32[]{:S(2)}) collective-permute-start(f32[66,512]{1,0:T(8,128)S(1)} %pad_maximum_fusion.7), channel_id=1, source_target_pairs={{0,1},{1,0},{2,3},{3,2},{4,5},{5,4},{6,7},{7,6},{8,9},{9,8},{10,11... | collective-permute-start | bytes 405512 | tf_op jit(solution)/shard_map/ppermute | solution.py:183
  122.9 11.6 %collective-permute-start.12 = (f32[66,512]{1,0:T(8,128)S(1)}, f32[66,512]{1,0:T(8,128)S(1)}, u32[]{:S(2)}, u32[]{:S(2)}) collective-permute-start(f32[66,512]{1,0:T(8,128)S(1)} %pad_maximum_fusion.8), channel_id=1, source_target_pairs={{0,2},{1,3},{2,0},{3,1},{4,6},{5,7},{6,4},{7,5},{8,10},{9,11},{10,... | collective-permute-start | bytes 405512 | tf_op jit(solution)/shard_map/ppermute | solution.py:183
  134.6 18.6 %collective-permute-start.13 = (f32[66,512]{1,0:T(8,128)S(1)}, f32[66,512]{1,0:T(8,128)S(1)}, u32[]{:S(2)}, u32[]{:S(2)}) collective-permute-start(f32[66,512]{1,0:T(8,128)S(1)} %pad_maximum_fusion.9), channel_id=1, source_target_pairs={{0,4},{1,5},{2,6},{3,7},{4,0},{5,1},{6,2},{7,3},{8,12},{9,13},{10,... | collective-permute-start | bytes 405512 | tf_op jit(solution)/shard_map/ppermute | solution.py:183
  153.3 5.0 %collective-permute-start.14 = (bf16[64,512]{1,0:T(8,128)(2,1)S(1)}, bf16[64,512]{1,0:T(8,128)(2,1)S(1)}, u32[]{:S(2)}, u32[]{:S(2)}) collective-permute-start(bf16[64,512]{1,0:T(8,128)(2,1)S(1)} %fusion.11), channel_id=1, source_target_pairs={{0,8},{1,9},{2,10},{3,11},{4,12},{5,13},{6,14},{7,15},{8,0},{9,1},... | collective-permute-start | bytes 196616 | tf_op jit(solution)/shard_map/ppermute | solution.py:190

commit v11 on v10

--- a/solution.py
+++ b/solution.py
@@ -150,11 +150,16 @@
 
 
 HALVING_BITS = (3,)
-EXCHANGE_BITS = (0, 1, 2)
+FAR_PARTNER = (6, 7, 4, 5, 2, 3, 0, 1)
+EXCHANGES = (lambda y: y ^ 1, lambda y: y ^ 2, lambda y: FAR_PARTNER[y])
 
 
 def xor_perm(size, bit):
     return [(i, i ^ (1 << bit)) for i in range(size)]
+
+
+def exchange_perm(size, partner):
+    return [(i, (i // 8) * 8 + partner(i % 8)) for i in range(size)]
 
 
 def merge(mine, theirs):
@@ -179,8 +184,8 @@
         got = lax.ppermute(send, "src", xor_perm(src_size, bit))
         packed = merge(keep, got)
         exercise = lax.dynamic_slice_in_dim(exercise, mine_hi * half, half, 0)
-    for bit in EXCHANGE_BITS:
-        got = lax.ppermute(packed, "src", xor_perm(src_size, bit))
+    for partner in EXCHANGES:
+        got = lax.ppermute(packed, "src", exchange_perm(src_size, partner))
         packed = merge(packed, got)
     width = packed.shape[0] - 2
     continuation = packed[:width] / packed[width : width + 1]

time: 160 us -> 156 us (0.975)
  the two profiles are of different devices: /device:TPU:1 before, /device:TPU:48 now
where the time goes in v11:
time: 156 us; the launch traced here: 155 us
  starting transfers between devices  71.7 us (46%)
  waiting for transfers between devices  50.2 us (32%)
  Pallas kernels  17.1 us (11%)
  local copies, waits for them, and re-layouts  9.37 us (6%)
  matrix products  2.67 us (2%)
  other arithmetic  2.35 us (2%)
    ppermute x6, waiting for transfers between devices, finish(): got = lax.ppermute(packed, 'src', exchange_perm(src_size, partner))  37.6 us
    ppermute x6, starting transfers between devices, finish(): got = lax.ppermute(packed, 'src', exchange_perm(src_size, partner))  36.3 us
    ppermute x2, starting transfers between devices, finish(): got = lax.ppermute(send, 'src', xor_perm(src_size, bit))  12.5 us
    ppermute x1, starting transfers between devices, regroup_offsets(): return lax.ppermute(offsets, ('tgt', 'src'), pairs)  10.8 us
    pallas_call x2, Pallas kernels, date_weights_kernel(): pl.pallas_call(kernel, out_shape=(jax.ShapeDtypeStruct((cols, rows), jnp....  10.3 us
    ppermute x2, waiting for transfers between devices, finish(): got = lax.ppermute(send, 'src', xor_perm(src_size, bit))  6.82 us
    pallas_call x1, Pallas kernels, date_partials_kernel(): pl.pallas_call(kernel, out_shape=jax.ShapeDtypeStruct((width + 2, rows),...  6.76 us
    ppermute x4, starting transfers between devices, regroup(): return [lax.ppermute(block_rows, ('tgt', 'src'), p) for p in perms]  6.11 us
  transfers between devices with their start and end apart: 15, of which 10 were waited for; matrix products, arithmetic and copies ran while one was open for 7% of the time, Pallas kernels for 11%

profile of v11, /device:TPU:48, one launch (start us, length us, event | category | flops | bytes accessed | tf_op | source)
XLA Modules:
  0.0 154.6 jit_solution(6896342514916176936)
XLA Ops:
  4.2 10.8 %collective-permute-start.2 = (bf16[2048]{0:T(1024)(128)(2,1)}, bf16[2048]{0:T(1024)(128)(2,1)S(1)}, u32[]{:S(2)}, u32[]{:S(2)}) collective-permute-start(bf16[2048]{0:T(1024)(128)(2,1)} %param.14), channel_id=1, source_target_pairs={{12,0},{13,1},{14,2},{15,3},{8,4},{10,5},{0,6},{2,7},{4,8},{5,9},{... | collective-permute-start | bytes 12296 | tf_op jit(solution)/shard_map/ppermute | solution.py:260
  17.1 1.9 %copy.18.refs_4_ = bf16[2048,64]{1,0:T(8,128)(2,1)} copy(bf16[2048,64]{0,1:T(8,128)(2,1)} %param.12) | data formatting | bytes 524288 | tf_op args[2]
  20.3 6.8 %shard_map.113 = f32[66,1024]{1,0:T(8,128)} custom-call(s32[8]{0:T(128)} %reshape.63.refs_0_, bf16[1024,128]{1,0:T(8,128)(2,1)} %refs_1_.1, bf16[2048,128]{1,0:T(8,128)(2,1)} %refs_2_.1, f32[8,2048]{1,0:T(8,128)} %broadcast_in_dim.4.refs_3_, bf16[2048,64]{1,0:T(8,128)(2,1)} %copy.18.refs_4_), custom_call_target="tpu_custom_call" | custom-call | tf_op jit(solution)/shard_map/pallas_call | solution.py:58
  28.1 8.6 %collective-permute-start.3 = (f32[66,512]{1,0:T(8,128)S(1)}, f32[66,512]{1,0:T(8,128)S(1)}, u32[]{:S(2)}, u32[]{:S(2)}) collective-permute-start(f32[66,512]{1,0:T(8,128)S(1)} %constant_dynamic-slice_fusion.1), channel_id=1, source_target_pairs={{0,8},{1,9},{2,10},{3,11},{4,12},{5,13},{6,14},{7,15},{8,0},{9,1},... | collective-permute-start | bytes 405512 | tf_op jit(solution)/shard_map/ppermute | solution.py:184
  36.6 3.7 %collective-permute-done.3 = f32[66,512]{1,0:T(8,128)S(1)} collective-permute-done((f32[66,512]{1,0:T(8,128)S(1)}, f32[66,512]{1,0:T(8,128)S(1)}, u32[]{:S(2)}, u32[]{:S(2)}) %collective-permute-start.3) | collective-permute-done | bytes 135200 | tf_op jit(solution)/shard_map/ppermute | solution.py:184
  40.5 1.9 %collective-permute-start.4 = (f32[66,512]{1,0:T(8,128)S(1)}, f32[66,512]{1,0:T(8,128)S(1)}, u32[]{:S(2)}, u32[]{:S(2)}) collective-permute-start(f32[66,512]{1,0:T(8,128)S(1)} %pad_maximum_fusion.4), channel_id=1, source_target_pairs={{0,1},{1,0},{2,3},{3,2},{4,5},{5,4},{6,7},{7,6},{8,9},{9,8},{10,11... | collective-permute-start | bytes 405512 | tf_op jit(solution)/shard_map/ppermute | solution.py:188
  42.4 5.1 %collective-permute-done.4 = f32[66,512]{1,0:T(8,128)S(1)} collective-permute-done((f32[66,512]{1,0:T(8,128)S(1)}, f32[66,512]{1,0:T(8,128)S(1)}, u32[]{:S(2)}, u32[]{:S(2)}) %collective-permute-start.4) | collective-permute-done | bytes 135200 | tf_op jit(solution)/shard_map/ppermute | solution.py:188
  47.6 10.0 %collective-permute-start.5 = (f32[66,512]{1,0:T(8,128)S(1)}, f32[66,512]{1,0:T(8,128)S(1)}, u32[]{:S(2)}, u32[]{:S(2)}) collective-permute-start(f32[66,512]{1,0:T(8,128)S(1)} %pad_maximum_fusion.5), channel_id=1, source_target_pairs={{0,2},{1,3},{2,0},{3,1},{4,6},{5,7},{6,4},{7,5},{8,10},{9,11},{10,... | collective-permute-start | bytes 405512 | tf_op jit(solution)/shard_map/ppermute | solution.py:188
  57.6 4.0 %collective-permute-done.5 = f32[66,512]{1,0:T(8,128)S(1)} collective-permute-done((f32[66,512]{1,0:T(8,128)S(1)}, f32[66,512]{1,0:T(8,128)S(1)}, u32[]{:S(2)}, u32[]{:S(2)}) %collective-permute-start.5) | collective-permute-done | bytes 135200 | tf_op jit(solution)/shard_map/ppermute | solution.py:188
  61.7 3.3 %collective-permute-start.6 = (f32[66,512]{1,0:T(8,128)S(1)}, f32[66,512]{1,0:T(8,128)S(1)}, u32[]{:S(2)}, u32[]{:S(2)}) collective-permute-start(f32[66,512]{1,0:T(8,128)S(1)} %pad_maximum_fusion.6), channel_id=1, source_target_pairs={{0,6},{1,7},{2,4},{3,5},{4,2},{5,3},{6,0},{7,1},{8,14},{9,15},{10,... | collective-permute-start | bytes 405512 | tf_op jit(solution)/shard_map/ppermute | solution.py:188
  65.0 7.4 %collective-permute-done.6 = f32[66,512]{1,0:T(8,128)S(1)} collective-permute-done((f32[66,512]{1,0:T(8,128)S(1)}, f32[66,512]{1,0:T(8,128)S(1)}, u32[]{:S(2)}, u32[]{:S(2)}) %collective-permute-start.6) | collective-permute-done | bytes 135200 | tf_op jit(solution)/shard_map/ppermute | solution.py:188
  72.5 4.1 %collective-permute-start.7 = (bf16[64,512]{1,0:T(8,128)(2,1)S(1)}, bf16[64,512]{1,0:T(8,128)(2,1)S(1)}, u32[]{:S(2)}, u32[]{:S(2)}) collective-permute-start(bf16[64,512]{1,0:T(8,128)(2,1)S(1)} %fusion.13), channel_id=1, source_target_pairs={{0,8},{1,9},{2,10},{3,11},{4,12},{5,13},{6,14},{7,15},{8,0},{9,1},... | collective-permute-start | bytes 196616 | tf_op jit(solution)/shard_map/ppermute | solution.py:195
  84.9 5.6 %shard_map.115 = (bf16[2048,512]{1,0:T(8,128)(2,1)}, f32[2,512]{1,0:T(2,128)}) custom-call(s32[4]{0:T(128)} %get-tuple-element.17.refs_0_, bf16[512,128]{1,0:T(8,128)(2,1)} %get-tuple-element.35.refs_1_, bf16[2048,128]{1,0:T(8,128)(2,1)} %pad_maximum_fusion.refs_2_, f32[8,2048]{1,0:T(8,128)} %broadcast_in_dim.5.refs_3_), custom_call_target="tpu_custom_call" | custom-call | tf_op jit(solution)/shard_map/pallas_call | solution.py:118
  90.5 4.8 %shard_map.114 = (bf16[2048,512]{1,0:T(8,128)(2,1)}, f32[2,512]{1,0:T(2,128)}) custom-call(s32[4]{0:T(128)} %get-tuple-element.16.refs_0_, bf16[512,128]{1,0:T(8,128)(2,1)} %get-tuple-element.34.refs_1_, bf16[2048,128]{1,0:T(8,128)(2,1)} %pad_maximum_fusion.refs_2_, f32[8,2048]{1,0:T(8,128)} %broadcast_in_dim.5.refs_3_), custom_call_target="tpu_custom_call" | custom-call | tf_op jit(solution)/shard_map/pallas_call | solution.py:118
  95.3 2.2 %fusion = f32[64,512]{1,0:T(8,128)S(1)} fusion(bf16[2048,512]{1,0:T(8,128)(2,1)} %get-tuple-element.13, bf16[64,1024]{1,0:T(8,128)(2,1)S(1)} %get-tuple-element.33, bf16[64,1024]{1,0:T(8,128)(2,1)S(1)} %get-tuple-element.32), kind=kOutput, calls=%fused_computation.9 | convolution fusion | flops 134742016 | bytes 2490368 | tf_op jit(solution)/shard_map/dot_general | solution.py:295
  98.1 3.9 %collective-permute-start.10 = (f32[66,512]{1,0:T(8,128)S(1)}, f32[66,512]{1,0:T(8,128)S(1)}, u32[]{:S(2)}, u32[]{:S(2)}) collective-permute-start(f32[66,512]{1,0:T(8,128)S(1)} %constant_dynamic-slice_fusion), channel_id=1, source_target_pairs={{0,8},{1,9},{2,10},{3,11},{4,12},{5,13},{6,14},{7,15},{8,0},{9,1},... | collective-permute-start | bytes 405512 | tf_op jit(solution)/shard_map/ppermute | solution.py:184
  102.0 3.1 %collective-permute-done.10 = f32[66,512]{1,0:T(8,128)S(1)} collective-permute-done((f32[66,512]{1,0:T(8,128)S(1)}, f32[66,512]{1,0:T(8,128)S(1)}, u32[]{:S(2)}, u32[]{:S(2)}) %collective-permute-start.10) | collective-permute-done | bytes 135200 | tf_op jit(solution)/shard_map/ppermute | solution.py:184
  105.3 8.6 %collective-permute-start.11 = (f32[66,512]{1,0:T(8,128)S(1)}, f32[66,512]{1,0:T(8,128)S(1)}, u32[]{:S(2)}, u32[]{:S(2)}) collective-permute-start(f32[66,512]{1,0:T(8,128)S(1)} %pad_maximum_fusion.7), channel_id=1, source_target_pairs={{0,1},{1,0},{2,3},{3,2},{4,5},{5,4},{6,7},{7,6},{8,9},{9,8},{10,11... | collective-permute-start | bytes 405512 | tf_op jit(solution)/shard_map/ppermute | solution.py:188
  113.9 4.6 %collective-permute-done.11 = f32[66,512]{1,0:T(8,128)S(1)} collective-permute-done((f32[66,512]{1,0:T(8,128)S(1)}, f32[66,512]{1,0:T(8,128)S(1)}, u32[]{:S(2)}, u32[]{:S(2)}) %collective-permute-start.11) | collective-permute-done | bytes 135200 | tf_op jit(solution)/shard_map/ppermute | solution.py:188
  118.6 10.6 %collective-permute-start.12 = (f32[66,512]{1,0:T(8,128)S(1)}, f32[66,512]{1,0:T(8,128)S(1)}, u32[]{:S(2)}, u32[]{:S(2)}) collective-permute-start(f32[66,512]{1,0:T(8,128)S(1)} %pad_maximum_fusion.8), channel_id=1, source_target_pairs={{0,2},{1,3},{2,0},{3,1},{4,6},{5,7},{6,4},{7,5},{8,10},{9,11},{10,... | collective-permute-start | bytes 405512 | tf_op jit(solution)/shard_map/ppermute | solution.py:188
  129.2 5.6 %collective-permute-done.12 = f32[66,512]{1,0:T(8,128)S(1)} collective-permute-done((f32[66,512]{1,0:T(8,128)S(1)}, f32[66,512]{1,0:T(8,128)S(1)}, u32[]{:S(2)}, u32[]{:S(2)}) %collective-permute-start.12) | collective-permute-done | bytes 135200 | tf_op jit(solution)/shard_map/ppermute | solution.py:188
  134.9 1.9 %collective-permute-start.13 = (f32[66,512]{1,0:T(8,128)S(1)}, f32[66,512]{1,0:T(8,128)S(1)}, u32[]{:S(2)}, u32[]{:S(2)}) collective-permute-start(f32[66,512]{1,0:T(8,128)S(1)} %pad_maximum_fusion.9), channel_id=1, source_target_pairs={{0,6},{1,7},{2,4},{3,5},{4,2},{5,3},{6,0},{7,1},{8,14},{9,15},{10,... | collective-permute-start | bytes 405512 | tf_op jit(solution)/shard_map/ppermute | solution.py:188
  136.8 10.9 %collective-permute-done.13 = f32[66,512]{1,0:T(8,128)S(1)} collective-permute-done((f32[66,512]{1,0:T(8,128)S(1)}, f32[66,512]{1,0:T(8,128)S(1)}, u32[]{:S(2)}, u32[]{:S(2)}) %collective-permute-start.13) | collective-permute-done | bytes 135200 | tf_op jit(solution)/shard_map/ppermute | solution.py:188
  149.7 4.2 %collective-permute-done.14 = bf16[64,512]{1,0:T(8,128)(2,1)S(1)} collective-permute-done((bf16[64,512]{1,0:T(8,128)(2,1)S(1)}, bf16[64,512]{1,0:T(8,128)(2,1)S(1)}, u32[]{:S(2)}, u32[]{:S(2)}) %collective-permute-start.14) | collective-permute-done | bytes 65568 | tf_op jit(solution)/shard_map/ppermute | solution.py:195
  (87 shorter events, 19.8 us)
Async XLA Ops:
  0.6 14.5 %copy-start = (s32[64,64]{1,0:T(8,128)S(1)}, s32[64,64]{1,0:T(8,128)}, u32[]{:S(2)}) copy-start(s32[64,64]{1,0:T(8,128)} %param.16) | copy-start | bytes 49156
  0.6 26.4 %collective-permute-start.1 = (bf16[1024,128]{1,0:T(8,128)(2,1)}, bf16[1024,128]{1,0:T(8,128)(2,1)S(1)}, u32[]{:S(2)}, u32[]{:S(2)}) collective-permute-start(bf16[1024,128]{1,0:T(8,128)(2,1)} %refs_1_.1), channel_id=1, source_target_pairs={{392,0},{425,1},{458,2},{491,3},{268,4},{333,5},{6,6},{71,7},{128,... | collective-permute-start | bytes 786440 | tf_op jit(solution)/shard_map/ppermute | solution.py:244
  2.3 24.8 %collective-permute-start = (bf16[1024,128]{1,0:T(8,128)(2,1)}, bf16[1024,128]{1,0:T(8,128)(2,1)S(1)}, u32[]{:S(2)}, u32[]{:S(2)}) collective-permute-start(bf16[1024,128]{1,0:T(8,128)(2,1)} %refs_1_.1), channel_id=1, source_target_pairs={{408,0},{441,1},{474,2},{507,3},{284,4},{349,5},{22,6},{87,7},{144... | collective-permute-start | bytes 786440 | tf_op jit(solution)/shard_map/ppermute | solution.py:244
  4.2 23.8 %collective-permute-start.2 = (bf16[2048]{0:T(1024)(128)(2,1)}, bf16[2048]{0:T(1024)(128)(2,1)S(1)}, u32[]{:S(2)}, u32[]{:S(2)}) collective-permute-start(bf16[2048]{0:T(1024)(128)(2,1)} %param.14), channel_id=1, source_target_pairs={{12,0},{13,1},{14,2},{15,3},{8,4},{10,5},{0,6},{2,7},{4,8},{5,9},{... | collective-permute-start | bytes 12296 | tf_op jit(solution)/shard_map/ppermute | solution.py:260
  27.1 1.0 copy-start.2
  27.1 45.4 %copy-start.5 = (bf16[1024,64]{0,1:T(8,128)(2,1)S(1)}, bf16[1024,64]{0,1:T(8,128)(2,1)}, u32[]{:S(2)}) copy-start(bf16[1024,64]{0,1:T(8,128)(2,1)} %param.15) | copy-start | bytes 393220
  27.2 49.5 %copy-start.3 = (bf16[1024,128]{1,0:T(8,128)(2,1)S(1)}, bf16[1024,128]{1,0:T(8,128)(2,1)}, u32[]{:S(2)}) copy-start(bf16[1024,128]{1,0:T(8,128)(2,1)} %param.17) | copy-start | bytes 786436
  28.1 12.3 %collective-permute-start.3 = (f32[66,512]{1,0:T(8,128)S(1)}, f32[66,512]{1,0:T(8,128)S(1)}, u32[]{:S(2)}, u32[]{:S(2)}) collective-permute-start(f32[66,512]{1,0:T(8,128)S(1)} %constant_dynamic-slice_fusion.1), channel_id=1, source_target_pairs={{0,8},{1,9},{2,10},{3,11},{4,12},{5,13},{6,14},{7,15},{8,0},{9,1},... | collective-permute-start | bytes 405512 | tf_op jit(solution)/shard_map/ppermute | solution.py:184
  40.5 7.0 %collective-permute-start.4 = (f32[66,512]{1,0:T(8,128)S(1)}, f32[66,512]{1,0:T(8,128)S(1)}, u32[]{:S(2)}, u32[]{:S(2)}) collective-permute-start(f32[66,512]{1,0:T(8,128)S(1)} %pad_maximum_fusion.4), channel_id=1, source_target_pairs={{0,1},{1,0},{2,3},{3,2},{4,5},{5,4},{6,7},{7,6},{8,9},{9,8},{10,11... | collective-permute-start | bytes 405512 | tf_op jit(solution)/shard_map/ppermute | solution.py:188
  47.6 14.0 %collective-permute-start.5 = (f32[66,512]{1,0:T(8,128)S(1)}, f32[66,512]{1,0:T(8,128)S(1)}, u32[]{:S(2)}, u32[]{:S(2)}) collective-permute-start(f32[66,512]{1,0:T(8,128)S(1)} %pad_maximum_fusion.5), channel_id=1, source_target_pairs={{0,2},{1,3},{2,0},{3,1},{4,6},{5,7},{6,4},{7,5},{8,10},{9,11},{10,... | collective-permute-start | bytes 405512 | tf_op jit(solution)/shard_map/ppermute | solution.py:188
  61.7 10.7 %collective-permute-start.6 = (f32[66,512]{1,0:T(8,128)S(1)}, f32[66,512]{1,0:T(8,128)S(1)}, u32[]{:S(2)}, u32[]{:S(2)}) collective-permute-start(f32[66,512]{1,0:T(8,128)S(1)} %pad_maximum_fusion.6), channel_id=1, source_target_pairs={{0,6},{1,7},{2,4},{3,5},{4,2},{5,3},{6,0},{7,1},{8,14},{9,15},{10,... | collective-permute-start | bytes 405512 | tf_op jit(solution)/shard_map/ppermute | solution.py:188
  72.5 6.3 %collective-permute-start.7 = (bf16[64,512]{1,0:T(8,128)(2,1)S(1)}, bf16[64,512]{1,0:T(8,128)(2,1)S(1)}, u32[]{:S(2)}, u32[]{:S(2)}) collective-permute-start(bf16[64,512]{1,0:T(8,128)(2,1)S(1)} %fusion.13), channel_id=1, source_target_pairs={{0,8},{1,9},{2,10},{3,11},{4,12},{5,13},{6,14},{7,15},{8,0},{9,1},... | collective-permute-start | bytes 196616 | tf_op jit(solution)/shard_map/ppermute | solution.py:195
  78.9 18.6 %copy-start.4 = (bf16[64,1024]{1,0:T(8,128)(2,1)}, bf16[64,1024]{1,0:T(8,128)(2,1)S(1)}, u32[]{:S(2)}) copy-start(bf16[64,1024]{1,0:T(8,128)(2,1)S(1)} %maximum_select_fusion) | copy-start | bytes 393220
  78.9 16.3 %collective-permute-start.9 = (bf16[64,1024]{1,0:T(8,128)(2,1)S(1)}, bf16[64,1024]{1,0:T(8,128)(2,1)S(1)}, u32[]{:S(2)}, u32[]{:S(2)}) collective-permute-start(bf16[64,1024]{1,0:T(8,128)(2,1)S(1)} %maximum_select_fusion), channel_id=1, source_target_pairs={{392,0},{425,1},{458,2},{491,3},{268,4},{333,5},{6,6},{71,7},{128,... | collective-permute-start | bytes 393224 | tf_op jit(solution)/shard_map/ppermute | solution.py:244
  79.6 15.6 %collective-permute-start.8 = (bf16[64,1024]{1,0:T(8,128)(2,1)S(1)}, bf16[64,1024]{1,0:T(8,128)(2,1)S(1)}, u32[]{:S(2)}, u32[]{:S(2)}) collective-permute-start(bf16[64,1024]{1,0:T(8,128)(2,1)S(1)} %maximum_select_fusion), channel_id=1, source_target_pairs={{408,0},{441,1},{474,2},{507,3},{284,4},{349,5},{22,6},{87,7},{144... | collective-permute-start | bytes 393224 | tf_op jit(solution)/shard_map/ppermute | solution.py:244
  95.2 2.3 %copy-start.1 = (bf16[2048,512]{1,0:T(8,128)(2,1)S(1)}, bf16[2048,512]{1,0:T(8,128)(2,1)}, u32[]{:S(2)}) copy-start(bf16[2048,512]{1,0:T(8,128)(2,1)} %get-tuple-element.12) | copy-start | bytes 6291460
  95.3 2.7 %copy-start.7 = (f32[2,512]{1,0:T(2,128)S(1)}, f32[2,512]{1,0:T(2,128)}, u32[]{:S(2)}) copy-start(f32[2,512]{1,0:T(2,128)} %get-tuple-element.15) | copy-start | bytes 12292
  95.3 2.7 %copy-start.8 = (f32[2,512]{1,0:T(2,128)S(1)}, f32[2,512]{1,0:T(2,128)}, u32[]{:S(2)}) copy-start(f32[2,512]{1,0:T(2,128)} %get-tuple-element.14) | copy-start | bytes 12292
  98.0 49.8 %copy-start.6 = (bf16[1024,64]{0,1:T(8,128)(2,1)S(1)}, bf16[1024,64]{0,1:T(8,128)(2,1)}, u32[]{:S(2)}) copy-start(bf16[1024,64]{0,1:T(8,128)(2,1)} %param.18) | copy-start | bytes 393220
  98.1 7.0 %collective-permute-start.10 = (f32[66,512]{1,0:T(8,128)S(1)}, f32[66,512]{1,0:T(8,128)S(1)}, u32[]{:S(2)}, u32[]{:S(2)}) collective-permute-start(f32[66,512]{1,0:T(8,128)S(1)} %constant_dynamic-slice_fusion), channel_id=1, source_target_pairs={{0,8},{1,9},{2,10},{3,11},{4,12},{5,13},{6,14},{7,15},{8,0},{9,1},... | collective-permute-start | bytes 405512 | tf_op jit(solution)/shard_map/ppermute | solution.py:184
  105.3 13.3 %collective-permute-start.11 = (f32[66,512]{1,0:T(8,128)S(1)}, f32[66,512]{1,0:T(8,128)S(1)}, u32[]{:S(2)}, u32[]{:S(2)}) collective-permute-start(f32[66,512]{1,0:T(8,128)S(1)} %pad_maximum_fusion.7), channel_id=1, source_target_pairs={{0,1},{1,0},{2,3},{3,2},{4,5},{5,4},{6,7},{7,6},{8,9},{9,8},{10,11... | collective-permute-start | bytes 405512 | tf_op jit(solution)/shard_map/ppermute | solution.py:188
  118.6 16.2 %collective-permute-start.12 = (f32[66,512]{1,0:T(8,128)S(1)}, f32[66,512]{1,0:T(8,128)S(1)}, u32[]{:S(2)}, u32[]{:S(2)}) collective-permute-start(f32[66,512]{1,0:T(8,128)S(1)} %pad_maximum_fusion.8), channel_id=1, source_target_pairs={{0,2},{1,3},{2,0},{3,1},{4,6},{5,7},{6,4},{7,5},{8,10},{9,11},{10,... | collective-permute-start | bytes 405512 | tf_op jit(solution)/shard_map/ppermute | solution.py:188
  134.9 12.8 %collective-permute-start.13 = (f32[66,512]{1,0:T(8,128)S(1)}, f32[66,512]{1,0:T(8,128)S(1)}, u32[]{:S(2)}, u32[]{:S(2)}) collective-permute-start(f32[66,512]{1,0:T(8,128)S(1)} %pad_maximum_fusion.9), channel_id=1, source_target_pairs={{0,6},{1,7},{2,4},{3,5},{4,2},{5,3},{6,0},{7,1},{8,14},{9,15},{10,... | collective-permute-start | bytes 405512 | tf_op jit(solution)/shard_map/ppermute | solution.py:188
  147.8 6.2 %collective-permute-start.14 = (bf16[64,512]{1,0:T(8,128)(2,1)S(1)}, bf16[64,512]{1,0:T(8,128)(2,1)S(1)}, u32[]{:S(2)}, u32[]{:S(2)}) collective-permute-start(bf16[64,512]{1,0:T(8,128)(2,1)S(1)} %fusion.11), channel_id=1, source_target_pairs={{0,8},{1,9},{2,10},{3,11},{4,12},{5,13},{6,14},{7,15},{8,0},{9,1},... | collective-permute-start | bytes 196616 | tf_op jit(solution)/shard_map/ppermute | solution.py:195

commit v12 on v9

--- a/solution.py
+++ b/solution.py
@@ -13,7 +13,16 @@
 very_low = -1e30
 
 
-def partials_kernel(mask_ref, x_ref, y_ref, off_ref, v_ref, out_ref, m_ref, l_ref, acc_ref, *, scale, col_tiles):
+def row_tile_base(row_tiles):
+    return lax.axis_index("tgt") * row_tiles
+
+
+def offset_column(off_row):
+    wide = jnp.broadcast_to(off_row.astype(jnp.float32), (8, off_row.shape[1]))
+    return jnp.transpose(wide)[:, 0:1]
+
+
+def partials_kernel(mask_ref, x_ref, y_ref, off_ref, v_ref, out_ref, m_ref, l_ref, acc_ref, *, scale, row_tiles, col_tiles, col_base):
     i = pl.program_id(0)
     j = pl.program_id(1)
 
@@ -23,10 +32,10 @@
         l_ref[...] = jnp.zeros(l_ref.shape, jnp.float32)
         acc_ref[...] = jnp.zeros(acc_ref.shape, jnp.float32)
 
-    @pl.when(mask_ref[i * col_tiles + j] > 0)
+    @pl.when(mask_ref[row_tile_base(row_tiles) + i, col_base() + j] > 0)
     def _():
         s = lax.dot_general(y_ref[...], x_ref[...], (((1,), (1,)), ((), ())), preferred_element_type=jnp.float32)
-        s = s * scale - off_ref[...]
+        s = s * scale - offset_column(off_ref[...])
         m_old = m_ref[...]
         m_new = jnp.maximum(m_old, jnp.max(s, axis=0, keepdims=True))
         shrink = jnp.exp(m_old - m_new)
@@ -43,12 +52,14 @@
         out_ref[w + 1:w + 2, :] = m_ref[...]
 
 
-def date_partials_kernel(targets, sources, offsets, values_t, live):
+def date_partials_kernel(targets, sources, offsets, values_t, tile_mask, col_base):
     rows, factors = targets.shape
     cols = sources.shape[0]
     width = values_t.shape[0]
     row_tiles, col_tiles = rows // BLOCK, cols // BLOCK
-    kernel = lambda *refs: partials_kernel(*refs, scale=sharpness / factors**0.5, col_tiles=col_tiles)
+    kernel = lambda *refs: partials_kernel(
+        *refs, scale=sharpness / factors**0.5, row_tiles=row_tiles, col_tiles=col_tiles, col_base=col_base
+    )
     return pl.pallas_call(
         kernel,
         out_shape=jax.ShapeDtypeStruct((width + 2, rows), jnp.float32),
@@ -58,7 +69,7 @@
             in_specs=[
                 pl.BlockSpec((BLOCK, factors), lambda i, j, m: (i, 0)),
                 pl.BlockSpec((BLOCK, factors), lambda i, j, m: (j, 0)),
-                pl.BlockSpec((BLOCK, 1), lambda i, j, m: (j, 0)),
+                pl.BlockSpec((1, BLOCK), lambda i, j, m: (0, j)),
                 pl.BlockSpec((width, BLOCK), lambda i, j, m: (0, j)),
             ],
             out_specs=pl.BlockSpec((width + 2, BLOCK), lambda i, j, m: (0, i)),
@@ -69,29 +80,30 @@
             ],
         ),
         compiler_params=pltpu.CompilerParams(dimension_semantics=("arbitrary", "arbitrary")),
-    )(live.reshape(-1).astype(jnp.int32), targets, sources, offsets.astype(jnp.float32).reshape(cols, 1), values_t)
-
-
-def weights_kernel(mask_ref, x_ref, y_ref, off_ref, p_ref, stats_ref, *, scale, col_tiles):
-    i = pl.program_id(0)
+    )(tile_mask, targets, sources, offsets.reshape(1, cols), values_t)
+
+
+def weights_kernel(mask_ref, x_ref, y_ref, off_ref, p_ref, stats_ref, *, scale, row_tile, col_tiles, col_base):
+    row = row_tile_base(2) + row_tile
+    col0 = col_base()
 
     def scores(j):
         y = y_ref[j * BLOCK : (j + 1) * BLOCK, :]
         s = lax.dot_general(y, x_ref[...], (((1,), (1,)), ((), ())), preferred_element_type=jnp.float32)
-        return s * scale - off_ref[j * BLOCK : (j + 1) * BLOCK, :]
+        return s * scale - offset_column(off_ref[:, j * BLOCK : (j + 1) * BLOCK])
 
     stats_ref[...] = jnp.concatenate(
         [jnp.zeros((1, BLOCK), jnp.float32), jnp.full((1, BLOCK), very_low, jnp.float32)], 0
     )
     for j in range(col_tiles):
 
-        @pl.when(mask_ref[i * col_tiles + j] > 0)
+        @pl.when(mask_ref[row, col0 + j] > 0)
         def _():
             tile_peak = jnp.max(scores(j), axis=0, keepdims=True)
             stats_ref[1:2, :] = jnp.maximum(stats_ref[1:2, :], tile_peak)
 
     for j in range(col_tiles):
-        live = mask_ref[i * col_tiles + j] > 0
+        live = mask_ref[row, col0 + j] > 0
 
         @pl.when(live)
         def _():
@@ -104,11 +116,13 @@
             p_ref[j * BLOCK : (j + 1) * BLOCK, :] = jnp.zeros((BLOCK, BLOCK), jnp.bfloat16)
 
 
-def date_weights_kernel(targets, sources, offsets, live):
+def date_weights_kernel(targets, sources, offsets, tile_mask, row_tile, col_base):
     rows, factors = targets.shape
     cols = sources.shape[0]
-    row_tiles, col_tiles = rows // BLOCK, cols // BLOCK
-    kernel = lambda *refs: weights_kernel(*refs, scale=sharpness / factors**0.5, col_tiles=col_tiles)
+    col_tiles = cols // BLOCK
+    kernel = lambda *refs: weights_kernel(
+        *refs, scale=sharpness / factors**0.5, row_tile=row_tile, col_tiles=col_tiles, col_base=col_base
+    )
     return pl.pallas_call(
         kernel,
         out_shape=(
@@ -117,38 +131,32 @@
         ),
         grid_spec=pltpu.PrefetchScalarGridSpec(
             num_scalar_prefetch=1,
-            grid=(row_tiles,),
+            grid=(1,),
             in_specs=[
-                pl.BlockSpec((BLOCK, factors), lambda i, m: (i, 0)),
+                pl.BlockSpec((BLOCK, factors), lambda i, m: (0, 0)),
                 pl.BlockSpec((cols, factors), lambda i, m: (0, 0)),
-                pl.BlockSpec((cols, 1), lambda i, m: (0, 0)),
+                pl.BlockSpec((1, cols), lambda i, m: (0, 0)),
             ],
             out_specs=(
-                pl.BlockSpec((cols, BLOCK), lambda i, m: (0, i)),
-                pl.BlockSpec((2, BLOCK), lambda i, m: (0, i)),
+                pl.BlockSpec((cols, BLOCK), lambda i, m: (0, 0)),
+                pl.BlockSpec((2, BLOCK), lambda i, m: (0, 0)),
             ),
         ),
         compiler_params=pltpu.CompilerParams(dimension_semantics=("arbitrary",)),
-    )(live.reshape(-1).astype(jnp.int32), targets, sources, offsets.astype(jnp.float32).reshape(cols, 1))
-
-
-def local_live(targets, tile_mask, col_tile_ids):
-    row_tiles = targets.shape[0] // BLOCK
-    row_ids = lax.axis_index("tgt") * row_tiles + jnp.arange(row_tiles)
-    return tile_mask[row_ids][:, col_tile_ids]
-
-
-def date_partials(targets, sources, offsets, values_t, tile_mask, col_tile_ids):
-    live = local_live(targets, tile_mask, col_tile_ids)
-    return date_partials_kernel(targets, sources, offsets, values_t, live)
+    )(tile_mask, targets, sources, offsets.reshape(1, cols))
 
 
 HALVING_BITS = (3,)
-EXCHANGE_BITS = (0, 1, 2)
+FAR_PARTNER = (6, 7, 4, 5, 2, 3, 0, 1)
+EXCHANGES = (lambda y: y ^ 1, lambda y: y ^ 2, lambda y: FAR_PARTNER[y])
 
 
 def xor_perm(size, bit):
     return [(i, i ^ (1 << bit)) for i in range(size)]
+
+
+def exchange_perm(size, partner):
+    return [(i, (i // 8) * 8 + partner(i % 8)) for i in range(size)]
 
 
 def merge(mine, theirs):
@@ -173,8 +181,8 @@
         got = lax.ppermute(send, "src", xor_perm(src_size, bit))
         packed = merge(keep, got)
         exercise = lax.dynamic_slice_in_dim(exercise, mine_hi * half, half, 0)
-    for bit in EXCHANGE_BITS:
-        got = lax.ppermute(packed, "src", xor_perm(src_size, bit))
+    for partner in EXCHANGES:
+        got = lax.ppermute(packed, "src", exchange_perm(src_size, partner))
         packed = merge(packed, got)
     width = packed.shape[0] - 2
     continuation = packed[:width] / packed[width : width + 1]
@@ -262,21 +270,28 @@
     mask_early,
 ):
     src_tiles = states_late.shape[0] // BLOCK
-    col_ids = lax.axis_index("src") * src_tiles + jnp.arange(src_tiles)
-    pair = source_pair(lax.axis_index("tgt"), lax.axis_index("src"))
-    early_col_ids = pair * src_tiles + jnp.arange(src_tiles)
+
+    def mid_col_base():
+        return lax.axis_index("src") * src_tiles
+
+    def early_col_base():
+        return source_pair(lax.axis_index("tgt"), lax.axis_index("src")) * src_tiles
+
     mid_sources = regroup_order(regroup(states_mid))
     mid_offsets = regroup_offsets(offset_mid)
-    partials = date_partials(states_mid, states_late, offset_late, values_late.T, mask_mid, col_ids)
+    partials = date_partials_kernel(
+        states_mid, states_late, offset_late, values_late.T, mask_mid, mid_col_base
+    )
     partials, mid_sources, mid_offsets = lax.optimization_barrier(
         (partials, mid_sources, mid_offsets)
     )
-    early_live = local_live(states_early, mask_early, early_col_ids)
     early_parts = []
-    for row_tile in range(early_live.shape[0]):
+    for row_tile in range(states_early.shape[0] // BLOCK):
         rows = states_early[row_tile * BLOCK : (row_tile + 1) * BLOCK]
         early_parts.append(
-            date_weights_kernel(rows, mid_sources, mid_offsets, early_live[row_tile : row_tile + 1])
+            date_weights_kernel(
+                rows, mid_sources, mid_offsets, mask_early, row_tile, early_col_base
+            )
         )
     value_mid_t = finish(partials, exercise_mid)
     mid_values_t = regroup_order(regroup(value_mid_t), axis=1)

time: 160 us -> 154 us (0.963)
  the two profiles are of different devices: /device:TPU:1 before, /device:TPU:48 now
where the time goes in v12:
time: 154 us; the launch traced here: 153 us
  starting transfers between devices  73.8 us (48%)
  waiting for transfers between devices  52.4 us (34%)
  Pallas kernels  18.4 us (12%)
  local copies, waits for them, and re-layouts  2.68 us (2%)
  matrix products  2.67 us (2%)
  other arithmetic  2.31 us (2%)
    ppermute x6, waiting for transfers between devices, finish(): got = lax.ppermute(packed, 'src', exchange_perm(src_size, partner))  38.9 us
    ppermute x6, starting transfers between devices, finish(): got = lax.ppermute(packed, 'src', exchange_perm(src_size, partner))  38.5 us
    ppermute x2, starting transfers between devices, finish(): got = lax.ppermute(send, 'src', xor_perm(src_size, bit))  12.4 us
    pallas_call x2, Pallas kernels, date_weights_kernel(): pl.pallas_call(kernel, out_shape=(jax.ShapeDtypeStruct((cols, rows), jnp....  11.4 us
    ppermute x1, starting transfers between devices, regroup_offsets(): return lax.ppermute(offsets, ('tgt', 'src'), pairs)  10.8 us
    pallas_call x1, Pallas kernels, date_partials_kernel(): pl.pallas_call(kernel, out_shape=jax.ShapeDtypeStruct((width + 2, rows),...  7.04 us
    ppermute x2, waiting for transfers between devices, finish(): got = lax.ppermute(send, 'src', xor_perm(src_size, bit))  7 us
    ppermute x2, waiting for transfers between devices, finish(): got = lax.ppermute(value, 'src', xor_perm(src_size, bit))  6.46 us
  transfers between devices with their start and end apart: 15, of which 10 were waited for; matrix products, arithmetic and copies ran while one was open for 2% of the time, Pallas kernels for 12%

profile of v12, /device:TPU:48, one launch (start us, length us, event | category | flops | bytes accessed | tf_op | source)
XLA Modules:
  0.0 153.4 jit_solution(14656012232975003311)
XLA Ops:
  4.2 10.8 %collective-permute-start.2 = (bf16[2048]{0:T(1024)(128)(2,1)}, bf16[2048]{0:T(1024)(128)(2,1)S(1)}, u32[]{:S(2)}, u32[]{:S(2)}) collective-permute-start(bf16[2048]{0:T(1024)(128)(2,1)} %param.14), channel_id=1, source_target_pairs={{12,0},{13,1},{14,2},{15,3},{8,4},{10,5},{0,6},{2,7},{4,8},{5,9},{... | collective-permute-start | bytes 12296 | tf_op jit(solution)/shard_map/ppermute | solution.py:257
  16.3 7.0 %shard_map.113 = f32[66,1024]{1,0:T(8,128)} custom-call(s32[64,64]{1,0:T(8,128)} %refs_0_.3, bf16[1024,128]{1,0:T(8,128)(2,1)} %refs_1_.1, bf16[2048,128]{1,0:T(8,128)(2,1)} %refs_2_.1, bf16[1,2048]{1,0:T(2,128)(2,1)} %reshape.11.refs_3_, bf16[64,2048]{1,0:T(8,128)(2,1)} %bitcast.28), custom_call_target="tpu_custom_call" | custom-call | tf_op jit(solution)/shard_map/pallas_call | solution.py:63
  24.3 8.5 %collective-permute-start.3 = (f32[66,512]{1,0:T(8,128)S(1)}, f32[66,512]{1,0:T(8,128)S(1)}, u32[]{:S(2)}, u32[]{:S(2)}) collective-permute-start(f32[66,512]{1,0:T(8,128)S(1)} %constant_dynamic-slice_fusion.1), channel_id=1, source_target_pairs={{0,8},{1,9},{2,10},{3,11},{4,12},{5,13},{6,14},{7,15},{8,0},{9,1},... | collective-permute-start | bytes 405512 | tf_op jit(solution)/shard_map/ppermute | solution.py:181
  32.8 3.9 %collective-permute-done.3 = f32[66,512]{1,0:T(8,128)S(1)} collective-permute-done((f32[66,512]{1,0:T(8,128)S(1)}, f32[66,512]{1,0:T(8,128)S(1)}, u32[]{:S(2)}, u32[]{:S(2)}) %collective-permute-start.3) | collective-permute-done | bytes 135200 | tf_op jit(solution)/shard_map/ppermute | solution.py:181
  36.8 1.9 %collective-permute-start.4 = (f32[66,512]{1,0:T(8,128)S(1)}, f32[66,512]{1,0:T(8,128)S(1)}, u32[]{:S(2)}, u32[]{:S(2)}) collective-permute-start(f32[66,512]{1,0:T(8,128)S(1)} %pad_maximum_fusion.4), channel_id=1, source_target_pairs={{0,1},{1,0},{2,3},{3,2},{4,5},{5,4},{6,7},{7,6},{8,9},{9,8},{10,11... | collective-permute-start | bytes 405512 | tf_op jit(solution)/shard_map/ppermute | solution.py:185
  38.7 5.1 %collective-permute-done.4 = f32[66,512]{1,0:T(8,128)S(1)} collective-permute-done((f32[66,512]{1,0:T(8,128)S(1)}, f32[66,512]{1,0:T(8,128)S(1)}, u32[]{:S(2)}, u32[]{:S(2)}) %collective-permute-start.4) | collective-permute-done | bytes 135200 | tf_op jit(solution)/shard_map/ppermute | solution.py:185
  43.9 13.7 %collective-permute-start.5 = (f32[66,512]{1,0:T(8,128)S(1)}, f32[66,512]{1,0:T(8,128)S(1)}, u32[]{:S(2)}, u32[]{:S(2)}) collective-permute-start(f32[66,512]{1,0:T(8,128)S(1)} %pad_maximum_fusion.5), channel_id=1, source_target_pairs={{0,2},{1,3},{2,0},{3,1},{4,6},{5,7},{6,4},{7,5},{8,10},{9,11},{10,... | collective-permute-start | bytes 405512 | tf_op jit(solution)/shard_map/ppermute | solution.py:185
  57.6 4.0 %collective-permute-done.5 = f32[66,512]{1,0:T(8,128)S(1)} collective-permute-done((f32[66,512]{1,0:T(8,128)S(1)}, f32[66,512]{1,0:T(8,128)S(1)}, u32[]{:S(2)}, u32[]{:S(2)}) %collective-permute-start.5) | collective-permute-done | bytes 135200 | tf_op jit(solution)/shard_map/ppermute | solution.py:185
  61.7 1.9 %collective-permute-start.6 = (f32[66,512]{1,0:T(8,128)S(1)}, f32[66,512]{1,0:T(8,128)S(1)}, u32[]{:S(2)}, u32[]{:S(2)}) collective-permute-start(f32[66,512]{1,0:T(8,128)S(1)} %pad_maximum_fusion.6), channel_id=1, source_target_pairs={{0,6},{1,7},{2,4},{3,5},{4,2},{5,3},{6,0},{7,1},{8,14},{9,15},{10,... | collective-permute-start | bytes 405512 | tf_op jit(solution)/shard_map/ppermute | solution.py:185
  63.6 8.8 %collective-permute-done.6 = f32[66,512]{1,0:T(8,128)S(1)} collective-permute-done((f32[66,512]{1,0:T(8,128)S(1)}, f32[66,512]{1,0:T(8,128)S(1)}, u32[]{:S(2)}, u32[]{:S(2)}) %collective-permute-start.6) | collective-permute-done | bytes 135200 | tf_op jit(solution)/shard_map/ppermute | solution.py:185
  72.5 4.1 %collective-permute-start.7 = (bf16[64,512]{1,0:T(8,128)(2,1)S(1)}, bf16[64,512]{1,0:T(8,128)(2,1)S(1)}, u32[]{:S(2)}, u32[]{:S(2)}) collective-permute-start(bf16[64,512]{1,0:T(8,128)(2,1)S(1)} %fusion.13), channel_id=1, source_target_pairs={{0,8},{1,9},{2,10},{3,11},{4,12},{5,13},{6,14},{7,15},{8,0},{9,1},... | collective-permute-start | bytes 196616 | tf_op jit(solution)/shard_map/ppermute | solution.py:192
  76.6 2.2 %collective-permute-done.7 = bf16[64,512]{1,0:T(8,128)(2,1)S(1)} collective-permute-done((bf16[64,512]{1,0:T(8,128)(2,1)S(1)}, bf16[64,512]{1,0:T(8,128)(2,1)S(1)}, u32[]{:S(2)}, u32[]{:S(2)}) %collective-permute-start.7) | collective-permute-done | bytes 65568 | tf_op jit(solution)/shard_map/ppermute | solution.py:192
  79.6 1.9 %collective-permute-start.8 = (bf16[64,1024]{1,0:T(8,128)(2,1)S(1)}, bf16[64,1024]{1,0:T(8,128)(2,1)S(1)}, u32[]{:S(2)}, u32[]{:S(2)}) collective-permute-start(bf16[64,1024]{1,0:T(8,128)(2,1)S(1)} %maximum_select_fusion), channel_id=1, source_target_pairs={{408,0},{441,1},{474,2},{507,3},{284,4},{349,5},{22,6},{87,7},{144... | collective-permute-start | bytes 393224 | tf_op jit(solution)/shard_map/ppermute | solution.py:241
  82.8 6.1 %shard_map.115 = (bf16[2048,512]{1,0:T(8,128)(2,1)}, f32[2,512]{1,0:T(2,128)}) custom-call(s32[64,64]{1,0:T(8,128)} %refs_0_.5, bf16[512,128]{1,0:T(8,128)(2,1)} %get-tuple-element.33.refs_1_, bf16[2048,128]{1,0:T(8,128)(2,1)} %pad_maximum_fusion.refs_2_, bf16[1,2048]{1,0:T(2,128)(2,1)} %reshape.12.refs_3_), custom_call_target="tpu_custom_call" | custom-call | tf_op jit(solution)/shard_map/pallas_call | solution.py:126
  88.9 5.3 %shard_map.114 = (bf16[2048,512]{1,0:T(8,128)(2,1)}, f32[2,512]{1,0:T(2,128)}) custom-call(s32[64,64]{1,0:T(8,128)} %refs_0_.5, bf16[512,128]{1,0:T(8,128)(2,1)} %get-tuple-element.32.refs_1_, bf16[2048,128]{1,0:T(8,128)(2,1)} %pad_maximum_fusion.refs_2_, bf16[1,2048]{1,0:T(2,128)(2,1)} %reshape.12.refs_3_), custom_call_target="tpu_custom_call" | custom-call | tf_op jit(solution)/shard_map/pallas_call | solution.py:126
  94.2 2.2 %fusion = f32[64,512]{1,0:T(8,128)S(1)} fusion(bf16[2048,512]{1,0:T(8,128)(2,1)} %get-tuple-element.13, bf16[64,1024]{1,0:T(8,128)(2,1)S(1)} %get-tuple-element.31, bf16[64,1024]{1,0:T(8,128)(2,1)S(1)} %get-tuple-element.30), kind=kOutput, calls=%fused_computation.5 | convolution fusion | flops 134742016 | bytes 2490368 | tf_op jit(solution)/shard_map/dot_general | solution.py:299
  97.0 3.9 %collective-permute-start.10 = (f32[66,512]{1,0:T(8,128)S(1)}, f32[66,512]{1,0:T(8,128)S(1)}, u32[]{:S(2)}, u32[]{:S(2)}) collective-permute-start(f32[66,512]{1,0:T(8,128)S(1)} %constant_dynamic-slice_fusion), channel_id=1, source_target_pairs={{0,8},{1,9},{2,10},{3,11},{4,12},{5,13},{6,14},{7,15},{8,0},{9,1},... | collective-permute-start | bytes 405512 | tf_op jit(solution)/shard_map/ppermute | solution.py:181
  100.9 3.1 %collective-permute-done.10 = f32[66,512]{1,0:T(8,128)S(1)} collective-permute-done((f32[66,512]{1,0:T(8,128)S(1)}, f32[66,512]{1,0:T(8,128)S(1)}, u32[]{:S(2)}, u32[]{:S(2)}) %collective-permute-start.10) | collective-permute-done | bytes 135200 | tf_op jit(solution)/shard_map/ppermute | solution.py:181
  104.2 8.7 %collective-permute-start.11 = (f32[66,512]{1,0:T(8,128)S(1)}, f32[66,512]{1,0:T(8,128)S(1)}, u32[]{:S(2)}, u32[]{:S(2)}) collective-permute-start(f32[66,512]{1,0:T(8,128)S(1)} %pad_maximum_fusion.7), channel_id=1, source_target_pairs={{0,1},{1,0},{2,3},{3,2},{4,5},{5,4},{6,7},{7,6},{8,9},{9,8},{10,11... | collective-permute-start | bytes 405512 | tf_op jit(solution)/shard_map/ppermute | solution.py:185
  112.9 4.6 %collective-permute-done.11 = f32[66,512]{1,0:T(8,128)S(1)} collective-permute-done((f32[66,512]{1,0:T(8,128)S(1)}, f32[66,512]{1,0:T(8,128)S(1)}, u32[]{:S(2)}, u32[]{:S(2)}) %collective-permute-start.11) | collective-permute-done | bytes 135200 | tf_op jit(solution)/shard_map/ppermute | solution.py:185
  117.6 10.4 %collective-permute-start.12 = (f32[66,512]{1,0:T(8,128)S(1)}, f32[66,512]{1,0:T(8,128)S(1)}, u32[]{:S(2)}, u32[]{:S(2)}) collective-permute-start(f32[66,512]{1,0:T(8,128)S(1)} %pad_maximum_fusion.8), channel_id=1, source_target_pairs={{0,2},{1,3},{2,0},{3,1},{4,6},{5,7},{6,4},{7,5},{8,10},{9,11},{10,... | collective-permute-start | bytes 405512 | tf_op jit(solution)/shard_map/ppermute | solution.py:185
  128.0 5.6 %collective-permute-done.12 = f32[66,512]{1,0:T(8,128)S(1)} collective-permute-done((f32[66,512]{1,0:T(8,128)S(1)}, f32[66,512]{1,0:T(8,128)S(1)}, u32[]{:S(2)}, u32[]{:S(2)}) %collective-permute-start.12) | collective-permute-done | bytes 135200 | tf_op jit(solution)/shard_map/ppermute | solution.py:185
  135.6 10.9 %collective-permute-done.13 = f32[66,512]{1,0:T(8,128)S(1)} collective-permute-done((f32[66,512]{1,0:T(8,128)S(1)}, f32[66,512]{1,0:T(8,128)S(1)}, u32[]{:S(2)}, u32[]{:S(2)}) %collective-permute-start.13) | collective-permute-done | bytes 135200 | tf_op jit(solution)/shard_map/ppermute | solution.py:185
  148.5 4.2 %collective-permute-done.14 = bf16[64,512]{1,0:T(8,128)(2,1)S(1)} collective-permute-done((bf16[64,512]{1,0:T(8,128)(2,1)S(1)}, bf16[64,512]{1,0:T(8,128)(2,1)S(1)}, u32[]{:S(2)}, u32[]{:S(2)}) %collective-permute-start.14) | collective-permute-done | bytes 65568 | tf_op jit(solution)/shard_map/ppermute | solution.py:192
  (70 shorter events, 13.5 us)
Async XLA Ops:
  0.6 22.7 %collective-permute-start.1 = (bf16[1024,128]{1,0:T(8,128)(2,1)}, bf16[1024,128]{1,0:T(8,128)(2,1)S(1)}, u32[]{:S(2)}, u32[]{:S(2)}) collective-permute-start(bf16[1024,128]{1,0:T(8,128)(2,1)} %refs_1_.1), channel_id=1, source_target_pairs={{392,0},{425,1},{458,2},{491,3},{268,4},{333,5},{6,6},{71,7},{128,... | collective-permute-start | bytes 786440 | tf_op jit(solution)/shard_map/ppermute | solution.py:241
  2.2 21.1 %collective-permute-start = (bf16[1024,128]{1,0:T(8,128)(2,1)}, bf16[1024,128]{1,0:T(8,128)(2,1)S(1)}, u32[]{:S(2)}, u32[]{:S(2)}) collective-permute-start(bf16[1024,128]{1,0:T(8,128)(2,1)} %refs_1_.1), channel_id=1, source_target_pairs={{408,0},{441,1},{474,2},{507,3},{284,4},{349,5},{22,6},{87,7},{144... | collective-permute-start | bytes 786440 | tf_op jit(solution)/shard_map/ppermute | solution.py:241
  4.2 20.1 %collective-permute-start.2 = (bf16[2048]{0:T(1024)(128)(2,1)}, bf16[2048]{0:T(1024)(128)(2,1)S(1)}, u32[]{:S(2)}, u32[]{:S(2)}) collective-permute-start(bf16[2048]{0:T(1024)(128)(2,1)} %param.14), channel_id=1, source_target_pairs={{12,0},{13,1},{14,2},{15,3},{8,4},{10,5},{0,6},{2,7},{4,8},{5,9},{... | collective-permute-start | bytes 12296 | tf_op jit(solution)/shard_map/ppermute | solution.py:257
  23.3 1.0 copy-start.1
  23.4 49.1 %copy-start.4 = (bf16[1024,64]{0,1:T(8,128)(2,1)S(1)}, bf16[1024,64]{0,1:T(8,128)(2,1)}, u32[]{:S(2)}) copy-start(bf16[1024,64]{0,1:T(8,128)(2,1)} %param.15) | copy-start | bytes 393220
  23.4 58.1 %copy-start.2 = (bf16[1024,128]{1,0:T(8,128)(2,1)S(1)}, bf16[1024,128]{1,0:T(8,128)(2,1)}, u32[]{:S(2)}) copy-start(bf16[1024,128]{1,0:T(8,128)(2,1)} %param.17) | copy-start | bytes 786436
  24.3 12.4 %collective-permute-start.3 = (f32[66,512]{1,0:T(8,128)S(1)}, f32[66,512]{1,0:T(8,128)S(1)}, u32[]{:S(2)}, u32[]{:S(2)}) collective-permute-start(f32[66,512]{1,0:T(8,128)S(1)} %constant_dynamic-slice_fusion.1), channel_id=1, source_target_pairs={{0,8},{1,9},{2,10},{3,11},{4,12},{5,13},{6,14},{7,15},{8,0},{9,1},... | collective-permute-start | bytes 405512 | tf_op jit(solution)/shard_map/ppermute | solution.py:181
  36.8 7.0 %collective-permute-start.4 = (f32[66,512]{1,0:T(8,128)S(1)}, f32[66,512]{1,0:T(8,128)S(1)}, u32[]{:S(2)}, u32[]{:S(2)}) collective-permute-start(f32[66,512]{1,0:T(8,128)S(1)} %pad_maximum_fusion.4), channel_id=1, source_target_pairs={{0,1},{1,0},{2,3},{3,2},{4,5},{5,4},{6,7},{7,6},{8,9},{9,8},{10,11... | collective-permute-start | bytes 405512 | tf_op jit(solution)/shard_map/ppermute | solution.py:185
  43.9 17.7 %collective-permute-start.5 = (f32[66,512]{1,0:T(8,128)S(1)}, f32[66,512]{1,0:T(8,128)S(1)}, u32[]{:S(2)}, u32[]{:S(2)}) collective-permute-start(f32[66,512]{1,0:T(8,128)S(1)} %pad_maximum_fusion.5), channel_id=1, source_target_pairs={{0,2},{1,3},{2,0},{3,1},{4,6},{5,7},{6,4},{7,5},{8,10},{9,11},{10,... | collective-permute-start | bytes 405512 | tf_op jit(solution)/shard_map/ppermute | solution.py:185
  61.7 10.7 %collective-permute-start.6 = (f32[66,512]{1,0:T(8,128)S(1)}, f32[66,512]{1,0:T(8,128)S(1)}, u32[]{:S(2)}, u32[]{:S(2)}) collective-permute-start(f32[66,512]{1,0:T(8,128)S(1)} %pad_maximum_fusion.6), channel_id=1, source_target_pairs={{0,6},{1,7},{2,4},{3,5},{4,2},{5,3},{6,0},{7,1},{8,14},{9,15},{10,... | collective-permute-start | bytes 405512 | tf_op jit(solution)/shard_map/ppermute | solution.py:185
  72.5 6.3 %collective-permute-start.7 = (bf16[64,512]{1,0:T(8,128)(2,1)S(1)}, bf16[64,512]{1,0:T(8,128)(2,1)S(1)}, u32[]{:S(2)}, u32[]{:S(2)}) collective-permute-start(bf16[64,512]{1,0:T(8,128)(2,1)S(1)} %fusion.13), channel_id=1, source_target_pairs={{0,8},{1,9},{2,10},{3,11},{4,12},{5,13},{6,14},{7,15},{8,0},{9,1},... | collective-permute-start | bytes 196616 | tf_op jit(solution)/shard_map/ppermute | solution.py:192
  78.9 17.6 %copy-start.3 = (bf16[64,1024]{1,0:T(8,128)(2,1)}, bf16[64,1024]{1,0:T(8,128)(2,1)S(1)}, u32[]{:S(2)}) copy-start(bf16[64,1024]{1,0:T(8,128)(2,1)S(1)} %maximum_select_fusion) | copy-start | bytes 393220
  78.9 15.3 %collective-permute-start.9 = (bf16[64,1024]{1,0:T(8,128)(2,1)S(1)}, bf16[64,1024]{1,0:T(8,128)(2,1)S(1)}, u32[]{:S(2)}, u32[]{:S(2)}) collective-permute-start(bf16[64,1024]{1,0:T(8,128)(2,1)S(1)} %maximum_select_fusion), channel_id=1, source_target_pairs={{392,0},{425,1},{458,2},{491,3},{268,4},{333,5},{6,6},{71,7},{128,... | collective-permute-start | bytes 393224 | tf_op jit(solution)/shard_map/ppermute | solution.py:241
  79.6 14.6 %collective-permute-start.8 = (bf16[64,1024]{1,0:T(8,128)(2,1)S(1)}, bf16[64,1024]{1,0:T(8,128)(2,1)S(1)}, u32[]{:S(2)}, u32[]{:S(2)}) collective-permute-start(bf16[64,1024]{1,0:T(8,128)(2,1)S(1)} %maximum_select_fusion), channel_id=1, source_target_pairs={{408,0},{441,1},{474,2},{507,3},{284,4},{349,5},{22,6},{87,7},{144... | collective-permute-start | bytes 393224 | tf_op jit(solution)/shard_map/ppermute | solution.py:241
  94.2 2.3 %copy-start = (bf16[2048,512]{1,0:T(8,128)(2,1)S(1)}, bf16[2048,512]{1,0:T(8,128)(2,1)}, u32[]{:S(2)}) copy-start(bf16[2048,512]{1,0:T(8,128)(2,1)} %get-tuple-element.12) | copy-start | bytes 6291460
  94.2 2.7 %copy-start.6 = (f32[2,512]{1,0:T(2,128)S(1)}, f32[2,512]{1,0:T(2,128)}, u32[]{:S(2)}) copy-start(f32[2,512]{1,0:T(2,128)} %get-tuple-element.15) | copy-start | bytes 12292
  94.2 2.7 %copy-start.7 = (f32[2,512]{1,0:T(2,128)S(1)}, f32[2,512]{1,0:T(2,128)}, u32[]{:S(2)}) copy-start(f32[2,512]{1,0:T(2,128)} %get-tuple-element.14) | copy-start | bytes 12292
  96.9 49.6 %copy-start.5 = (bf16[1024,64]{0,1:T(8,128)(2,1)S(1)}, bf16[1024,64]{0,1:T(8,128)(2,1)}, u32[]{:S(2)}) copy-start(bf16[1024,64]{0,1:T(8,128)(2,1)} %param.18) | copy-start | bytes 393220
  97.0 7.0 %collective-permute-start.10 = (f32[66,512]{1,0:T(8,128)S(1)}, f32[66,512]{1,0:T(8,128)S(1)}, u32[]{:S(2)}, u32[]{:S(2)}) collective-permute-start(f32[66,512]{1,0:T(8,128)S(1)} %constant_dynamic-slice_fusion), channel_id=1, source_target_pairs={{0,8},{1,9},{2,10},{3,11},{4,12},{5,13},{6,14},{7,15},{8,0},{9,1},... | collective-permute-start | bytes 405512 | tf_op jit(solution)/shard_map/ppermute | solution.py:181
  104.2 13.3 %collective-permute-start.11 = (f32[66,512]{1,0:T(8,128)S(1)}, f32[66,512]{1,0:T(8,128)S(1)}, u32[]{:S(2)}, u32[]{:S(2)}) collective-permute-start(f32[66,512]{1,0:T(8,128)S(1)} %pad_maximum_fusion.7), channel_id=1, source_target_pairs={{0,1},{1,0},{2,3},{3,2},{4,5},{5,4},{6,7},{7,6},{8,9},{9,8},{10,11... | collective-permute-start | bytes 405512 | tf_op jit(solution)/shard_map/ppermute | solution.py:185
  117.6 15.9 %collective-permute-start.12 = (f32[66,512]{1,0:T(8,128)S(1)}, f32[66,512]{1,0:T(8,128)S(1)}, u32[]{:S(2)}, u32[]{:S(2)}) collective-permute-start(f32[66,512]{1,0:T(8,128)S(1)} %pad_maximum_fusion.8), channel_id=1, source_target_pairs={{0,2},{1,3},{2,0},{3,1},{4,6},{5,7},{6,4},{7,5},{8,10},{9,11},{10,... | collective-permute-start | bytes 405512 | tf_op jit(solution)/shard_map/ppermute | solution.py:185
  133.7 12.8 %collective-permute-start.13 = (f32[66,512]{1,0:T(8,128)S(1)}, f32[66,512]{1,0:T(8,128)S(1)}, u32[]{:S(2)}, u32[]{:S(2)}) collective-permute-start(f32[66,512]{1,0:T(8,128)S(1)} %pad_maximum_fusion.9), channel_id=1, source_target_pairs={{0,6},{1,7},{2,4},{3,5},{4,2},{5,3},{6,0},{7,1},{8,14},{9,15},{10,... | collective-permute-start | bytes 405512 | tf_op jit(solution)/shard_map/ppermute | solution.py:185
  146.6 6.2 %collective-permute-start.14 = (bf16[64,512]{1,0:T(8,128)(2,1)S(1)}, bf16[64,512]{1,0:T(8,128)(2,1)S(1)}, u32[]{:S(2)}, u32[]{:S(2)}) collective-permute-start(bf16[64,512]{1,0:T(8,128)(2,1)S(1)} %fusion.11), channel_id=1, source_target_pairs={{0,8},{1,9},{2,10},{3,11},{4,12},{5,13},{6,14},{7,15},{8,0},{9,1},... | collective-permute-start | bytes 196616 | tf_op jit(solution)/shard_map/ppermute | solution.py:192

commit v13 on v12

--- a/solution.py
+++ b/solution.py
@@ -22,34 +22,29 @@
     return jnp.transpose(wide)[:, 0:1]
 
 
-def partials_kernel(mask_ref, x_ref, y_ref, off_ref, v_ref, out_ref, m_ref, l_ref, acc_ref, *, scale, row_tiles, col_tiles, col_base):
+def partials_kernel(mask_ref, x_ref, y_ref, off_ref, v_ref, out_ref, *, scale, row_tiles, col_tiles, col_base):
     i = pl.program_id(0)
-    j = pl.program_id(1)
-
-    @pl.when(j == 0)
-    def _():
-        m_ref[...] = jnp.full(m_ref.shape, very_low, jnp.float32)
-        l_ref[...] = jnp.zeros(l_ref.shape, jnp.float32)
-        acc_ref[...] = jnp.zeros(acc_ref.shape, jnp.float32)
-
-    @pl.when(mask_ref[row_tile_base(row_tiles) + i, col_base() + j] > 0)
-    def _():
-        s = lax.dot_general(y_ref[...], x_ref[...], (((1,), (1,)), ((), ())), preferred_element_type=jnp.float32)
-        s = s * scale - offset_column(off_ref[...])
-        m_old = m_ref[...]
-        m_new = jnp.maximum(m_old, jnp.max(s, axis=0, keepdims=True))
-        shrink = jnp.exp(m_old - m_new)
-        p = jnp.exp(s - m_new)
-        l_ref[...] = l_ref[...] * shrink + jnp.sum(p, axis=0, keepdims=True)
-        acc_ref[...] = acc_ref[...] * shrink + jnp.dot(v_ref[...], p.astype(jnp.bfloat16), preferred_element_type=jnp.float32)
-        m_ref[...] = m_new
-
-    @pl.when(j == col_tiles - 1)
-    def _():
-        w = acc_ref.shape[0]
-        out_ref[0:w, :] = acc_ref[...]
-        out_ref[w:w + 1, :] = l_ref[...]
-        out_ref[w + 1:w + 2, :] = m_ref[...]
+    row = row_tile_base(row_tiles) + i
+    col0 = col_base()
+    width = v_ref.shape[0]
+    out_ref[0 : width + 1, :] = jnp.zeros((width + 1, BLOCK), jnp.float32)
+    out_ref[width + 1 : width + 2, :] = jnp.full((1, BLOCK), very_low, jnp.float32)
+    for j in range(col_tiles):
+
+        @pl.when(mask_ref[row, col0 + j] > 0)
+        def _():
+            y = y_ref[j * BLOCK : (j + 1) * BLOCK, :]
+            s = lax.dot_general(y, x_ref[...], (((1,), (1,)), ((), ())), preferred_element_type=jnp.float32)
+            s = s * scale - offset_column(off_ref[:, j * BLOCK : (j + 1) * BLOCK])
+            m_old = out_ref[width + 1 : width + 2, :]
+            m_new = jnp.maximum(m_old, jnp.max(s, axis=0, keepdims=True))
+            shrink = jnp.exp(m_old - m_new)
+            p = jnp.exp(s - m_new)
+            out_ref[width : width + 1, :] = out_ref[width : width + 1, :] * shrink + jnp.sum(p, axis=0, keepdims=True)
+            out_ref[0:width, :] = out_ref[0:width, :] * shrink + jnp.dot(
+                v_ref[:, j * BLOCK : (j + 1) * BLOCK], p.astype(jnp.bfloat16), preferred_element_type=jnp.float32
+            )
+            out_ref[width + 1 : width + 2, :] = m_new
 
 
 def date_partials_kernel(targets, sources, offsets, values_t, tile_mask, col_base):
@@ -65,21 +60,16 @@
         out_shape=jax.ShapeDtypeStruct((width + 2, rows), jnp.float32),
         grid_spec=pltpu.PrefetchScalarGridSpec(
             num_scalar_prefetch=1,
-            grid=(row_tiles, col_tiles),
+            grid=(row_tiles,),
             in_specs=[
-                pl.BlockSpec((BLOCK, factors), lambda i, j, m: (i, 0)),
-                pl.BlockSpec((BLOCK, factors), lambda i, j, m: (j, 0)),
-                pl.BlockSpec((1, BLOCK), lambda i, j, m: (0, j)),
-                pl.BlockSpec((width, BLOCK), lambda i, j, m: (0, j)),
+                pl.BlockSpec((BLOCK, factors), lambda i, m: (i, 0)),
+                pl.BlockSpec((cols, factors), lambda i, m: (0, 0)),
+                pl.BlockSpec((1, cols), lambda i, m: (0, 0)),
+                pl.BlockSpec((width, cols), lambda i, m: (0, 0)),
             ],
-            out_specs=pl.BlockSpec((width + 2, BLOCK), lambda i, j, m: (0, i)),
-            scratch_shapes=[
-                pltpu.VMEM((1, BLOCK), jnp.float32),
-                pltpu.VMEM((1, BLOCK), jnp.float32),
-                pltpu.VMEM((width, BLOCK), jnp.float32),
-            ],
+            out_specs=pl.BlockSpec((width + 2, BLOCK), lambda i, m: (0, i)),
         ),
-        compiler_params=pltpu.CompilerParams(dimension_semantics=("arbitrary", "arbitrary")),
+        compiler_params=pltpu.CompilerParams(dimension_semantics=("arbitrary",)),
     )(tile_mask, targets, sources, offsets.reshape(1, cols), values_t)
 
 

time: 154 us -> 154 us (level)
  starting transfers between devices: 73.8 us -> 76.5 us
  Pallas kernels: 18.4 us -> 15.9 us
    ppermute x6, starting transfers between devices: 38.5 us -> 41.4 us  [finish(): got = lax.ppermute(packed, 'src', exchange_perm(src_size, partner))]
    pallas_call x1, Pallas kernels: 7.04 us -> 4.55 us  [date_partials_kernel(): pl.pallas_call(kernel, out_shape=jax.ShapeDtypeStruct((width + 2, rows),...]
  transfers between devices with their start and end apart: 15 -> 15, of which waited for: 10 -> 10; matrix products, arithmetic and copies ran while one was open for 2% -> 2% of each run, Pallas kernels for 12% -> 10%
where the time goes in v13:
time: 154 us; the launch traced here: 153 us
  starting transfers between devices  76.5 us (50%)
  waiting for transfers between devices  52.2 us (34%)
  Pallas kernels  15.9 us (10%)
  local copies, waits for them, and re-layouts  2.68 us (2%)
  matrix products  2.67 us (2%)
  other arithmetic  2.31 us (2%)
    ppermute x6, starting transfers between devices, finish(): got = lax.ppermute(packed, 'src', exchange_perm(src_size, partner))  41.4 us
    ppermute x6, waiting for transfers between devices, finish(): got = lax.ppermute(packed, 'src', exchange_perm(src_size, partner))  38.8 us
    ppermute x2, starting transfers between devices, finish(): got = lax.ppermute(send, 'src', xor_perm(src_size, bit))  12.1 us
    pallas_call x2, Pallas kernels, date_weights_kernel(): pl.pallas_call(kernel, out_shape=(jax.ShapeDtypeStruct((cols, rows), jnp....  11.4 us
    ppermute x1, starting transfers between devices, regroup_offsets(): return lax.ppermute(offsets, ('tgt', 'src'), pairs)  10.8 us
    ppermute x2, waiting for transfers between devices, finish(): got = lax.ppermute(send, 'src', xor_perm(src_size, bit))  6.95 us
    ppermute x2, waiting for transfers between devices, finish(): got = lax.ppermute(value, 'src', xor_perm(src_size, bit))  6.46 us
    ppermute x4, starting transfers between devices, regroup(): return [lax.ppermute(block_rows, ('tgt', 'src'), p) for p in perms]  6.11 us
  transfers between devices with their start and end apart: 15, of which 10 were waited for; matrix products, arithmetic and copies ran while one was open for 2% of the time, Pallas kernels for 10%

profile of v13, /device:TPU:48, one launch (start us, length us, event | category | flops | bytes accessed | tf_op | source)
XLA Modules:
  0.0 153.4 jit_solution(92217209782119923)
XLA Ops:
  4.2 10.8 %collective-permute-start.2 = (bf16[2048]{0:T(1024)(128)(2,1)}, bf16[2048]{0:T(1024)(128)(2,1)S(1)}, u32[]{:S(2)}, u32[]{:S(2)}) collective-permute-start(bf16[2048]{0:T(1024)(128)(2,1)} %param.14), channel_id=1, source_target_pairs={{12,0},{13,1},{14,2},{15,3},{8,4},{10,5},{0,6},{2,7},{4,8},{5,9},{... | collective-permute-start | bytes 12296 | tf_op jit(solution)/shard_map/ppermute | solution.py:247
  16.3 4.6 %shard_map.113 = f32[66,1024]{1,0:T(8,128)} custom-call(s32[64,64]{1,0:T(8,128)} %refs_0_.3, bf16[1024,128]{1,0:T(8,128)(2,1)} %refs_1_.1, bf16[2048,128]{1,0:T(8,128)(2,1)} %refs_2_.1, bf16[1,2048]{1,0:T(2,128)(2,1)} %reshape.11.refs_3_, bf16[64,2048]{1,0:T(8,128)(2,1)} %bitcast.28), custom_call_target="tpu_custom_call" | custom-call | tf_op jit(solution)/shard_map/pallas_call | solution.py:58
  21.8 8.3 %collective-permute-start.3 = (f32[66,512]{1,0:T(8,128)S(1)}, f32[66,512]{1,0:T(8,128)S(1)}, u32[]{:S(2)}, u32[]{:S(2)}) collective-permute-start(f32[66,512]{1,0:T(8,128)S(1)} %constant_dynamic-slice_fusion.1), channel_id=1, source_target_pairs={{0,8},{1,9},{2,10},{3,11},{4,12},{5,13},{6,14},{7,15},{8,0},{9,1},... | collective-permute-start | bytes 405512 | tf_op jit(solution)/shard_map/ppermute | solution.py:171
  30.0 3.8 %collective-permute-done.3 = f32[66,512]{1,0:T(8,128)S(1)} collective-permute-done((f32[66,512]{1,0:T(8,128)S(1)}, f32[66,512]{1,0:T(8,128)S(1)}, u32[]{:S(2)}, u32[]{:S(2)}) %collective-permute-start.3) | collective-permute-done | bytes 135200 | tf_op jit(solution)/shard_map/ppermute | solution.py:171
  34.0 2.3 %collective-permute-start.4 = (f32[66,512]{1,0:T(8,128)S(1)}, f32[66,512]{1,0:T(8,128)S(1)}, u32[]{:S(2)}, u32[]{:S(2)}) collective-permute-start(f32[66,512]{1,0:T(8,128)S(1)} %pad_maximum_fusion.4), channel_id=1, source_target_pairs={{0,1},{1,0},{2,3},{3,2},{4,5},{5,4},{6,7},{7,6},{8,9},{9,8},{10,11... | collective-permute-start | bytes 405512 | tf_op jit(solution)/shard_map/ppermute | solution.py:175
  36.4 5.0 %collective-permute-done.4 = f32[66,512]{1,0:T(8,128)S(1)} collective-permute-done((f32[66,512]{1,0:T(8,128)S(1)}, f32[66,512]{1,0:T(8,128)S(1)}, u32[]{:S(2)}, u32[]{:S(2)}) %collective-permute-start.4) | collective-permute-done | bytes 135200 | tf_op jit(solution)/shard_map/ppermute | solution.py:175
  41.4 16.2 %collective-permute-start.5 = (f32[66,512]{1,0:T(8,128)S(1)}, f32[66,512]{1,0:T(8,128)S(1)}, u32[]{:S(2)}, u32[]{:S(2)}) collective-permute-start(f32[66,512]{1,0:T(8,128)S(1)} %pad_maximum_fusion.5), channel_id=1, source_target_pairs={{0,2},{1,3},{2,0},{3,1},{4,6},{5,7},{6,4},{7,5},{8,10},{9,11},{10,... | collective-permute-start | bytes 405512 | tf_op jit(solution)/shard_map/ppermute | solution.py:175
  57.6 4.0 %collective-permute-done.5 = f32[66,512]{1,0:T(8,128)S(1)} collective-permute-done((f32[66,512]{1,0:T(8,128)S(1)}, f32[66,512]{1,0:T(8,128)S(1)}, u32[]{:S(2)}, u32[]{:S(2)}) %collective-permute-start.5) | collective-permute-done | bytes 135200 | tf_op jit(solution)/shard_map/ppermute | solution.py:175
  61.7 1.9 %collective-permute-start.6 = (f32[66,512]{1,0:T(8,128)S(1)}, f32[66,512]{1,0:T(8,128)S(1)}, u32[]{:S(2)}, u32[]{:S(2)}) collective-permute-start(f32[66,512]{1,0:T(8,128)S(1)} %pad_maximum_fusion.6), channel_id=1, source_target_pairs={{0,6},{1,7},{2,4},{3,5},{4,2},{5,3},{6,0},{7,1},{8,14},{9,15},{10,... | collective-permute-start | bytes 405512 | tf_op jit(solution)/shard_map/ppermute | solution.py:175
  63.6 8.8 %collective-permute-done.6 = f32[66,512]{1,0:T(8,128)S(1)} collective-permute-done((f32[66,512]{1,0:T(8,128)S(1)}, f32[66,512]{1,0:T(8,128)S(1)}, u32[]{:S(2)}, u32[]{:S(2)}) %collective-permute-start.6) | collective-permute-done | bytes 135200 | tf_op jit(solution)/shard_map/ppermute | solution.py:175
  72.5 4.1 %collective-permute-start.7 = (bf16[64,512]{1,0:T(8,128)(2,1)S(1)}, bf16[64,512]{1,0:T(8,128)(2,1)S(1)}, u32[]{:S(2)}, u32[]{:S(2)}) collective-permute-start(bf16[64,512]{1,0:T(8,128)(2,1)S(1)} %fusion.13), channel_id=1, source_target_pairs={{0,8},{1,9},{2,10},{3,11},{4,12},{5,13},{6,14},{7,15},{8,0},{9,1},... | collective-permute-start | bytes 196616 | tf_op jit(solution)/shard_map/ppermute | solution.py:182
  76.6 2.2 %collective-permute-done.7 = bf16[64,512]{1,0:T(8,128)(2,1)S(1)} collective-permute-done((bf16[64,512]{1,0:T(8,128)(2,1)S(1)}, bf16[64,512]{1,0:T(8,128)(2,1)S(1)}, u32[]{:S(2)}, u32[]{:S(2)}) %collective-permute-start.7) | collective-permute-done | bytes 65568 | tf_op jit(solution)/shard_map/ppermute | solution.py:182
  79.6 1.9 %collective-permute-start.8 = (bf16[64,1024]{1,0:T(8,128)(2,1)S(1)}, bf16[64,1024]{1,0:T(8,128)(2,1)S(1)}, u32[]{:S(2)}, u32[]{:S(2)}) collective-permute-start(bf16[64,1024]{1,0:T(8,128)(2,1)S(1)} %maximum_select_fusion), channel_id=1, source_target_pairs={{408,0},{441,1},{474,2},{507,3},{284,4},{349,5},{22,6},{87,7},{144... | collective-permute-start | bytes 393224 | tf_op jit(solution)/shard_map/ppermute | solution.py:231
  82.8 6.1 %shard_map.115 = (bf16[2048,512]{1,0:T(8,128)(2,1)}, f32[2,512]{1,0:T(2,128)}) custom-call(s32[64,64]{1,0:T(8,128)} %refs_0_.5, bf16[512,128]{1,0:T(8,128)(2,1)} %get-tuple-element.33.refs_1_, bf16[2048,128]{1,0:T(8,128)(2,1)} %pad_maximum_fusion.refs_2_, bf16[1,2048]{1,0:T(2,128)(2,1)} %reshape.12.refs_3_), custom_call_target="tpu_custom_call" | custom-call | tf_op jit(solution)/shard_map/pallas_call | solution.py:116
  88.9 5.3 %shard_map.114 = (bf16[2048,512]{1,0:T(8,128)(2,1)}, f32[2,512]{1,0:T(2,128)}) custom-call(s32[64,64]{1,0:T(8,128)} %refs_0_.5, bf16[512,128]{1,0:T(8,128)(2,1)} %get-tuple-element.32.refs_1_, bf16[2048,128]{1,0:T(8,128)(2,1)} %pad_maximum_fusion.refs_2_, bf16[1,2048]{1,0:T(2,128)(2,1)} %reshape.12.refs_3_), custom_call_target="tpu_custom_call" | custom-call | tf_op jit(solution)/shard_map/pallas_call | solution.py:116
  94.2 2.2 %fusion = f32[64,512]{1,0:T(8,128)S(1)} fusion(bf16[2048,512]{1,0:T(8,128)(2,1)} %get-tuple-element.13, bf16[64,1024]{1,0:T(8,128)(2,1)S(1)} %get-tuple-element.31, bf16[64,1024]{1,0:T(8,128)(2,1)S(1)} %get-tuple-element.30), kind=kOutput, calls=%fused_computation.5 | convolution fusion | flops 134742016 | bytes 2490368 | tf_op jit(solution)/shard_map/dot_general | solution.py:289
  97.0 3.9 %collective-permute-start.10 = (f32[66,512]{1,0:T(8,128)S(1)}, f32[66,512]{1,0:T(8,128)S(1)}, u32[]{:S(2)}, u32[]{:S(2)}) collective-permute-start(f32[66,512]{1,0:T(8,128)S(1)} %constant_dynamic-slice_fusion), channel_id=1, source_target_pairs={{0,8},{1,9},{2,10},{3,11},{4,12},{5,13},{6,14},{7,15},{8,0},{9,1},... | collective-permute-start | bytes 405512 | tf_op jit(solution)/shard_map/ppermute | solution.py:171
  100.9 3.1 %collective-permute-done.10 = f32[66,512]{1,0:T(8,128)S(1)} collective-permute-done((f32[66,512]{1,0:T(8,128)S(1)}, f32[66,512]{1,0:T(8,128)S(1)}, u32[]{:S(2)}, u32[]{:S(2)}) %collective-permute-start.10) | collective-permute-done | bytes 135200 | tf_op jit(solution)/shard_map/ppermute | solution.py:171
  104.2 8.7 %collective-permute-start.11 = (f32[66,512]{1,0:T(8,128)S(1)}, f32[66,512]{1,0:T(8,128)S(1)}, u32[]{:S(2)}, u32[]{:S(2)}) collective-permute-start(f32[66,512]{1,0:T(8,128)S(1)} %pad_maximum_fusion.7), channel_id=1, source_target_pairs={{0,1},{1,0},{2,3},{3,2},{4,5},{5,4},{6,7},{7,6},{8,9},{9,8},{10,11... | collective-permute-start | bytes 405512 | tf_op jit(solution)/shard_map/ppermute | solution.py:175
  112.9 4.6 %collective-permute-done.11 = f32[66,512]{1,0:T(8,128)S(1)} collective-permute-done((f32[66,512]{1,0:T(8,128)S(1)}, f32[66,512]{1,0:T(8,128)S(1)}, u32[]{:S(2)}, u32[]{:S(2)}) %collective-permute-start.11) | collective-permute-done | bytes 135200 | tf_op jit(solution)/shard_map/ppermute | solution.py:175
  117.6 10.4 %collective-permute-start.12 = (f32[66,512]{1,0:T(8,128)S(1)}, f32[66,512]{1,0:T(8,128)S(1)}, u32[]{:S(2)}, u32[]{:S(2)}) collective-permute-start(f32[66,512]{1,0:T(8,128)S(1)} %pad_maximum_fusion.8), channel_id=1, source_target_pairs={{0,2},{1,3},{2,0},{3,1},{4,6},{5,7},{6,4},{7,5},{8,10},{9,11},{10,... | collective-permute-start | bytes 405512 | tf_op jit(solution)/shard_map/ppermute | solution.py:175
  128.0 5.6 %collective-permute-done.12 = f32[66,512]{1,0:T(8,128)S(1)} collective-permute-done((f32[66,512]{1,0:T(8,128)S(1)}, f32[66,512]{1,0:T(8,128)S(1)}, u32[]{:S(2)}, u32[]{:S(2)}) %collective-permute-start.12) | collective-permute-done | bytes 135200 | tf_op jit(solution)/shard_map/ppermute | solution.py:175
  135.6 10.9 %collective-permute-done.13 = f32[66,512]{1,0:T(8,128)S(1)} collective-permute-done((f32[66,512]{1,0:T(8,128)S(1)}, f32[66,512]{1,0:T(8,128)S(1)}, u32[]{:S(2)}, u32[]{:S(2)}) %collective-permute-start.13) | collective-permute-done | bytes 135200 | tf_op jit(solution)/shard_map/ppermute | solution.py:175
  148.5 4.2 %collective-permute-done.14 = bf16[64,512]{1,0:T(8,128)(2,1)S(1)} collective-permute-done((bf16[64,512]{1,0:T(8,128)(2,1)S(1)}, bf16[64,512]{1,0:T(8,128)(2,1)S(1)}, u32[]{:S(2)}, u32[]{:S(2)}) %collective-permute-start.14) | collective-permute-done | bytes 65568 | tf_op jit(solution)/shard_map/ppermute | solution.py:182
  (70 shorter events, 13.5 us)
Async XLA Ops:
  0.6 20.2 %collective-permute-start.1 = (bf16[1024,128]{1,0:T(8,128)(2,1)}, bf16[1024,128]{1,0:T(8,128)(2,1)S(1)}, u32[]{:S(2)}, u32[]{:S(2)}) collective-permute-start(bf16[1024,128]{1,0:T(8,128)(2,1)} %refs_1_.1), channel_id=1, source_target_pairs={{392,0},{425,1},{458,2},{491,3},{268,4},{333,5},{6,6},{71,7},{128,... | collective-permute-start | bytes 786440 | tf_op jit(solution)/shard_map/ppermute | solution.py:231
  2.2 18.6 %collective-permute-start = (bf16[1024,128]{1,0:T(8,128)(2,1)}, bf16[1024,128]{1,0:T(8,128)(2,1)S(1)}, u32[]{:S(2)}, u32[]{:S(2)}) collective-permute-start(bf16[1024,128]{1,0:T(8,128)(2,1)} %refs_1_.1), channel_id=1, source_target_pairs={{408,0},{441,1},{474,2},{507,3},{284,4},{349,5},{22,6},{87,7},{144... | collective-permute-start | bytes 786440 | tf_op jit(solution)/shard_map/ppermute | solution.py:231
  4.2 17.6 %collective-permute-start.2 = (bf16[2048]{0:T(1024)(128)(2,1)}, bf16[2048]{0:T(1024)(128)(2,1)S(1)}, u32[]{:S(2)}, u32[]{:S(2)}) collective-permute-start(bf16[2048]{0:T(1024)(128)(2,1)} %param.14), channel_id=1, source_target_pairs={{12,0},{13,1},{14,2},{15,3},{8,4},{10,5},{0,6},{2,7},{4,8},{5,9},{... | collective-permute-start | bytes 12296 | tf_op jit(solution)/shard_map/ppermute | solution.py:247
  20.8 1.0 copy-start.1
  20.9 51.6 %copy-start.4 = (bf16[1024,64]{0,1:T(8,128)(2,1)S(1)}, bf16[1024,64]{0,1:T(8,128)(2,1)}, u32[]{:S(2)}) copy-start(bf16[1024,64]{0,1:T(8,128)(2,1)} %param.15) | copy-start | bytes 393220
  20.9 60.6 %copy-start.2 = (bf16[1024,128]{1,0:T(8,128)(2,1)S(1)}, bf16[1024,128]{1,0:T(8,128)(2,1)}, u32[]{:S(2)}) copy-start(bf16[1024,128]{1,0:T(8,128)(2,1)} %param.17) | copy-start | bytes 786436
  21.8 12.1 %collective-permute-start.3 = (f32[66,512]{1,0:T(8,128)S(1)}, f32[66,512]{1,0:T(8,128)S(1)}, u32[]{:S(2)}, u32[]{:S(2)}) collective-permute-start(f32[66,512]{1,0:T(8,128)S(1)} %constant_dynamic-slice_fusion.1), channel_id=1, source_target_pairs={{0,8},{1,9},{2,10},{3,11},{4,12},{5,13},{6,14},{7,15},{8,0},{9,1},... | collective-permute-start | bytes 405512 | tf_op jit(solution)/shard_map/ppermute | solution.py:171
  34.0 7.3 %collective-permute-start.4 = (f32[66,512]{1,0:T(8,128)S(1)}, f32[66,512]{1,0:T(8,128)S(1)}, u32[]{:S(2)}, u32[]{:S(2)}) collective-permute-start(f32[66,512]{1,0:T(8,128)S(1)} %pad_maximum_fusion.4), channel_id=1, source_target_pairs={{0,1},{1,0},{2,3},{3,2},{4,5},{5,4},{6,7},{7,6},{8,9},{9,8},{10,11... | collective-permute-start | bytes 405512 | tf_op jit(solution)/shard_map/ppermute | solution.py:175
  41.4 20.2 %collective-permute-start.5 = (f32[66,512]{1,0:T(8,128)S(1)}, f32[66,512]{1,0:T(8,128)S(1)}, u32[]{:S(2)}, u32[]{:S(2)}) collective-permute-start(f32[66,512]{1,0:T(8,128)S(1)} %pad_maximum_fusion.5), channel_id=1, source_target_pairs={{0,2},{1,3},{2,0},{3,1},{4,6},{5,7},{6,4},{7,5},{8,10},{9,11},{10,... | collective-permute-start | bytes 405512 | tf_op jit(solution)/shard_map/ppermute | solution.py:175
  61.7 10.7 %collective-permute-start.6 = (f32[66,512]{1,0:T(8,128)S(1)}, f32[66,512]{1,0:T(8,128)S(1)}, u32[]{:S(2)}, u32[]{:S(2)}) collective-permute-start(f32[66,512]{1,0:T(8,128)S(1)} %pad_maximum_fusion.6), channel_id=1, source_target_pairs={{0,6},{1,7},{2,4},{3,5},{4,2},{5,3},{6,0},{7,1},{8,14},{9,15},{10,... | collective-permute-start | bytes 405512 | tf_op jit(solution)/shard_map/ppermute | solution.py:175
  72.5 6.3 %collective-permute-start.7 = (bf16[64,512]{1,0:T(8,128)(2,1)S(1)}, bf16[64,512]{1,0:T(8,128)(2,1)S(1)}, u32[]{:S(2)}, u32[]{:S(2)}) collective-permute-start(bf16[64,512]{1,0:T(8,128)(2,1)S(1)} %fusion.13), channel_id=1, source_target_pairs={{0,8},{1,9},{2,10},{3,11},{4,12},{5,13},{6,14},{7,15},{8,0},{9,1},... | collective-permute-start | bytes 196616 | tf_op jit(solution)/shard_map/ppermute | solution.py:182
  78.9 17.6 %copy-start.3 = (bf16[64,1024]{1,0:T(8,128)(2,1)}, bf16[64,1024]{1,0:T(8,128)(2,1)S(1)}, u32[]{:S(2)}) copy-start(bf16[64,1024]{1,0:T(8,128)(2,1)S(1)} %maximum_select_fusion) | copy-start | bytes 393220
  78.9 15.3 %collective-permute-start.9 = (bf16[64,1024]{1,0:T(8,128)(2,1)S(1)}, bf16[64,1024]{1,0:T(8,128)(2,1)S(1)}, u32[]{:S(2)}, u32[]{:S(2)}) collective-permute-start(bf16[64,1024]{1,0:T(8,128)(2,1)S(1)} %maximum_select_fusion), channel_id=1, source_target_pairs={{392,0},{425,1},{458,2},{491,3},{268,4},{333,5},{6,6},{71,7},{128,... | collective-permute-start | bytes 393224 | tf_op jit(solution)/shard_map/ppermute | solution.py:231
  79.6 14.6 %collective-permute-start.8 = (bf16[64,1024]{1,0:T(8,128)(2,1)S(1)}, bf16[64,1024]{1,0:T(8,128)(2,1)S(1)}, u32[]{:S(2)}, u32[]{:S(2)}) collective-permute-start(bf16[64,1024]{1,0:T(8,128)(2,1)S(1)} %maximum_select_fusion), channel_id=1, source_target_pairs={{408,0},{441,1},{474,2},{507,3},{284,4},{349,5},{22,6},{87,7},{144... | collective-permute-start | bytes 393224 | tf_op jit(solution)/shard_map/ppermute | solution.py:231
  94.2 2.3 %copy-start = (bf16[2048,512]{1,0:T(8,128)(2,1)S(1)}, bf16[2048,512]{1,0:T(8,128)(2,1)}, u32[]{:S(2)}) copy-start(bf16[2048,512]{1,0:T(8,128)(2,1)} %get-tuple-element.12) | copy-start | bytes 6291460
  94.2 2.7 %copy-start.6 = (f32[2,512]{1,0:T(2,128)S(1)}, f32[2,512]{1,0:T(2,128)}, u32[]{:S(2)}) copy-start(f32[2,512]{1,0:T(2,128)} %get-tuple-element.15) | copy-start | bytes 12292
  94.2 2.7 %copy-start.7 = (f32[2,512]{1,0:T(2,128)S(1)}, f32[2,512]{1,0:T(2,128)}, u32[]{:S(2)}) copy-start(f32[2,512]{1,0:T(2,128)} %get-tuple-element.14) | copy-start | bytes 12292
  96.9 49.6 %copy-start.5 = (bf16[1024,64]{0,1:T(8,128)(2,1)S(1)}, bf16[1024,64]{0,1:T(8,128)(2,1)}, u32[]{:S(2)}) copy-start(bf16[1024,64]{0,1:T(8,128)(2,1)} %param.18) | copy-start | bytes 393220
  97.0 7.0 %collective-permute-start.10 = (f32[66,512]{1,0:T(8,128)S(1)}, f32[66,512]{1,0:T(8,128)S(1)}, u32[]{:S(2)}, u32[]{:S(2)}) collective-permute-start(f32[66,512]{1,0:T(8,128)S(1)} %constant_dynamic-slice_fusion), channel_id=1, source_target_pairs={{0,8},{1,9},{2,10},{3,11},{4,12},{5,13},{6,14},{7,15},{8,0},{9,1},... | collective-permute-start | bytes 405512 | tf_op jit(solution)/shard_map/ppermute | solution.py:171
  104.2 13.3 %collective-permute-start.11 = (f32[66,512]{1,0:T(8,128)S(1)}, f32[66,512]{1,0:T(8,128)S(1)}, u32[]{:S(2)}, u32[]{:S(2)}) collective-permute-start(f32[66,512]{1,0:T(8,128)S(1)} %pad_maximum_fusion.7), channel_id=1, source_target_pairs={{0,1},{1,0},{2,3},{3,2},{4,5},{5,4},{6,7},{7,6},{8,9},{9,8},{10,11... | collective-permute-start | bytes 405512 | tf_op jit(solution)/shard_map/ppermute | solution.py:175
  117.6 15.9 %collective-permute-start.12 = (f32[66,512]{1,0:T(8,128)S(1)}, f32[66,512]{1,0:T(8,128)S(1)}, u32[]{:S(2)}, u32[]{:S(2)}) collective-permute-start(f32[66,512]{1,0:T(8,128)S(1)} %pad_maximum_fusion.8), channel_id=1, source_target_pairs={{0,2},{1,3},{2,0},{3,1},{4,6},{5,7},{6,4},{7,5},{8,10},{9,11},{10,... | collective-permute-start | bytes 405512 | tf_op jit(solution)/shard_map/ppermute | solution.py:175
  133.7 12.8 %collective-permute-start.13 = (f32[66,512]{1,0:T(8,128)S(1)}, f32[66,512]{1,0:T(8,128)S(1)}, u32[]{:S(2)}, u32[]{:S(2)}) collective-permute-start(f32[66,512]{1,0:T(8,128)S(1)} %pad_maximum_fusion.9), channel_id=1, source_target_pairs={{0,6},{1,7},{2,4},{3,5},{4,2},{5,3},{6,0},{7,1},{8,14},{9,15},{10,... | collective-permute-start | bytes 405512 | tf_op jit(solution)/shard_map/ppermute | solution.py:175
  146.6 6.2 %collective-permute-start.14 = (bf16[64,512]{1,0:T(8,128)(2,1)S(1)}, bf16[64,512]{1,0:T(8,128)(2,1)S(1)}, u32[]{:S(2)}, u32[]{:S(2)}) collective-permute-start(bf16[64,512]{1,0:T(8,128)(2,1)S(1)} %fusion.11), channel_id=1, source_target_pairs={{0,8},{1,9},{2,10},{3,11},{4,12},{5,13},{6,14},{7,15},{8,0},{9,1},... | collective-permute-start | bytes 196616 | tf_op jit(solution)/shard_map/ppermute | solution.py:182

commit v14 on v13

--- a/solution.py
+++ b/solution.py
@@ -30,21 +30,19 @@
     out_ref[0 : width + 1, :] = jnp.zeros((width + 1, BLOCK), jnp.float32)
     out_ref[width + 1 : width + 2, :] = jnp.full((1, BLOCK), very_low, jnp.float32)
     for j in range(col_tiles):
-
-        @pl.when(mask_ref[row, col0 + j] > 0)
-        def _():
-            y = y_ref[j * BLOCK : (j + 1) * BLOCK, :]
-            s = lax.dot_general(y, x_ref[...], (((1,), (1,)), ((), ())), preferred_element_type=jnp.float32)
-            s = s * scale - offset_column(off_ref[:, j * BLOCK : (j + 1) * BLOCK])
-            m_old = out_ref[width + 1 : width + 2, :]
-            m_new = jnp.maximum(m_old, jnp.max(s, axis=0, keepdims=True))
-            shrink = jnp.exp(m_old - m_new)
-            p = jnp.exp(s - m_new)
-            out_ref[width : width + 1, :] = out_ref[width : width + 1, :] * shrink + jnp.sum(p, axis=0, keepdims=True)
-            out_ref[0:width, :] = out_ref[0:width, :] * shrink + jnp.dot(
-                v_ref[:, j * BLOCK : (j + 1) * BLOCK], p.astype(jnp.bfloat16), preferred_element_type=jnp.float32
-            )
-            out_ref[width + 1 : width + 2, :] = m_new
+        live = mask_ref[row, col0 + j] > 0
+        y = y_ref[j * BLOCK : (j + 1) * BLOCK, :]
+        s = lax.dot_general(y, x_ref[...], (((1,), (1,)), ((), ())), preferred_element_type=jnp.float32)
+        s = s * scale - offset_column(off_ref[:, j * BLOCK : (j + 1) * BLOCK])
+        m_old = out_ref[width + 1 : width + 2, :]
+        m_new = jnp.where(live, jnp.maximum(m_old, jnp.max(s, axis=0, keepdims=True)), m_old)
+        shrink = jnp.exp(m_old - m_new)
+        p = jnp.where(live, jnp.exp(s - m_new), 0.0)
+        out_ref[width : width + 1, :] = out_ref[width : width + 1, :] * shrink + jnp.sum(p, axis=0, keepdims=True)
+        out_ref[0:width, :] = out_ref[0:width, :] * shrink + jnp.dot(
+            v_ref[:, j * BLOCK : (j + 1) * BLOCK], p.astype(jnp.bfloat16), preferred_element_type=jnp.float32
+        )
+        out_ref[width + 1 : width + 2, :] = m_new
 
 
 def date_partials_kernel(targets, sources, offsets, values_t, tile_mask, col_base):
@@ -82,28 +80,18 @@
         s = lax.dot_general(y, x_ref[...], (((1,), (1,)), ((), ())), preferred_element_type=jnp.float32)
         return s * scale - offset_column(off_ref[:, j * BLOCK : (j + 1) * BLOCK])
 
-    stats_ref[...] = jnp.concatenate(
-        [jnp.zeros((1, BLOCK), jnp.float32), jnp.full((1, BLOCK), very_low, jnp.float32)], 0
-    )
-    for j in range(col_tiles):
-
-        @pl.when(mask_ref[row, col0 + j] > 0)
-        def _():
-            tile_peak = jnp.max(scores(j), axis=0, keepdims=True)
-            stats_ref[1:2, :] = jnp.maximum(stats_ref[1:2, :], tile_peak)
-
+    peak = jnp.full((1, BLOCK), very_low, jnp.float32)
     for j in range(col_tiles):
         live = mask_ref[row, col0 + j] > 0
-
-        @pl.when(live)
-        def _():
-            p = jnp.exp(scores(j) - stats_ref[1:2, :])
-            p_ref[j * BLOCK : (j + 1) * BLOCK, :] = p.astype(jnp.bfloat16)
-            stats_ref[0:1, :] = stats_ref[0:1, :] + jnp.sum(p, axis=0, keepdims=True)
-
-        @pl.when(jnp.logical_not(live))
-        def _():
-            p_ref[j * BLOCK : (j + 1) * BLOCK, :] = jnp.zeros((BLOCK, BLOCK), jnp.bfloat16)
+        peak = jnp.where(live, jnp.maximum(peak, jnp.max(scores(j), axis=0, keepdims=True)), peak)
+    total = jnp.zeros((1, BLOCK), jnp.float32)
+    for j in range(col_tiles):
+        live = mask_ref[row, col0 + j] > 0
+        p = jnp.where(live, jnp.exp(scores(j) - peak), 0.0)
+        p_ref[j * BLOCK : (j + 1) * BLOCK, :] = p.astype(jnp.bfloat16)
+        total = total + jnp.sum(p, axis=0, keepdims=True)
+    stats_ref[0:1, :] = total
+    stats_ref[1:2, :] = peak
 
 
 def date_weights_kernel(targets, sources, offsets, tile_mask, row_tile, col_base):

time: 154 us -> 151 us (0.981)
  the two profiles are of different devices: /device:TPU:48 before, /device:TPU:6 now
where the time goes in v14:
time: 151 us; the launch traced here: 149 us
  starting transfers between devices  76.6 us (51%)
  waiting for transfers between devices  43 us (28%)
  Pallas kernels  20.2 us (13%)
  local copies, waits for them, and re-layouts  2.68 us (2%)
  matrix products  2.67 us (2%)
  other arithmetic  2.31 us (2%)
    ppermute x6, starting transfers between devices, finish(): got = lax.ppermute(packed, 'src', exchange_perm(src_size, partner))  31.9 us
    ppermute x6, waiting for transfers between devices, finish(): got = lax.ppermute(packed, 'src', exchange_perm(src_size, partner))  28.6 us
    ppermute x4, starting transfers between devices, regroup(): return [lax.ppermute(block_rows, ('tgt', 'src'), p) for p in perms]  23.6 us
    pallas_call x2, Pallas kernels, date_weights_kernel(): pl.pallas_call(kernel, out_shape=(jax.ShapeDtypeStruct((cols, rows), jnp....  11.8 us
    ppermute x2, starting transfers between devices, finish(): got = lax.ppermute(send, 'src', xor_perm(src_size, bit))  10.2 us
    ppermute x2, waiting for transfers between devices, finish(): got = lax.ppermute(send, 'src', xor_perm(src_size, bit))  9.67 us
    ppermute x2, starting transfers between devices, finish(): got = lax.ppermute(value, 'src', xor_perm(src_size, bit))  9.09 us
    pallas_call x1, Pallas kernels, date_partials_kernel(): pl.pallas_call(kernel, out_shape=jax.ShapeDtypeStruct((width + 2, rows),...  8.43 us
  transfers between devices with their start and end apart: 15, of which 10 were waited for; matrix products, arithmetic and copies ran while one was open for 2% of the time, Pallas kernels for 14%

profile of v14, /device:TPU:6, one launch (start us, length us, event | category | flops | bytes accessed | tf_op | source)
XLA Modules:
  0.0 148.7 jit_solution(13522514536264015263)
XLA Ops:
  0.6 10.9 %collective-permute-start.1 = (bf16[1024,128]{1,0:T(8,128)(2,1)}, bf16[1024,128]{1,0:T(8,128)(2,1)S(1)}, u32[]{:S(2)}, u32[]{:S(2)}) collective-permute-start(bf16[1024,128]{1,0:T(8,128)(2,1)} %refs_1_.1), channel_id=1, source_target_pairs={{392,0},{425,1},{458,2},{491,3},{268,4},{333,5},{6,6},{71,7},{128,... | collective-permute-start | bytes 786440 | tf_op jit(solution)/shard_map/ppermute | solution.py:219
  16.8 8.4 %shard_map.113 = f32[66,1024]{1,0:T(8,128)} custom-call(s32[64,64]{1,0:T(8,128)} %refs_0_.3, bf16[1024,128]{1,0:T(8,128)(2,1)} %refs_1_.1, bf16[2048,128]{1,0:T(8,128)(2,1)} %refs_2_.1, bf16[1,2048]{1,0:T(2,128)(2,1)} %reshape.11.refs_3_, bf16[64,2048]{1,0:T(8,128)(2,1)} %bitcast.28), custom_call_target="tpu_custom_call" | custom-call | tf_op jit(solution)/shard_map/pallas_call | solution.py:56
  26.2 8.2 %collective-permute-start.3 = (f32[66,512]{1,0:T(8,128)S(1)}, f32[66,512]{1,0:T(8,128)S(1)}, u32[]{:S(2)}, u32[]{:S(2)}) collective-permute-start(f32[66,512]{1,0:T(8,128)S(1)} %constant_dynamic-slice_fusion.1), channel_id=1, source_target_pairs={{0,8},{1,9},{2,10},{3,11},{4,12},{5,13},{6,14},{7,15},{8,0},{9,1},... | collective-permute-start | bytes 405512 | tf_op jit(solution)/shard_map/ppermute | solution.py:159
  34.4 3.8 %collective-permute-done.3 = f32[66,512]{1,0:T(8,128)S(1)} collective-permute-done((f32[66,512]{1,0:T(8,128)S(1)}, f32[66,512]{1,0:T(8,128)S(1)}, u32[]{:S(2)}, u32[]{:S(2)}) %collective-permute-start.3) | collective-permute-done | bytes 135200 | tf_op jit(solution)/shard_map/ppermute | solution.py:159
  38.4 3.4 %collective-permute-start.4 = (f32[66,512]{1,0:T(8,128)S(1)}, f32[66,512]{1,0:T(8,128)S(1)}, u32[]{:S(2)}, u32[]{:S(2)}) collective-permute-start(f32[66,512]{1,0:T(8,128)S(1)} %pad_maximum_fusion.4), channel_id=1, source_target_pairs={{0,1},{1,0},{2,3},{3,2},{4,5},{5,4},{6,7},{7,6},{8,9},{9,8},{10,11... | collective-permute-start | bytes 405512 | tf_op jit(solution)/shard_map/ppermute | solution.py:163
  41.8 3.6 %collective-permute-done.4 = f32[66,512]{1,0:T(8,128)S(1)} collective-permute-done((f32[66,512]{1,0:T(8,128)S(1)}, f32[66,512]{1,0:T(8,128)S(1)}, u32[]{:S(2)}, u32[]{:S(2)}) %collective-permute-start.4) | collective-permute-done | bytes 135200 | tf_op jit(solution)/shard_map/ppermute | solution.py:163
  45.5 3.4 %collective-permute-start.5 = (f32[66,512]{1,0:T(8,128)S(1)}, f32[66,512]{1,0:T(8,128)S(1)}, u32[]{:S(2)}, u32[]{:S(2)}) collective-permute-start(f32[66,512]{1,0:T(8,128)S(1)} %pad_maximum_fusion.5), channel_id=1, source_target_pairs={{0,2},{1,3},{2,0},{3,1},{4,6},{5,7},{6,4},{7,5},{8,10},{9,11},{10,... | collective-permute-start | bytes 405512 | tf_op jit(solution)/shard_map/ppermute | solution.py:163
  49.0 6.4 %collective-permute-done.5 = f32[66,512]{1,0:T(8,128)S(1)} collective-permute-done((f32[66,512]{1,0:T(8,128)S(1)}, f32[66,512]{1,0:T(8,128)S(1)}, u32[]{:S(2)}, u32[]{:S(2)}) %collective-permute-start.5) | collective-permute-done | bytes 135200 | tf_op jit(solution)/shard_map/ppermute | solution.py:163
  55.4 8.6 %collective-permute-start.6 = (f32[66,512]{1,0:T(8,128)S(1)}, f32[66,512]{1,0:T(8,128)S(1)}, u32[]{:S(2)}, u32[]{:S(2)}) collective-permute-start(f32[66,512]{1,0:T(8,128)S(1)} %pad_maximum_fusion.6), channel_id=1, source_target_pairs={{0,6},{1,7},{2,4},{3,5},{4,2},{5,3},{6,0},{7,1},{8,14},{9,15},{10,... | collective-permute-start | bytes 405512 | tf_op jit(solution)/shard_map/ppermute | solution.py:163
  64.0 4.3 %collective-permute-done.6 = f32[66,512]{1,0:T(8,128)S(1)} collective-permute-done((f32[66,512]{1,0:T(8,128)S(1)}, f32[66,512]{1,0:T(8,128)S(1)}, u32[]{:S(2)}, u32[]{:S(2)}) %collective-permute-start.6) | collective-permute-done | bytes 135200 | tf_op jit(solution)/shard_map/ppermute | solution.py:163
  68.4 5.4 %collective-permute-start.7 = (bf16[64,512]{1,0:T(8,128)(2,1)S(1)}, bf16[64,512]{1,0:T(8,128)(2,1)S(1)}, u32[]{:S(2)}, u32[]{:S(2)}) collective-permute-start(bf16[64,512]{1,0:T(8,128)(2,1)S(1)} %fusion.13), channel_id=1, source_target_pairs={{0,8},{1,9},{2,10},{3,11},{4,12},{5,13},{6,14},{7,15},{8,0},{9,1},... | collective-permute-start | bytes 196616 | tf_op jit(solution)/shard_map/ppermute | solution.py:170
  73.8 2.2 %collective-permute-done.7 = bf16[64,512]{1,0:T(8,128)(2,1)S(1)} collective-permute-done((bf16[64,512]{1,0:T(8,128)(2,1)S(1)}, bf16[64,512]{1,0:T(8,128)(2,1)S(1)}, u32[]{:S(2)}, u32[]{:S(2)}) %collective-permute-start.7) | collective-permute-done | bytes 65568 | tf_op jit(solution)/shard_map/ppermute | solution.py:170
  76.1 8.8 %collective-permute-start.9 = (bf16[64,1024]{1,0:T(8,128)(2,1)S(1)}, bf16[64,1024]{1,0:T(8,128)(2,1)S(1)}, u32[]{:S(2)}, u32[]{:S(2)}) collective-permute-start(bf16[64,1024]{1,0:T(8,128)(2,1)S(1)} %maximum_select_fusion), channel_id=1, source_target_pairs={{392,0},{425,1},{458,2},{491,3},{268,4},{333,5},{6,6},{71,7},{128,... | collective-permute-start | bytes 393224 | tf_op jit(solution)/shard_map/ppermute | solution.py:219
  88.1 5.9 %shard_map.115 = (bf16[2048,512]{1,0:T(8,128)(2,1)}, f32[2,512]{1,0:T(2,128)}) custom-call(s32[64,64]{1,0:T(8,128)} %refs_0_.5, bf16[512,128]{1,0:T(8,128)(2,1)} %get-tuple-element.33.refs_1_, bf16[2048,128]{1,0:T(8,128)(2,1)} %pad_maximum_fusion.refs_2_, bf16[1,2048]{1,0:T(2,128)(2,1)} %reshape.12.refs_3_), custom_call_target="tpu_custom_call" | custom-call | tf_op jit(solution)/shard_map/pallas_call | solution.py:104
  94.0 5.9 %shard_map.114 = (bf16[2048,512]{1,0:T(8,128)(2,1)}, f32[2,512]{1,0:T(2,128)}) custom-call(s32[64,64]{1,0:T(8,128)} %refs_0_.5, bf16[512,128]{1,0:T(8,128)(2,1)} %get-tuple-element.32.refs_1_, bf16[2048,128]{1,0:T(8,128)(2,1)} %pad_maximum_fusion.refs_2_, bf16[1,2048]{1,0:T(2,128)(2,1)} %reshape.12.refs_3_), custom_call_target="tpu_custom_call" | custom-call | tf_op jit(solution)/shard_map/pallas_call | solution.py:104
  104.7 5.8 %collective-permute-done.10 = f32[66,512]{1,0:T(8,128)S(1)} collective-permute-done((f32[66,512]{1,0:T(8,128)S(1)}, f32[66,512]{1,0:T(8,128)S(1)}, u32[]{:S(2)}, u32[]{:S(2)}) %collective-permute-start.10) | collective-permute-done | bytes 135200 | tf_op jit(solution)/shard_map/ppermute | solution.py:159
  110.7 3.9 %collective-permute-start.11 = (f32[66,512]{1,0:T(8,128)S(1)}, f32[66,512]{1,0:T(8,128)S(1)}, u32[]{:S(2)}, u32[]{:S(2)}) collective-permute-start(f32[66,512]{1,0:T(8,128)S(1)} %pad_maximum_fusion.7), channel_id=1, source_target_pairs={{0,1},{1,0},{2,3},{3,2},{4,5},{5,4},{6,7},{7,6},{8,9},{9,8},{10,11... | collective-permute-start | bytes 405512 | tf_op jit(solution)/shard_map/ppermute | solution.py:163
  114.5 3.3 %collective-permute-done.11 = f32[66,512]{1,0:T(8,128)S(1)} collective-permute-done((f32[66,512]{1,0:T(8,128)S(1)}, f32[66,512]{1,0:T(8,128)S(1)}, u32[]{:S(2)}, u32[]{:S(2)}) %collective-permute-start.11) | collective-permute-done | bytes 135200 | tf_op jit(solution)/shard_map/ppermute | solution.py:163
  117.9 5.8 %collective-permute-start.12 = (f32[66,512]{1,0:T(8,128)S(1)}, f32[66,512]{1,0:T(8,128)S(1)}, u32[]{:S(2)}, u32[]{:S(2)}) collective-permute-start(f32[66,512]{1,0:T(8,128)S(1)} %pad_maximum_fusion.8), channel_id=1, source_target_pairs={{0,2},{1,3},{2,0},{3,1},{4,6},{5,7},{6,4},{7,5},{8,10},{9,11},{10,... | collective-permute-start | bytes 405512 | tf_op jit(solution)/shard_map/ppermute | solution.py:163
  123.7 5.3 %collective-permute-done.12 = f32[66,512]{1,0:T(8,128)S(1)} collective-permute-done((f32[66,512]{1,0:T(8,128)S(1)}, f32[66,512]{1,0:T(8,128)S(1)}, u32[]{:S(2)}, u32[]{:S(2)}) %collective-permute-start.12) | collective-permute-done | bytes 135200 | tf_op jit(solution)/shard_map/ppermute | solution.py:163
  129.0 6.8 %collective-permute-start.13 = (f32[66,512]{1,0:T(8,128)S(1)}, f32[66,512]{1,0:T(8,128)S(1)}, u32[]{:S(2)}, u32[]{:S(2)}) collective-permute-start(f32[66,512]{1,0:T(8,128)S(1)} %pad_maximum_fusion.9), channel_id=1, source_target_pairs={{0,6},{1,7},{2,4},{3,5},{4,2},{5,3},{6,0},{7,1},{8,14},{9,15},{10,... | collective-permute-start | bytes 405512 | tf_op jit(solution)/shard_map/ppermute | solution.py:163
  135.9 5.8 %collective-permute-done.13 = f32[66,512]{1,0:T(8,128)S(1)} collective-permute-done((f32[66,512]{1,0:T(8,128)S(1)}, f32[66,512]{1,0:T(8,128)S(1)}, u32[]{:S(2)}, u32[]{:S(2)}) %collective-permute-start.13) | collective-permute-done | bytes 135200 | tf_op jit(solution)/shard_map/ppermute | solution.py:163
  141.8 3.7 %collective-permute-start.14 = (bf16[64,512]{1,0:T(8,128)(2,1)S(1)}, bf16[64,512]{1,0:T(8,128)(2,1)S(1)}, u32[]{:S(2)}, u32[]{:S(2)}) collective-permute-start(bf16[64,512]{1,0:T(8,128)(2,1)S(1)} %fusion.11), channel_id=1, source_target_pairs={{0,8},{1,9},{2,10},{3,11},{4,12},{5,13},{6,14},{7,15},{8,0},{9,1},... | collective-permute-start | bytes 196616 | tf_op jit(solution)/shard_map/ppermute | solution.py:170
  145.5 2.5 %collective-permute-done.14 = bf16[64,512]{1,0:T(8,128)(2,1)S(1)} collective-permute-done((bf16[64,512]{1,0:T(8,128)(2,1)S(1)}, bf16[64,512]{1,0:T(8,128)(2,1)S(1)}, u32[]{:S(2)}, u32[]{:S(2)}) %collective-permute-start.14) | collective-permute-done | bytes 65568 | tf_op jit(solution)/shard_map/ppermute | solution.py:170
  (70 shorter events, 15.4 us)
Async XLA Ops:
  0.6 24.6 %collective-permute-start.1 = (bf16[1024,128]{1,0:T(8,128)(2,1)}, bf16[1024,128]{1,0:T(8,128)(2,1)S(1)}, u32[]{:S(2)}, u32[]{:S(2)}) collective-permute-start(bf16[1024,128]{1,0:T(8,128)(2,1)} %refs_1_.1), channel_id=1, source_target_pairs={{392,0},{425,1},{458,2},{491,3},{268,4},{333,5},{6,6},{71,7},{128,... | collective-permute-start | bytes 786440 | tf_op jit(solution)/shard_map/ppermute | solution.py:219
  11.6 13.6 %collective-permute-start = (bf16[1024,128]{1,0:T(8,128)(2,1)}, bf16[1024,128]{1,0:T(8,128)(2,1)S(1)}, u32[]{:S(2)}, u32[]{:S(2)}) collective-permute-start(bf16[1024,128]{1,0:T(8,128)(2,1)} %refs_1_.1), channel_id=1, source_target_pairs={{408,0},{441,1},{474,2},{507,3},{284,4},{349,5},{22,6},{87,7},{144... | collective-permute-start | bytes 786440 | tf_op jit(solution)/shard_map/ppermute | solution.py:219
  13.5 12.6 %collective-permute-start.2 = (bf16[2048]{0:T(1024)(128)(2,1)}, bf16[2048]{0:T(1024)(128)(2,1)S(1)}, u32[]{:S(2)}, u32[]{:S(2)}) collective-permute-start(bf16[2048]{0:T(1024)(128)(2,1)} %param.14), channel_id=1, source_target_pairs={{12,0},{13,1},{14,2},{15,3},{8,4},{10,5},{0,6},{2,7},{4,8},{5,9},{... | collective-permute-start | bytes 12296 | tf_op jit(solution)/shard_map/ppermute | solution.py:235
  25.2 1.0 copy-start.1
  25.2 43.1 %copy-start.4 = (bf16[1024,64]{0,1:T(8,128)(2,1)S(1)}, bf16[1024,64]{0,1:T(8,128)(2,1)}, u32[]{:S(2)}) copy-start(bf16[1024,64]{0,1:T(8,128)(2,1)} %param.15) | copy-start | bytes 393220
  25.3 61.6 %copy-start.2 = (bf16[1024,128]{1,0:T(8,128)(2,1)S(1)}, bf16[1024,128]{1,0:T(8,128)(2,1)}, u32[]{:S(2)}) copy-start(bf16[1024,128]{1,0:T(8,128)(2,1)} %param.17) | copy-start | bytes 786436
  26.2 12.1 %collective-permute-start.3 = (f32[66,512]{1,0:T(8,128)S(1)}, f32[66,512]{1,0:T(8,128)S(1)}, u32[]{:S(2)}, u32[]{:S(2)}) collective-permute-start(f32[66,512]{1,0:T(8,128)S(1)} %constant_dynamic-slice_fusion.1), channel_id=1, source_target_pairs={{0,8},{1,9},{2,10},{3,11},{4,12},{5,13},{6,14},{7,15},{8,0},{9,1},... | collective-permute-start | bytes 405512 | tf_op jit(solution)/shard_map/ppermute | solution.py:159
  38.4 7.0 %collective-permute-start.4 = (f32[66,512]{1,0:T(8,128)S(1)}, f32[66,512]{1,0:T(8,128)S(1)}, u32[]{:S(2)}, u32[]{:S(2)}) collective-permute-start(f32[66,512]{1,0:T(8,128)S(1)} %pad_maximum_fusion.4), channel_id=1, source_target_pairs={{0,1},{1,0},{2,3},{3,2},{4,5},{5,4},{6,7},{7,6},{8,9},{9,8},{10,11... | collective-permute-start | bytes 405512 | tf_op jit(solution)/shard_map/ppermute | solution.py:163
  45.5 9.8 %collective-permute-start.5 = (f32[66,512]{1,0:T(8,128)S(1)}, f32[66,512]{1,0:T(8,128)S(1)}, u32[]{:S(2)}, u32[]{:S(2)}) collective-permute-start(f32[66,512]{1,0:T(8,128)S(1)} %pad_maximum_fusion.5), channel_id=1, source_target_pairs={{0,2},{1,3},{2,0},{3,1},{4,6},{5,7},{6,4},{7,5},{8,10},{9,11},{10,... | collective-permute-start | bytes 405512 | tf_op jit(solution)/shard_map/ppermute | solution.py:163
  55.4 12.8 %collective-permute-start.6 = (f32[66,512]{1,0:T(8,128)S(1)}, f32[66,512]{1,0:T(8,128)S(1)}, u32[]{:S(2)}, u32[]{:S(2)}) collective-permute-start(f32[66,512]{1,0:T(8,128)S(1)} %pad_maximum_fusion.6), channel_id=1, source_target_pairs={{0,6},{1,7},{2,4},{3,5},{4,2},{5,3},{6,0},{7,1},{8,14},{9,15},{10,... | collective-permute-start | bytes 405512 | tf_op jit(solution)/shard_map/ppermute | solution.py:163
  68.4 7.6 %collective-permute-start.7 = (bf16[64,512]{1,0:T(8,128)(2,1)S(1)}, bf16[64,512]{1,0:T(8,128)(2,1)S(1)}, u32[]{:S(2)}, u32[]{:S(2)}) collective-permute-start(bf16[64,512]{1,0:T(8,128)(2,1)S(1)} %fusion.13), channel_id=1, source_target_pairs={{0,8},{1,9},{2,10},{3,11},{4,12},{5,13},{6,14},{7,15},{8,0},{9,1},... | collective-permute-start | bytes 196616 | tf_op jit(solution)/shard_map/ppermute | solution.py:170
  76.0 26.1 %copy-start.3 = (bf16[64,1024]{1,0:T(8,128)(2,1)}, bf16[64,1024]{1,0:T(8,128)(2,1)S(1)}, u32[]{:S(2)}) copy-start(bf16[64,1024]{1,0:T(8,128)(2,1)S(1)} %maximum_select_fusion) | copy-start | bytes 393220
  76.1 23.8 %collective-permute-start.9 = (bf16[64,1024]{1,0:T(8,128)(2,1)S(1)}, bf16[64,1024]{1,0:T(8,128)(2,1)S(1)}, u32[]{:S(2)}, u32[]{:S(2)}) collective-permute-start(bf16[64,1024]{1,0:T(8,128)(2,1)S(1)} %maximum_select_fusion), channel_id=1, source_target_pairs={{392,0},{425,1},{458,2},{491,3},{268,4},{333,5},{6,6},{71,7},{128,... | collective-permute-start | bytes 393224 | tf_op jit(solution)/shard_map/ppermute | solution.py:219
  84.9 15.0 %collective-permute-start.8 = (bf16[64,1024]{1,0:T(8,128)(2,1)S(1)}, bf16[64,1024]{1,0:T(8,128)(2,1)S(1)}, u32[]{:S(2)}, u32[]{:S(2)}) collective-permute-start(bf16[64,1024]{1,0:T(8,128)(2,1)S(1)} %maximum_select_fusion), channel_id=1, source_target_pairs={{408,0},{441,1},{474,2},{507,3},{284,4},{349,5},{22,6},{87,7},{144... | collective-permute-start | bytes 393224 | tf_op jit(solution)/shard_map/ppermute | solution.py:219
  99.9 2.3 %copy-start = (bf16[2048,512]{1,0:T(8,128)(2,1)S(1)}, bf16[2048,512]{1,0:T(8,128)(2,1)}, u32[]{:S(2)}) copy-start(bf16[2048,512]{1,0:T(8,128)(2,1)} %get-tuple-element.12) | copy-start | bytes 6291460
  99.9 2.7 %copy-start.6 = (f32[2,512]{1,0:T(2,128)S(1)}, f32[2,512]{1,0:T(2,128)}, u32[]{:S(2)}) copy-start(f32[2,512]{1,0:T(2,128)} %get-tuple-element.15) | copy-start | bytes 12292
  99.9 2.7 %copy-start.7 = (f32[2,512]{1,0:T(2,128)S(1)}, f32[2,512]{1,0:T(2,128)}, u32[]{:S(2)}) copy-start(f32[2,512]{1,0:T(2,128)} %get-tuple-element.14) | copy-start | bytes 12292
  102.6 39.1 %copy-start.5 = (bf16[1024,64]{0,1:T(8,128)(2,1)S(1)}, bf16[1024,64]{0,1:T(8,128)(2,1)}, u32[]{:S(2)}) copy-start(bf16[1024,64]{0,1:T(8,128)(2,1)} %param.18) | copy-start | bytes 393220
  102.7 7.8 %collective-permute-start.10 = (f32[66,512]{1,0:T(8,128)S(1)}, f32[66,512]{1,0:T(8,128)S(1)}, u32[]{:S(2)}, u32[]{:S(2)}) collective-permute-start(f32[66,512]{1,0:T(8,128)S(1)} %constant_dynamic-slice_fusion), channel_id=1, source_target_pairs={{0,8},{1,9},{2,10},{3,11},{4,12},{5,13},{6,14},{7,15},{8,0},{9,1},... | collective-permute-start | bytes 405512 | tf_op jit(solution)/shard_map/ppermute | solution.py:159
  110.7 7.1 %collective-permute-start.11 = (f32[66,512]{1,0:T(8,128)S(1)}, f32[66,512]{1,0:T(8,128)S(1)}, u32[]{:S(2)}, u32[]{:S(2)}) collective-permute-start(f32[66,512]{1,0:T(8,128)S(1)} %pad_maximum_fusion.7), channel_id=1, source_target_pairs={{0,1},{1,0},{2,3},{3,2},{4,5},{5,4},{6,7},{7,6},{8,9},{9,8},{10,11... | collective-permute-start | bytes 405512 | tf_op jit(solution)/shard_map/ppermute | solution.py:163
  117.9 11.1 %collective-permute-start.12 = (f32[66,512]{1,0:T(8,128)S(1)}, f32[66,512]{1,0:T(8,128)S(1)}, u32[]{:S(2)}, u32[]{:S(2)}) collective-permute-start(f32[66,512]{1,0:T(8,128)S(1)} %pad_maximum_fusion.8), channel_id=1, source_target_pairs={{0,2},{1,3},{2,0},{3,1},{4,6},{5,7},{6,4},{7,5},{8,10},{9,11},{10,... | collective-permute-start | bytes 405512 | tf_op jit(solution)/shard_map/ppermute | solution.py:163
  129.0 12.7 %collective-permute-start.13 = (f32[66,512]{1,0:T(8,128)S(1)}, f32[66,512]{1,0:T(8,128)S(1)}, u32[]{:S(2)}, u32[]{:S(2)}) collective-permute-start(f32[66,512]{1,0:T(8,128)S(1)} %pad_maximum_fusion.9), channel_id=1, source_target_pairs={{0,6},{1,7},{2,4},{3,5},{4,2},{5,3},{6,0},{7,1},{8,14},{9,15},{10,... | collective-permute-start | bytes 405512 | tf_op jit(solution)/shard_map/ppermute | solution.py:163
  141.8 6.2 %collective-permute-start.14 = (bf16[64,512]{1,0:T(8,128)(2,1)S(1)}, bf16[64,512]{1,0:T(8,128)(2,1)S(1)}, u32[]{:S(2)}, u32[]{:S(2)}) collective-permute-start(bf16[64,512]{1,0:T(8,128)(2,1)S(1)} %fusion.11), channel_id=1, source_target_pairs={{0,8},{1,9},{2,10},{3,11},{4,12},{5,13},{6,14},{7,15},{8,0},{9,1},... | collective-permute-start | bytes 196616 | tf_op jit(solution)/shard_map/ppermute | solution.py:170

commit v15 on v14

--- a/solution.py
+++ b/solution.py
@@ -219,6 +219,18 @@
     return [lax.ppermute(block_rows, ("tgt", "src"), p) for p in perms]
 
 
+def forward_perms():
+    tgt_size = lax.axis_size("tgt")
+    src_size = lax.axis_size("src")
+    direct, swap = [], []
+    for t in range(tgt_size):
+        for s in range(src_size):
+            u = 2 * source_pair(t, s) + t % 2
+            direct.append((lin(u, holder(s)), lin(t, s)))
+            swap.append((lin(t ^ 1, s), lin(t, s)))
+    return direct, swap
+
+
 def regroup_order(got, axis=0):
     odd = lax.axis_index("tgt") % 2 == 1
     return jnp.concatenate(
@@ -255,13 +267,17 @@
     def early_col_base():
         return source_pair(lax.axis_index("tgt"), lax.axis_index("src")) * src_tiles
 
-    mid_sources = regroup_order(regroup(states_mid))
+    direct, swap = forward_perms()
+    own_sources = lax.ppermute(states_mid, ("tgt", "src"), direct)
     mid_offsets = regroup_offsets(offset_mid)
     partials = date_partials_kernel(
         states_mid, states_late, offset_late, values_late.T, mask_mid, mid_col_base
     )
-    partials, mid_sources, mid_offsets = lax.optimization_barrier(
-        (partials, mid_sources, mid_offsets)
+    partials, own_sources, mid_offsets = lax.optimization_barrier(
+        (partials, own_sources, mid_offsets)
+    )
+    mid_sources = regroup_order(
+        [own_sources, lax.ppermute(own_sources, ("tgt", "src"), swap)]
     )
     early_parts = []
     for row_tile in range(states_early.shape[0] // BLOCK):

time: 151 us -> 140 us (0.927)
  the two profiles are of different devices: /device:TPU:6 before, /device:TPU:10 now
where the time goes in v15:
time: 140 us; the launch traced here: 139 us
  starting transfers between devices  63.2 us (45%)
  waiting for transfers between devices  44.2 us (32%)
  Pallas kernels  20.2 us (14%)
  other arithmetic  3.95 us (3%)
  local copies, waits for them, and re-layouts  3.63 us (3%)
  matrix products  2.67 us (2%)
    ppermute x6, waiting for transfers between devices, finish(): got = lax.ppermute(packed, 'src', exchange_perm(src_size, partner))  28.3 us
    ppermute x6, starting transfers between devices, finish(): got = lax.ppermute(packed, 'src', exchange_perm(src_size, partner))  22.3 us
    pallas_call x2, Pallas kernels, date_weights_kernel(): pl.pallas_call(kernel, out_shape=(jax.ShapeDtypeStruct((cols, rows), jnp....  11.8 us
    ppermute x1, starting transfers between devices, per_device(): own_sources = lax.ppermute(states_mid, ('tgt', 'src'), direct)  11.1 us
    ppermute x2, starting transfers between devices, finish(): got = lax.ppermute(send, 'src', xor_perm(src_size, bit))  10.1 us
    ppermute x2, starting transfers between devices, regroup(): return [lax.ppermute(block_rows, ('tgt', 'src'), p) for p in perms]  9.79 us
    ppermute x2, waiting for transfers between devices, finish(): got = lax.ppermute(send, 'src', xor_perm(src_size, bit))  9.77 us
    pallas_call x1, Pallas kernels, date_partials_kernel(): pl.pallas_call(kernel, out_shape=jax.ShapeDtypeStruct((width + 2, rows),...  8.42 us
  transfers between devices with their start and end apart: 15, of which 10 were waited for; matrix products, arithmetic and copies ran while one was open for 3% of the time, Pallas kernels for 15%

profile of v15, /device:TPU:10, one launch (start us, length us, event | category | flops | bytes accessed | tf_op | source)
XLA Modules:
  0.0 139.0 jit_solution(17062780460164876950)
XLA Ops:
  0.6 11.1 %collective-permute-start = (bf16[1024,128]{1,0:T(8,128)(2,1)}, bf16[1024,128]{1,0:T(8,128)(2,1)S(1)}, u32[]{:S(2)}, u32[]{:S(2)}) collective-permute-start(bf16[1024,128]{1,0:T(8,128)(2,1)} %refs_1_.1), channel_id=1, source_target_pairs={{392,0},{425,1},{458,2},{491,3},{268,4},{333,5},{6,6},{71,7},{128,... | collective-permute-start | bytes 786440 | tf_op jit(solution)/shard_map/ppermute | solution.py:271
  14.9 8.4 %shard_map.113 = f32[66,1024]{1,0:T(8,128)} custom-call(s32[64,64]{1,0:T(8,128)} %refs_0_.3, bf16[1024,128]{1,0:T(8,128)(2,1)} %refs_1_.1, bf16[2048,128]{1,0:T(8,128)(2,1)} %refs_2_.1, bf16[1,2048]{1,0:T(2,128)(2,1)} %reshape.11.refs_3_, bf16[64,2048]{1,0:T(8,128)(2,1)} %bitcast.28), custom_call_target="tpu_custom_call" | custom-call | tf_op jit(solution)/shard_map/pallas_call | solution.py:56
  24.3 8.1 %collective-permute-start.2 = (f32[66,512]{1,0:T(8,128)S(1)}, f32[66,512]{1,0:T(8,128)S(1)}, u32[]{:S(2)}, u32[]{:S(2)}) collective-permute-start(f32[66,512]{1,0:T(8,128)S(1)} %constant_dynamic-slice_fusion.1), channel_id=1, source_target_pairs={{0,8},{1,9},{2,10},{3,11},{4,12},{5,13},{6,14},{7,15},{8,0},{9,1},... | collective-permute-start | bytes 405512 | tf_op jit(solution)/shard_map/ppermute | solution.py:159
  32.5 3.3 %collective-permute-done.2 = f32[66,512]{1,0:T(8,128)S(1)} collective-permute-done((f32[66,512]{1,0:T(8,128)S(1)}, f32[66,512]{1,0:T(8,128)S(1)}, u32[]{:S(2)}, u32[]{:S(2)}) %collective-permute-start.2) | collective-permute-done | bytes 135200 | tf_op jit(solution)/shard_map/ppermute | solution.py:159
  37.5 3.3 %collective-permute-start.3 = (f32[66,512]{1,0:T(8,128)S(1)}, f32[66,512]{1,0:T(8,128)S(1)}, u32[]{:S(2)}, u32[]{:S(2)}) collective-permute-start(f32[66,512]{1,0:T(8,128)S(1)} %pad_maximum_fusion.4), channel_id=1, source_target_pairs={{0,1},{1,0},{2,3},{3,2},{4,5},{5,4},{6,7},{7,6},{8,9},{9,8},{10,11... | collective-permute-start | bytes 405512 | tf_op jit(solution)/shard_map/ppermute | solution.py:163
  40.8 3.8 %collective-permute-done.3 = f32[66,512]{1,0:T(8,128)S(1)} collective-permute-done((f32[66,512]{1,0:T(8,128)S(1)}, f32[66,512]{1,0:T(8,128)S(1)}, u32[]{:S(2)}, u32[]{:S(2)}) %collective-permute-start.3) | collective-permute-done | bytes 135200 | tf_op jit(solution)/shard_map/ppermute | solution.py:163
  44.7 3.5 %collective-permute-start.4 = (f32[66,512]{1,0:T(8,128)S(1)}, f32[66,512]{1,0:T(8,128)S(1)}, u32[]{:S(2)}, u32[]{:S(2)}) collective-permute-start(f32[66,512]{1,0:T(8,128)S(1)} %pad_maximum_fusion.5), channel_id=1, source_target_pairs={{0,2},{1,3},{2,0},{3,1},{4,6},{5,7},{6,4},{7,5},{8,10},{9,11},{10,... | collective-permute-start | bytes 405512 | tf_op jit(solution)/shard_map/ppermute | solution.py:163
  48.2 4.5 %collective-permute-done.4 = f32[66,512]{1,0:T(8,128)S(1)} collective-permute-done((f32[66,512]{1,0:T(8,128)S(1)}, f32[66,512]{1,0:T(8,128)S(1)}, u32[]{:S(2)}, u32[]{:S(2)}) %collective-permute-start.4) | collective-permute-done | bytes 135200 | tf_op jit(solution)/shard_map/ppermute | solution.py:163
  52.8 4.8 %collective-permute-start.5 = (f32[66,512]{1,0:T(8,128)S(1)}, f32[66,512]{1,0:T(8,128)S(1)}, u32[]{:S(2)}, u32[]{:S(2)}) collective-permute-start(f32[66,512]{1,0:T(8,128)S(1)} %pad_maximum_fusion.6), channel_id=1, source_target_pairs={{0,6},{1,7},{2,4},{3,5},{4,2},{5,3},{6,0},{7,1},{8,14},{9,15},{10,... | collective-permute-start | bytes 405512 | tf_op jit(solution)/shard_map/ppermute | solution.py:163
  62.0 3.7 %collective-permute-start.6 = (bf16[64,512]{1,0:T(8,128)(2,1)S(1)}, bf16[64,512]{1,0:T(8,128)(2,1)S(1)}, u32[]{:S(2)}, u32[]{:S(2)}) collective-permute-start(bf16[64,512]{1,0:T(8,128)(2,1)S(1)} %fusion.13), channel_id=1, source_target_pairs={{0,8},{1,9},{2,10},{3,11},{4,12},{5,13},{6,14},{7,15},{8,0},{9,1},... | collective-permute-start | bytes 196616 | tf_op jit(solution)/shard_map/ppermute | solution.py:170
  65.8 2.4 %collective-permute-done.6 = bf16[64,512]{1,0:T(8,128)(2,1)S(1)} collective-permute-done((bf16[64,512]{1,0:T(8,128)(2,1)S(1)}, bf16[64,512]{1,0:T(8,128)(2,1)S(1)}, u32[]{:S(2)}, u32[]{:S(2)}) %collective-permute-start.6) | collective-permute-done | bytes 65568 | tf_op jit(solution)/shard_map/ppermute | solution.py:170
  68.2 7.9 %collective-permute-start.8 = (bf16[64,1024]{1,0:T(8,128)(2,1)S(1)}, bf16[64,1024]{1,0:T(8,128)(2,1)S(1)}, u32[]{:S(2)}, u32[]{:S(2)}) collective-permute-start(bf16[64,1024]{1,0:T(8,128)(2,1)S(1)} %maximum_select_fusion), channel_id=1, source_target_pairs={{392,0},{425,1},{458,2},{491,3},{268,4},{333,5},{6,6},{71,7},{128,... | collective-permute-start | bytes 393224 | tf_op jit(solution)/shard_map/ppermute | solution.py:219
  76.1 1.9 %collective-permute-start.7 = (bf16[64,1024]{1,0:T(8,128)(2,1)S(1)}, bf16[64,1024]{1,0:T(8,128)(2,1)S(1)}, u32[]{:S(2)}, u32[]{:S(2)}) collective-permute-start(bf16[64,1024]{1,0:T(8,128)(2,1)S(1)} %maximum_select_fusion), channel_id=1, source_target_pairs={{408,0},{441,1},{474,2},{507,3},{284,4},{349,5},{22,6},{87,7},{144... | collective-permute-start | bytes 393224 | tf_op jit(solution)/shard_map/ppermute | solution.py:219
  78.9 5.9 %shard_map.115 = (bf16[2048,512]{1,0:T(8,128)(2,1)}, f32[2,512]{1,0:T(2,128)}) custom-call(s32[64,64]{1,0:T(8,128)} %refs_0_.5, bf16[512,128]{1,0:T(8,128)(2,1)} %get-tuple-element.33.refs_1_, bf16[2048,128]{1,0:T(8,128)(2,1)} %pad_maximum_fusion.refs_2_, bf16[1,2048]{1,0:T(2,128)(2,1)} %reshape.12.refs_3_), custom_call_target="tpu_custom_call" | custom-call | tf_op jit(solution)/shard_map/pallas_call | solution.py:104
  84.8 5.9 %shard_map.114 = (bf16[2048,512]{1,0:T(8,128)(2,1)}, f32[2,512]{1,0:T(2,128)}) custom-call(s32[64,64]{1,0:T(8,128)} %refs_0_.5, bf16[512,128]{1,0:T(8,128)(2,1)} %get-tuple-element.32.refs_1_, bf16[2048,128]{1,0:T(8,128)(2,1)} %pad_maximum_fusion.refs_2_, bf16[1,2048]{1,0:T(2,128)(2,1)} %reshape.12.refs_3_), custom_call_target="tpu_custom_call" | custom-call | tf_op jit(solution)/shard_map/pallas_call | solution.py:104
  90.7 2.2 %fusion = f32[64,512]{1,0:T(8,128)S(1)} fusion(bf16[2048,512]{1,0:T(8,128)(2,1)} %get-tuple-element.13, bf16[64,1024]{1,0:T(8,128)(2,1)S(1)} %get-tuple-element.31, bf16[64,1024]{1,0:T(8,128)(2,1)S(1)} %get-tuple-element.30), kind=kOutput, calls=%fused_computation.5 | convolution fusion | flops 134742016 | bytes 2490368 | tf_op jit(solution)/shard_map/dot_general | solution.py:293
  95.5 6.5 %collective-permute-done.10 = f32[66,512]{1,0:T(8,128)S(1)} collective-permute-done((f32[66,512]{1,0:T(8,128)S(1)}, f32[66,512]{1,0:T(8,128)S(1)}, u32[]{:S(2)}, u32[]{:S(2)}) %collective-permute-start.10) | collective-permute-done | bytes 135200 | tf_op jit(solution)/shard_map/ppermute | solution.py:159
  104.0 5.8 %collective-permute-done.11 = f32[66,512]{1,0:T(8,128)S(1)} collective-permute-done((f32[66,512]{1,0:T(8,128)S(1)}, f32[66,512]{1,0:T(8,128)S(1)}, u32[]{:S(2)}, u32[]{:S(2)}) %collective-permute-start.11) | collective-permute-done | bytes 135200 | tf_op jit(solution)/shard_map/ppermute | solution.py:163
  110.0 2.0 %collective-permute-start.12 = (f32[66,512]{1,0:T(8,128)S(1)}, f32[66,512]{1,0:T(8,128)S(1)}, u32[]{:S(2)}, u32[]{:S(2)}) collective-permute-start(f32[66,512]{1,0:T(8,128)S(1)} %pad_maximum_fusion.8), channel_id=1, source_target_pairs={{0,2},{1,3},{2,0},{3,1},{4,6},{5,7},{6,4},{7,5},{8,10},{9,11},{10,... | collective-permute-start | bytes 405512 | tf_op jit(solution)/shard_map/ppermute | solution.py:163
  112.0 5.9 %collective-permute-done.12 = f32[66,512]{1,0:T(8,128)S(1)} collective-permute-done((f32[66,512]{1,0:T(8,128)S(1)}, f32[66,512]{1,0:T(8,128)S(1)}, u32[]{:S(2)}, u32[]{:S(2)}) %collective-permute-start.12) | collective-permute-done | bytes 135200 | tf_op jit(solution)/shard_map/ppermute | solution.py:163
  118.0 6.8 %collective-permute-start.13 = (f32[66,512]{1,0:T(8,128)S(1)}, f32[66,512]{1,0:T(8,128)S(1)}, u32[]{:S(2)}, u32[]{:S(2)}) collective-permute-start(f32[66,512]{1,0:T(8,128)S(1)} %pad_maximum_fusion.9), channel_id=1, source_target_pairs={{0,6},{1,7},{2,4},{3,5},{4,2},{5,3},{6,0},{7,1},{8,14},{9,15},{10,... | collective-permute-start | bytes 405512 | tf_op jit(solution)/shard_map/ppermute | solution.py:163
  124.8 7.2 %collective-permute-done.13 = f32[66,512]{1,0:T(8,128)S(1)} collective-permute-done((f32[66,512]{1,0:T(8,128)S(1)}, f32[66,512]{1,0:T(8,128)S(1)}, u32[]{:S(2)}, u32[]{:S(2)}) %collective-permute-start.13) | collective-permute-done | bytes 135200 | tf_op jit(solution)/shard_map/ppermute | solution.py:163
  132.1 2.4 %collective-permute-start.14 = (bf16[64,512]{1,0:T(8,128)(2,1)S(1)}, bf16[64,512]{1,0:T(8,128)(2,1)S(1)}, u32[]{:S(2)}, u32[]{:S(2)}) collective-permute-start(bf16[64,512]{1,0:T(8,128)(2,1)S(1)} %fusion.11), channel_id=1, source_target_pairs={{0,8},{1,9},{2,10},{3,11},{4,12},{5,13},{6,14},{7,15},{8,0},{9,1},... | collective-permute-start | bytes 196616 | tf_op jit(solution)/shard_map/ppermute | solution.py:170
  134.5 3.7 %collective-permute-done.14 = bf16[64,512]{1,0:T(8,128)(2,1)S(1)} collective-permute-done((bf16[64,512]{1,0:T(8,128)(2,1)S(1)}, bf16[64,512]{1,0:T(8,128)(2,1)S(1)}, u32[]{:S(2)}, u32[]{:S(2)}) %collective-permute-start.14) | collective-permute-done | bytes 65568 | tf_op jit(solution)/shard_map/ppermute | solution.py:170
  (68 shorter events, 16.8 us)
Async XLA Ops:
  0.6 56.9 %copy-start.1 = (bf16[1024,128]{1,0:T(8,128)(2,1)S(1)}, bf16[1024,128]{1,0:T(8,128)(2,1)}, u32[]{:S(2)}) copy-start(bf16[1024,128]{1,0:T(8,128)(2,1)} %param.17) | copy-start | bytes 786436
  0.6 22.7 %collective-permute-start = (bf16[1024,128]{1,0:T(8,128)(2,1)}, bf16[1024,128]{1,0:T(8,128)(2,1)S(1)}, u32[]{:S(2)}, u32[]{:S(2)}) collective-permute-start(bf16[1024,128]{1,0:T(8,128)(2,1)} %refs_1_.1), channel_id=1, source_target_pairs={{392,0},{425,1},{458,2},{491,3},{268,4},{333,5},{6,6},{71,7},{128,... | collective-permute-start | bytes 786440 | tf_op jit(solution)/shard_map/ppermute | solution.py:271
  11.7 11.7 %collective-permute-start.1 = (bf16[2048]{0:T(1024)(128)(2,1)}, bf16[2048]{0:T(1024)(128)(2,1)S(1)}, u32[]{:S(2)}, u32[]{:S(2)}) collective-permute-start(bf16[2048]{0:T(1024)(128)(2,1)} %param.14), channel_id=1, source_target_pairs={{12,0},{13,1},{14,2},{15,3},{8,4},{10,5},{0,6},{2,7},{4,8},{5,9},{... | collective-permute-start | bytes 12296 | tf_op jit(solution)/shard_map/ppermute | solution.py:247
  23.3 38.6 %copy-start.3 = (bf16[1024,64]{0,1:T(8,128)(2,1)S(1)}, bf16[1024,64]{0,1:T(8,128)(2,1)}, u32[]{:S(2)}) copy-start(bf16[1024,64]{0,1:T(8,128)(2,1)} %param.15) | copy-start | bytes 393220
  24.3 11.4 %collective-permute-start.2 = (f32[66,512]{1,0:T(8,128)S(1)}, f32[66,512]{1,0:T(8,128)S(1)}, u32[]{:S(2)}, u32[]{:S(2)}) collective-permute-start(f32[66,512]{1,0:T(8,128)S(1)} %constant_dynamic-slice_fusion.1), channel_id=1, source_target_pairs={{0,8},{1,9},{2,10},{3,11},{4,12},{5,13},{6,14},{7,15},{8,0},{9,1},... | collective-permute-start | bytes 405512 | tf_op jit(solution)/shard_map/ppermute | solution.py:159
  37.5 7.0 %collective-permute-start.3 = (f32[66,512]{1,0:T(8,128)S(1)}, f32[66,512]{1,0:T(8,128)S(1)}, u32[]{:S(2)}, u32[]{:S(2)}) collective-permute-start(f32[66,512]{1,0:T(8,128)S(1)} %pad_maximum_fusion.4), channel_id=1, source_target_pairs={{0,1},{1,0},{2,3},{3,2},{4,5},{5,4},{6,7},{7,6},{8,9},{9,8},{10,11... | collective-permute-start | bytes 405512 | tf_op jit(solution)/shard_map/ppermute | solution.py:163
  44.7 8.0 %collective-permute-start.4 = (f32[66,512]{1,0:T(8,128)S(1)}, f32[66,512]{1,0:T(8,128)S(1)}, u32[]{:S(2)}, u32[]{:S(2)}) collective-permute-start(f32[66,512]{1,0:T(8,128)S(1)} %pad_maximum_fusion.5), channel_id=1, source_target_pairs={{0,2},{1,3},{2,0},{3,1},{4,6},{5,7},{6,4},{7,5},{8,10},{9,11},{10,... | collective-permute-start | bytes 405512 | tf_op jit(solution)/shard_map/ppermute | solution.py:163
  52.8 9.1 %collective-permute-start.5 = (f32[66,512]{1,0:T(8,128)S(1)}, f32[66,512]{1,0:T(8,128)S(1)}, u32[]{:S(2)}, u32[]{:S(2)}) collective-permute-start(f32[66,512]{1,0:T(8,128)S(1)} %pad_maximum_fusion.6), channel_id=1, source_target_pairs={{0,6},{1,7},{2,4},{3,5},{4,2},{5,3},{6,0},{7,1},{8,14},{9,15},{10,... | collective-permute-start | bytes 405512 | tf_op jit(solution)/shard_map/ppermute | solution.py:163
  58.9 6.9 %collective-permute-start.9 = (bf16[1024,128]{1,0:T(8,128)(2,1)S(1)}, bf16[1024,128]{1,0:T(8,128)(2,1)S(1)}, u32[]{:S(2)}, u32[]{:S(2)}) collective-permute-start(bf16[1024,128]{1,0:T(8,128)(2,1)S(1)} %collective-permute-done), channel_id=1, source_target_pairs={{16,0},{17,1},{18,2},{19,3},{20,4},{21,5},{22,6},{23,7},{24,8},{25... | collective-permute-start | bytes 786440 | tf_op jit(solution)/shard_map/ppermute | solution.py:280
  62.0 6.2 %collective-permute-start.6 = (bf16[64,512]{1,0:T(8,128)(2,1)S(1)}, bf16[64,512]{1,0:T(8,128)(2,1)S(1)}, u32[]{:S(2)}, u32[]{:S(2)}) collective-permute-start(bf16[64,512]{1,0:T(8,128)(2,1)S(1)} %fusion.13), channel_id=1, source_target_pairs={{0,8},{1,9},{2,10},{3,11},{4,12},{5,13},{6,14},{7,15},{8,0},{9,1},... | collective-permute-start | bytes 196616 | tf_op jit(solution)/shard_map/ppermute | solution.py:170
  68.2 24.7 %copy-start.2 = (bf16[64,1024]{1,0:T(8,128)(2,1)}, bf16[64,1024]{1,0:T(8,128)(2,1)S(1)}, u32[]{:S(2)}) copy-start(bf16[64,1024]{1,0:T(8,128)(2,1)S(1)} %maximum_select_fusion) | copy-start | bytes 393220
  68.2 22.4 %collective-permute-start.8 = (bf16[64,1024]{1,0:T(8,128)(2,1)S(1)}, bf16[64,1024]{1,0:T(8,128)(2,1)S(1)}, u32[]{:S(2)}, u32[]{:S(2)}) collective-permute-start(bf16[64,1024]{1,0:T(8,128)(2,1)S(1)} %maximum_select_fusion), channel_id=1, source_target_pairs={{392,0},{425,1},{458,2},{491,3},{268,4},{333,5},{6,6},{71,7},{128,... | collective-permute-start | bytes 393224 | tf_op jit(solution)/shard_map/ppermute | solution.py:219
  76.1 14.6 %collective-permute-start.7 = (bf16[64,1024]{1,0:T(8,128)(2,1)S(1)}, bf16[64,1024]{1,0:T(8,128)(2,1)S(1)}, u32[]{:S(2)}, u32[]{:S(2)}) collective-permute-start(bf16[64,1024]{1,0:T(8,128)(2,1)S(1)} %maximum_select_fusion), channel_id=1, source_target_pairs={{408,0},{441,1},{474,2},{507,3},{284,4},{349,5},{22,6},{87,7},{144... | collective-permute-start | bytes 393224 | tf_op jit(solution)/shard_map/ppermute | solution.py:219
  90.7 2.3 %copy-start = (bf16[2048,512]{1,0:T(8,128)(2,1)S(1)}, bf16[2048,512]{1,0:T(8,128)(2,1)}, u32[]{:S(2)}) copy-start(bf16[2048,512]{1,0:T(8,128)(2,1)} %get-tuple-element.12) | copy-start | bytes 6291460
  90.7 2.7 %copy-start.5 = (f32[2,512]{1,0:T(2,128)S(1)}, f32[2,512]{1,0:T(2,128)}, u32[]{:S(2)}) copy-start(f32[2,512]{1,0:T(2,128)} %get-tuple-element.15) | copy-start | bytes 12292
  90.7 2.7 %copy-start.6 = (f32[2,512]{1,0:T(2,128)S(1)}, f32[2,512]{1,0:T(2,128)}, u32[]{:S(2)}) copy-start(f32[2,512]{1,0:T(2,128)} %get-tuple-element.14) | copy-start | bytes 12292
  93.4 38.6 %copy-start.4 = (bf16[1024,64]{0,1:T(8,128)(2,1)S(1)}, bf16[1024,64]{0,1:T(8,128)(2,1)}, u32[]{:S(2)}) copy-start(bf16[1024,64]{0,1:T(8,128)(2,1)} %param.18) | copy-start | bytes 393220
  93.5 8.4 %collective-permute-start.10 = (f32[66,512]{1,0:T(8,128)S(1)}, f32[66,512]{1,0:T(8,128)S(1)}, u32[]{:S(2)}, u32[]{:S(2)}) collective-permute-start(f32[66,512]{1,0:T(8,128)S(1)} %constant_dynamic-slice_fusion), channel_id=1, source_target_pairs={{0,8},{1,9},{2,10},{3,11},{4,12},{5,13},{6,14},{7,15},{8,0},{9,1},... | collective-permute-start | bytes 405512 | tf_op jit(solution)/shard_map/ppermute | solution.py:159
  102.1 7.8 %collective-permute-start.11 = (f32[66,512]{1,0:T(8,128)S(1)}, f32[66,512]{1,0:T(8,128)S(1)}, u32[]{:S(2)}, u32[]{:S(2)}) collective-permute-start(f32[66,512]{1,0:T(8,128)S(1)} %pad_maximum_fusion.7), channel_id=1, source_target_pairs={{0,1},{1,0},{2,3},{3,2},{4,5},{5,4},{6,7},{7,6},{8,9},{9,8},{10,11... | collective-permute-start | bytes 405512 | tf_op jit(solution)/shard_map/ppermute | solution.py:163
  110.0 7.9 %collective-permute-start.12 = (f32[66,512]{1,0:T(8,128)S(1)}, f32[66,512]{1,0:T(8,128)S(1)}, u32[]{:S(2)}, u32[]{:S(2)}) collective-permute-start(f32[66,512]{1,0:T(8,128)S(1)} %pad_maximum_fusion.8), channel_id=1, source_target_pairs={{0,2},{1,3},{2,0},{3,1},{4,6},{5,7},{6,4},{7,5},{8,10},{9,11},{10,... | collective-permute-start | bytes 405512 | tf_op jit(solution)/shard_map/ppermute | solution.py:163
  118.0 14.0 %collective-permute-start.13 = (f32[66,512]{1,0:T(8,128)S(1)}, f32[66,512]{1,0:T(8,128)S(1)}, u32[]{:S(2)}, u32[]{:S(2)}) collective-permute-start(f32[66,512]{1,0:T(8,128)S(1)} %pad_maximum_fusion.9), channel_id=1, source_target_pairs={{0,6},{1,7},{2,4},{3,5},{4,2},{5,3},{6,0},{7,1},{8,14},{9,15},{10,... | collective-permute-start | bytes 405512 | tf_op jit(solution)/shard_map/ppermute | solution.py:163
  132.1 6.2 %collective-permute-start.14 = (bf16[64,512]{1,0:T(8,128)(2,1)S(1)}, bf16[64,512]{1,0:T(8,128)(2,1)S(1)}, u32[]{:S(2)}, u32[]{:S(2)}) collective-permute-start(bf16[64,512]{1,0:T(8,128)(2,1)S(1)} %fusion.11), channel_id=1, source_target_pairs={{0,8},{1,9},{2,10},{3,11},{4,12},{5,13},{6,14},{7,15},{8,0},{9,1},... | collective-permute-start | bytes 196616 | tf_op jit(solution)/shard_map/ppermute | solution.py:170

commit v16 on v15

--- a/solution.py
+++ b/solution.py
@@ -273,12 +273,8 @@
     partials = date_partials_kernel(
         states_mid, states_late, offset_late, values_late.T, mask_mid, mid_col_base
     )
-    partials, own_sources, mid_offsets = lax.optimization_barrier(
-        (partials, own_sources, mid_offsets)
-    )
-    mid_sources = regroup_order(
-        [own_sources, lax.ppermute(own_sources, ("tgt", "src"), swap)]
-    )
+    swapped = lax.ppermute(own_sources, ("tgt", "src"), swap)
+    mid_sources = regroup_order([own_sources, swapped])
     early_parts = []
     for row_tile in range(states_early.shape[0] // BLOCK):
         rows = states_early[row_tile * BLOCK : (row_tile + 1) * BLOCK]

time: 140 us -> 134 us (0.957)
  the two profiles are of different devices: /device:TPU:10 before, /device:TPU:6 now
where the time goes in v16:
time: 134 us; the launch traced here: 132 us
  starting transfers between devices  64 us (48%)
  waiting for transfers between devices  36 us (27%)
  Pallas kernels  20.1 us (15%)
  other arithmetic  3.94 us (3%)
  local copies, waits for them, and re-layouts  3.69 us (3%)
  matrix products  2.67 us (2%)
    ppermute x6, starting transfers between devices, finish(): got = lax.ppermute(packed, 'src', exchange_perm(src_size, partner))  28.8 us
    ppermute x6, waiting for transfers between devices, finish(): got = lax.ppermute(packed, 'src', exchange_perm(src_size, partner))  20.3 us
    pallas_call x2, Pallas kernels, date_weights_kernel(): pl.pallas_call(kernel, out_shape=(jax.ShapeDtypeStruct((cols, rows), jnp....  11.7 us
    ppermute x1, starting transfers between devices, per_device(): own_sources = lax.ppermute(states_mid, ('tgt', 'src'), direct)  10.3 us
    ppermute x2, starting transfers between devices, finish(): got = lax.ppermute(value, 'src', xor_perm(src_size, bit))  8.99 us
    pallas_call x1, Pallas kernels, date_partials_kernel(): pl.pallas_call(kernel, out_shape=jax.ShapeDtypeStruct((width + 2, rows),...  8.4 us
    ppermute x2, starting transfers between devices, finish(): got = lax.ppermute(send, 'src', xor_perm(src_size, bit))  8.22 us
    ppermute x2, waiting for transfers between devices, finish(): got = lax.ppermute(send, 'src', xor_perm(src_size, bit))  6.94 us
  transfers between devices with their start and end apart: 15, of which 10 were waited for; matrix products, arithmetic and copies ran while one was open for 2% of the time, Pallas kernels for 9%

profile of v16, /device:TPU:6, one launch (start us, length us, event | category | flops | bytes accessed | tf_op | source)
XLA Modules:
  0.0 131.5 jit_solution(3962664734915850024)
XLA Ops:
  2.0 8.4 %shard_map.113 = f32[66,1024]{1,0:T(8,128)} custom-call(s32[64,64]{1,0:T(8,128)} %refs_0_.3, bf16[1024,128]{1,0:T(8,128)(2,1)} %refs_1_.1, bf16[2048,128]{1,0:T(8,128)(2,1)} %refs_2_.1, bf16[1,2048]{1,0:T(2,128)(2,1)} %reshape.11.refs_3_, bf16[64,2048]{1,0:T(8,128)(2,1)} %bitcast.28), custom_call_target="tpu_custom_call" | custom-call | tf_op jit(solution)/shard_map/pallas_call | solution.py:56
  11.4 4.3 %collective-permute-start = (f32[66,512]{1,0:T(8,128)S(1)}, f32[66,512]{1,0:T(8,128)S(1)}, u32[]{:S(2)}, u32[]{:S(2)}) collective-permute-start(f32[66,512]{1,0:T(8,128)S(1)} %constant_dynamic-slice_fusion.1), channel_id=1, source_target_pairs={{0,8},{1,9},{2,10},{3,11},{4,12},{5,13},{6,14},{7,15},{8,0},{9,1},... | collective-permute-start | bytes 405512 | tf_op jit(solution)/shard_map/ppermute | solution.py:159
  15.7 3.8 %collective-permute-done = f32[66,512]{1,0:T(8,128)S(1)} collective-permute-done((f32[66,512]{1,0:T(8,128)S(1)}, f32[66,512]{1,0:T(8,128)S(1)}, u32[]{:S(2)}, u32[]{:S(2)}) %collective-permute-start) | collective-permute-done | bytes 135200 | tf_op jit(solution)/shard_map/ppermute | solution.py:159
  21.3 3.5 %collective-permute-start.1 = (f32[66,512]{1,0:T(8,128)S(1)}, f32[66,512]{1,0:T(8,128)S(1)}, u32[]{:S(2)}, u32[]{:S(2)}) collective-permute-start(f32[66,512]{1,0:T(8,128)S(1)} %pad_maximum_fusion.4), channel_id=1, source_target_pairs={{0,1},{1,0},{2,3},{3,2},{4,5},{5,4},{6,7},{7,6},{8,9},{9,8},{10,11... | collective-permute-start | bytes 405512 | tf_op jit(solution)/shard_map/ppermute | solution.py:163
  24.8 3.5 %collective-permute-done.1 = f32[66,512]{1,0:T(8,128)S(1)} collective-permute-done((f32[66,512]{1,0:T(8,128)S(1)}, f32[66,512]{1,0:T(8,128)S(1)}, u32[]{:S(2)}, u32[]{:S(2)}) %collective-permute-start.1) | collective-permute-done | bytes 135200 | tf_op jit(solution)/shard_map/ppermute | solution.py:163
  28.4 4.5 %collective-permute-start.2 = (f32[66,512]{1,0:T(8,128)S(1)}, f32[66,512]{1,0:T(8,128)S(1)}, u32[]{:S(2)}, u32[]{:S(2)}) collective-permute-start(f32[66,512]{1,0:T(8,128)S(1)} %pad_maximum_fusion.5), channel_id=1, source_target_pairs={{0,2},{1,3},{2,0},{3,1},{4,6},{5,7},{6,4},{7,5},{8,10},{9,11},{10,... | collective-permute-start | bytes 405512 | tf_op jit(solution)/shard_map/ppermute | solution.py:163
  32.9 10.3 %collective-permute-start.7 = (bf16[1024,128]{1,0:T(8,128)(2,1)S(1)}, bf16[1024,128]{1,0:T(8,128)(2,1)S(1)}, u32[]{:S(2)}, u32[]{:S(2)}) collective-permute-start(bf16[1024,128]{1,0:T(8,128)(2,1)S(1)} %copy-done.2), channel_id=1, source_target_pairs={{392,0},{425,1},{458,2},{491,3},{268,4},{333,5},{6,6},{71,7},{128,... | collective-permute-start | bytes 786440 | tf_op jit(solution)/shard_map/ppermute | solution.py:271
  43.2 1.9 %collective-permute-start.9 = (bf16[2048]{0:T(1024)(128)(2,1)S(1)}, bf16[2048]{0:T(1024)(128)(2,1)S(1)}, u32[]{:S(2)}, u32[]{:S(2)}) collective-permute-start(bf16[2048]{0:T(1024)(128)(2,1)S(1)} %copy-done.8), channel_id=1, source_target_pairs={{12,0},{13,1},{14,2},{15,3},{8,4},{10,5},{0,6},{2,7},{4,8},{5,9},{... | collective-permute-start | bytes 12296 | tf_op jit(solution)/shard_map/ppermute | solution.py:247
  47.9 2.9 %collective-permute-done.9 = bf16[2048]{0:T(1024)(128)(2,1)S(1)} collective-permute-done((bf16[2048]{0:T(1024)(128)(2,1)S(1)}, bf16[2048]{0:T(1024)(128)(2,1)S(1)}, u32[]{:S(2)}, u32[]{:S(2)}) %collective-permute-start.9) | collective-permute-done | bytes 4128 | tf_op jit(solution)/shard_map/ppermute | solution.py:247
  54.6 6.5 %collective-permute-start.4 = (bf16[64,512]{1,0:T(8,128)(2,1)S(1)}, bf16[64,512]{1,0:T(8,128)(2,1)S(1)}, u32[]{:S(2)}, u32[]{:S(2)}) collective-permute-start(bf16[64,512]{1,0:T(8,128)(2,1)S(1)} %fusion.13), channel_id=1, source_target_pairs={{0,8},{1,9},{2,10},{3,11},{4,12},{5,13},{6,14},{7,15},{8,0},{9,1},... | collective-permute-start | bytes 196616 | tf_op jit(solution)/shard_map/ppermute | solution.py:170
  61.1 2.2 %collective-permute-done.4 = bf16[64,512]{1,0:T(8,128)(2,1)S(1)} collective-permute-done((bf16[64,512]{1,0:T(8,128)(2,1)S(1)}, bf16[64,512]{1,0:T(8,128)(2,1)S(1)}, u32[]{:S(2)}, u32[]{:S(2)}) %collective-permute-start.4) | collective-permute-done | bytes 65568 | tf_op jit(solution)/shard_map/ppermute | solution.py:170
  68.1 5.9 %shard_map.115 = (bf16[2048,512]{1,0:T(8,128)(2,1)}, f32[2,512]{1,0:T(2,128)}) custom-call(s32[64,64]{1,0:T(8,128)} %refs_0_.5, bf16[512,128]{1,0:T(8,128)(2,1)} %get-tuple-element.27.refs_1_, bf16[2048,128]{1,0:T(8,128)(2,1)} %pad_maximum_fusion.refs_2_, bf16[1,2048]{1,0:T(2,128)(2,1)} %reshape.12.refs_3_), custom_call_target="tpu_custom_call" | custom-call | tf_op jit(solution)/shard_map/pallas_call | solution.py:104
  73.9 5.9 %shard_map.114 = (bf16[2048,512]{1,0:T(8,128)(2,1)}, f32[2,512]{1,0:T(2,128)}) custom-call(s32[64,64]{1,0:T(8,128)} %refs_0_.5, bf16[512,128]{1,0:T(8,128)(2,1)} %get-tuple-element.26.refs_1_, bf16[2048,128]{1,0:T(8,128)(2,1)} %pad_maximum_fusion.refs_2_, bf16[1,2048]{1,0:T(2,128)(2,1)} %reshape.12.refs_3_), custom_call_target="tpu_custom_call" | custom-call | tf_op jit(solution)/shard_map/pallas_call | solution.py:104
  79.9 2.2 %fusion = f32[64,512]{1,0:T(8,128)S(1)} fusion(bf16[2048,512]{1,0:T(8,128)(2,1)} %get-tuple-element.7, bf16[64,1024]{1,0:T(8,128)(2,1)S(1)} %get-tuple-element.25, bf16[64,1024]{1,0:T(8,128)(2,1)S(1)} %get-tuple-element.24), kind=kOutput, calls=%fused_computation.5 | convolution fusion | flops 134742016 | bytes 2490368 | tf_op jit(solution)/shard_map/dot_general | solution.py:289
  82.7 3.9 %collective-permute-start.10 = (f32[66,512]{1,0:T(8,128)S(1)}, f32[66,512]{1,0:T(8,128)S(1)}, u32[]{:S(2)}, u32[]{:S(2)}) collective-permute-start(f32[66,512]{1,0:T(8,128)S(1)} %constant_dynamic-slice_fusion), channel_id=1, source_target_pairs={{0,8},{1,9},{2,10},{3,11},{4,12},{5,13},{6,14},{7,15},{8,0},{9,1},... | collective-permute-start | bytes 405512 | tf_op jit(solution)/shard_map/ppermute | solution.py:159
  86.6 3.1 %collective-permute-done.10 = f32[66,512]{1,0:T(8,128)S(1)} collective-permute-done((f32[66,512]{1,0:T(8,128)S(1)}, f32[66,512]{1,0:T(8,128)S(1)}, u32[]{:S(2)}, u32[]{:S(2)}) %collective-permute-start.10) | collective-permute-done | bytes 135200 | tf_op jit(solution)/shard_map/ppermute | solution.py:159
  89.9 4.8 %collective-permute-start.11 = (f32[66,512]{1,0:T(8,128)S(1)}, f32[66,512]{1,0:T(8,128)S(1)}, u32[]{:S(2)}, u32[]{:S(2)}) collective-permute-start(f32[66,512]{1,0:T(8,128)S(1)} %pad_maximum_fusion.7), channel_id=1, source_target_pairs={{0,1},{1,0},{2,3},{3,2},{4,5},{5,4},{6,7},{7,6},{8,9},{9,8},{10,11... | collective-permute-start | bytes 405512 | tf_op jit(solution)/shard_map/ppermute | solution.py:163
  94.7 3.1 %collective-permute-done.11 = f32[66,512]{1,0:T(8,128)S(1)} collective-permute-done((f32[66,512]{1,0:T(8,128)S(1)}, f32[66,512]{1,0:T(8,128)S(1)}, u32[]{:S(2)}, u32[]{:S(2)}) %collective-permute-start.11) | collective-permute-done | bytes 135200 | tf_op jit(solution)/shard_map/ppermute | solution.py:163
  97.9 5.3 %collective-permute-start.12 = (f32[66,512]{1,0:T(8,128)S(1)}, f32[66,512]{1,0:T(8,128)S(1)}, u32[]{:S(2)}, u32[]{:S(2)}) collective-permute-start(f32[66,512]{1,0:T(8,128)S(1)} %pad_maximum_fusion.8), channel_id=1, source_target_pairs={{0,2},{1,3},{2,0},{3,1},{4,6},{5,7},{6,4},{7,5},{8,10},{9,11},{10,... | collective-permute-start | bytes 405512 | tf_op jit(solution)/shard_map/ppermute | solution.py:163
  103.2 6.7 %collective-permute-done.12 = f32[66,512]{1,0:T(8,128)S(1)} collective-permute-done((f32[66,512]{1,0:T(8,128)S(1)}, f32[66,512]{1,0:T(8,128)S(1)}, u32[]{:S(2)}, u32[]{:S(2)}) %collective-permute-start.12) | collective-permute-done | bytes 135200 | tf_op jit(solution)/shard_map/ppermute | solution.py:163
  110.0 8.8 %collective-permute-start.13 = (f32[66,512]{1,0:T(8,128)S(1)}, f32[66,512]{1,0:T(8,128)S(1)}, u32[]{:S(2)}, u32[]{:S(2)}) collective-permute-start(f32[66,512]{1,0:T(8,128)S(1)} %pad_maximum_fusion.9), channel_id=1, source_target_pairs={{0,6},{1,7},{2,4},{3,5},{4,2},{5,3},{6,0},{7,1},{8,14},{9,15},{10,... | collective-permute-start | bytes 405512 | tf_op jit(solution)/shard_map/ppermute | solution.py:163
  118.7 5.8 %collective-permute-done.13 = f32[66,512]{1,0:T(8,128)S(1)} collective-permute-done((f32[66,512]{1,0:T(8,128)S(1)}, f32[66,512]{1,0:T(8,128)S(1)}, u32[]{:S(2)}, u32[]{:S(2)}) %collective-permute-start.13) | collective-permute-done | bytes 135200 | tf_op jit(solution)/shard_map/ppermute | solution.py:163
  124.7 2.5 %collective-permute-start.14 = (bf16[64,512]{1,0:T(8,128)(2,1)S(1)}, bf16[64,512]{1,0:T(8,128)(2,1)S(1)}, u32[]{:S(2)}, u32[]{:S(2)}) collective-permute-start(bf16[64,512]{1,0:T(8,128)(2,1)S(1)} %fusion.11), channel_id=1, source_target_pairs={{0,8},{1,9},{2,10},{3,11},{4,12},{5,13},{6,14},{7,15},{8,0},{9,1},... | collective-permute-start | bytes 196616 | tf_op jit(solution)/shard_map/ppermute | solution.py:170
  127.2 3.6 %collective-permute-done.14 = bf16[64,512]{1,0:T(8,128)(2,1)S(1)} collective-permute-done((bf16[64,512]{1,0:T(8,128)(2,1)S(1)}, bf16[64,512]{1,0:T(8,128)(2,1)S(1)}, u32[]{:S(2)}, u32[]{:S(2)}) %collective-permute-start.14) | collective-permute-done | bytes 65568 | tf_op jit(solution)/shard_map/ppermute | solution.py:170
  (72 shorter events, 16.9 us)
Async XLA Ops:
  0.6 32.3 %copy-start.2 = (bf16[1024,128]{1,0:T(8,128)(2,1)S(1)}, bf16[1024,128]{1,0:T(8,128)(2,1)}, u32[]{:S(2)}) copy-start(bf16[1024,128]{1,0:T(8,128)(2,1)} %refs_1_.1) | copy-start | bytes 786436
  0.6 42.6 %copy-start.8 = (bf16[2048]{0:T(1024)(128)(2,1)S(1)}, bf16[2048]{0:T(1024)(128)(2,1)}, u32[]{:S(2)}) copy-start(bf16[2048]{0:T(1024)(128)(2,1)} %param.14) | copy-start | bytes 12292
  0.7 46.5 %copy-start.1 = (bf16[1024,128]{1,0:T(8,128)(2,1)S(1)}, bf16[1024,128]{1,0:T(8,128)(2,1)}, u32[]{:S(2)}) copy-start(bf16[1024,128]{1,0:T(8,128)(2,1)} %param.17) | copy-start | bytes 786436
  10.4 44.2 %copy-start.4 = (bf16[1024,64]{0,1:T(8,128)(2,1)S(1)}, bf16[1024,64]{0,1:T(8,128)(2,1)}, u32[]{:S(2)}) copy-start(bf16[1024,64]{0,1:T(8,128)(2,1)} %param.15) | copy-start | bytes 393220
  11.4 8.1 %collective-permute-start = (f32[66,512]{1,0:T(8,128)S(1)}, f32[66,512]{1,0:T(8,128)S(1)}, u32[]{:S(2)}, u32[]{:S(2)}) collective-permute-start(f32[66,512]{1,0:T(8,128)S(1)} %constant_dynamic-slice_fusion.1), channel_id=1, source_target_pairs={{0,8},{1,9},{2,10},{3,11},{4,12},{5,13},{6,14},{7,15},{8,0},{9,1},... | collective-permute-start | bytes 405512 | tf_op jit(solution)/shard_map/ppermute | solution.py:159
  21.3 7.0 %collective-permute-start.1 = (f32[66,512]{1,0:T(8,128)S(1)}, f32[66,512]{1,0:T(8,128)S(1)}, u32[]{:S(2)}, u32[]{:S(2)}) collective-permute-start(f32[66,512]{1,0:T(8,128)S(1)} %pad_maximum_fusion.4), channel_id=1, source_target_pairs={{0,1},{1,0},{2,3},{3,2},{4,5},{5,4},{6,7},{7,6},{8,9},{9,8},{10,11... | collective-permute-start | bytes 405512 | tf_op jit(solution)/shard_map/ppermute | solution.py:163
  28.4 16.7 %collective-permute-start.2 = (f32[66,512]{1,0:T(8,128)S(1)}, f32[66,512]{1,0:T(8,128)S(1)}, u32[]{:S(2)}, u32[]{:S(2)}) collective-permute-start(f32[66,512]{1,0:T(8,128)S(1)} %pad_maximum_fusion.5), channel_id=1, source_target_pairs={{0,2},{1,3},{2,0},{3,1},{4,6},{5,7},{6,4},{7,5},{8,10},{9,11},{10,... | collective-permute-start | bytes 405512 | tf_op jit(solution)/shard_map/ppermute | solution.py:163
  32.9 18.5 %collective-permute-start.7 = (bf16[1024,128]{1,0:T(8,128)(2,1)S(1)}, bf16[1024,128]{1,0:T(8,128)(2,1)S(1)}, u32[]{:S(2)}, u32[]{:S(2)}) collective-permute-start(bf16[1024,128]{1,0:T(8,128)(2,1)S(1)} %copy-done.2), channel_id=1, source_target_pairs={{392,0},{425,1},{458,2},{491,3},{268,4},{333,5},{6,6},{71,7},{128,... | collective-permute-start | bytes 786440 | tf_op jit(solution)/shard_map/ppermute | solution.py:271
  43.2 7.6 %collective-permute-start.9 = (bf16[2048]{0:T(1024)(128)(2,1)S(1)}, bf16[2048]{0:T(1024)(128)(2,1)S(1)}, u32[]{:S(2)}, u32[]{:S(2)}) collective-permute-start(bf16[2048]{0:T(1024)(128)(2,1)S(1)} %copy-done.8), channel_id=1, source_target_pairs={{12,0},{13,1},{14,2},{15,3},{8,4},{10,5},{0,6},{2,7},{4,8},{5,9},{... | collective-permute-start | bytes 12296 | tf_op jit(solution)/shard_map/ppermute | solution.py:247
  45.3 9.2 %collective-permute-start.3 = (f32[66,512]{1,0:T(8,128)S(1)}, f32[66,512]{1,0:T(8,128)S(1)}, u32[]{:S(2)}, u32[]{:S(2)}) collective-permute-start(f32[66,512]{1,0:T(8,128)S(1)} %pad_maximum_fusion.6), channel_id=1, source_target_pairs={{0,6},{1,7},{2,4},{3,5},{4,2},{5,3},{6,0},{7,1},{8,14},{9,15},{10,... | collective-permute-start | bytes 405512 | tf_op jit(solution)/shard_map/ppermute | solution.py:163
  51.4 9.6 %collective-permute-start.8 = (bf16[1024,128]{1,0:T(8,128)(2,1)S(1)}, bf16[1024,128]{1,0:T(8,128)(2,1)S(1)}, u32[]{:S(2)}, u32[]{:S(2)}) collective-permute-start(bf16[1024,128]{1,0:T(8,128)(2,1)S(1)} %collective-permute-done.7), channel_id=1, source_target_pairs={{16,0},{17,1},{18,2},{19,3},{20,4},{21,5},{22,6},{23,7},{24,8},{25... | collective-permute-start | bytes 786440 | tf_op jit(solution)/shard_map/ppermute | solution.py:276
  54.6 8.7 %collective-permute-start.4 = (bf16[64,512]{1,0:T(8,128)(2,1)S(1)}, bf16[64,512]{1,0:T(8,128)(2,1)S(1)}, u32[]{:S(2)}, u32[]{:S(2)}) collective-permute-start(bf16[64,512]{1,0:T(8,128)(2,1)S(1)} %fusion.13), channel_id=1, source_target_pairs={{0,8},{1,9},{2,10},{3,11},{4,12},{5,13},{6,14},{7,15},{8,0},{9,1},... | collective-permute-start | bytes 196616 | tf_op jit(solution)/shard_map/ppermute | solution.py:170
  63.3 18.7 %copy-start.3 = (bf16[64,1024]{1,0:T(8,128)(2,1)}, bf16[64,1024]{1,0:T(8,128)(2,1)S(1)}, u32[]{:S(2)}) copy-start(bf16[64,1024]{1,0:T(8,128)(2,1)S(1)} %maximum_select_fusion) | copy-start | bytes 393220
  63.4 16.5 %collective-permute-start.6 = (bf16[64,1024]{1,0:T(8,128)(2,1)S(1)}, bf16[64,1024]{1,0:T(8,128)(2,1)S(1)}, u32[]{:S(2)}, u32[]{:S(2)}) collective-permute-start(bf16[64,1024]{1,0:T(8,128)(2,1)S(1)} %maximum_select_fusion), channel_id=1, source_target_pairs={{392,0},{425,1},{458,2},{491,3},{268,4},{333,5},{6,6},{71,7},{128,... | collective-permute-start | bytes 393224 | tf_op jit(solution)/shard_map/ppermute | solution.py:219
  65.3 14.5 %collective-permute-start.5 = (bf16[64,1024]{1,0:T(8,128)(2,1)S(1)}, bf16[64,1024]{1,0:T(8,128)(2,1)S(1)}, u32[]{:S(2)}, u32[]{:S(2)}) collective-permute-start(bf16[64,1024]{1,0:T(8,128)(2,1)S(1)} %maximum_select_fusion), channel_id=1, source_target_pairs={{408,0},{441,1},{474,2},{507,3},{284,4},{349,5},{22,6},{87,7},{144... | collective-permute-start | bytes 393224 | tf_op jit(solution)/shard_map/ppermute | solution.py:219
  79.8 2.3 %copy-start = (bf16[2048,512]{1,0:T(8,128)(2,1)S(1)}, bf16[2048,512]{1,0:T(8,128)(2,1)}, u32[]{:S(2)}) copy-start(bf16[2048,512]{1,0:T(8,128)(2,1)} %get-tuple-element.6) | copy-start | bytes 6291460
  79.8 2.7 %copy-start.6 = (f32[2,512]{1,0:T(2,128)S(1)}, f32[2,512]{1,0:T(2,128)}, u32[]{:S(2)}) copy-start(f32[2,512]{1,0:T(2,128)} %get-tuple-element.9) | copy-start | bytes 12292
  79.9 2.7 %copy-start.7 = (f32[2,512]{1,0:T(2,128)S(1)}, f32[2,512]{1,0:T(2,128)}, u32[]{:S(2)}) copy-start(f32[2,512]{1,0:T(2,128)} %get-tuple-element.8) | copy-start | bytes 12292
  82.6 42.1 %copy-start.5 = (bf16[1024,64]{0,1:T(8,128)(2,1)S(1)}, bf16[1024,64]{0,1:T(8,128)(2,1)}, u32[]{:S(2)}) copy-start(bf16[1024,64]{0,1:T(8,128)(2,1)} %param.18) | copy-start | bytes 393220
  82.7 7.0 %collective-permute-start.10 = (f32[66,512]{1,0:T(8,128)S(1)}, f32[66,512]{1,0:T(8,128)S(1)}, u32[]{:S(2)}, u32[]{:S(2)}) collective-permute-start(f32[66,512]{1,0:T(8,128)S(1)} %constant_dynamic-slice_fusion), channel_id=1, source_target_pairs={{0,8},{1,9},{2,10},{3,11},{4,12},{5,13},{6,14},{7,15},{8,0},{9,1},... | collective-permute-start | bytes 405512 | tf_op jit(solution)/shard_map/ppermute | solution.py:159
  89.9 7.9 %collective-permute-start.11 = (f32[66,512]{1,0:T(8,128)S(1)}, f32[66,512]{1,0:T(8,128)S(1)}, u32[]{:S(2)}, u32[]{:S(2)}) collective-permute-start(f32[66,512]{1,0:T(8,128)S(1)} %pad_maximum_fusion.7), channel_id=1, source_target_pairs={{0,1},{1,0},{2,3},{3,2},{4,5},{5,4},{6,7},{7,6},{8,9},{9,8},{10,11... | collective-permute-start | bytes 405512 | tf_op jit(solution)/shard_map/ppermute | solution.py:163
  97.9 12.0 %collective-permute-start.12 = (f32[66,512]{1,0:T(8,128)S(1)}, f32[66,512]{1,0:T(8,128)S(1)}, u32[]{:S(2)}, u32[]{:S(2)}) collective-permute-start(f32[66,512]{1,0:T(8,128)S(1)} %pad_maximum_fusion.8), channel_id=1, source_target_pairs={{0,2},{1,3},{2,0},{3,1},{4,6},{5,7},{6,4},{7,5},{8,10},{9,11},{10,... | collective-permute-start | bytes 405512 | tf_op jit(solution)/shard_map/ppermute | solution.py:163
  110.0 14.6 %collective-permute-start.13 = (f32[66,512]{1,0:T(8,128)S(1)}, f32[66,512]{1,0:T(8,128)S(1)}, u32[]{:S(2)}, u32[]{:S(2)}) collective-permute-start(f32[66,512]{1,0:T(8,128)S(1)} %pad_maximum_fusion.9), channel_id=1, source_target_pairs={{0,6},{1,7},{2,4},{3,5},{4,2},{5,3},{6,0},{7,1},{8,14},{9,15},{10,... | collective-permute-start | bytes 405512 | tf_op jit(solution)/shard_map/ppermute | solution.py:163
  124.7 6.2 %collective-permute-start.14 = (bf16[64,512]{1,0:T(8,128)(2,1)S(1)}, bf16[64,512]{1,0:T(8,128)(2,1)S(1)}, u32[]{:S(2)}, u32[]{:S(2)}) collective-permute-start(bf16[64,512]{1,0:T(8,128)(2,1)S(1)} %fusion.11), channel_id=1, source_target_pairs={{0,8},{1,9},{2,10},{3,11},{4,12},{5,13},{6,14},{7,15},{8,0},{9,1},... | collective-permute-start | bytes 196616 | tf_op jit(solution)/shard_map/ppermute | solution.py:170

commit v17 on v15

--- a/solution.py
+++ b/solution.py
@@ -206,19 +206,6 @@
     return ((z_hi + dz) % 4) * x_count + (x + dx) % x_count
 
 
-def regroup(block_rows):
-    tgt_size = lax.axis_size("tgt")
-    src_size = lax.axis_size("src")
-    perms = ([], [])
-    for t in range(tgt_size):
-        for s in range(src_size):
-            pair = source_pair(t, s)
-            for flip in range(2):
-                u = 2 * pair + ((t % 2) ^ flip)
-                perms[flip].append((lin(u, holder(s)), lin(t, s)))
-    return [lax.ppermute(block_rows, ("tgt", "src"), p) for p in perms]
-
-
 def forward_perms():
     tgt_size = lax.axis_size("tgt")
     src_size = lax.axis_size("src")
@@ -288,10 +275,18 @@
             )
         )
     value_mid_t = finish(partials, exercise_mid)
-    mid_values_t = regroup_order(regroup(value_mid_t), axis=1)
-    early_weighted = jnp.concatenate(
-        [jnp.dot(mid_values_t, w, preferred_element_type=jnp.float32) for w, _ in early_parts], 1
-    )
+    own_values = lax.ppermute(value_mid_t, ("tgt", "src"), direct)
+    other_values = lax.ppermute(own_values, ("tgt", "src"), swap)
+    half = own_values.shape[1]
+    odd = lax.axis_index("tgt") % 2
+
+    def weighted_part(w):
+        own_w = lax.dynamic_slice_in_dim(w, odd * half, half, 0)
+        other_w = lax.dynamic_slice_in_dim(w, (1 - odd) * half, half, 0)
+        own_part = jnp.dot(own_values, own_w, preferred_element_type=jnp.float32)
+        return own_part + jnp.dot(other_values, other_w, preferred_element_type=jnp.float32)
+
+    early_weighted = jnp.concatenate([weighted_part(w) for w, _ in early_parts], 1)
     early_stats = jnp.concatenate([s for _, s in early_parts], 1)
     value_early_t = finish(jnp.concatenate([early_weighted, early_stats], 0), exercise_early)
     value_mid, value_early = value_mid_t.T, value_early_t.T

time: 140 us -> 142 us (1.014)
  the two profiles are of different devices: /device:TPU:10 before, /device:TPU:16 now
where the time goes in v17:
time: 142 us; the launch traced here: 141 us
  starting transfers between devices  65.6 us (46%)
  waiting for transfers between devices  42.5 us (30%)
  Pallas kernels  20.3 us (14%)
  other arithmetic  3.92 us (3%)
  matrix products  3.65 us (3%)
  local copies, waits for them, and re-layouts  3.63 us (3%)
    ppermute x6, starting transfers between devices, finish(): got = lax.ppermute(packed, 'src', exchange_perm(src_size, partner))  28.1 us
    ppermute x6, waiting for transfers between devices, finish(): got = lax.ppermute(packed, 'src', exchange_perm(src_size, partner))  27.2 us
    ppermute x1, starting transfers between devices, per_device(): own_sources = lax.ppermute(states_mid, ('tgt', 'src'), direct)  13.5 us
    pallas_call x2, Pallas kernels, date_weights_kernel(): pl.pallas_call(kernel, out_shape=(jax.ShapeDtypeStruct((cols, rows), jnp....  11.9 us
    ppermute x2, waiting for transfers between devices, finish(): got = lax.ppermute(send, 'src', xor_perm(src_size, bit))  9.49 us
    pallas_call x1, Pallas kernels, date_partials_kernel(): pl.pallas_call(kernel, out_shape=jax.ShapeDtypeStruct((width + 2, rows),...  8.42 us
    ppermute x2, starting transfers between devices, finish(): got = lax.ppermute(send, 'src', xor_perm(src_size, bit))  7.64 us
    ppermute x2, starting transfers between devices, finish(): got = lax.ppermute(value, 'src', xor_perm(src_size, bit))  6.41 us
  transfers between devices with their start and end apart: 15, of which 10 were waited for; matrix products, arithmetic and copies ran while one was open for 5% of the time, Pallas kernels for 14%

profile of v17, /device:TPU:16, one launch (start us, length us, event | category | flops | bytes accessed | tf_op | source)
XLA Modules:
  0.0 140.8 jit_solution(12766682100431450503)
XLA Ops:
  0.6 13.5 %collective-permute-start = (bf16[1024,128]{1,0:T(8,128)(2,1)}, bf16[1024,128]{1,0:T(8,128)(2,1)S(1)}, u32[]{:S(2)}, u32[]{:S(2)}) collective-permute-start(bf16[1024,128]{1,0:T(8,128)(2,1)} %refs_1_.1), channel_id=1, source_target_pairs={{392,0},{425,1},{458,2},{491,3},{268,4},{333,5},{6,6},{71,7},{128,... | collective-permute-start | bytes 786440 | tf_op jit(solution)/shard_map/ppermute | solution.py:258
  17.4 8.4 %shard_map.113 = f32[66,1024]{1,0:T(8,128)} custom-call(s32[64,64]{1,0:T(8,128)} %refs_0_.3, bf16[1024,128]{1,0:T(8,128)(2,1)} %refs_1_.1, bf16[2048,128]{1,0:T(8,128)(2,1)} %refs_2_.1, bf16[1,2048]{1,0:T(2,128)(2,1)} %reshape.11.refs_3_, bf16[64,2048]{1,0:T(8,128)(2,1)} %bitcast.30), custom_call_target="tpu_custom_call" | custom-call | tf_op jit(solution)/shard_map/pallas_call | solution.py:56
  26.8 5.7 %collective-permute-start.2 = (f32[66,512]{1,0:T(8,128)S(1)}, f32[66,512]{1,0:T(8,128)S(1)}, u32[]{:S(2)}, u32[]{:S(2)}) collective-permute-start(f32[66,512]{1,0:T(8,128)S(1)} %constant_dynamic-slice_fusion.1), channel_id=1, source_target_pairs={{0,8},{1,9},{2,10},{3,11},{4,12},{5,13},{6,14},{7,15},{8,0},{9,1},... | collective-permute-start | bytes 405512 | tf_op jit(solution)/shard_map/ppermute | solution.py:159
  32.5 3.3 %collective-permute-done.2 = f32[66,512]{1,0:T(8,128)S(1)} collective-permute-done((f32[66,512]{1,0:T(8,128)S(1)}, f32[66,512]{1,0:T(8,128)S(1)}, u32[]{:S(2)}, u32[]{:S(2)}) %collective-permute-start.2) | collective-permute-done | bytes 135200 | tf_op jit(solution)/shard_map/ppermute | solution.py:159
  37.6 3.1 %collective-permute-start.3 = (f32[66,512]{1,0:T(8,128)S(1)}, f32[66,512]{1,0:T(8,128)S(1)}, u32[]{:S(2)}, u32[]{:S(2)}) collective-permute-start(f32[66,512]{1,0:T(8,128)S(1)} %pad_maximum_fusion.1), channel_id=1, source_target_pairs={{0,1},{1,0},{2,3},{3,2},{4,5},{5,4},{6,7},{7,6},{8,9},{9,8},{10,11... | collective-permute-start | bytes 405512 | tf_op jit(solution)/shard_map/ppermute | solution.py:163
  40.7 3.9 %collective-permute-done.3 = f32[66,512]{1,0:T(8,128)S(1)} collective-permute-done((f32[66,512]{1,0:T(8,128)S(1)}, f32[66,512]{1,0:T(8,128)S(1)}, u32[]{:S(2)}, u32[]{:S(2)}) %collective-permute-start.3) | collective-permute-done | bytes 135200 | tf_op jit(solution)/shard_map/ppermute | solution.py:163
  44.7 5.4 %collective-permute-start.4 = (f32[66,512]{1,0:T(8,128)S(1)}, f32[66,512]{1,0:T(8,128)S(1)}, u32[]{:S(2)}, u32[]{:S(2)}) collective-permute-start(f32[66,512]{1,0:T(8,128)S(1)} %pad_maximum_fusion.2), channel_id=1, source_target_pairs={{0,2},{1,3},{2,0},{3,1},{4,6},{5,7},{6,4},{7,5},{8,10},{9,11},{10,... | collective-permute-start | bytes 405512 | tf_op jit(solution)/shard_map/ppermute | solution.py:163
  50.2 3.7 %collective-permute-done.4 = f32[66,512]{1,0:T(8,128)S(1)} collective-permute-done((f32[66,512]{1,0:T(8,128)S(1)}, f32[66,512]{1,0:T(8,128)S(1)}, u32[]{:S(2)}, u32[]{:S(2)}) %collective-permute-start.4) | collective-permute-done | bytes 135200 | tf_op jit(solution)/shard_map/ppermute | solution.py:163
  53.9 4.0 %collective-permute-start.5 = (f32[66,512]{1,0:T(8,128)S(1)}, f32[66,512]{1,0:T(8,128)S(1)}, u32[]{:S(2)}, u32[]{:S(2)}) collective-permute-start(f32[66,512]{1,0:T(8,128)S(1)} %pad_maximum_fusion.3), channel_id=1, source_target_pairs={{0,6},{1,7},{2,4},{3,5},{4,2},{5,3},{6,0},{7,1},{8,14},{9,15},{10,... | collective-permute-start | bytes 405512 | tf_op jit(solution)/shard_map/ppermute | solution.py:163
  61.2 3.5 %collective-permute-done.5 = f32[66,512]{1,0:T(8,128)S(1)} collective-permute-done((f32[66,512]{1,0:T(8,128)S(1)}, f32[66,512]{1,0:T(8,128)S(1)}, u32[]{:S(2)}, u32[]{:S(2)}) %collective-permute-start.5) | collective-permute-done | bytes 135200 | tf_op jit(solution)/shard_map/ppermute | solution.py:163
  64.8 3.7 %collective-permute-start.6 = (bf16[64,512]{1,0:T(8,128)(2,1)S(1)}, bf16[64,512]{1,0:T(8,128)(2,1)S(1)}, u32[]{:S(2)}, u32[]{:S(2)}) collective-permute-start(bf16[64,512]{1,0:T(8,128)(2,1)S(1)} %fusion.17), channel_id=1, source_target_pairs={{0,8},{1,9},{2,10},{3,11},{4,12},{5,13},{6,14},{7,15},{8,0},{9,1},... | collective-permute-start | bytes 196616 | tf_op jit(solution)/shard_map/ppermute | solution.py:170
  68.5 2.4 %collective-permute-done.6 = bf16[64,512]{1,0:T(8,128)(2,1)S(1)} collective-permute-done((bf16[64,512]{1,0:T(8,128)(2,1)S(1)}, bf16[64,512]{1,0:T(8,128)(2,1)S(1)}, u32[]{:S(2)}, u32[]{:S(2)}) %collective-permute-start.6) | collective-permute-done | bytes 65568 | tf_op jit(solution)/shard_map/ppermute | solution.py:170
  71.0 4.0 %collective-permute-start.7 = (bf16[64,1024]{1,0:T(8,128)(2,1)S(1)}, bf16[64,1024]{1,0:T(8,128)(2,1)S(1)}, u32[]{:S(2)}, u32[]{:S(2)}) collective-permute-start(bf16[64,1024]{1,0:T(8,128)(2,1)S(1)} %maximum_select_fusion), channel_id=1, source_target_pairs={{392,0},{425,1},{458,2},{491,3},{268,4},{333,5},{6,6},{71,7},{128,... | collective-permute-start | bytes 393224 | tf_op jit(solution)/shard_map/ppermute | solution.py:278
  75.9 5.9 %shard_map.115 = (bf16[2048,512]{1,0:T(8,128)(2,1)}, f32[2,512]{1,0:T(2,128)}) custom-call(s32[64,64]{1,0:T(8,128)} %refs_0_.5, bf16[512,128]{1,0:T(8,128)(2,1)} %get-tuple-element.31.refs_1_, bf16[2048,128]{1,0:T(8,128)(2,1)} %pad_maximum_fusion.refs_2_, bf16[1,2048]{1,0:T(2,128)(2,1)} %reshape.12.refs_3_), custom_call_target="tpu_custom_call" | custom-call | tf_op jit(solution)/shard_map/pallas_call | solution.py:104
  81.8 6.0 %shard_map.114 = (bf16[2048,512]{1,0:T(8,128)(2,1)}, f32[2,512]{1,0:T(2,128)}) custom-call(s32[64,64]{1,0:T(8,128)} %refs_0_.5, bf16[512,128]{1,0:T(8,128)(2,1)} %get-tuple-element.30.refs_1_, bf16[2048,128]{1,0:T(8,128)(2,1)} %pad_maximum_fusion.refs_2_, bf16[1,2048]{1,0:T(2,128)(2,1)} %reshape.12.refs_3_), custom_call_target="tpu_custom_call" | custom-call | tf_op jit(solution)/shard_map/pallas_call | solution.py:104
  95.6 6.2 %collective-permute-done.10 = f32[66,512]{1,0:T(8,128)S(1)} collective-permute-done((f32[66,512]{1,0:T(8,128)S(1)}, f32[66,512]{1,0:T(8,128)S(1)}, u32[]{:S(2)}, u32[]{:S(2)}) %collective-permute-start.10) | collective-permute-done | bytes 135200 | tf_op jit(solution)/shard_map/ppermute | solution.py:159
  102.0 3.6 %collective-permute-start.11 = (f32[66,512]{1,0:T(8,128)S(1)}, f32[66,512]{1,0:T(8,128)S(1)}, u32[]{:S(2)}, u32[]{:S(2)}) collective-permute-start(f32[66,512]{1,0:T(8,128)S(1)} %pad_maximum_fusion.4), channel_id=1, source_target_pairs={{0,1},{1,0},{2,3},{3,2},{4,5},{5,4},{6,7},{7,6},{8,9},{9,8},{10,11... | collective-permute-start | bytes 405512 | tf_op jit(solution)/shard_map/ppermute | solution.py:163
  105.6 3.7 %collective-permute-done.11 = f32[66,512]{1,0:T(8,128)S(1)} collective-permute-done((f32[66,512]{1,0:T(8,128)S(1)}, f32[66,512]{1,0:T(8,128)S(1)}, u32[]{:S(2)}, u32[]{:S(2)}) %collective-permute-start.11) | collective-permute-done | bytes 135200 | tf_op jit(solution)/shard_map/ppermute | solution.py:163
  109.3 4.6 %collective-permute-start.12 = (f32[66,512]{1,0:T(8,128)S(1)}, f32[66,512]{1,0:T(8,128)S(1)}, u32[]{:S(2)}, u32[]{:S(2)}) collective-permute-start(f32[66,512]{1,0:T(8,128)S(1)} %pad_maximum_fusion.5), channel_id=1, source_target_pairs={{0,2},{1,3},{2,0},{3,1},{4,6},{5,7},{6,4},{7,5},{8,10},{9,11},{10,... | collective-permute-start | bytes 405512 | tf_op jit(solution)/shard_map/ppermute | solution.py:163
  114.0 5.5 %collective-permute-done.12 = f32[66,512]{1,0:T(8,128)S(1)} collective-permute-done((f32[66,512]{1,0:T(8,128)S(1)}, f32[66,512]{1,0:T(8,128)S(1)}, u32[]{:S(2)}, u32[]{:S(2)}) %collective-permute-start.12) | collective-permute-done | bytes 135200 | tf_op jit(solution)/shard_map/ppermute | solution.py:163
  119.5 7.3 %collective-permute-start.13 = (f32[66,512]{1,0:T(8,128)S(1)}, f32[66,512]{1,0:T(8,128)S(1)}, u32[]{:S(2)}, u32[]{:S(2)}) collective-permute-start(f32[66,512]{1,0:T(8,128)S(1)} %pad_maximum_fusion.6), channel_id=1, source_target_pairs={{0,6},{1,7},{2,4},{3,5},{4,2},{5,3},{6,0},{7,1},{8,14},{9,15},{10,... | collective-permute-start | bytes 405512 | tf_op jit(solution)/shard_map/ppermute | solution.py:163
  126.9 6.9 %collective-permute-done.13 = f32[66,512]{1,0:T(8,128)S(1)} collective-permute-done((f32[66,512]{1,0:T(8,128)S(1)}, f32[66,512]{1,0:T(8,128)S(1)}, u32[]{:S(2)}, u32[]{:S(2)}) %collective-permute-start.13) | collective-permute-done | bytes 135200 | tf_op jit(solution)/shard_map/ppermute | solution.py:163
  133.9 2.7 %collective-permute-start.14 = (bf16[64,512]{1,0:T(8,128)(2,1)S(1)}, bf16[64,512]{1,0:T(8,128)(2,1)S(1)}, u32[]{:S(2)}, u32[]{:S(2)}) collective-permute-start(bf16[64,512]{1,0:T(8,128)(2,1)S(1)} %fusion.15), channel_id=1, source_target_pairs={{0,8},{1,9},{2,10},{3,11},{4,12},{5,13},{6,14},{7,15},{8,0},{9,1},... | collective-permute-start | bytes 196616 | tf_op jit(solution)/shard_map/ppermute | solution.py:170
  136.6 3.4 %collective-permute-done.14 = bf16[64,512]{1,0:T(8,128)(2,1)S(1)} collective-permute-done((bf16[64,512]{1,0:T(8,128)(2,1)S(1)}, bf16[64,512]{1,0:T(8,128)(2,1)S(1)}, u32[]{:S(2)}, u32[]{:S(2)}) %collective-permute-start.14) | collective-permute-done | bytes 65568 | tf_op jit(solution)/shard_map/ppermute | solution.py:170
  (71 shorter events, 19.0 us)
Async XLA Ops:
  0.6 57.3 %copy-start.2 = (bf16[1024,128]{1,0:T(8,128)(2,1)S(1)}, bf16[1024,128]{1,0:T(8,128)(2,1)}, u32[]{:S(2)}) copy-start(bf16[1024,128]{1,0:T(8,128)(2,1)} %param.17) | copy-start | bytes 786436
  0.6 25.2 %collective-permute-start = (bf16[1024,128]{1,0:T(8,128)(2,1)}, bf16[1024,128]{1,0:T(8,128)(2,1)S(1)}, u32[]{:S(2)}, u32[]{:S(2)}) collective-permute-start(bf16[1024,128]{1,0:T(8,128)(2,1)} %refs_1_.1), channel_id=1, source_target_pairs={{392,0},{425,1},{458,2},{491,3},{268,4},{333,5},{6,6},{71,7},{128,... | collective-permute-start | bytes 786440 | tf_op jit(solution)/shard_map/ppermute | solution.py:258
  14.2 11.7 %collective-permute-start.1 = (bf16[2048]{0:T(1024)(128)(2,1)}, bf16[2048]{0:T(1024)(128)(2,1)S(1)}, u32[]{:S(2)}, u32[]{:S(2)}) collective-permute-start(bf16[2048]{0:T(1024)(128)(2,1)} %param.14), channel_id=1, source_target_pairs={{12,0},{13,1},{14,2},{15,3},{8,4},{10,5},{0,6},{2,7},{4,8},{5,9},{... | collective-permute-start | bytes 12296 | tf_op jit(solution)/shard_map/ppermute | solution.py:234
  25.8 38.9 %copy-start.4 = (bf16[1024,64]{0,1:T(8,128)(2,1)S(1)}, bf16[1024,64]{0,1:T(8,128)(2,1)}, u32[]{:S(2)}) copy-start(bf16[1024,64]{0,1:T(8,128)(2,1)} %param.15) | copy-start | bytes 393220
  26.8 9.0 %collective-permute-start.2 = (f32[66,512]{1,0:T(8,128)S(1)}, f32[66,512]{1,0:T(8,128)S(1)}, u32[]{:S(2)}, u32[]{:S(2)}) collective-permute-start(f32[66,512]{1,0:T(8,128)S(1)} %constant_dynamic-slice_fusion.1), channel_id=1, source_target_pairs={{0,8},{1,9},{2,10},{3,11},{4,12},{5,13},{6,14},{7,15},{8,0},{9,1},... | collective-permute-start | bytes 405512 | tf_op jit(solution)/shard_map/ppermute | solution.py:159
  37.6 7.0 %collective-permute-start.3 = (f32[66,512]{1,0:T(8,128)S(1)}, f32[66,512]{1,0:T(8,128)S(1)}, u32[]{:S(2)}, u32[]{:S(2)}) collective-permute-start(f32[66,512]{1,0:T(8,128)S(1)} %pad_maximum_fusion.1), channel_id=1, source_target_pairs={{0,1},{1,0},{2,3},{3,2},{4,5},{5,4},{6,7},{7,6},{8,9},{9,8},{10,11... | collective-permute-start | bytes 405512 | tf_op jit(solution)/shard_map/ppermute | solution.py:163
  44.7 9.1 %collective-permute-start.4 = (f32[66,512]{1,0:T(8,128)S(1)}, f32[66,512]{1,0:T(8,128)S(1)}, u32[]{:S(2)}, u32[]{:S(2)}) collective-permute-start(f32[66,512]{1,0:T(8,128)S(1)} %pad_maximum_fusion.2), channel_id=1, source_target_pairs={{0,2},{1,3},{2,0},{3,1},{4,6},{5,7},{6,4},{7,5},{8,10},{9,11},{10,... | collective-permute-start | bytes 405512 | tf_op jit(solution)/shard_map/ppermute | solution.py:163
  53.9 10.7 %collective-permute-start.5 = (f32[66,512]{1,0:T(8,128)S(1)}, f32[66,512]{1,0:T(8,128)S(1)}, u32[]{:S(2)}, u32[]{:S(2)}) collective-permute-start(f32[66,512]{1,0:T(8,128)S(1)} %pad_maximum_fusion.3), channel_id=1, source_target_pairs={{0,6},{1,7},{2,4},{3,5},{4,2},{5,3},{6,0},{7,1},{8,14},{9,15},{10,... | collective-permute-start | bytes 405512 | tf_op jit(solution)/shard_map/ppermute | solution.py:163
  59.3 9.2 %collective-permute-start.8 = (bf16[1024,128]{1,0:T(8,128)(2,1)S(1)}, bf16[1024,128]{1,0:T(8,128)(2,1)S(1)}, u32[]{:S(2)}, u32[]{:S(2)}) collective-permute-start(bf16[1024,128]{1,0:T(8,128)(2,1)S(1)} %collective-permute-done), channel_id=1, source_target_pairs={{16,0},{17,1},{18,2},{19,3},{20,4},{21,5},{22,6},{23,7},{24,8},{25... | collective-permute-start | bytes 786440 | tf_op jit(solution)/shard_map/ppermute | solution.py:267
  64.8 6.2 %collective-permute-start.6 = (bf16[64,512]{1,0:T(8,128)(2,1)S(1)}, bf16[64,512]{1,0:T(8,128)(2,1)S(1)}, u32[]{:S(2)}, u32[]{:S(2)}) collective-permute-start(bf16[64,512]{1,0:T(8,128)(2,1)S(1)} %fusion.17), channel_id=1, source_target_pairs={{0,8},{1,9},{2,10},{3,11},{4,12},{5,13},{6,14},{7,15},{8,0},{9,1},... | collective-permute-start | bytes 196616 | tf_op jit(solution)/shard_map/ppermute | solution.py:170
  71.0 21.9 %copy-start.3 = (bf16[64,1024]{1,0:T(8,128)(2,1)}, bf16[64,1024]{1,0:T(8,128)(2,1)S(1)}, u32[]{:S(2)}) copy-start(bf16[64,1024]{1,0:T(8,128)(2,1)S(1)} %maximum_select_fusion) | copy-start | bytes 393220
  71.0 16.8 %collective-permute-start.7 = (bf16[64,1024]{1,0:T(8,128)(2,1)S(1)}, bf16[64,1024]{1,0:T(8,128)(2,1)S(1)}, u32[]{:S(2)}, u32[]{:S(2)}) collective-permute-start(bf16[64,1024]{1,0:T(8,128)(2,1)S(1)} %maximum_select_fusion), channel_id=1, source_target_pairs={{392,0},{425,1},{458,2},{491,3},{268,4},{333,5},{6,6},{71,7},{128,... | collective-permute-start | bytes 393224 | tf_op jit(solution)/shard_map/ppermute | solution.py:278
  81.8 11.2 %copy-start = (bf16[2048,512]{1,0:T(8,128)(2,1)S(1)}, bf16[2048,512]{1,0:T(8,128)(2,1)}, u32[]{:S(2)}) copy-start(bf16[2048,512]{1,0:T(8,128)(2,1)} %get-tuple-element.13) | copy-start | bytes 6291460
  87.8 5.5 %copy-start.1 = (bf16[2048,512]{1,0:T(8,128)(2,1)S(1)}, bf16[2048,512]{1,0:T(8,128)(2,1)}, u32[]{:S(2)}) copy-start(bf16[2048,512]{1,0:T(8,128)(2,1)} %get-tuple-element.12) | copy-start | bytes 6291460
  87.8 5.1 %collective-permute-start.9 = (bf16[64,1024]{1,0:T(8,128)(2,1)S(1)}, bf16[64,1024]{1,0:T(8,128)(2,1)S(1)}, u32[]{:S(2)}, u32[]{:S(2)}) collective-permute-start(bf16[64,1024]{1,0:T(8,128)(2,1)S(1)} %collective-permute-done.7), channel_id=1, source_target_pairs={{16,0},{17,1},{18,2},{19,3},{20,4},{21,5},{22,6},{23,7},{24,8},{25... | collective-permute-start | bytes 393224 | tf_op jit(solution)/shard_map/ppermute | solution.py:279
  91.4 2.2 %copy-start.6 = (f32[2,512]{1,0:T(2,128)S(1)}, f32[2,512]{1,0:T(2,128)}, u32[]{:S(2)}) copy-start(f32[2,512]{1,0:T(2,128)} %get-tuple-element.15) | copy-start | bytes 12292
  91.4 2.2 %copy-start.7 = (f32[2,512]{1,0:T(2,128)S(1)}, f32[2,512]{1,0:T(2,128)}, u32[]{:S(2)}) copy-start(f32[2,512]{1,0:T(2,128)} %get-tuple-element.14) | copy-start | bytes 12292
  93.6 40.3 %copy-start.5 = (bf16[1024,64]{0,1:T(8,128)(2,1)S(1)}, bf16[1024,64]{0,1:T(8,128)(2,1)}, u32[]{:S(2)}) copy-start(bf16[1024,64]{0,1:T(8,128)(2,1)} %param.18) | copy-start | bytes 393220
  93.7 8.1 %collective-permute-start.10 = (f32[66,512]{1,0:T(8,128)S(1)}, f32[66,512]{1,0:T(8,128)S(1)}, u32[]{:S(2)}, u32[]{:S(2)}) collective-permute-start(f32[66,512]{1,0:T(8,128)S(1)} %constant_dynamic-slice_fusion), channel_id=1, source_target_pairs={{0,8},{1,9},{2,10},{3,11},{4,12},{5,13},{6,14},{7,15},{8,0},{9,1},... | collective-permute-start | bytes 405512 | tf_op jit(solution)/shard_map/ppermute | solution.py:159
  102.0 7.3 %collective-permute-start.11 = (f32[66,512]{1,0:T(8,128)S(1)}, f32[66,512]{1,0:T(8,128)S(1)}, u32[]{:S(2)}, u32[]{:S(2)}) collective-permute-start(f32[66,512]{1,0:T(8,128)S(1)} %pad_maximum_fusion.4), channel_id=1, source_target_pairs={{0,1},{1,0},{2,3},{3,2},{4,5},{5,4},{6,7},{7,6},{8,9},{9,8},{10,11... | collective-permute-start | bytes 405512 | tf_op jit(solution)/shard_map/ppermute | solution.py:163
  109.3 10.1 %collective-permute-start.12 = (f32[66,512]{1,0:T(8,128)S(1)}, f32[66,512]{1,0:T(8,128)S(1)}, u32[]{:S(2)}, u32[]{:S(2)}) collective-permute-start(f32[66,512]{1,0:T(8,128)S(1)} %pad_maximum_fusion.5), channel_id=1, source_target_pairs={{0,2},{1,3},{2,0},{3,1},{4,6},{5,7},{6,4},{7,5},{8,10},{9,11},{10,... | collective-permute-start | bytes 405512 | tf_op jit(solution)/shard_map/ppermute | solution.py:163
  119.5 14.3 %collective-permute-start.13 = (f32[66,512]{1,0:T(8,128)S(1)}, f32[66,512]{1,0:T(8,128)S(1)}, u32[]{:S(2)}, u32[]{:S(2)}) collective-permute-start(f32[66,512]{1,0:T(8,128)S(1)} %pad_maximum_fusion.6), channel_id=1, source_target_pairs={{0,6},{1,7},{2,4},{3,5},{4,2},{5,3},{6,0},{7,1},{8,14},{9,15},{10,... | collective-permute-start | bytes 405512 | tf_op jit(solution)/shard_map/ppermute | solution.py:163
  133.9 6.2 %collective-permute-start.14 = (bf16[64,512]{1,0:T(8,128)(2,1)S(1)}, bf16[64,512]{1,0:T(8,128)(2,1)S(1)}, u32[]{:S(2)}, u32[]{:S(2)}) collective-permute-start(bf16[64,512]{1,0:T(8,128)(2,1)S(1)} %fusion.15), channel_id=1, source_target_pairs={{0,8},{1,9},{2,10},{3,11},{4,12},{5,13},{6,14},{7,15},{8,0},{9,1},... | collective-permute-start | bytes 196616 | tf_op jit(solution)/shard_map/ppermute | solution.py:170

commit v18 on v15

--- a/solution.py
+++ b/solution.py
@@ -18,7 +18,7 @@
 
 
 def offset_column(off_row):
-    wide = jnp.broadcast_to(off_row.astype(jnp.float32), (8, off_row.shape[1]))
+    wide = jnp.broadcast_to(off_row.astype(jnp.float32)[None, :], (8, off_row.shape[0]))
     return jnp.transpose(wide)[:, 0:1]
 
 
@@ -33,7 +33,7 @@
         live = mask_ref[row, col0 + j] > 0
         y = y_ref[j * BLOCK : (j + 1) * BLOCK, :]
         s = lax.dot_general(y, x_ref[...], (((1,), (1,)), ((), ())), preferred_element_type=jnp.float32)
-        s = s * scale - offset_column(off_ref[:, j * BLOCK : (j + 1) * BLOCK])
+        s = s * scale - offset_column(off_ref[j * BLOCK : (j + 1) * BLOCK])
         m_old = out_ref[width + 1 : width + 2, :]
         m_new = jnp.where(live, jnp.maximum(m_old, jnp.max(s, axis=0, keepdims=True)), m_old)
         shrink = jnp.exp(m_old - m_new)
@@ -62,13 +62,13 @@
             in_specs=[
                 pl.BlockSpec((BLOCK, factors), lambda i, m: (i, 0)),
                 pl.BlockSpec((cols, factors), lambda i, m: (0, 0)),
-                pl.BlockSpec((1, cols), lambda i, m: (0, 0)),
+                pl.BlockSpec((cols,), lambda i, m: (0,)),
                 pl.BlockSpec((width, cols), lambda i, m: (0, 0)),
             ],
             out_specs=pl.BlockSpec((width + 2, BLOCK), lambda i, m: (0, i)),
         ),
         compiler_params=pltpu.CompilerParams(dimension_semantics=("arbitrary",)),
-    )(tile_mask, targets, sources, offsets.reshape(1, cols), values_t)
+    )(tile_mask, targets, sources, offsets, values_t)
 
 
 def weights_kernel(mask_ref, x_ref, y_ref, off_ref, p_ref, stats_ref, *, scale, row_tile, col_tiles, col_base):
@@ -78,7 +78,7 @@
     def scores(j):
         y = y_ref[j * BLOCK : (j + 1) * BLOCK, :]
         s = lax.dot_general(y, x_ref[...], (((1,), (1,)), ((), ())), preferred_element_type=jnp.float32)
-        return s * scale - offset_column(off_ref[:, j * BLOCK : (j + 1) * BLOCK])
+        return s * scale - offset_column(off_ref[j * BLOCK : (j + 1) * BLOCK])
 
     peak = jnp.full((1, BLOCK), very_low, jnp.float32)
     for j in range(col_tiles):
@@ -113,7 +113,7 @@
             in_specs=[
                 pl.BlockSpec((BLOCK, factors), lambda i, m: (0, 0)),
                 pl.BlockSpec((cols, factors), lambda i, m: (0, 0)),
-                pl.BlockSpec((1, cols), lambda i, m: (0, 0)),
+                pl.BlockSpec((cols,), lambda i, m: (0,)),
             ],
             out_specs=(
                 pl.BlockSpec((cols, BLOCK), lambda i, m: (0, 0)),
@@ -121,7 +121,7 @@
             ),
         ),
         compiler_params=pltpu.CompilerParams(dimension_semantics=("arbitrary",)),
-    )(tile_mask, targets, sources, offsets.reshape(1, cols))
+    )(tile_mask, targets, sources, offsets)
 
 
 HALVING_BITS = (3,)

time: 140 us -> 139 us (level)
  the two profiles are of different devices: /device:TPU:10 before, /device:TPU:8 now
where the time goes in v18:
time: 139 us; the launch traced here: 138 us
  starting transfers between devices  64.3 us (46%)
  waiting for transfers between devices  44.2 us (32%)
  Pallas kernels  20.1 us (14%)
  other arithmetic  3.94 us (3%)
  matrix products  2.67 us (2%)
  local copies, waits for them, and re-layouts  1.69 us (1%)
    ppermute x6, waiting for transfers between devices, finish(): got = lax.ppermute(packed, 'src', exchange_perm(src_size, partner))  29.2 us
    ppermute x6, starting transfers between devices, finish(): got = lax.ppermute(packed, 'src', exchange_perm(src_size, partner))  23 us
    ppermute x1, starting transfers between devices, per_device(): own_sources = lax.ppermute(states_mid, ('tgt', 'src'), direct)  13.3 us
    pallas_call x2, Pallas kernels, date_weights_kernel(): pl.pallas_call(kernel, out_shape=(jax.ShapeDtypeStruct((cols, rows), jnp....  11.7 us
    ppermute x2, starting transfers between devices, regroup(): return [lax.ppermute(block_rows, ('tgt', 'src'), p) for p in perms]  10.9 us
    ppermute x2, waiting for transfers between devices, finish(): got = lax.ppermute(send, 'src', xor_perm(src_size, bit))  9.11 us
    pallas_call x1, Pallas kernels, date_partials_kernel(): pl.pallas_call(kernel, out_shape=jax.ShapeDtypeStruct((width + 2, rows),...  8.38 us
    ppermute x2, starting transfers between devices, finish(): got = lax.ppermute(send, 'src', xor_perm(src_size, bit))  6.8 us
  transfers between devices with their start and end apart: 15, of which 11 were waited for; matrix products, arithmetic and copies ran while one was open for 1% of the time, Pallas kernels for 15%

profile of v18, /device:TPU:8, one launch (start us, length us, event | category | flops | bytes accessed | tf_op | source)
XLA Modules:
  0.0 138.1 jit_solution(16648246546724664083)
XLA Ops:
  0.6 13.3 %collective-permute-start = (bf16[1024,128]{1,0:T(8,128)(2,1)}, bf16[1024,128]{1,0:T(8,128)(2,1)S(1)}, u32[]{:S(2)}, u32[]{:S(2)}) collective-permute-start(bf16[1024,128]{1,0:T(8,128)(2,1)} %refs_1_.1), channel_id=1, source_target_pairs={{392,0},{425,1},{458,2},{491,3},{268,4},{333,5},{6,6},{71,7},{128,... | collective-permute-start | bytes 786440 | tf_op jit(solution)/shard_map/ppermute | solution.py:271
  15.9 8.4 %shard_map.113 = f32[66,1024]{1,0:T(8,128)} custom-call(s32[64,64]{1,0:T(8,128)} %refs_0_.3, bf16[1024,128]{1,0:T(8,128)(2,1)} %refs_1_.1, bf16[2048,128]{1,0:T(8,128)(2,1)} %refs_2_.1, bf16[2048]{0:T(1024)(128)(2,1)} %refs_3_.1, bf16[64,2048]{1,0:T(8,128)(2,1)} %bitcast.28), custom_call_target="tpu_custom_call" | custom-call | tf_op jit(solution)/shard_map/pallas_call | solution.py:56
  25.4 4.9 %collective-permute-start.2 = (f32[66,512]{1,0:T(8,128)S(1)}, f32[66,512]{1,0:T(8,128)S(1)}, u32[]{:S(2)}, u32[]{:S(2)}) collective-permute-start(f32[66,512]{1,0:T(8,128)S(1)} %constant_dynamic-slice_fusion.1), channel_id=1, source_target_pairs={{0,8},{1,9},{2,10},{3,11},{4,12},{5,13},{6,14},{7,15},{8,0},{9,1},... | collective-permute-start | bytes 405512 | tf_op jit(solution)/shard_map/ppermute | solution.py:159
  30.3 3.3 %collective-permute-done.2 = f32[66,512]{1,0:T(8,128)S(1)} collective-permute-done((f32[66,512]{1,0:T(8,128)S(1)}, f32[66,512]{1,0:T(8,128)S(1)}, u32[]{:S(2)}, u32[]{:S(2)}) %collective-permute-start.2) | collective-permute-done | bytes 135200 | tf_op jit(solution)/shard_map/ppermute | solution.py:159
  35.3 6.5 %collective-permute-start.3 = (f32[66,512]{1,0:T(8,128)S(1)}, f32[66,512]{1,0:T(8,128)S(1)}, u32[]{:S(2)}, u32[]{:S(2)}) collective-permute-start(f32[66,512]{1,0:T(8,128)S(1)} %pad_maximum_fusion.4), channel_id=1, source_target_pairs={{0,1},{1,0},{2,3},{3,2},{4,5},{5,4},{6,7},{7,6},{8,9},{9,8},{10,11... | collective-permute-start | bytes 405512 | tf_op jit(solution)/shard_map/ppermute | solution.py:163
  41.8 3.1 %collective-permute-done.3 = f32[66,512]{1,0:T(8,128)S(1)} collective-permute-done((f32[66,512]{1,0:T(8,128)S(1)}, f32[66,512]{1,0:T(8,128)S(1)}, u32[]{:S(2)}, u32[]{:S(2)}) %collective-permute-start.3) | collective-permute-done | bytes 135200 | tf_op jit(solution)/shard_map/ppermute | solution.py:163
  45.0 2.5 %collective-permute-start.4 = (f32[66,512]{1,0:T(8,128)S(1)}, f32[66,512]{1,0:T(8,128)S(1)}, u32[]{:S(2)}, u32[]{:S(2)}) collective-permute-start(f32[66,512]{1,0:T(8,128)S(1)} %pad_maximum_fusion.5), channel_id=1, source_target_pairs={{0,2},{1,3},{2,0},{3,1},{4,6},{5,7},{6,4},{7,5},{8,10},{9,11},{10,... | collective-permute-start | bytes 405512 | tf_op jit(solution)/shard_map/ppermute | solution.py:163
  47.5 5.5 %collective-permute-done.4 = f32[66,512]{1,0:T(8,128)S(1)} collective-permute-done((f32[66,512]{1,0:T(8,128)S(1)}, f32[66,512]{1,0:T(8,128)S(1)}, u32[]{:S(2)}, u32[]{:S(2)}) %collective-permute-start.4) | collective-permute-done | bytes 135200 | tf_op jit(solution)/shard_map/ppermute | solution.py:163
  53.1 4.0 %collective-permute-start.5 = (f32[66,512]{1,0:T(8,128)S(1)}, f32[66,512]{1,0:T(8,128)S(1)}, u32[]{:S(2)}, u32[]{:S(2)}) collective-permute-start(f32[66,512]{1,0:T(8,128)S(1)} %pad_maximum_fusion.6), channel_id=1, source_target_pairs={{0,6},{1,7},{2,4},{3,5},{4,2},{5,3},{6,0},{7,1},{8,14},{9,15},{10,... | collective-permute-start | bytes 405512 | tf_op jit(solution)/shard_map/ppermute | solution.py:163
  59.8 2.5 %collective-permute-done.5 = f32[66,512]{1,0:T(8,128)S(1)} collective-permute-done((f32[66,512]{1,0:T(8,128)S(1)}, f32[66,512]{1,0:T(8,128)S(1)}, u32[]{:S(2)}, u32[]{:S(2)}) %collective-permute-start.5) | collective-permute-done | bytes 135200 | tf_op jit(solution)/shard_map/ppermute | solution.py:163
  62.4 3.7 %collective-permute-start.6 = (bf16[64,512]{1,0:T(8,128)(2,1)S(1)}, bf16[64,512]{1,0:T(8,128)(2,1)S(1)}, u32[]{:S(2)}, u32[]{:S(2)}) collective-permute-start(bf16[64,512]{1,0:T(8,128)(2,1)S(1)} %fusion.13), channel_id=1, source_target_pairs={{0,8},{1,9},{2,10},{3,11},{4,12},{5,13},{6,14},{7,15},{8,0},{9,1},... | collective-permute-start | bytes 196616 | tf_op jit(solution)/shard_map/ppermute | solution.py:170
  66.2 2.3 %collective-permute-done.6 = bf16[64,512]{1,0:T(8,128)(2,1)S(1)} collective-permute-done((bf16[64,512]{1,0:T(8,128)(2,1)S(1)}, bf16[64,512]{1,0:T(8,128)(2,1)S(1)}, u32[]{:S(2)}, u32[]{:S(2)}) %collective-permute-start.6) | collective-permute-done | bytes 65568 | tf_op jit(solution)/shard_map/ppermute | solution.py:170
  68.6 9.0 %collective-permute-start.8 = (bf16[64,1024]{1,0:T(8,128)(2,1)S(1)}, bf16[64,1024]{1,0:T(8,128)(2,1)S(1)}, u32[]{:S(2)}, u32[]{:S(2)}) collective-permute-start(bf16[64,1024]{1,0:T(8,128)(2,1)S(1)} %maximum_select_fusion), channel_id=1, source_target_pairs={{392,0},{425,1},{458,2},{491,3},{268,4},{333,5},{6,6},{71,7},{128,... | collective-permute-start | bytes 393224 | tf_op jit(solution)/shard_map/ppermute | solution.py:219
  80.4 5.9 %shard_map.115 = (bf16[2048,512]{1,0:T(8,128)(2,1)}, f32[2,512]{1,0:T(2,128)}) custom-call(s32[64,64]{1,0:T(8,128)} %refs_0_.5, bf16[512,128]{1,0:T(8,128)(2,1)} %get-tuple-element.33.refs_1_, bf16[2048,128]{1,0:T(8,128)(2,1)} %pad_maximum_fusion.refs_2_, bf16[2048]{0:T(1024)(128)(2,1)} %copy-done.5), custom_call_target="tpu_custom_call" | custom-call | tf_op jit(solution)/shard_map/pallas_call | solution.py:104
  86.2 5.9 %shard_map.114 = (bf16[2048,512]{1,0:T(8,128)(2,1)}, f32[2,512]{1,0:T(2,128)}) custom-call(s32[64,64]{1,0:T(8,128)} %refs_0_.5, bf16[512,128]{1,0:T(8,128)(2,1)} %get-tuple-element.32.refs_1_, bf16[2048,128]{1,0:T(8,128)(2,1)} %pad_maximum_fusion.refs_2_, bf16[2048]{0:T(1024)(128)(2,1)} %copy-done.5), custom_call_target="tpu_custom_call" | custom-call | tf_op jit(solution)/shard_map/pallas_call | solution.py:104
  92.1 2.2 %fusion = f32[64,512]{1,0:T(8,128)S(1)} fusion(bf16[2048,512]{1,0:T(8,128)(2,1)} %get-tuple-element.13, bf16[64,1024]{1,0:T(8,128)(2,1)S(1)} %get-tuple-element.31, bf16[64,1024]{1,0:T(8,128)(2,1)S(1)} %get-tuple-element.30), kind=kOutput, calls=%fused_computation.5 | convolution fusion | flops 134742016 | bytes 2490368 | tf_op jit(solution)/shard_map/dot_general | solution.py:293
  96.9 5.8 %collective-permute-done.10 = f32[66,512]{1,0:T(8,128)S(1)} collective-permute-done((f32[66,512]{1,0:T(8,128)S(1)}, f32[66,512]{1,0:T(8,128)S(1)}, u32[]{:S(2)}, u32[]{:S(2)}) %collective-permute-start.10) | collective-permute-done | bytes 135200 | tf_op jit(solution)/shard_map/ppermute | solution.py:159
  104.8 5.1 %collective-permute-done.11 = f32[66,512]{1,0:T(8,128)S(1)} collective-permute-done((f32[66,512]{1,0:T(8,128)S(1)}, f32[66,512]{1,0:T(8,128)S(1)}, u32[]{:S(2)}, u32[]{:S(2)}) %collective-permute-start.11) | collective-permute-done | bytes 135200 | tf_op jit(solution)/shard_map/ppermute | solution.py:163
  110.0 2.1 %collective-permute-start.12 = (f32[66,512]{1,0:T(8,128)S(1)}, f32[66,512]{1,0:T(8,128)S(1)}, u32[]{:S(2)}, u32[]{:S(2)}) collective-permute-start(f32[66,512]{1,0:T(8,128)S(1)} %pad_maximum_fusion.8), channel_id=1, source_target_pairs={{0,2},{1,3},{2,0},{3,1},{4,6},{5,7},{6,4},{7,5},{8,10},{9,11},{10,... | collective-permute-start | bytes 405512 | tf_op jit(solution)/shard_map/ppermute | solution.py:163
  112.1 5.9 %collective-permute-done.12 = f32[66,512]{1,0:T(8,128)S(1)} collective-permute-done((f32[66,512]{1,0:T(8,128)S(1)}, f32[66,512]{1,0:T(8,128)S(1)}, u32[]{:S(2)}, u32[]{:S(2)}) %collective-permute-start.12) | collective-permute-done | bytes 135200 | tf_op jit(solution)/shard_map/ppermute | solution.py:163
  118.1 6.0 %collective-permute-start.13 = (f32[66,512]{1,0:T(8,128)S(1)}, f32[66,512]{1,0:T(8,128)S(1)}, u32[]{:S(2)}, u32[]{:S(2)}) collective-permute-start(f32[66,512]{1,0:T(8,128)S(1)} %pad_maximum_fusion.9), channel_id=1, source_target_pairs={{0,6},{1,7},{2,4},{3,5},{4,2},{5,3},{6,0},{7,1},{8,14},{9,15},{10,... | collective-permute-start | bytes 405512 | tf_op jit(solution)/shard_map/ppermute | solution.py:163
  124.1 7.0 %collective-permute-done.13 = f32[66,512]{1,0:T(8,128)S(1)} collective-permute-done((f32[66,512]{1,0:T(8,128)S(1)}, f32[66,512]{1,0:T(8,128)S(1)}, u32[]{:S(2)}, u32[]{:S(2)}) %collective-permute-start.13) | collective-permute-done | bytes 135200 | tf_op jit(solution)/shard_map/ppermute | solution.py:163
  131.3 2.7 %collective-permute-start.14 = (bf16[64,512]{1,0:T(8,128)(2,1)S(1)}, bf16[64,512]{1,0:T(8,128)(2,1)S(1)}, u32[]{:S(2)}, u32[]{:S(2)}) collective-permute-start(bf16[64,512]{1,0:T(8,128)(2,1)S(1)} %fusion.11), channel_id=1, source_target_pairs={{0,8},{1,9},{2,10},{3,11},{4,12},{5,13},{6,14},{7,15},{8,0},{9,1},... | collective-permute-start | bytes 196616 | tf_op jit(solution)/shard_map/ppermute | solution.py:170
  134.0 3.4 %collective-permute-done.14 = bf16[64,512]{1,0:T(8,128)(2,1)S(1)} collective-permute-done((bf16[64,512]{1,0:T(8,128)(2,1)S(1)}, bf16[64,512]{1,0:T(8,128)(2,1)S(1)}, u32[]{:S(2)}, u32[]{:S(2)}) %collective-permute-start.14) | collective-permute-done | bytes 65568 | tf_op jit(solution)/shard_map/ppermute | solution.py:170
  (68 shorter events, 15.9 us)
Async XLA Ops:
  0.6 56.5 %copy-start.1 = (bf16[1024,128]{1,0:T(8,128)(2,1)S(1)}, bf16[1024,128]{1,0:T(8,128)(2,1)}, u32[]{:S(2)}) copy-start(bf16[1024,128]{1,0:T(8,128)(2,1)} %param.17) | copy-start | bytes 786436
  0.6 23.8 %collective-permute-start = (bf16[1024,128]{1,0:T(8,128)(2,1)}, bf16[1024,128]{1,0:T(8,128)(2,1)S(1)}, u32[]{:S(2)}, u32[]{:S(2)}) collective-permute-start(bf16[1024,128]{1,0:T(8,128)(2,1)} %refs_1_.1), channel_id=1, source_target_pairs={{392,0},{425,1},{458,2},{491,3},{268,4},{333,5},{6,6},{71,7},{128,... | collective-permute-start | bytes 786440 | tf_op jit(solution)/shard_map/ppermute | solution.py:271
  13.9 10.5 %collective-permute-start.1 = (bf16[2048]{0:T(1024)(128)(2,1)}, bf16[2048]{0:T(1024)(128)(2,1)S(1)}, u32[]{:S(2)}, u32[]{:S(2)}) collective-permute-start(bf16[2048]{0:T(1024)(128)(2,1)} %param.14), channel_id=1, source_target_pairs={{12,0},{13,1},{14,2},{15,3},{8,4},{10,5},{0,6},{2,7},{4,8},{5,9},{... | collective-permute-start | bytes 12296 | tf_op jit(solution)/shard_map/ppermute | solution.py:247
  24.2 38.1 %copy-start.3 = (bf16[1024,64]{0,1:T(8,128)(2,1)S(1)}, bf16[1024,64]{0,1:T(8,128)(2,1)}, u32[]{:S(2)}) copy-start(bf16[1024,64]{0,1:T(8,128)(2,1)} %param.15) | copy-start | bytes 393220
  24.4 41.8 %copy-start.5 = (bf16[2048]{0:T(1024)(128)(2,1)}, bf16[2048]{0:T(1024)(128)(2,1)S(1)}, u32[]{:S(2)}) copy-start(bf16[2048]{0:T(1024)(128)(2,1)S(1)} %collective-permute-done.1.refs_3_) | copy-start | bytes 12292
  25.4 8.2 %collective-permute-start.2 = (f32[66,512]{1,0:T(8,128)S(1)}, f32[66,512]{1,0:T(8,128)S(1)}, u32[]{:S(2)}, u32[]{:S(2)}) collective-permute-start(f32[66,512]{1,0:T(8,128)S(1)} %constant_dynamic-slice_fusion.1), channel_id=1, source_target_pairs={{0,8},{1,9},{2,10},{3,11},{4,12},{5,13},{6,14},{7,15},{8,0},{9,1},... | collective-permute-start | bytes 405512 | tf_op jit(solution)/shard_map/ppermute | solution.py:159
  35.3 9.6 %collective-permute-start.3 = (f32[66,512]{1,0:T(8,128)S(1)}, f32[66,512]{1,0:T(8,128)S(1)}, u32[]{:S(2)}, u32[]{:S(2)}) collective-permute-start(f32[66,512]{1,0:T(8,128)S(1)} %pad_maximum_fusion.4), channel_id=1, source_target_pairs={{0,1},{1,0},{2,3},{3,2},{4,5},{5,4},{6,7},{7,6},{8,9},{9,8},{10,11... | collective-permute-start | bytes 405512 | tf_op jit(solution)/shard_map/ppermute | solution.py:163
  45.0 8.0 %collective-permute-start.4 = (f32[66,512]{1,0:T(8,128)S(1)}, f32[66,512]{1,0:T(8,128)S(1)}, u32[]{:S(2)}, u32[]{:S(2)}) collective-permute-start(f32[66,512]{1,0:T(8,128)S(1)} %pad_maximum_fusion.5), channel_id=1, source_target_pairs={{0,2},{1,3},{2,0},{3,1},{4,6},{5,7},{6,4},{7,5},{8,10},{9,11},{10,... | collective-permute-start | bytes 405512 | tf_op jit(solution)/shard_map/ppermute | solution.py:163
  53.1 9.1 %collective-permute-start.5 = (f32[66,512]{1,0:T(8,128)S(1)}, f32[66,512]{1,0:T(8,128)S(1)}, u32[]{:S(2)}, u32[]{:S(2)}) collective-permute-start(f32[66,512]{1,0:T(8,128)S(1)} %pad_maximum_fusion.6), channel_id=1, source_target_pairs={{0,6},{1,7},{2,4},{3,5},{4,2},{5,3},{6,0},{7,1},{8,14},{9,15},{10,... | collective-permute-start | bytes 405512 | tf_op jit(solution)/shard_map/ppermute | solution.py:163
  57.9 8.3 %collective-permute-start.9 = (bf16[1024,128]{1,0:T(8,128)(2,1)S(1)}, bf16[1024,128]{1,0:T(8,128)(2,1)S(1)}, u32[]{:S(2)}, u32[]{:S(2)}) collective-permute-start(bf16[1024,128]{1,0:T(8,128)(2,1)S(1)} %collective-permute-done), channel_id=1, source_target_pairs={{16,0},{17,1},{18,2},{19,3},{20,4},{21,5},{22,6},{23,7},{24,8},{25... | collective-permute-start | bytes 786440 | tf_op jit(solution)/shard_map/ppermute | solution.py:280
  62.4 6.2 %collective-permute-start.6 = (bf16[64,512]{1,0:T(8,128)(2,1)S(1)}, bf16[64,512]{1,0:T(8,128)(2,1)S(1)}, u32[]{:S(2)}, u32[]{:S(2)}) collective-permute-start(bf16[64,512]{1,0:T(8,128)(2,1)S(1)} %fusion.13), channel_id=1, source_target_pairs={{0,8},{1,9},{2,10},{3,11},{4,12},{5,13},{6,14},{7,15},{8,0},{9,1},... | collective-permute-start | bytes 196616 | tf_op jit(solution)/shard_map/ppermute | solution.py:170
  68.6 25.8 %copy-start.2 = (bf16[64,1024]{1,0:T(8,128)(2,1)}, bf16[64,1024]{1,0:T(8,128)(2,1)S(1)}, u32[]{:S(2)}) copy-start(bf16[64,1024]{1,0:T(8,128)(2,1)S(1)} %maximum_select_fusion) | copy-start | bytes 393220
  68.6 23.5 %collective-permute-start.8 = (bf16[64,1024]{1,0:T(8,128)(2,1)S(1)}, bf16[64,1024]{1,0:T(8,128)(2,1)S(1)}, u32[]{:S(2)}, u32[]{:S(2)}) collective-permute-start(bf16[64,1024]{1,0:T(8,128)(2,1)S(1)} %maximum_select_fusion), channel_id=1, source_target_pairs={{392,0},{425,1},{458,2},{491,3},{268,4},{333,5},{6,6},{71,7},{128,... | collective-permute-start | bytes 393224 | tf_op jit(solution)/shard_map/ppermute | solution.py:219
  77.6 14.5 %collective-permute-start.7 = (bf16[64,1024]{1,0:T(8,128)(2,1)S(1)}, bf16[64,1024]{1,0:T(8,128)(2,1)S(1)}, u32[]{:S(2)}, u32[]{:S(2)}) collective-permute-start(bf16[64,1024]{1,0:T(8,128)(2,1)S(1)} %maximum_select_fusion), channel_id=1, source_target_pairs={{408,0},{441,1},{474,2},{507,3},{284,4},{349,5},{22,6},{87,7},{144... | collective-permute-start | bytes 393224 | tf_op jit(solution)/shard_map/ppermute | solution.py:219
  92.1 2.3 %copy-start = (bf16[2048,512]{1,0:T(8,128)(2,1)S(1)}, bf16[2048,512]{1,0:T(8,128)(2,1)}, u32[]{:S(2)}) copy-start(bf16[2048,512]{1,0:T(8,128)(2,1)} %get-tuple-element.12) | copy-start | bytes 6291460
  92.1 2.7 %copy-start.6 = (f32[2,512]{1,0:T(2,128)S(1)}, f32[2,512]{1,0:T(2,128)}, u32[]{:S(2)}) copy-start(f32[2,512]{1,0:T(2,128)} %get-tuple-element.15) | copy-start | bytes 12292
  92.1 2.7 %copy-start.7 = (f32[2,512]{1,0:T(2,128)S(1)}, f32[2,512]{1,0:T(2,128)}, u32[]{:S(2)}) copy-start(f32[2,512]{1,0:T(2,128)} %get-tuple-element.14) | copy-start | bytes 12292
  94.8 36.4 %copy-start.4 = (bf16[1024,64]{0,1:T(8,128)(2,1)S(1)}, bf16[1024,64]{0,1:T(8,128)(2,1)}, u32[]{:S(2)}) copy-start(bf16[1024,64]{0,1:T(8,128)(2,1)} %param.18) | copy-start | bytes 393220
  94.9 7.8 %collective-permute-start.10 = (f32[66,512]{1,0:T(8,128)S(1)}, f32[66,512]{1,0:T(8,128)S(1)}, u32[]{:S(2)}, u32[]{:S(2)}) collective-permute-start(f32[66,512]{1,0:T(8,128)S(1)} %constant_dynamic-slice_fusion), channel_id=1, source_target_pairs={{0,8},{1,9},{2,10},{3,11},{4,12},{5,13},{6,14},{7,15},{8,0},{9,1},... | collective-permute-start | bytes 405512 | tf_op jit(solution)/shard_map/ppermute | solution.py:159
  102.9 7.0 %collective-permute-start.11 = (f32[66,512]{1,0:T(8,128)S(1)}, f32[66,512]{1,0:T(8,128)S(1)}, u32[]{:S(2)}, u32[]{:S(2)}) collective-permute-start(f32[66,512]{1,0:T(8,128)S(1)} %pad_maximum_fusion.7), channel_id=1, source_target_pairs={{0,1},{1,0},{2,3},{3,2},{4,5},{5,4},{6,7},{7,6},{8,9},{9,8},{10,11... | collective-permute-start | bytes 405512 | tf_op jit(solution)/shard_map/ppermute | solution.py:163
  110.0 8.0 %collective-permute-start.12 = (f32[66,512]{1,0:T(8,128)S(1)}, f32[66,512]{1,0:T(8,128)S(1)}, u32[]{:S(2)}, u32[]{:S(2)}) collective-permute-start(f32[66,512]{1,0:T(8,128)S(1)} %pad_maximum_fusion.8), channel_id=1, source_target_pairs={{0,2},{1,3},{2,0},{3,1},{4,6},{5,7},{6,4},{7,5},{8,10},{9,11},{10,... | collective-permute-start | bytes 405512 | tf_op jit(solution)/shard_map/ppermute | solution.py:163
  118.1 13.0 %collective-permute-start.13 = (f32[66,512]{1,0:T(8,128)S(1)}, f32[66,512]{1,0:T(8,128)S(1)}, u32[]{:S(2)}, u32[]{:S(2)}) collective-permute-start(f32[66,512]{1,0:T(8,128)S(1)} %pad_maximum_fusion.9), channel_id=1, source_target_pairs={{0,6},{1,7},{2,4},{3,5},{4,2},{5,3},{6,0},{7,1},{8,14},{9,15},{10,... | collective-permute-start | bytes 405512 | tf_op jit(solution)/shard_map/ppermute | solution.py:163
  131.3 6.2 %collective-permute-start.14 = (bf16[64,512]{1,0:T(8,128)(2,1)S(1)}, bf16[64,512]{1,0:T(8,128)(2,1)S(1)}, u32[]{:S(2)}, u32[]{:S(2)}) collective-permute-start(bf16[64,512]{1,0:T(8,128)(2,1)S(1)} %fusion.11), channel_id=1, source_target_pairs={{0,8},{1,9},{2,10},{3,11},{4,12},{5,13},{6,14},{7,15},{8,0},{9,1},... | collective-permute-start | bytes 196616 | tf_op jit(solution)/shard_map/ppermute | solution.py:170
